TPU v7x, 256 devices: a whole 4x4x8 slice. The times are simulated.
256 devices in a mesh: sec: 2 (over x_hi), gy: 16 (over y, x_lo, core), gz: 8 (over z).
Axes of the slice: x: 4 (x_hi: 2, x_lo: 2; x = x_hi * 2 + x_lo), y: 4, z: 8, core: 2. Of those that a mesh axis runs over, the one named last changes fastest.
Arguments:
- populations: float32 [56, 4, 128, 1024], P('sec', None, 'gy', 'gz'), may hold values from 0 to 1, as said below
- solid_mask: int32 [4, 128, 1024], P(None, 'gy', 'gz'), may hold values 0 or 1
- flow_rates: float32 [15], replicated, may hold values from 0.5 to 1.8
- species_rates: float32 [4], replicated, may hold values from 0.5 to 1.8
- cotangents: float32 [56, 4, 128, 1024], P('sec', None, 'gy', 'gz'), may hold values from -6 to 6
Outputs:
- next_pop: float32 [56, 4, 128, 1024], P('sec', None, 'gy', 'gz')
- pop_grad: float32 [56, 4, 128, 1024], P('sec', None, 'gy', 'gz')
- rate_grad: float32 [19], replicated
Inputs may be any that keep to these rules, and one draw needn't show every extreme that they name: `populations`: entries are positive.
All inputs are finite; a program needn't handle non-finite values. No bound on the sum of `solid_mask` on one device may be relied on, other than what follows from the above.
Results may differ from a plain program's by a relative error of at most 0.0003.
Values sent between devices are 32-bit elements; how exact they have to be, the bound alone decides.
No kernel may reach another device: no remote copies, remote signals or barrier semaphores. Data moves between devices by JAX's collectives and lax.ppermute only.
A program may use at most 64 MiB of HBM per device.

v0:
```python
from functools import partial

import jax
import jax.numpy as jnp
import numpy as np
from jax import lax
from jax.sharding import PartitionSpec as P


def extended(block, sides, width):
    for axis, dim in sides:
        count = lax.axis_size(axis)
        forward = [(i, i + 1) for i in range(count - 1)]
        forward.append((count - 1, 0))
        backward = [(target, source) for source, target in forward]
        low = lax.ppermute(
            lax.slice_in_dim(block, block.shape[dim] - width, None, axis=dim), axis, forward
        )
        high = lax.ppermute(lax.slice_in_dim(block, 0, width, axis=dim), axis, backward)
        block = jnp.concatenate([low, block, high], axis=dim)
    return block


def spread(shard, axis, root):
    mine = lax.axis_index(axis) == root
    return lax.psum(jnp.where(mine, shard, jnp.zeros_like(shard)), axis)


def orthonormal_columns(basis):
    result = []
    for column in range(basis.shape[1]):
        vector = basis[:, column] * 1.0
        for repeat in range(2):
            for earlier in result:
                vector = vector - np.sum(earlier * vector) * earlier
        vector = vector / np.sqrt(np.sum(vector * vector))
        result.append(vector)
    return np.stack(result, 1)


def lattice_tables():
    axis_moves = [(1, 0, 0), (-1, 0, 0), (0, 1, 0), (0, -1, 0), (0, 0, 1), (0, 0, -1)]
    edge_moves = []
    for first, second in ((0, 1), (0, 2), (1, 2)):
        for sign_first in (1, -1):
            for sign_second in (1, -1):
                move = [0, 0, 0]
                move[first] = sign_first
                move[second] = sign_second
                edge_moves.append(tuple(move))
    velocity = np.array([(0, 0, 0)] + axis_moves + edge_moves) * 1.0
    weights = np.array([1.0 / 3.0] + [1.0 / 18.0] * 6 + [1.0 / 36.0] * 12)
    opposite = np.array(
        [int(np.argmin(np.abs(velocity + velocity[channel]).sum(1))) for channel in range(19)]
    )
    along_x = velocity[:, 0]
    along_y = velocity[:, 1]
    along_z = velocity[:, 2]
    basis = np.stack(
        [
            np.ones(19),
            along_x,
            along_y,
            along_z,
            along_x**2,
            along_y**2,
            along_z**2,
            along_x * along_y,
            along_y * along_z,
            along_x * along_z,
            along_x * along_y**2,
            along_x * along_z**2,
            along_y * along_x**2,
            along_y * along_z**2,
            along_z * along_x**2,
            along_z * along_y**2,
            along_x**2 * along_y**2,
            along_x**2 * along_z**2,
            along_y**2 * along_z**2,
        ],
        1,
    )
    ortho = orthonormal_columns(basis)
    return (velocity, weights, opposite, ortho)


def expand(table, trailing):
    return jnp.asarray(table, jnp.float32).reshape(table.shape + (1,) * trailing)


def same_move(first_move, second_move):
    return tuple((int(value) for value in first_move)) == tuple(
        (int(value) for value in second_move)
    )


def flow_branch(is_fluid, rows, motion, flow_rates, species_rates):
    velocity, weights, opposite, ortho = lattice_tables()
    highest = lax.Precision.HIGHEST
    flow = rows[:19]
    trailing = flow.ndim - 1
    rates = jnp.concatenate([jnp.zeros((4,), flow_rates.dtype), flow_rates])
    ortho_table = jnp.asarray(ortho, jnp.float32)
    collision = jnp.dot(ortho_table * rates[None, :], ortho_table.T, precision=highest)
    velocity_table = jnp.asarray(velocity, jnp.float32)
    density = jnp.sum(flow, 0)
    projected = jnp.tensordot(velocity_table, motion, 1, precision=highest)
    squared = jnp.sum(motion * motion, 0)
    equilibrium = (
        expand(weights, trailing)
        * density
        * (1.0 + 3.0 * projected + 4.5 * projected * projected - 1.5 * squared)
    )
    relaxed = flow - jnp.tensordot(collision, flow - equilibrium, 1, precision=highest)
    flow_out = jnp.where(is_fluid, relaxed, flow[opposite])
    filler = jnp.zeros((rows.shape[0] - 19,) + rows.shape[1:], jnp.float32)
    return jnp.concatenate([flow_out, filler])


def species_branch(is_fluid, rows, motion, flow_rates, species_rates):
    velocity, weights, opposite, ortho = lattice_tables()
    highest = lax.Precision.HIGHEST
    trailing = rows.ndim - 1
    velocity_table = jnp.asarray(velocity[:7], jnp.float32)
    projected = jnp.tensordot(velocity_table, motion, 1, precision=highest)
    grouped = rows.reshape((rows.shape[0] // 7, 7) + rows.shape[1:])
    concentration = jnp.sum(grouped, 1)
    small_weights = np.array([0.25] + [0.125] * 6)
    species_eq = (
        expand(small_weights, trailing)[None]
        * concentration[:, None]
        * (1.0 + 4.0 * projected)[None]
    )
    rate_shape = species_rates.reshape((-1, 1) + (1,) * trailing)
    relaxed_species = grouped - rate_shape * (grouped - species_eq)
    return jnp.where(is_fluid, relaxed_species, grouped[:, opposite[:7]]).reshape(rows.shape)


def take_piece(padded, channel, move, size_y, size_z):
    step_x, step_y, step_z = (int(value) for value in move)
    piece = padded[channel, :, 1 - step_y : 1 - step_y + size_y, 1 - step_z : 1 - step_z + size_z]
    return jnp.roll(piece, step_x, 0)


def stream(field, table_flow, table_species, is_flow):
    padded = extended(field, (("gy", 2), ("gz", 3)), 1)
    size_y, size_z = (field.shape[2], field.shape[3])
    pieces = []
    for channel in range(field.shape[0]):
        first = take_piece(padded, channel, table_flow[channel], size_y, size_z)
        if same_move(table_flow[channel], table_species[channel]):
            pieces.append(first)
        else:
            second = take_piece(padded, channel, table_species[channel], size_y, size_z)
            pieces.append(jnp.where(is_flow, first, second))
    return jnp.stack(pieces)


def per_device(populations, solid_mask, flow_rates, species_rates, cotangents):
    velocity, weights, opposite, ortho = lattice_tables()
    highest = lax.Precision.HIGHEST
    rows_count = populations.shape[0]
    is_flow = lax.axis_index("sec") == 0
    is_fluid = solid_mask == 0
    velocity_table = jnp.asarray(velocity, jnp.float32)
    density = jnp.sum(populations[:19], 0)
    own_motion = jnp.tensordot(velocity_table.T, populations[:19], 1, precision=highest) / density
    motion = spread(own_motion, "sec", 0)

    def forward(rows, shared, rates_a, rates_b):
        return lax.cond(
            is_flow,
            partial(flow_branch, is_fluid),
            partial(species_branch, is_fluid),
            rows,
            shared,
            rates_a,
            rates_b,
        )

    post, pullback = jax.vjp(forward, populations, motion, flow_rates, species_rates)
    table_flow = np.concatenate([velocity, np.zeros((rows_count - 19, 3))])
    table_species = np.tile(velocity[:7], (rows_count // 7, 1))
    returned = stream(cotangents, -table_flow, -table_species, is_flow)
    moved = stream(post, table_flow, table_species, is_flow)
    grad_rows, grad_motion, local_flow_rates, local_species_rates = pullback(returned)
    from_species = spread(grad_motion, "sec", 1)
    total_motion = grad_motion + from_species
    along = jnp.tensordot(velocity_table, total_motion, 1, precision=highest)
    extra = (along - jnp.sum(own_motion * total_motion, 0)[None]) / density[None]
    filler = jnp.zeros((rows_count - 19,) + populations.shape[1:], jnp.float32)
    grad_rows = grad_rows + jnp.where(is_flow, jnp.concatenate([extra, filler]), 0.0)
    summed_flow_rates, summed_species_rates = lax.psum(
        (local_flow_rates, local_species_rates), ("sec", "gy", "gz")
    )
    rate_grad = jnp.concatenate([summed_flow_rates, summed_species_rates])
    return (moved, grad_rows, rate_grad)


def solution(mesh):
    placed = (P("sec", None, "gy", "gz"), P(None, "gy", "gz"), P(), P(), P("sec", None, "gy", "gz"))
    return jax.shard_map(
        per_device,
        mesh=mesh,
        in_specs=placed,
        out_specs=(P("sec", None, "gy", "gz"), P("sec", None, "gy", "gz"), P()),
        check_vma=False,
    )
```

profile of v0, /device:TPU:1, one launch (start us, length us, event | category | flops | bytes accessed | tf_op | source)
XLA Modules:
  0.0 205.7 jit_solution(12356524541416200816)
XLA Ops:
  3.5 10.7 %psum.28 = f32[3,4,8,128]{3,0,2,1:T(4,128)S(1)} all-reduce(f32[3,4,8,128]{3,0,2,1:T(4,128)S(1)} %get-tuple-element.572), channel_id=1, replica_groups=mesh['sec'=2,'gy'=16,'gz'=8] {'sec'}, use_global_device_ids=true, to_apply=%region_1.2 | all-reduce | flops 12288 | bytes 98304 | tf_op jit(solution)/shard_map/psum | solution.py:26
  14.9 8.5 %conditional.2 = (f32[28,4,8,128]{3,0,2,1:T(8,128)S(1)}, f32[7,3]{1,0:T(8,128)S(1)}, f32[1,7,1,1,1]{4,3,2,1,0:T(1,128)S(1)}, f32[1,7,4,8,128]{4,3,2,1,0:T(8,128)...) conditional(s32[]{:T(128)} %convert_element_type.3, ...), branch_computations={%region_2.4_spmd.clone, %region_4.7_spmd.clone} | conditional | flops 21583616 | bytes 10085426 | solution.py:171
  16.0 1.6 multiply_subtract_fusion.1
  28.3 2.9 %collective-permute-start = (f32[28,4,1,128]{3,2,1,0:T(1,128)}, f32[28,4,1,128]{3,2,1,0:T(1,128)S(1)}, u32[]{:S(2)}, u32[]{:S(2)}) collective-permute-start(f32[28,4,1,128]{3,2,1,0:T(1,128)} %copy.353), channel_id=1, source_target_pairs={{0,8},{8,16},{16,24},{24,32},{32,40},{40,48},{48,56},{56,64},{64,7... | collective-permute-start | bytes 172040 | tf_op jit(solution)/shard_map/ppermute | solution.py:16
  32.6 3.8 %collective-permute-start.4 = (f32[28,4,1,128]{3,2,1,0:T(1,128)}, f32[28,4,1,128]{3,2,1,0:T(1,128)S(1)}, u32[]{:S(2)}, u32[]{:S(2)}) collective-permute-start(f32[28,4,1,128]{3,2,1,0:T(1,128)} %get-tuple-element.553), channel_id=1, source_target_pairs={{8,0},{16,8},{24,16},{32,24},{40,32},{48,40},{56,48},{64,56},{72,6... | collective-permute-start | bytes 172040 | tf_op jit(solution)/shard_map/ppermute | solution.py:19
  42.6 2.8 %dynamic-update-slice.59 = f32[28,4,9,128]{3,2,1,0:T(8,128)} dynamic-update-slice(f32[28,4,9,128]{3,2,1,0:T(8,128)} %get-tuple-element.508, f32[28,4,1,128]{3,2,1,0:T(1,128)S(1)} %collective-permute-done.1, s32[]{} %constant.121, s32[]{} %constant.121, s32[]{} %constant.129, s32[]{} %constant.121) | dynamic-update-slice | bytes 114692 | tf_op jit(solution)/shard_map/concatenate | solution.py:20
  45.4 1.4 fusion.65
  47.4 1.4 constant_dynamic-update-slice_fusion.24
  49.3 1.3 fusion.66
  50.6 2.8 %dynamic-update-slice.29 = f32[28,4,9,128]{3,2,1,0:T(8,128)} dynamic-update-slice(f32[28,4,9,128]{3,2,1,0:T(8,128)} %constant_dynamic-update-slice_fusion.29, f32[28,4,1,128]{3,2,1,0:T(1,128)S(1)} %collective-permute-done.4, s32[]{} %constant.121, s32[]{} %constant.121, s32[]{} %constant.129, s32[]{} %constant.121) | dynamic-update-slice | bytes 114692 | tf_op jit(solution)/shard_map/concatenate | solution.py:20
  53.4 1.4 fusion.63
  55.5 1.3 fusion.62
  56.8 1.3 copy.358
  58.0 1.5 collective-permute-start.2
  59.5 1.3 copy.360
  60.8 3.9 %collective-permute-start.3 = (f32[28,4,10,1]{0,2,3,1:T(8,128)}, f32[28,4,10,1]{0,2,3,1:T(8,128)}, u32[]{:S(2)}, u32[]{:S(2)}) collective-permute-start(f32[28,4,10,1]{0,2,3,1:T(8,128)} %copy.360), channel_id=1, source_target_pairs={{1,0},{2,1},{3,2},{4,3},{5,4},{6,5},{7,6},{0,7},{9,8},{10,9},{11,1... | collective-permute-start | bytes 13448 | tf_op jit(solution)/shard_map/ppermute | solution.py:19
  65.2 1.3 copy.385
  66.5 1.5 collective-permute-start.6
  68.0 1.3 copy.387
  69.2 1.7 copy.359
  70.9 1.7 copy.361
  77.3 1.4 constant_dynamic-update-slice_fusion.17
  83.0 1.4 constant_dynamic-update-slice_fusion.10
  88.4 1.4 constant_dynamic-update-slice_fusion.3
  89.8 2.5 %copy.386 = f32[28,4,10,1]{3,2,1,0:T(8,128)} copy(f32[28,4,10,1]{0,2,3,1:T(8,128)} %collective-permute-done.6) | data formatting | bytes 8960 | tf_op jit(solution)/shard_map/ppermute | solution.py:19
  92.3 2.5 %copy.388 = f32[28,4,10,1]{3,2,1,0:T(8,128)} copy(f32[28,4,10,1]{0,2,3,1:T(8,128)} %collective-permute-done.7) | data formatting | bytes 8960 | tf_op jit(solution)/shard_map/ppermute | solution.py:16
  103.5 9.2 %conditional.3 = (f32[3,4,8,128]{3,0,2,1:T(4,128)S(1)}, f32[15]{0:T(128)S(1)}, f32[4]{0:T(128)S(1)}, f32[28,4,8,128]{3,0,2,1:T(8,128)}) conditional(s32[]{:T(128)} %convert_element_type.3, (f32[28,4,8,128]{3,2,1,0:T(8,128)S(1)}, pred[4,7,4,8,128]{4,3,2,1,0:T(8,128)(4,1)}, f32[4,1,1,1,1]{4,3,2,1,0:T(1,128)S(1)}, f32[1,7,1,1,1]{4,3,2,1,0:T(1,128)}, ...), branch_computations={%region_7.12_spmd, %region_12.17_spmd} | conditional | flops 40199236 | bytes 13603772 | solution.py:171
  104.6 1.7 multiply_reduce_fusion.4
  106.4 1.5 fusion.15
  109.7 1.9 scatter_fusion.1
  113.3 8.1 %psum.29 = f32[3,4,8,128]{3,0,2,1:T(4,128)S(1)} all-reduce(f32[3,4,8,128]{3,0,2,1:T(4,128)S(1)} %broadcast_select_fusion.3), channel_id=1, replica_groups=mesh['sec'=2,'gy'=16,'gz'=8] {'sec'}, use_global_device_ids=true, to_apply=%region_17.18 | all-reduce | flops 12288 | bytes 98304 | tf_op jit(solution)/shard_map/psum | solution.py:26
  125.4 78.3 %all-reduce.4 = (f32[4]{0:T(128)S(1)}, f32[15]{0:T(128)S(1)}) all-reduce(f32[4]{0:T(128)S(1)} %get-tuple-element.174, f32[15]{0:T(128)S(1)} %copy-done.85), channel_id=1, replica_groups=mesh['sec'=2,'gy'=16,'gz'=8] {'sec','gy','gz'}, use_global_device_ids=true, to_apply=%region_20.21 | all-reduce | flops 19 | bytes 152 | tf_op jit(solution)/shard_map/psum | solution.py:193
  (280 shorter events, 57.0 us)
Async XLA Ops:
  1.4 1.0 copy-start.86
  2.4 1.2 copy-start.49
  2.4 11.9 %copy-start.3 = (f32[28,4,8,128]{3,2,1,0:T(8,128)S(1)}, f32[28,4,8,128]{3,2,1,0:T(8,128)}, u32[]{:S(2)}) copy-start(f32[28,4,8,128]{3,2,1,0:T(8,128)} %param.19) | copy-start | bytes 1376260
  14.9 4.4 %copy-start.8 = (pred[19,4,8,128]{3,0,2,1:T(8,128)(4,1)}, pred[19,4,8,128]{3,0,2,1:T(8,128)(4,1)S(1)}, u32[]{:S(2)}) copy-start(pred[19,4,8,128]{3,0,2,1:T(8,128)(4,1)S(1)} %broadcast_in_dim.48) | copy-start | bytes 233476 | tf_op jit(solution)/shard_map/jvp()/cond
  17.6 1.8 copy-start.4
  17.7 0.8 copy-start.80
  22.5 0.9 copy-start.9
  22.6 0.9 copy-start.17
  27.0 4.8 %copy-start.12 = (f32[3,4,8,128]{3,0,2,1:T(4,128)}, f32[3,4,8,128]{3,0,2,1:T(4,128)S(1)}, u32[]{:S(2)}) copy-start(f32[3,4,8,128]{3,0,2,1:T(4,128)S(1)} %get-tuple-element.164) | copy-start | bytes 147460
  27.0 10.5 %copy-start.6 = (f32[19,4,8,128]{3,0,2,1:T(8,128)}, f32[19,4,8,128]{3,0,2,1:T(8,128)S(1)}, u32[]{:S(2)}) copy-start(f32[19,4,8,128]{3,0,2,1:T(8,128)S(1)} %get-tuple-element.163) | copy-start | bytes 933892
  27.0 10.5 %copy-start.10 = (f32[4,7,4,8,128]{4,3,2,1,0:T(8,128)}, f32[4,7,4,8,128]{4,3,2,1,0:T(8,128)S(1)}, u32[]{:S(2)}) copy-start(f32[4,7,4,8,128]{4,3,2,1,0:T(8,128)S(1)} %get-tuple-element.157) | copy-start | bytes 1376260
  27.0 10.5 %copy-start.11 = (f32[4,7,4,8,128]{4,3,2,1,0:T(8,128)}, f32[4,7,4,8,128]{4,3,2,1,0:T(8,128)S(1)}, u32[]{:S(2)}) copy-start(f32[4,7,4,8,128]{4,3,2,1,0:T(8,128)S(1)} %get-tuple-element.155) | copy-start | bytes 1376260
  27.0 10.4 %copy-start.14 = (f32[19,4,8,128]{3,0,2,1:T(8,128)}, f32[19,4,8,128]{3,0,2,1:T(8,128)S(1)}, u32[]{:S(2)}) copy-start(f32[19,4,8,128]{3,0,2,1:T(8,128)S(1)} %get-tuple-element.166) | copy-start | bytes 933892
  27.0 4.8 %copy-start = (f32[28,4,8,128]{3,2,1,0:T(8,128)S(1)}, f32[28,4,8,128]{3,2,1,0:T(8,128)}, u32[]{:S(2)}) copy-start(f32[28,4,8,128]{3,2,1,0:T(8,128)} %param.23) | copy-start | bytes 1376260
  28.3 18.5 %collective-permute-start = (f32[28,4,1,128]{3,2,1,0:T(1,128)}, f32[28,4,1,128]{3,2,1,0:T(1,128)S(1)}, u32[]{:S(2)}, u32[]{:S(2)}) collective-permute-start(f32[28,4,1,128]{3,2,1,0:T(1,128)} %copy.353), channel_id=1, source_target_pairs={{0,8},{8,16},{16,24},{24,32},{32,40},{40,48},{48,56},{56,64},{64,7... | collective-permute-start | bytes 172040 | tf_op jit(solution)/shard_map/ppermute | solution.py:16
  31.8 10.8 %collective-permute-start.1 = (f32[28,4,1,128]{3,2,1,0:T(1,128)}, f32[28,4,1,128]{3,2,1,0:T(1,128)S(1)}, u32[]{:S(2)}, u32[]{:S(2)}) collective-permute-start(f32[28,4,1,128]{3,2,1,0:T(1,128)} %copy.355), channel_id=1, source_target_pairs={{8,0},{16,8},{24,16},{32,24},{40,32},{48,40},{56,48},{64,56},{72,6... | collective-permute-start | bytes 172040 | tf_op jit(solution)/shard_map/ppermute | solution.py:19
  32.6 18.0 %collective-permute-start.4 = (f32[28,4,1,128]{3,2,1,0:T(1,128)}, f32[28,4,1,128]{3,2,1,0:T(1,128)S(1)}, u32[]{:S(2)}, u32[]{:S(2)}) collective-permute-start(f32[28,4,1,128]{3,2,1,0:T(1,128)} %get-tuple-element.553), channel_id=1, source_target_pairs={{8,0},{16,8},{24,16},{32,24},{40,32},{48,40},{56,48},{64,56},{72,6... | collective-permute-start | bytes 172040 | tf_op jit(solution)/shard_map/ppermute | solution.py:19
  36.4 28.4 %collective-permute-start.5 = (f32[28,4,1,128]{3,2,1,0:T(1,128)}, f32[28,4,1,128]{3,2,1,0:T(1,128)S(1)}, u32[]{:S(2)}, u32[]{:S(2)}) collective-permute-start(f32[28,4,1,128]{3,2,1,0:T(1,128)} %get-tuple-element.552), channel_id=1, source_target_pairs={{0,8},{8,16},{16,24},{24,32},{32,40},{40,48},{48,56},{56,64},{64,7... | collective-permute-start | bytes 172040 | tf_op jit(solution)/shard_map/ppermute | solution.py:16
  58.0 11.2 %collective-permute-start.2 = (f32[28,4,10,1]{0,2,3,1:T(8,128)}, f32[28,4,10,1]{0,2,3,1:T(8,128)}, u32[]{:S(2)}, u32[]{:S(2)}) collective-permute-start(f32[28,4,10,1]{0,2,3,1:T(8,128)} %copy.358), channel_id=1, source_target_pairs={{0,1},{1,2},{2,3},{3,4},{4,5},{5,6},{6,7},{7,0},{8,9},{9,10},{10,1... | collective-permute-start | bytes 13448 | tf_op jit(solution)/shard_map/ppermute | solution.py:16
  60.8 10.1 %collective-permute-start.3 = (f32[28,4,10,1]{0,2,3,1:T(8,128)}, f32[28,4,10,1]{0,2,3,1:T(8,128)}, u32[]{:S(2)}, u32[]{:S(2)}) collective-permute-start(f32[28,4,10,1]{0,2,3,1:T(8,128)} %copy.360), channel_id=1, source_target_pairs={{1,0},{2,1},{3,2},{4,3},{5,4},{6,5},{7,6},{0,7},{9,8},{10,9},{11,1... | collective-permute-start | bytes 13448 | tf_op jit(solution)/shard_map/ppermute | solution.py:19
  66.5 23.3 %collective-permute-start.6 = (f32[28,4,10,1]{0,2,3,1:T(8,128)}, f32[28,4,10,1]{0,2,3,1:T(8,128)}, u32[]{:S(2)}, u32[]{:S(2)}) collective-permute-start(f32[28,4,10,1]{0,2,3,1:T(8,128)} %copy.385), channel_id=1, source_target_pairs={{1,0},{2,1},{3,2},{4,3},{5,4},{6,5},{7,6},{0,7},{9,8},{10,9},{11,1... | collective-permute-start | bytes 13448 | tf_op jit(solution)/shard_map/ppermute | solution.py:19
  69.2 23.1 %collective-permute-start.7 = (f32[28,4,10,1]{0,2,3,1:T(8,128)}, f32[28,4,10,1]{0,2,3,1:T(8,128)}, u32[]{:S(2)}, u32[]{:S(2)}) collective-permute-start(f32[28,4,10,1]{0,2,3,1:T(8,128)} %copy.387), channel_id=1, source_target_pairs={{0,1},{1,2},{2,3},{3,4},{4,5},{5,6},{6,7},{7,0},{8,9},{9,10},{10,1... | collective-permute-start | bytes 13448 | tf_op jit(solution)/shard_map/ppermute | solution.py:16
  85.1 2.0 copy-start.28
  94.8 1.2 copy-start.2
  96.0 0.7 copy-start.33
  96.1 1.4 copy-start.1
  100.4 0.8 copy-start.25
  103.6 1.0 copy-start.7
  104.6 1.7 copy-start.13
  104.6 1.8 copy-start.15
  106.4 1.6 copy-start.5
  113.2 8.1 %copy-start.20 = (f32[3,4,8,128]{3,0,2,1:T(4,128)S(1)}, f32[3,4,8,128]{3,0,2,1:T(4,128)}, u32[]{:S(2)}) copy-start(f32[3,4,8,128]{3,0,2,1:T(4,128)} %get-tuple-element.573) | copy-start | bytes 147460
  (55 other events, 37.6 us)
where the time goes:
time: 208 us; the launch traced here: 206 us
  blocking collectives  97.1 us (47%)
  local copies, waits for them, and re-layouts  56.7 us (27%)
  other arithmetic  29 us (14%)
  starting transfers between devices  13.6 us (7%)
  matrix products  7.89 us (4%)
    psum x1, blocking collectives, per_device(): lax.psum((local_flow_rates, local_species_rates), ('sec', 'gy', 'gz'))  78.3 us
    unnamed x48, other arithmetic  22.2 us
    psum x2, blocking collectives, spread(): return lax.psum(jnp.where(mine, shard, jnp.zeros_like(shard)), axis)  18.8 us
    unnamed x131, local copies, waits for them, and re-layouts  18.2 us
    ppermute x4, starting transfers between devices, extended(): lax.ppermute(lax.slice_in_dim(block, 0, width, axis=dim), axis, backward)  9.2 us
    slice x8, local copies, waits for them, and re-layouts, take_piece(): return jnp.roll(piece, step_x, 0)  7.86 us
    concatenate x2, local copies, waits for them, and re-layouts, extended(): block = jnp.concatenate([low, block, high], axis=dim)  5.54 us
    cond x40, local copies, waits for them, and re-layouts  5.1 us
  transfers between devices with their start and end apart: 8, of which 0 were waited for; matrix products, arithmetic and copies ran while one was open for 24% of the time, Pallas kernels for 0%

commit v1 on v0

v1 whole, which is shorter than its diff:
```python
import jax
import jax.numpy as jnp
import numpy as np
from jax import lax
from jax.sharding import PartitionSpec as P


def orthonormal_columns(basis):
    result = []
    for column in range(basis.shape[1]):
        vector = basis[:, column] * 1.0
        for repeat in range(2):
            for earlier in result:
                vector = vector - np.sum(earlier * vector) * earlier
        vector = vector / np.sqrt(np.sum(vector * vector))
        result.append(vector)
    return np.stack(result, 1)


def lattice_tables():
    axis_moves = [(1, 0, 0), (-1, 0, 0), (0, 1, 0), (0, -1, 0), (0, 0, 1), (0, 0, -1)]
    edge_moves = []
    for first, second in ((0, 1), (0, 2), (1, 2)):
        for sign_first in (1, -1):
            for sign_second in (1, -1):
                move = [0, 0, 0]
                move[first] = sign_first
                move[second] = sign_second
                edge_moves.append(tuple(move))
    velocity = np.array([(0, 0, 0)] + axis_moves + edge_moves) * 1.0
    weights = np.array([1.0 / 3.0] + [1.0 / 18.0] * 6 + [1.0 / 36.0] * 12)
    opposite = np.array(
        [int(np.argmin(np.abs(velocity + velocity[channel]).sum(1))) for channel in range(19)]
    )
    along_x = velocity[:, 0]
    along_y = velocity[:, 1]
    along_z = velocity[:, 2]
    basis = np.stack(
        [
            np.ones(19),
            along_x,
            along_y,
            along_z,
            along_x**2,
            along_y**2,
            along_z**2,
            along_x * along_y,
            along_y * along_z,
            along_x * along_z,
            along_x * along_y**2,
            along_x * along_z**2,
            along_y * along_x**2,
            along_y * along_z**2,
            along_z * along_x**2,
            along_z * along_y**2,
            along_x**2 * along_y**2,
            along_x**2 * along_z**2,
            along_y**2 * along_z**2,
        ],
        1,
    )
    ortho = orthonormal_columns(basis)
    return (velocity, weights, opposite, ortho)


def column(values):
    return jnp.asarray(np.asarray(values, np.float32).reshape(-1, 1, 1, 1))


def ring(axis, step):
    count = lax.axis_size(axis)
    return [(i, (i + step) % count) for i in range(count)]


def shift_rows(field, moves):
    move_x, move_y, move_z = moves
    size_y, size_z = field.shape[2], field.shape[3]
    low = lax.ppermute(field[:, :, size_y - 1 :, :], "gy", ring("gy", 1))
    high = lax.ppermute(field[:, :, :1, :], "gy", ring("gy", -1))
    from_low = jnp.concatenate([low, field[:, :, : size_y - 1, :]], axis=2)
    from_high = jnp.concatenate([field[:, :, 1:, :], high], axis=2)
    field = jnp.where(move_y > 0, from_low, jnp.where(move_y < 0, from_high, field))
    low = lax.ppermute(field[:, :, :, size_z - 1 :], "gz", ring("gz", 1))
    high = lax.ppermute(field[:, :, :, :1], "gz", ring("gz", -1))
    from_low = jnp.concatenate([low, field[:, :, :, : size_z - 1]], axis=3)
    from_high = jnp.concatenate([field[:, :, :, 1:], high], axis=3)
    field = jnp.where(move_z > 0, from_low, jnp.where(move_z < 0, from_high, field))
    from_low = jnp.roll(field, 1, axis=1)
    from_high = jnp.roll(field, -1, axis=1)
    return jnp.where(move_x > 0, from_low, jnp.where(move_x < 0, from_high, field))


def butterfly_sum(values):
    for axis in ("gy", "gz", "sec"):
        count = lax.axis_size(axis)
        step = 1
        while step < count:
            values = values + lax.ppermute(
                values, axis, [(i, i ^ step) for i in range(count)]
            )
            step *= 2
    return values


def per_device(populations, solid_mask, flow_rates, species_rates, cotangents):
    velocity, weights, opposite, ortho = lattice_tables()
    highest = lax.Precision.HIGHEST
    rows = populations.shape[0]
    groups = rows // 7
    is_flow = lax.axis_index("sec") == 0
    fluid = (solid_mask == 0)[None]

    flow_moves = np.concatenate([velocity, np.zeros((rows - 19, 3))])
    species_moves = np.tile(velocity[:7], (groups, 1))
    moves = [
        jnp.where(is_flow, column(flow_moves[:, d]), column(species_moves[:, d])) for d in range(3)
    ]
    returned = shift_rows(cotangents, [-m for m in moves])

    flow = populations[:19]
    vx, vy, vz = (column(velocity[:, d]) for d in range(3))
    density = jnp.sum(flow, 0)
    own_motion = jnp.stack(
        [jnp.sum(flow * vx, 0), jnp.sum(flow * vy, 0), jnp.sum(flow * vz, 0)]
    ) / density[None]
    sent_motion = lax.ppermute(own_motion, "sec", [(0, 1)])
    motion = jnp.where(is_flow, own_motion, sent_motion)

    small_weights = column([0.25] + [0.125] * 6)
    grouped = populations.reshape((groups, 7) + populations.shape[1:])
    back_species = returned.reshape(grouped.shape)
    species_r = species_rates.reshape((groups, 1, 1, 1, 1))
    concentration = jnp.sum(grouped, 1)
    sx, sy, sz = (column(velocity[:7, d])[None] for d in range(3))
    weighted_back = back_species * small_weights[None]
    species_motion_grad = 4.0 * jnp.sum(
        species_r * concentration[:, None] * jnp.stack(
            [jnp.sum(weighted_back * sx, 1), jnp.sum(weighted_back * sy, 1), jnp.sum(weighted_back * sz, 1)], 1
        ),
        0,
    )
    species_motion_grad = jnp.where(fluid, species_motion_grad, 0.0)
    sent_grad = lax.ppermute(species_motion_grad, "sec", [(1, 0)])

    projected_small = motion[0][None] * sx[0] + motion[1][None] * sy[0] + motion[2][None] * sz[0]
    factor = small_weights * (1.0 + 4.0 * projected_small)
    species_eq = factor[None] * concentration[:, None]
    species_gap = grouped - species_eq
    species_relaxed = grouped - species_r * species_gap
    species_bounce = grouped[:, opposite[:7]]
    species_post = jnp.where(fluid[None], species_relaxed, species_bounce).reshape(populations.shape)
    species_t = jnp.sum(back_species * factor[None], 1)
    species_grad_fluid = (1.0 - species_r) * back_species + species_r * species_t[:, None]
    species_grad = jnp.where(
        fluid[None], species_grad_fluid, back_species[:, opposite[:7]]
    ).reshape(populations.shape)
    species_rate_grad = -jnp.sum(
        jnp.where(fluid[None], back_species * species_gap, 0.0), axis=(1, 2, 3, 4)
    )

    q_table = jnp.asarray(ortho, jnp.float32)
    relax = jnp.concatenate([jnp.zeros((4,), flow_rates.dtype), flow_rates]).reshape(19, 1, 1, 1)
    w = column(weights)
    projected = vx * motion[0][None] + vy * motion[1][None] + vz * motion[2][None]
    squared = jnp.sum(motion * motion, 0)
    poly = w * (1.0 + 3.0 * projected + 4.5 * projected * projected - 1.5 * squared[None])
    equilibrium = density[None] * poly
    moments = jnp.einsum("ji,jxyz->ixyz", q_table, flow - equilibrium, precision=highest)
    flow_relaxed = flow - jnp.einsum("ij,jxyz->ixyz", q_table, relax * moments, precision=highest)
    flow_post = jnp.where(fluid, flow_relaxed, flow[opposite])

    back_flow = returned[:19]
    back_moments = jnp.einsum("ji,jxyz->ixyz", q_table, back_flow, precision=highest)
    through_eq = jnp.einsum("ij,jxyz->ixyz", q_table, relax * back_moments, precision=highest)
    flow_rate_grad = -jnp.sum(
        jnp.where(fluid, back_moments * moments, 0.0)[4:], axis=(1, 2, 3)
    )
    density_grad = jnp.sum(through_eq * poly, 0)
    hw = through_eq * w
    hw_sum = jnp.sum(hw, 0)
    hwp = hw * (3.0 + 9.0 * projected)
    motion_grad = density[None] * (
        jnp.stack([jnp.sum(hwp * vx, 0), jnp.sum(hwp * vy, 0), jnp.sum(hwp * vz, 0)])
        - 3.0 * motion * hw_sum[None]
    )
    motion_grad = jnp.where(fluid, motion_grad + sent_grad, 0.0)
    along = vx * motion_grad[0][None] + vy * motion_grad[1][None] + vz * motion_grad[2][None]
    extra = (along - jnp.sum(motion * motion_grad, 0)[None]) / density[None]
    flow_grad = jnp.where(
        fluid, back_flow - through_eq + density_grad[None] + extra, back_flow[opposite]
    )

    filler = jnp.zeros((rows - 19,) + populations.shape[1:], jnp.float32)
    post = jnp.where(is_flow, jnp.concatenate([flow_post, filler]), species_post)
    grad_rows = jnp.where(is_flow, jnp.concatenate([flow_grad, filler]), species_grad)
    local_rates = jnp.where(
        is_flow,
        jnp.concatenate([flow_rate_grad, jnp.zeros((groups,), jnp.float32)]),
        jnp.concatenate([jnp.zeros((15,), jnp.float32), species_rate_grad]),
    )
    rate_grad = butterfly_sum(local_rates)
    moved = shift_rows(post, moves)
    moved = jnp.where(is_flow, jnp.concatenate([moved[:19], filler]), moved)
    return (moved, grad_rows, rate_grad)


def solution(mesh):
    placed = (P("sec", None, "gy", "gz"), P(None, "gy", "gz"), P(), P(), P("sec", None, "gy", "gz"))
    return jax.shard_map(
        per_device,
        mesh=mesh,
        in_specs=placed,
        out_specs=(P("sec", None, "gy", "gz"), P("sec", None, "gy", "gz"), P()),
        check_vma=False,
    )
```

time: 208 us -> 115 us (0.55)
  the two profiles are of different devices: /device:TPU:1 before, /device:TPU:32 now
where the time goes in v1:
time: 115 us; the launch traced here: 114 us
  starting transfers between devices  37.5 us (33%)
  waiting for transfers between devices  32.5 us (28%)
  local copies, waits for them, and re-layouts  27.5 us (24%)
  other arithmetic  11.5 us (10%)
  matrix products  3.3 us (3%)
  between operations  1.43 us (1%)
    ppermute x8, starting transfers between devices, butterfly_sum(): lax.ppermute(values, axis, [(i, i ^ step) for i in range(count)])  22.4 us
    ppermute x2, waiting for transfers between devices, shift_rows(): low = lax.ppermute(field[:, :, :, size_z - 1:], 'gz', ring('gz', 1))  17.1 us
    unnamed x121, local copies, waits for them, and re-layouts  16.2 us
    ppermute x8, waiting for transfers between devices, butterfly_sum(): lax.ppermute(values, axis, [(i, i ^ step) for i in range(count)])  11.6 us
    ppermute x1, starting transfers between devices, per_device(): sent_motion = lax.ppermute(own_motion, 'sec', [(0, 1)])  5.55 us
    ppermute x2, starting transfers between devices, shift_rows(): high = lax.ppermute(field[:, :, :1, :], 'gy', ring('gy', -1))  3.89 us
    ppermute x2, waiting for transfers between devices, shift_rows(): high = lax.ppermute(field[:, :, :, :1], 'gz', ring('gz', -1))  3.77 us
    ppermute x2, starting transfers between devices, shift_rows(): low = lax.ppermute(field[:, :, :, size_z - 1:], 'gz', ring('gz', 1))  3.53 us
  transfers between devices with their start and end apart: 18, of which 10 were waited for; matrix products, arithmetic and copies ran while one was open for 19% of the time, Pallas kernels for 0%

profile of v1, /device:TPU:32, one launch (start us, length us, event | category | flops | bytes accessed | tf_op | source)
XLA Modules:
  0.0 113.7 jit_solution(3515554771531535045)
XLA Ops:
  0.7 1.3 %copy.66 = f32[28,4,8,128]{3,0,2,1:T(8,128)S(1)} copy(f32[28,4,8,128]{3,2,1,0:T(8,128)} %param.27) | data formatting | bytes 917504 | tf_op args[0]
  2.4 5.5 %collective-permute-start = (f32[3,4,8,128]{3,2,1,0:T(8,128)S(1)}, f32[3,4,8,128]{3,2,1,0:T(8,128)}, u32[]{:S(2)}, u32[]{:S(2)}) collective-permute-start(f32[3,4,8,128]{3,2,1,0:T(8,128)S(1)} %maximum_divide_fusion), channel_id=1, source_target_pairs={{0,128},{1,129},{2,130},{3,131},{4,132},{5,133},{6,134},{7,135},{8... | collective-permute-start | bytes 147464 | tf_op jit(solution)/shard_map/ppermute | solution.py:126
  9.3 3.9 %collective-permute-start.6 = (f32[28,4,1,128]{3,0,2,1:T(8,128)}, f32[28,4,1,128]{3,0,2,1:T(8,128)}, u32[]{:S(2)}, u32[]{:S(2)}) collective-permute-start(f32[28,4,1,128]{3,0,2,1:T(8,128)} %copy.115), channel_id=1, source_target_pairs={{0,120},{8,0},{16,8},{24,16},{32,24},{40,32},{48,40},{56,48},{64,5... | collective-permute-start | bytes 172040 | tf_op jit(solution)/shard_map/ppermute | solution.py:79
  23.6 2.3 %gather_fusion = f32[19,4,8,128]{3,2,1,0:T(8,128)} fusion(f32[19,4,8,128]{3,2,1,0:T(8,128)} %copy.68, s32[1024]{0:T(1024)S(1)} %pad_clamp_fusion.1), kind=kCustom, calls=%fused_computation | custom fusion | bytes 622668 | tf_op jit(solution)/shard_map/gather | solution.py:170
  26.8 1.2 %maximum_select_fusion.6 = f32[28,4,8,128]{3,0,2,1:T(8,128)S(1)} fusion(f32[28,4,7,128]{3,0,2,1:T(8,128)S(1)} %copy.113, f32[28,4,1,128]{3,0,2,1:T(8,128)S(1)} %collective-permute-done.5, f32[28,4,1,128]{3,0,2,1:T(8,128)} %collective-permute-done.6, f32[28,4,7,128]{3,0,2,1:T(8,128)S(1)} %copy.116, pred[28]{0:T(512)(128)(4,1)S(1)} %get-tuple-element.74, ...), kind=kLoop, calls=%fused_computation.18 | loop fusion | flops 458752 | bytes 1835064 | tf_op jit(solution)/shard_map/jit(_where)/select_n | solution.py:82
  28.2 2.0 %collective-permute-start.7 = (f32[28,4,8,1]{3,0,2,1:T(8,128)S(1)}, f32[28,4,8,1]{3,0,2,1:T(8,128)S(1)}, u32[]{:S(2)}, u32[]{:S(2)}) collective-permute-start(f32[28,4,8,1]{3,0,2,1:T(8,128)S(1)} %get-tuple-element.47), channel_id=1, source_target_pairs={{0,1},{1,2},{2,3},{3,4},{4,5},{5,6},{6,7},{7,0},{8,9},{9,10},{10,1... | collective-permute-start | bytes 10760 | tf_op jit(solution)/shard_map/ppermute | solution.py:83
  30.5 8.4 %collective-permute-done.7 = f32[28,4,8,1]{3,0,2,1:T(8,128)S(1)} collective-permute-done((f32[28,4,8,1]{3,0,2,1:T(8,128)S(1)}, f32[28,4,8,1]{3,0,2,1:T(8,128)S(1)}, u32[]{:S(2)}, u32[]{:S(2)}) %collective-permute-start.7) | collective-permute-done | bytes 3616 | tf_op jit(solution)/shard_map/ppermute | solution.py:83
  39.0 1.8 %collective-permute-done.8 = f32[28,4,8,1]{3,0,2,1:T(8,128)S(1)} collective-permute-done((f32[28,4,8,1]{3,0,2,1:T(8,128)S(1)}, f32[28,4,8,1]{3,0,2,1:T(8,128)S(1)}, u32[]{:S(2)}, u32[]{:S(2)}) %collective-permute-start.8) | collective-permute-done | bytes 3616 | tf_op jit(solution)/shard_map/ppermute | solution.py:84
  41.9 1.4 %select_reduce_fusion = (f32[28]{0:T(128)}, f32[28,4,8,128]{3,0,2,1:T(8,128)S(1)}) fusion(pred[4,8,128]{2,1,0:T(8,128)(4,1)S(1)} %broadcast_compare_fusion, f32[28,4,8,128]{3,2,1,0:T(8,128)S(1)} %bitcast.74, f32[28,4,8,128]{3,2,1,0:T(8,128)S(1)} %copy-done, f32[28,4,8,128]{3,0,2,1:T(8,128)S(1)} %maximum_select_fusion.8, ...), kind=kLoop, calls=%fused_computation.30 | loop fusion | flops 917476 | bytes 2756776 | tf_op jit(solution)/shard_map/reduce_sum | solution.py:157
  44.5 1.4 %collective-permute-start.9 = (f32[3,4,8,128]{3,2,1,0:T(8,128)}, f32[3,4,8,128]{3,2,1,0:T(8,128)}, u32[]{:S(2)}, u32[]{:S(2)}) collective-permute-start(f32[3,4,8,128]{3,2,1,0:T(8,128)} %multiply_select_fusion), channel_id=1, source_target_pairs={{128,0},{129,1},{130,2},{131,3},{132,4},{133,5},{134,6},{135,7},{1... | collective-permute-start | bytes 147464 | tf_op jit(solution)/shard_map/ppermute | solution.py:143
  46.5 1.4 %add_multiply_fusion = (f32[19,4,8,128]{3,0,2,1:T(8,128)S(1)}, f32[4,8,128]{2,1,0:T(8,128)S(1)}, f32[19,4,8,128]{3,0,2,1:T(8,128)}) fusion(f32[4,8,128]{2,1,0:T(8,128)S(1)} %get-tuple-element.59, f32[4,8,128]{2,1,0:T(8,128)S(1)} %get-tuple-element.60, f32[4,8,128]{2,1,0:T(8,128)S(1)} %get-tuple-element.58, f32[19]{0:T(128)S(1)} %copy-done.37, ...), kind=kOutput, calls=%fused_computation.45 | convolution fusion | flops 18595840 | bytes 1001248 | tf_op jit(solution)/shard_map/ij,jxyz->ixyz/dot_general | solution.py:174
  50.6 1.1 copy.82
  51.6 1.4 %gather_fusion.2 = f32[19,4,8,128]{3,2,1,0:T(8,128)} fusion(f32[19,4,8,128]{3,2,1,0:T(8,128)S(1)} %copy.82, s32[1024]{0:T(1024)} %copy-done.15), kind=kCustom, calls=%fused_computation.2 | custom fusion | bytes 622668 | tf_op jit(solution)/shard_map/gather | solution.py:190
  53.1 0.8 multiply_reduce_fusion.11
  57.4 2.7 %collective-permute-start.11 = (f32[19]{0:T(128)S(1)}, f32[19]{0:T(128)S(1)}, u32[]{:S(2)}, u32[]{:S(2)}) collective-permute-start(f32[19]{0:T(128)S(1)} %add.139), channel_id=1, source_target_pairs={{0,16},{8,24},{16,0},{24,8},{32,48},{40,56},{48,32},{56,40},{64,80... | collective-permute-start | bytes 236 | tf_op jit(solution)/shard_map/ppermute | solution.py:98
  60.8 0.8 collective-permute-done.11
  61.6 1.6 %collective-permute-start.12 = (f32[19]{0:T(128)S(1)}, f32[19]{0:T(128)S(1)}, u32[]{:S(2)}, u32[]{:S(2)}) collective-permute-start(f32[19]{0:T(128)S(1)} %add.140), channel_id=1, source_target_pairs={{0,32},{8,40},{16,48},{24,56},{32,0},{40,8},{48,16},{56,24},{64,96... | collective-permute-start | bytes 236 | tf_op jit(solution)/shard_map/ppermute | solution.py:98
  63.9 2.1 %fusion.5 = (f32[28,4,8,128]{3,0,2,1:T(8,128)S(1)}, f32[28,4,8,128]{3,0,2,1:T(8,128)S(1)}) fusion(f32[28,4,8,128]{3,2,1,0:T(8,128)S(1)} %bitcast.79, f32[28,4,8,128]{3,2,1,0:T(8,128)S(1)} %bitcast.80, f32[28,4,8,128]{3,0,2,1:T(8,128)S(1)} %get-tuple-element.26, f32[19,4,8,128]{3,0,2,1:T(8,128)S(1)} %fusion.4, f32[28]{0:T(128)S(1)} %copy-done.17, ...), kind=kLoop, calls=%fused_computation.25 | loop fusion | flops 1032192 | bytes 4296929 | tf_op jit(solution)/shard_map/jit(_where)/select_n | solution.py:195
  66.1 2.6 %collective-permute-start.13 = (f32[19]{0:T(128)S(1)}, f32[19]{0:T(128)S(1)}, u32[]{:S(2)}, u32[]{:S(2)}) collective-permute-start(f32[19]{0:T(128)S(1)} %add.141), channel_id=1, source_target_pairs={{0,64},{8,72},{16,80},{24,88},{32,96},{40,104},{48,112},{56,120},{... | collective-permute-start | bytes 236 | tf_op jit(solution)/shard_map/ppermute | solution.py:98
  68.6 2.6 %collective-permute-done.13 = f32[19]{0:T(128)S(1)} collective-permute-done((f32[19]{0:T(128)S(1)}, f32[19]{0:T(128)S(1)}, u32[]{:S(2)}, u32[]{:S(2)}) %collective-permute-start.13) | collective-permute-done | bytes 108 | tf_op jit(solution)/shard_map/ppermute | solution.py:98
  71.2 2.2 %collective-permute-start.14 = (f32[19]{0:T(128)S(1)}, f32[19]{0:T(128)S(1)}, u32[]{:S(2)}, u32[]{:S(2)}) collective-permute-start(f32[19]{0:T(128)S(1)} %add.142), channel_id=1, source_target_pairs={{0,1},{1,0},{2,3},{3,2},{4,5},{5,4},{6,7},{7,6},{8,9},{9,8},{10,11... | collective-permute-start | bytes 236 | tf_op jit(solution)/shard_map/ppermute | solution.py:98
  73.4 1.5 %collective-permute-done.14 = f32[19]{0:T(128)S(1)} collective-permute-done((f32[19]{0:T(128)S(1)}, f32[19]{0:T(128)S(1)}, u32[]{:S(2)}, u32[]{:S(2)}) %collective-permute-start.14) | collective-permute-done | bytes 108 | tf_op jit(solution)/shard_map/ppermute | solution.py:98
  74.9 5.4 %collective-permute-start.15 = (f32[19]{0:T(128)S(1)}, f32[19]{0:T(128)S(1)}, u32[]{:S(2)}, u32[]{:S(2)}) collective-permute-start(f32[19]{0:T(128)S(1)} %add.143), channel_id=1, source_target_pairs={{0,2},{1,3},{2,0},{3,1},{4,6},{5,7},{6,4},{7,5},{8,10},{9,11},{10,... | collective-permute-start | bytes 236 | tf_op jit(solution)/shard_map/ppermute | solution.py:98
  80.3 1.5 %collective-permute-done.15 = f32[19]{0:T(128)S(1)} collective-permute-done((f32[19]{0:T(128)S(1)}, f32[19]{0:T(128)S(1)}, u32[]{:S(2)}, u32[]{:S(2)}) %collective-permute-start.15) | collective-permute-done | bytes 108 | tf_op jit(solution)/shard_map/ppermute | solution.py:98
  81.8 2.6 %collective-permute-start.16 = (f32[19]{0:T(128)S(1)}, f32[19]{0:T(128)S(1)}, u32[]{:S(2)}, u32[]{:S(2)}) collective-permute-start(f32[19]{0:T(128)S(1)} %add.144), channel_id=1, source_target_pairs={{0,4},{1,5},{2,6},{3,7},{4,0},{5,1},{6,2},{7,3},{8,12},{9,13},{10,... | collective-permute-start | bytes 236 | tf_op jit(solution)/shard_map/ppermute | solution.py:98
  84.5 4.7 %collective-permute-done.16 = f32[19]{0:T(128)S(1)} collective-permute-done((f32[19]{0:T(128)S(1)}, f32[19]{0:T(128)S(1)}, u32[]{:S(2)}, u32[]{:S(2)}) %collective-permute-start.16) | collective-permute-done | bytes 108 | tf_op jit(solution)/shard_map/ppermute | solution.py:98
  89.2 5.4 %collective-permute-start.17 = (f32[19]{0:T(128)S(1)}, f32[19]{0:T(128)S(1)}, u32[]{:S(2)}, u32[]{:S(2)}) collective-permute-start(f32[19]{0:T(128)S(1)} %add.145), channel_id=1, source_target_pairs={{0,128},{128,0},{1,129},{129,1},{2,130},{130,2},{3,131},{131,3},{4... | collective-permute-start | bytes 236 | tf_op jit(solution)/shard_map/ppermute | solution.py:98
  94.6 1.0 copy.88
  97.6 1.5 %collective-permute-start.3 = (f32[28,4,8,1]{3,0,2,1:T(8,128)S(1)}, f32[28,4,8,1]{3,0,2,1:T(8,128)S(1)}, u32[]{:S(2)}, u32[]{:S(2)}) collective-permute-start(f32[28,4,8,1]{3,0,2,1:T(8,128)S(1)} %get-tuple-element.35), channel_id=1, source_target_pairs={{0,1},{1,2},{2,3},{3,4},{4,5},{5,6},{6,7},{7,0},{8,9},{9,10},{10,1... | collective-permute-start | bytes 10760 | tf_op jit(solution)/shard_map/ppermute | solution.py:83
  100.0 8.7 %collective-permute-done.3 = f32[28,4,8,1]{3,0,2,1:T(8,128)S(1)} collective-permute-done((f32[28,4,8,1]{3,0,2,1:T(8,128)S(1)}, f32[28,4,8,1]{3,0,2,1:T(8,128)S(1)}, u32[]{:S(2)}, u32[]{:S(2)}) %collective-permute-start.3) | collective-permute-done | bytes 3616 | tf_op jit(solution)/shard_map/ppermute | solution.py:83
  108.6 2.0 %collective-permute-done.4 = f32[28,4,8,1]{3,0,2,1:T(8,128)S(1)} collective-permute-done((f32[28,4,8,1]{3,0,2,1:T(8,128)S(1)}, f32[28,4,8,1]{3,0,2,1:T(8,128)S(1)}, u32[]{:S(2)}, u32[]{:S(2)}) %collective-permute-start.4) | collective-permute-done | bytes 3616 | tf_op jit(solution)/shard_map/ppermute | solution.py:84
  112.6 1.0 copy.87
  (202 shorter events, 28.6 us)
Async XLA Ops:
  2.0 5.9 %copy-start.1 = (f32[28,4,8,128]{3,2,1,0:T(8,128)S(1)}, f32[28,4,8,128]{3,2,1,0:T(8,128)}, u32[]{:S(2)}) copy-start(f32[28,4,8,128]{3,2,1,0:T(8,128)} %param.31) | copy-start | bytes 1376260
  2.4 23.5 %collective-permute-start = (f32[3,4,8,128]{3,2,1,0:T(8,128)S(1)}, f32[3,4,8,128]{3,2,1,0:T(8,128)}, u32[]{:S(2)}, u32[]{:S(2)}) collective-permute-start(f32[3,4,8,128]{3,2,1,0:T(8,128)S(1)} %maximum_divide_fusion), channel_id=1, source_target_pairs={{0,128},{1,129},{2,130},{3,131},{4,132},{5,133},{6,134},{7,135},{8... | collective-permute-start | bytes 147464 | tf_op jit(solution)/shard_map/ppermute | solution.py:126
  8.6 18.2 %collective-permute-start.5 = (f32[28,4,1,128]{3,0,2,1:T(8,128)}, f32[28,4,1,128]{3,0,2,1:T(8,128)S(1)}, u32[]{:S(2)}, u32[]{:S(2)}) collective-permute-start(f32[28,4,1,128]{3,0,2,1:T(8,128)} %copy.114), channel_id=1, source_target_pairs={{0,8},{8,16},{16,24},{24,32},{32,40},{40,48},{48,56},{56,64},{64,7... | collective-permute-start | bytes 172040 | tf_op jit(solution)/shard_map/ppermute | solution.py:78
  9.3 17.6 %collective-permute-start.6 = (f32[28,4,1,128]{3,0,2,1:T(8,128)}, f32[28,4,1,128]{3,0,2,1:T(8,128)}, u32[]{:S(2)}, u32[]{:S(2)}) collective-permute-start(f32[28,4,1,128]{3,0,2,1:T(8,128)} %copy.115), channel_id=1, source_target_pairs={{0,120},{8,0},{16,8},{24,16},{32,24},{40,32},{48,40},{56,48},{64,5... | collective-permute-start | bytes 172040 | tf_op jit(solution)/shard_map/ppermute | solution.py:79
  15.1 8.5 %copy-start.15 = (s32[1024]{0:T(1024)}, s32[1024]{0:T(1024)S(1)}, u32[]{:S(2)}) copy-start(s32[1024]{0:T(1024)S(1)} %pad_clamp_fusion.1) | copy-start | bytes 12292
  17.7 3.3 %copy-start.14 = (s32[1024]{0:T(1024)}, s32[1024]{0:T(1024)S(1)}, u32[]{:S(2)}) copy-start(s32[1024]{0:T(1024)S(1)} %pad_clamp_fusion) | copy-start | bytes 12292
  25.9 20.5 %copy-start.6 = (f32[4,8,128]{2,1,0:T(8,128)}, f32[4,8,128]{2,1,0:T(8,128)S(1)}, u32[]{:S(2)}) copy-start(f32[4,8,128]{2,1,0:T(8,128)S(1)} %get-tuple-element.58) | copy-start | bytes 49156
  25.9 20.5 %copy-start.8 = (f32[4,8,128]{2,1,0:T(8,128)}, f32[4,8,128]{2,1,0:T(8,128)S(1)}, u32[]{:S(2)}) copy-start(f32[4,8,128]{2,1,0:T(8,128)S(1)} %get-tuple-element.59) | copy-start | bytes 49156
  26.0 20.5 %copy-start.10 = (f32[4,8,128]{2,1,0:T(8,128)}, f32[4,8,128]{2,1,0:T(8,128)S(1)}, u32[]{:S(2)}) copy-start(f32[4,8,128]{2,1,0:T(8,128)S(1)} %get-tuple-element.60) | copy-start | bytes 49156
  28.2 10.8 %collective-permute-start.7 = (f32[28,4,8,1]{3,0,2,1:T(8,128)S(1)}, f32[28,4,8,1]{3,0,2,1:T(8,128)S(1)}, u32[]{:S(2)}, u32[]{:S(2)}) collective-permute-start(f32[28,4,8,1]{3,0,2,1:T(8,128)S(1)} %get-tuple-element.47), channel_id=1, source_target_pairs={{0,1},{1,2},{2,3},{3,4},{4,5},{5,6},{6,7},{7,0},{8,9},{9,10},{10,1... | collective-permute-start | bytes 10760 | tf_op jit(solution)/shard_map/ppermute | solution.py:83
  30.2 10.6 %collective-permute-start.8 = (f32[28,4,8,1]{3,0,2,1:T(8,128)S(1)}, f32[28,4,8,1]{3,0,2,1:T(8,128)S(1)}, u32[]{:S(2)}, u32[]{:S(2)}) collective-permute-start(f32[28,4,8,1]{3,0,2,1:T(8,128)S(1)} %get-tuple-element.46), channel_id=1, source_target_pairs={{0,7},{1,0},{2,1},{3,2},{4,3},{5,4},{6,5},{7,6},{8,15},{9,8},{10,9... | collective-permute-start | bytes 10760 | tf_op jit(solution)/shard_map/ppermute | solution.py:84
  43.9 2.1 %copy-start.12 = (f32[19,19,1,1]{0,1,3,2:T(8,128)S(1)}, f32[19,19,1,1]{0,1,3,2:T(8,128)}, u32[]{:S(2)}) copy-start(f32[19,19,1,1]{0,1,3,2:T(8,128)} %constant.120) | copy-start | bytes 4336
  44.5 2.0 %copy-start.31 = (f32[19]{0:T(128)S(1)}, f32[19]{0:T(128)}, u32[]{:S(2)}) copy-start(f32[19]{0:T(128)} %constant.107) | copy-start | bytes 232
  44.5 2.0 %copy-start.34 = (f32[19]{0:T(128)S(1)}, f32[19]{0:T(128)}, u32[]{:S(2)}) copy-start(f32[19]{0:T(128)} %constant.108) | copy-start | bytes 232
  44.5 2.0 %copy-start.37 = (f32[19]{0:T(128)S(1)}, f32[19]{0:T(128)}, u32[]{:S(2)}) copy-start(f32[19]{0:T(128)} %constant.109) | copy-start | bytes 232
  44.5 2.0 %copy-start.42 = (f32[19]{0:T(128)S(1)}, f32[19]{0:T(128)}, u32[]{:S(2)}) copy-start(f32[19]{0:T(128)} %concatenate.56) | copy-start | bytes 232
  44.5 2.0 %copy-start.55 = (f32[19]{0:T(128)S(1)}, f32[19]{0:T(128)}, u32[]{:S(2)}) copy-start(f32[19]{0:T(128)} %constant.106) | copy-start | bytes 232
  44.5 8.5 %collective-permute-start.9 = (f32[3,4,8,128]{3,2,1,0:T(8,128)}, f32[3,4,8,128]{3,2,1,0:T(8,128)}, u32[]{:S(2)}, u32[]{:S(2)}) collective-permute-start(f32[3,4,8,128]{3,2,1,0:T(8,128)} %multiply_select_fusion), channel_id=1, source_target_pairs={{128,0},{129,1},{130,2},{131,3},{132,4},{133,5},{134,6},{135,7},{1... | collective-permute-start | bytes 147464 | tf_op jit(solution)/shard_map/ppermute | solution.py:143
  56.0 1.3 %collective-permute-start.10 = (f32[19]{0:T(128)S(1)}, f32[19]{0:T(128)S(1)}, u32[]{:S(2)}, u32[]{:S(2)}) collective-permute-start(f32[19]{0:T(128)S(1)} %broadcast_select_fusion.1), channel_id=1, source_target_pairs={{0,8},{8,0},{16,24},{24,16},{32,40},{40,32},{48,56},{56,48},{64,72... | collective-permute-start | bytes 236 | tf_op jit(solution)/shard_map/ppermute | solution.py:98
  56.8 3.3 %copy-start.2 = (f32[19,4,8,128]{3,2,1,0:T(8,128)S(1)}, f32[19,4,8,128]{3,2,1,0:T(8,128)}, u32[]{:S(2)}) copy-start(f32[19,4,8,128]{3,2,1,0:T(8,128)} %gather_fusion) | copy-start | bytes 933892
  57.3 2.8 %copy-start.43 = (f32[19]{0:T(128)S(1)}, f32[19]{0:T(128)}, u32[]{:S(2)}) copy-start(f32[19]{0:T(128)} %concatenate.56) | copy-start | bytes 232
  57.4 4.2 %collective-permute-start.11 = (f32[19]{0:T(128)S(1)}, f32[19]{0:T(128)S(1)}, u32[]{:S(2)}, u32[]{:S(2)}) collective-permute-start(f32[19]{0:T(128)S(1)} %add.139), channel_id=1, source_target_pairs={{0,16},{8,24},{16,0},{24,8},{32,48},{40,56},{48,32},{56,40},{64,80... | collective-permute-start | bytes 236 | tf_op jit(solution)/shard_map/ppermute | solution.py:98
  61.6 4.4 %collective-permute-start.12 = (f32[19]{0:T(128)S(1)}, f32[19]{0:T(128)S(1)}, u32[]{:S(2)}, u32[]{:S(2)}) collective-permute-start(f32[19]{0:T(128)S(1)} %add.140), channel_id=1, source_target_pairs={{0,32},{8,40},{16,48},{24,56},{32,0},{40,8},{48,16},{56,24},{64,96... | collective-permute-start | bytes 236 | tf_op jit(solution)/shard_map/ppermute | solution.py:98
  66.1 5.1 %collective-permute-start.13 = (f32[19]{0:T(128)S(1)}, f32[19]{0:T(128)S(1)}, u32[]{:S(2)}, u32[]{:S(2)}) collective-permute-start(f32[19]{0:T(128)S(1)} %add.141), channel_id=1, source_target_pairs={{0,64},{8,72},{16,80},{24,88},{32,96},{40,104},{48,112},{56,120},{... | collective-permute-start | bytes 236 | tf_op jit(solution)/shard_map/ppermute | solution.py:98
  71.2 3.7 %collective-permute-start.14 = (f32[19]{0:T(128)S(1)}, f32[19]{0:T(128)S(1)}, u32[]{:S(2)}, u32[]{:S(2)}) collective-permute-start(f32[19]{0:T(128)S(1)} %add.142), channel_id=1, source_target_pairs={{0,1},{1,0},{2,3},{3,2},{4,5},{5,4},{6,7},{7,6},{8,9},{9,8},{10,11... | collective-permute-start | bytes 236 | tf_op jit(solution)/shard_map/ppermute | solution.py:98
  73.4 23.3 %collective-permute-start.1 = (f32[28,4,1,128]{3,0,2,1:T(8,128)S(1)}, f32[28,4,1,128]{3,0,2,1:T(8,128)S(1)}, u32[]{:S(2)}, u32[]{:S(2)}) collective-permute-start(f32[28,4,1,128]{3,0,2,1:T(8,128)S(1)} %get-tuple-element.39), channel_id=1, source_target_pairs={{0,8},{8,16},{16,24},{24,32},{32,40},{40,48},{48,56},{56,64},{64,7... | collective-permute-start | bytes 172040 | tf_op jit(solution)/shard_map/ppermute | solution.py:78
  74.9 6.9 %collective-permute-start.15 = (f32[19]{0:T(128)S(1)}, f32[19]{0:T(128)S(1)}, u32[]{:S(2)}, u32[]{:S(2)}) collective-permute-start(f32[19]{0:T(128)S(1)} %add.143), channel_id=1, source_target_pairs={{0,2},{1,3},{2,0},{3,1},{4,6},{5,7},{6,4},{7,5},{8,10},{9,11},{10,... | collective-permute-start | bytes 236 | tf_op jit(solution)/shard_map/ppermute | solution.py:98
  80.3 16.4 %collective-permute-start.2 = (f32[28,4,1,128]{3,0,2,1:T(8,128)S(1)}, f32[28,4,1,128]{3,0,2,1:T(8,128)S(1)}, u32[]{:S(2)}, u32[]{:S(2)}) collective-permute-start(f32[28,4,1,128]{3,0,2,1:T(8,128)S(1)} %get-tuple-element.38), channel_id=1, source_target_pairs={{0,120},{8,0},{16,8},{24,16},{32,24},{40,32},{48,40},{56,48},{64,5... | collective-permute-start | bytes 172040 | tf_op jit(solution)/shard_map/ppermute | solution.py:79
  81.8 7.4 %collective-permute-start.16 = (f32[19]{0:T(128)S(1)}, f32[19]{0:T(128)S(1)}, u32[]{:S(2)}, u32[]{:S(2)}) collective-permute-start(f32[19]{0:T(128)S(1)} %add.144), channel_id=1, source_target_pairs={{0,4},{1,5},{2,6},{3,7},{4,0},{5,1},{6,2},{7,3},{8,12},{9,13},{10,... | collective-permute-start | bytes 236 | tf_op jit(solution)/shard_map/ppermute | solution.py:98
  89.2 6.9 %collective-permute-start.17 = (f32[19]{0:T(128)S(1)}, f32[19]{0:T(128)S(1)}, u32[]{:S(2)}, u32[]{:S(2)}) collective-permute-start(f32[19]{0:T(128)S(1)} %add.145), channel_id=1, source_target_pairs={{0,128},{128,0},{1,129},{129,1},{2,130},{130,2},{3,131},{131,3},{4... | collective-permute-start | bytes 236 | tf_op jit(solution)/shard_map/ppermute | solution.py:98
  97.6 11.0 %collective-permute-start.3 = (f32[28,4,8,1]{3,0,2,1:T(8,128)S(1)}, f32[28,4,8,1]{3,0,2,1:T(8,128)S(1)}, u32[]{:S(2)}, u32[]{:S(2)}) collective-permute-start(f32[28,4,8,1]{3,0,2,1:T(8,128)S(1)} %get-tuple-element.35), channel_id=1, source_target_pairs={{0,1},{1,2},{2,3},{3,4},{4,5},{5,6},{6,7},{7,0},{8,9},{9,10},{10,1... | collective-permute-start | bytes 10760 | tf_op jit(solution)/shard_map/ppermute | solution.py:83
  99.2 11.4 %collective-permute-start.4 = (f32[28,4,8,1]{3,0,2,1:T(8,128)S(1)}, f32[28,4,8,1]{3,0,2,1:T(8,128)S(1)}, u32[]{:S(2)}, u32[]{:S(2)}) collective-permute-start(f32[28,4,8,1]{3,0,2,1:T(8,128)S(1)} %get-tuple-element.34), channel_id=1, source_target_pairs={{0,7},{1,0},{2,1},{3,2},{4,3},{5,4},{6,5},{7,6},{8,15},{9,8},{10,9... | collective-permute-start | bytes 10760 | tf_op jit(solution)/shard_map/ppermute | solution.py:84
  (43 other events, 34.0 us)

commit v2 on v1

--- a/solution.py
+++ b/solution.py
@@ -90,8 +90,8 @@
     return jnp.where(move_x > 0, from_low, jnp.where(move_x < 0, from_high, field))
 
 
-def butterfly_sum(values):
-    for axis in ("gy", "gz", "sec"):
+def butterfly_sum(values, axes):
+    for axis in axes:
         count = lax.axis_size(axis)
         step = 1
         while step < count:
@@ -110,13 +110,6 @@
     is_flow = lax.axis_index("sec") == 0
     fluid = (solid_mask == 0)[None]
 
-    flow_moves = np.concatenate([velocity, np.zeros((rows - 19, 3))])
-    species_moves = np.tile(velocity[:7], (groups, 1))
-    moves = [
-        jnp.where(is_flow, column(flow_moves[:, d]), column(species_moves[:, d])) for d in range(3)
-    ]
-    returned = shift_rows(cotangents, [-m for m in moves])
-
     flow = populations[:19]
     vx, vy, vz = (column(velocity[:, d]) for d in range(3))
     density = jnp.sum(flow, 0)
@@ -128,20 +121,9 @@
 
     small_weights = column([0.25] + [0.125] * 6)
     grouped = populations.reshape((groups, 7) + populations.shape[1:])
-    back_species = returned.reshape(grouped.shape)
     species_r = species_rates.reshape((groups, 1, 1, 1, 1))
     concentration = jnp.sum(grouped, 1)
     sx, sy, sz = (column(velocity[:7, d])[None] for d in range(3))
-    weighted_back = back_species * small_weights[None]
-    species_motion_grad = 4.0 * jnp.sum(
-        species_r * concentration[:, None] * jnp.stack(
-            [jnp.sum(weighted_back * sx, 1), jnp.sum(weighted_back * sy, 1), jnp.sum(weighted_back * sz, 1)], 1
-        ),
-        0,
-    )
-    species_motion_grad = jnp.where(fluid, species_motion_grad, 0.0)
-    sent_grad = lax.ppermute(species_motion_grad, "sec", [(1, 0)])
-
     projected_small = motion[0][None] * sx[0] + motion[1][None] * sy[0] + motion[2][None] * sz[0]
     factor = small_weights * (1.0 + 4.0 * projected_small)
     species_eq = factor[None] * concentration[:, None]
@@ -149,14 +131,6 @@
     species_relaxed = grouped - species_r * species_gap
     species_bounce = grouped[:, opposite[:7]]
     species_post = jnp.where(fluid[None], species_relaxed, species_bounce).reshape(populations.shape)
-    species_t = jnp.sum(back_species * factor[None], 1)
-    species_grad_fluid = (1.0 - species_r) * back_species + species_r * species_t[:, None]
-    species_grad = jnp.where(
-        fluid[None], species_grad_fluid, back_species[:, opposite[:7]]
-    ).reshape(populations.shape)
-    species_rate_grad = -jnp.sum(
-        jnp.where(fluid[None], back_species * species_gap, 0.0), axis=(1, 2, 3, 4)
-    )
 
     q_table = jnp.asarray(ortho, jnp.float32)
     relax = jnp.concatenate([jnp.zeros((4,), flow_rates.dtype), flow_rates]).reshape(19, 1, 1, 1)
@@ -168,6 +142,37 @@
     moments = jnp.einsum("ji,jxyz->ixyz", q_table, flow - equilibrium, precision=highest)
     flow_relaxed = flow - jnp.einsum("ij,jxyz->ixyz", q_table, relax * moments, precision=highest)
     flow_post = jnp.where(fluid, flow_relaxed, flow[opposite])
+    filler = jnp.zeros((rows - 19,) + populations.shape[1:], jnp.float32)
+    post = jnp.where(is_flow, jnp.concatenate([flow_post, filler]), species_post)
+
+    flow_moves = np.concatenate([velocity, np.zeros((rows - 19, 3))])
+    species_moves = np.tile(velocity[:7], (groups, 1))
+    both_moves = []
+    for d in range(3):
+        table = jnp.where(is_flow, column(flow_moves[:, d]), column(species_moves[:, d]))
+        both_moves.append(jnp.concatenate([table, -table]))
+    both = shift_rows(jnp.concatenate([post, cotangents]), both_moves)
+    moved = both[:rows]
+    returned = both[rows:]
+    moved = jnp.where(is_flow, jnp.concatenate([moved[:19], filler]), moved)
+
+    back_species = returned.reshape(grouped.shape)
+    weighted_back = back_species * small_weights[None]
+    species_motion_grad = 4.0 * jnp.sum(
+        species_r * concentration[:, None] * jnp.stack(
+            [jnp.sum(weighted_back * sx, 1), jnp.sum(weighted_back * sy, 1), jnp.sum(weighted_back * sz, 1)], 1
+        ),
+        0,
+    )
+    species_motion_grad = jnp.where(fluid, species_motion_grad, 0.0)
+    species_t = jnp.sum(back_species * factor[None], 1)
+    species_grad_fluid = (1.0 - species_r) * back_species + species_r * species_t[:, None]
+    species_grad = jnp.where(
+        fluid[None], species_grad_fluid, back_species[:, opposite[:7]]
+    ).reshape(populations.shape)
+    species_rate_grad = -jnp.sum(
+        jnp.where(fluid[None], back_species * species_gap, 0.0), axis=(1, 2, 3, 4)
+    )
 
     back_flow = returned[:19]
     back_moments = jnp.einsum("ji,jxyz->ixyz", q_table, back_flow, precision=highest)
@@ -183,24 +188,26 @@
         jnp.stack([jnp.sum(hwp * vx, 0), jnp.sum(hwp * vy, 0), jnp.sum(hwp * vz, 0)])
         - 3.0 * motion * hw_sum[None]
     )
-    motion_grad = jnp.where(fluid, motion_grad + sent_grad, 0.0)
+
+    local_rates = jnp.where(
+        is_flow,
+        jnp.concatenate([flow_rate_grad, jnp.zeros((groups,), jnp.float32)]),
+        jnp.concatenate([jnp.zeros((15,), jnp.float32), species_rate_grad]),
+    )
+    partial_rates = butterfly_sum(local_rates, ("gy", "gz"))
+    plane = populations.shape[1:]
+    rate_plane = jnp.zeros(plane, jnp.float32).at[0, 0, : partial_rates.shape[0]].set(partial_rates)
+    payload = jnp.concatenate([species_motion_grad, rate_plane[None]])
+    other = lax.ppermute(payload, "sec", [(0, 1), (1, 0)])
+    rate_grad = partial_rates + other[3, 0, 0, : partial_rates.shape[0]]
+
+    motion_grad = jnp.where(fluid, motion_grad + other[:3], 0.0)
     along = vx * motion_grad[0][None] + vy * motion_grad[1][None] + vz * motion_grad[2][None]
     extra = (along - jnp.sum(motion * motion_grad, 0)[None]) / density[None]
     flow_grad = jnp.where(
         fluid, back_flow - through_eq + density_grad[None] + extra, back_flow[opposite]
     )
-
-    filler = jnp.zeros((rows - 19,) + populations.shape[1:], jnp.float32)
-    post = jnp.where(is_flow, jnp.concatenate([flow_post, filler]), species_post)
     grad_rows = jnp.where(is_flow, jnp.concatenate([flow_grad, filler]), species_grad)
-    local_rates = jnp.where(
-        is_flow,
-        jnp.concatenate([flow_rate_grad, jnp.zeros((groups,), jnp.float32)]),
-        jnp.concatenate([jnp.zeros((15,), jnp.float32), species_rate_grad]),
-    )
-    rate_grad = butterfly_sum(local_rates)
-    moved = shift_rows(post, moves)
-    moved = jnp.where(is_flow, jnp.concatenate([moved[:19], filler]), moved)
     return (moved, grad_rows, rate_grad)
 
 

time: 115 us -> 84.9 us (0.74)
  starting transfers between devices: 37.5 us -> 26.8 us
  waiting for transfers between devices: 32.5 us -> 22.1 us
  local copies, waits for them, and re-layouts: 27.5 us -> 21.8 us
  other arithmetic: 11.5 us -> 9.84 us
    ppermute x2 -> x1, waiting for transfers between devices: 17.1 us -> 0.1 us  [shift_rows(): low = lax.ppermute(field[:, :, :, size_z - 1:], 'gz', ring('gz', 1))]
    ppermute x8 -> x7, starting transfers between devices: 22.4 us -> 15.6 us  [butterfly_sum(): lax.ppermute(values, axis, [(i, i ^ step) for i in range(count)])]
    unnamed x121 -> x90, local copies, waits for them, and re-layouts: 16.2 us -> 9.87 us
    ppermute x1, waiting for transfers between devices: 0.01 us -> 4.15 us  [per_device(): other = lax.ppermute(payload, 'sec', [(0, 1), (1, 0)])]
    ppermute x8 -> x7, waiting for transfers between devices: 11.6 us -> 14.5 us  [butterfly_sum(): lax.ppermute(values, axis, [(i, i ^ step) for i in range(count)])]
    ppermute x2 -> x1, waiting for transfers between devices: 3.77 us -> 0.95 us  [shift_rows(): high = lax.ppermute(field[:, :, :, :1], 'gz', ring('gz', -1))]
    ppermute x0 -> x2, local copies, waits for them, and re-layouts: none -> 2.66 us  [the longest x1 1.36 us: shift_rows(): low = lax.ppermute(field[:, :, :, size_z - 1:], 'gz', ring('gz', 1))]
    ppermute x2 -> x1, waiting for transfers between devices: 0.01 us -> 2.36 us  [shift_rows(): low = lax.ppermute(field[:, :, size_y - 1:, :], 'gy', ring('gy', 1))]
  transfers between devices with their start and end apart: 18 -> 13, of which waited for: 10 -> 10; matrix products, arithmetic and copies ran while one was open for 19% -> 13% of each run, Pallas kernels for 0% -> 0%
where the time goes in v2:
time: 84.9 us; the launch traced here: 84.5 us
  starting transfers between devices  26.8 us (32%)
  waiting for transfers between devices  22.1 us (26%)
  local copies, waits for them, and re-layouts  21.8 us (26%)
  other arithmetic  9.84 us (12%)
  matrix products  2.57 us (3%)
  between operations  1.42 us (2%)
    ppermute x7, starting transfers between devices, butterfly_sum(): lax.ppermute(values, axis, [(i, i ^ step) for i in range(count)])  15.6 us
    ppermute x7, waiting for transfers between devices, butterfly_sum(): lax.ppermute(values, axis, [(i, i ^ step) for i in range(count)])  14.5 us
    unnamed x90, local copies, waits for them, and re-layouts  9.87 us
    ppermute x1, starting transfers between devices, per_device(): sent_motion = lax.ppermute(own_motion, 'sec', [(0, 1)])  5.06 us
    ppermute x1, waiting for transfers between devices, per_device(): other = lax.ppermute(payload, 'sec', [(0, 1), (1, 0)])  4.15 us
    ppermute x1, starting transfers between devices, shift_rows(): high = lax.ppermute(field[:, :, :1, :], 'gy', ring('gy', -1))  3.84 us
    ppermute x1, waiting for transfers between devices, shift_rows(): low = lax.ppermute(field[:, :, size_y - 1:, :], 'gy', ring('gy', 1))  2.36 us
    select_n x1, other arithmetic, shift_rows(): jnp.where(move_z > 0, from_low, jnp.where(move_z < 0, from_high, field))  2.28 us
  transfers between devices with their start and end apart: 13, of which 10 were waited for; matrix products, arithmetic and copies ran while one was open for 13% of the time, Pallas kernels for 0%

profile of v2, /device:TPU:32, one launch (start us, length us, event | category | flops | bytes accessed | tf_op | source)
XLA Modules:
  0.0 84.5 jit_solution(13263052897531846300)
XLA Ops:
  0.7 1.3 %copy.81 = f32[28,4,8,128]{3,0,2,1:T(8,128)S(1)} copy(f32[28,4,8,128]{3,2,1,0:T(8,128)} %param.29) | data formatting | bytes 917504 | tf_op args[0]
  2.5 5.1 %collective-permute-start = (f32[3,4,8,128]{3,2,1,0:T(8,128)S(1)}, f32[3,4,8,128]{3,2,1,0:T(8,128)S(1)}, u32[]{:S(2)}, u32[]{:S(2)}) collective-permute-start(f32[3,4,8,128]{3,2,1,0:T(8,128)S(1)} %maximum_divide_fusion), channel_id=1, source_target_pairs={{0,128},{1,129},{2,130},{3,131},{4,132},{5,133},{6,134},{7,135},{8... | collective-permute-start | bytes 147464 | tf_op jit(solution)/shard_map/ppermute | solution.py:119
  15.8 0.8 fusion.19
  16.5 0.7 fusion.2
  17.9 0.8 fusion.10
  18.8 3.8 %collective-permute-start.2 = (f32[56,4,1,128]{3,0,2,1:T(8,128)S(1)}, f32[56,4,1,128]{3,0,2,1:T(8,128)S(1)}, u32[]{:S(2)}, u32[]{:S(2)}) collective-permute-start(f32[56,4,1,128]{3,0,2,1:T(8,128)S(1)} %get-tuple-element.44), channel_id=1, source_target_pairs={{0,120},{8,0},{16,8},{24,16},{32,24},{40,32},{48,40},{56,48},{64,5... | collective-permute-start | bytes 344072 | tf_op jit(solution)/shard_map/ppermute | solution.py:79
  22.8 2.4 %collective-permute-done.1 = f32[56,4,1,128]{3,0,2,1:T(8,128)S(1)} collective-permute-done((f32[56,4,1,128]{3,0,2,1:T(8,128)S(1)}, f32[56,4,1,128]{3,0,2,1:T(8,128)S(1)}, u32[]{:S(2)}, u32[]{:S(2)}) %collective-permute-start.1) | collective-permute-done | bytes 114720 | tf_op jit(solution)/shard_map/ppermute | solution.py:78
  26.1 1.2 %fusion.73 = (f32[56,4,8,1]{3,0,2,1:T(8,128)S(1)}, f32[56,4,8,1]{3,0,2,1:T(8,128)}) fusion(f32[56,4,8,128]{3,0,2,1:T(8,128)S(1)} %fusion.6), kind=kLoop, calls=%fused_computation.154 | loop fusion | bytes 28672 | tf_op jit(solution)/shard_map/slice | solution.py:84
  27.3 1.5 %copy.91 = f32[56,4,8,1]{0,2,3,1:T(8,128)S(1)} copy(f32[56,4,8,1]{3,0,2,1:T(8,128)} %get-tuple-element.57) | data formatting | bytes 14336 | tf_op jit(solution)/shard_map/slice | solution.py:83
  28.8 2.0 %collective-permute-start.3 = (f32[56,4,8,1]{0,2,3,1:T(8,128)S(1)}, f32[56,4,8,1]{0,2,3,1:T(8,128)S(1)}, u32[]{:S(2)}, u32[]{:S(2)}) collective-permute-start(f32[56,4,8,1]{0,2,3,1:T(8,128)S(1)} %copy.91), channel_id=1, source_target_pairs={{0,1},{1,2},{2,3},{3,4},{4,5},{5,6},{6,7},{7,0},{8,9},{9,10},{10,1... | collective-permute-start | bytes 21512 | tf_op jit(solution)/shard_map/ppermute | solution.py:83
  31.3 1.2 %fusion.72 = (f32[56,4,8,127]{3,0,2,1:T(8,128)S(1)}, f32[56,4,8,127]{3,0,2,1:T(8,128)}) fusion(f32[56,4,8,128]{3,0,2,1:T(8,128)S(1)} %fusion.6), kind=kLoop, calls=%fused_computation.153 | loop fusion | bytes 3641344 | tf_op jit(solution)/shard_map/slice | solution.py:86
  32.6 1.4 %copy.92 = f32[56,4,8,1]{3,0,2,1:T(8,128)} copy(f32[56,4,8,1]{0,2,3,1:T(8,128)S(1)} %collective-permute-done.3) | data formatting | bytes 14336 | tf_op jit(solution)/shard_map/ppermute | solution.py:83
  34.0 1.0 %collective-permute-done.4 = f32[56,4,8,1]{0,2,3,1:T(8,128)S(1)} collective-permute-done((f32[56,4,8,1]{0,2,3,1:T(8,128)S(1)}, f32[56,4,8,1]{0,2,3,1:T(8,128)S(1)}, u32[]{:S(2)}, u32[]{:S(2)}) %collective-permute-start.4) | collective-permute-done | bytes 7200 | tf_op jit(solution)/shard_map/ppermute | solution.py:84
  34.9 1.3 %copy.94 = f32[56,4,8,1]{3,0,2,1:T(8,128)} copy(f32[56,4,8,1]{0,2,3,1:T(8,128)S(1)} %collective-permute-done.4) | data formatting | bytes 14336 | tf_op jit(solution)/shard_map/ppermute | solution.py:84
  36.2 0.7 copy-done.6
  36.9 2.3 %maximum_select_fusion = f32[56,4,8,128]{3,0,2,1:T(8,128)S(1)} fusion(f32[56,4,8,127]{3,0,2,1:T(8,128)} %get-tuple-element.55, f32[56,4,8,1]{3,0,2,1:T(8,128)} %copy.92, f32[56,4,8,128]{3,0,2,1:T(8,128)S(1)} %fusion.6, f32[56,4,8,1]{3,0,2,1:T(8,128)} %copy.94, f32[56,4,8,127]{3,0,2,1:T(8,128)S(1)} %get-tuple-element.54, pred[56]{0:T(512)(128)(4,1)S(1)} %copy-done.7, ...), kind=kLoop, calls=%fused_computation.21 | loop fusion | flops 917504 | bytes 3670128 | tf_op jit(solution)/shard_map/jit(_where)/select_n | solution.py:87
  40.3 0.7 select_reduce_fusion
  44.0 3.1 %collective-permute-done.6 = f32[19]{0:T(128)S(1)} collective-permute-done((f32[19]{0:T(128)S(1)}, f32[19]{0:T(128)S(1)}, u32[]{:S(2)}, u32[]{:S(2)}) %collective-permute-start.6) | collective-permute-done | bytes 108 | tf_op jit(solution)/shard_map/ppermute | solution.py:98
  47.1 1.6 %collective-permute-start.7 = (f32[19]{0:T(128)S(1)}, f32[19]{0:T(128)S(1)}, u32[]{:S(2)}, u32[]{:S(2)}) collective-permute-start(f32[19]{0:T(128)S(1)} %add.136), channel_id=1, source_target_pairs={{0,32},{8,40},{16,48},{24,56},{32,0},{40,8},{48,16},{56,24},{64,96... | collective-permute-start | bytes 236 | tf_op jit(solution)/shard_map/ppermute | solution.py:98
  48.9 1.9 %collective-permute-done.7 = f32[19]{0:T(128)S(1)} collective-permute-done((f32[19]{0:T(128)S(1)}, f32[19]{0:T(128)S(1)}, u32[]{:S(2)}, u32[]{:S(2)}) %collective-permute-start.7) | collective-permute-done | bytes 108 | tf_op jit(solution)/shard_map/ppermute | solution.py:98
  50.8 3.1 %collective-permute-start.8 = (f32[19]{0:T(128)S(1)}, f32[19]{0:T(128)S(1)}, u32[]{:S(2)}, u32[]{:S(2)}) collective-permute-start(f32[19]{0:T(128)S(1)} %add.137), channel_id=1, source_target_pairs={{0,64},{8,72},{16,80},{24,88},{32,96},{40,104},{48,112},{56,120},{... | collective-permute-start | bytes 236 | tf_op jit(solution)/shard_map/ppermute | solution.py:98
  53.9 1.9 %collective-permute-done.8 = f32[19]{0:T(128)S(1)} collective-permute-done((f32[19]{0:T(128)S(1)}, f32[19]{0:T(128)S(1)}, u32[]{:S(2)}, u32[]{:S(2)}) %collective-permute-start.8) | collective-permute-done | bytes 108 | tf_op jit(solution)/shard_map/ppermute | solution.py:98
  55.8 3.0 %collective-permute-start.9 = (f32[19]{0:T(128)S(1)}, f32[19]{0:T(128)S(1)}, u32[]{:S(2)}, u32[]{:S(2)}) collective-permute-start(f32[19]{0:T(128)S(1)} %add.138), channel_id=1, source_target_pairs={{0,1},{1,0},{2,3},{3,2},{4,5},{5,4},{6,7},{7,6},{8,9},{9,8},{10,11... | collective-permute-start | bytes 236 | tf_op jit(solution)/shard_map/ppermute | solution.py:98
  58.8 1.5 %collective-permute-done.9 = f32[19]{0:T(128)S(1)} collective-permute-done((f32[19]{0:T(128)S(1)}, f32[19]{0:T(128)S(1)}, u32[]{:S(2)}, u32[]{:S(2)}) %collective-permute-start.9) | collective-permute-done | bytes 108 | tf_op jit(solution)/shard_map/ppermute | solution.py:98
  60.3 4.7 %collective-permute-start.10 = (f32[19]{0:T(128)S(1)}, f32[19]{0:T(128)S(1)}, u32[]{:S(2)}, u32[]{:S(2)}) collective-permute-start(f32[19]{0:T(128)S(1)} %add.139), channel_id=1, source_target_pairs={{0,2},{1,3},{2,0},{3,1},{4,6},{5,7},{6,4},{7,5},{8,10},{9,11},{10,... | collective-permute-start | bytes 236 | tf_op jit(solution)/shard_map/ppermute | solution.py:98
  65.1 1.5 %collective-permute-done.10 = f32[19]{0:T(128)S(1)} collective-permute-done((f32[19]{0:T(128)S(1)}, f32[19]{0:T(128)S(1)}, u32[]{:S(2)}, u32[]{:S(2)}) %collective-permute-start.10) | collective-permute-done | bytes 108 | tf_op jit(solution)/shard_map/ppermute | solution.py:98
  66.6 2.8 %collective-permute-start.11 = (f32[19]{0:T(128)S(1)}, f32[19]{0:T(128)S(1)}, u32[]{:S(2)}, u32[]{:S(2)}) collective-permute-start(f32[19]{0:T(128)S(1)} %add.140), channel_id=1, source_target_pairs={{0,4},{1,5},{2,6},{3,7},{4,0},{5,1},{6,2},{7,3},{8,12},{9,13},{10,... | collective-permute-start | bytes 236 | tf_op jit(solution)/shard_map/ppermute | solution.py:98
  69.4 4.7 %collective-permute-done.11 = f32[19]{0:T(128)S(1)} collective-permute-done((f32[19]{0:T(128)S(1)}, f32[19]{0:T(128)S(1)}, u32[]{:S(2)}, u32[]{:S(2)}) %collective-permute-start.11) | collective-permute-done | bytes 108 | tf_op jit(solution)/shard_map/ppermute | solution.py:98
  75.8 4.2 %collective-permute-done.12 = f32[4,4,8,128]{3,2,1,0:T(8,128)S(1)} collective-permute-done((f32[4,4,8,128]{3,2,1,0:T(8,128)S(1)}, f32[4,4,8,128]{3,2,1,0:T(8,128)S(1)}, u32[]{:S(2)}, u32[]{:S(2)}) %collective-permute-start.12) | collective-permute-done | bytes 65568 | tf_op jit(solution)/shard_map/ppermute | solution.py:201
  81.2 0.8 fusion.9
  81.9 1.0 %copy.102 = f32[28,4,8,128]{3,2,1,0:T(8,128)} copy(f32[28,4,8,128]{3,0,2,1:T(8,128)S(1)} %get-tuple-element.47) | data formatting | bytes 917504
  83.0 1.0 %copy.103 = f32[28,4,8,128]{3,2,1,0:T(8,128)} copy(f32[28,4,8,128]{3,0,2,1:T(8,128)S(1)} %get-tuple-element.46) | data formatting | bytes 917504
  (162 shorter events, 18.5 us)
Async XLA Ops:
  0.6 1.3 %copy-start.18 = (f32[19]{0:T(128)S(1)}, f32[19]{0:T(128)}, u32[]{:S(2)}) copy-start(f32[19]{0:T(128)} %constant.138) | copy-start | bytes 232
  0.6 1.3 %copy-start.21 = (f32[19]{0:T(128)S(1)}, f32[19]{0:T(128)}, u32[]{:S(2)}) copy-start(f32[19]{0:T(128)} %constant.139) | copy-start | bytes 232
  0.7 1.3 %copy-start.24 = (f32[19]{0:T(128)S(1)}, f32[19]{0:T(128)}, u32[]{:S(2)}) copy-start(f32[19]{0:T(128)} %constant.140) | copy-start | bytes 232
  2.0 5.6 %copy-start.38 = (s32[19]{0:T(128)S(1)}, s32[19]{0:T(128)}, u32[]{:S(2)}) copy-start(s32[19]{0:T(128)} %constant.147) | copy-start | bytes 232
  2.0 5.6 %copy-start.3 = (s32[4,8,128]{2,1,0:T(8,128)S(1)}, s32[4,8,128]{2,1,0:T(8,128)}, u32[]{:S(2)}) copy-start(s32[4,8,128]{2,1,0:T(8,128)} %param.30) | copy-start | bytes 49156
  2.0 5.6 %copy-start.37 = (s32[7]{0:T(128)S(1)}, s32[7]{0:T(128)}, u32[]{:S(2)}) copy-start(s32[7]{0:T(128)} %constant.148) | copy-start | bytes 88
  2.0 5.6 %copy-start.4 = (f32[4]{0:T(128)S(1)}, f32[4]{0:T(128)}, u32[]{:S(2)}) copy-start(f32[4]{0:T(128)} %param.32) | copy-start | bytes 52
  2.1 5.6 %copy-start.35 = (f32[28,1,1,1]{0,3,2,1:T(1,128)S(1)}, f32[28,1,1,1]{0,3,2,1:T(1,128)}, u32[]{:S(2)}) copy-start(f32[28,1,1,1]{0,3,2,1:T(1,128)} %constant.118.clone) | copy-start | bytes 340
  2.1 5.6 %copy-start.36 = (f32[28,1,1,1]{0,3,2,1:T(1,128)S(1)}, f32[28,1,1,1]{0,3,2,1:T(1,128)}, u32[]{:S(2)}) copy-start(f32[28,1,1,1]{0,3,2,1:T(1,128)} %constant.119.clone) | copy-start | bytes 340
  2.1 6.3 %copy-start.31 = (f32[28,1,1,1]{0,3,2,1:T(1,128)S(1)}, f32[28,1,1,1]{0,3,2,1:T(1,128)}, u32[]{:S(2)}) copy-start(f32[28,1,1,1]{0,3,2,1:T(1,128)} %constant.116.clone) | copy-start | bytes 340
  2.1 6.3 %copy-start.32 = (f32[28,1,1,1]{0,3,2,1:T(1,128)S(1)}, f32[28,1,1,1]{0,3,2,1:T(1,128)}, u32[]{:S(2)}) copy-start(f32[28,1,1,1]{0,3,2,1:T(1,128)} %constant.117.clone) | copy-start | bytes 340
  2.1 6.3 %copy-start.33 = (f32[28,1,1,1]{0,3,2,1:T(1,128)S(1)}, f32[28,1,1,1]{0,3,2,1:T(1,128)}, u32[]{:S(2)}) copy-start(f32[28,1,1,1]{0,3,2,1:T(1,128)} %constant.120.clone) | copy-start | bytes 340
  2.1 6.3 %copy-start.34 = (f32[28,1,1,1]{0,3,2,1:T(1,128)S(1)}, f32[28,1,1,1]{0,3,2,1:T(1,128)}, u32[]{:S(2)}) copy-start(f32[28,1,1,1]{0,3,2,1:T(1,128)} %constant.121.clone) | copy-start | bytes 340
  2.5 8.5 %copy-start = (f32[28,4,8,128]{3,2,1,0:T(8,128)S(1)}, f32[28,4,8,128]{3,2,1,0:T(8,128)}, u32[]{:S(2)}) copy-start(f32[28,4,8,128]{3,2,1,0:T(8,128)} %param.29) | copy-start | bytes 1376260
  2.5 11.7 %collective-permute-start = (f32[3,4,8,128]{3,2,1,0:T(8,128)S(1)}, f32[3,4,8,128]{3,2,1,0:T(8,128)S(1)}, u32[]{:S(2)}, u32[]{:S(2)}) collective-permute-start(f32[3,4,8,128]{3,2,1,0:T(8,128)S(1)} %maximum_divide_fusion), channel_id=1, source_target_pairs={{0,128},{1,129},{2,130},{3,131},{4,132},{5,133},{6,134},{7,135},{8... | collective-permute-start | bytes 147464 | tf_op jit(solution)/shard_map/ppermute | solution.py:119
  11.6 1.0 %copy-start.1 = (f32[28,4,8,128]{3,2,1,0:T(8,128)S(1)}, f32[28,4,8,128]{3,2,1,0:T(8,128)}, u32[]{:S(2)}) copy-start(f32[28,4,8,128]{3,2,1,0:T(8,128)} %param.33) | copy-start | bytes 1376260
  18.7 6.4 %collective-permute-start.1 = (f32[56,4,1,128]{3,0,2,1:T(8,128)S(1)}, f32[56,4,1,128]{3,0,2,1:T(8,128)S(1)}, u32[]{:S(2)}, u32[]{:S(2)}) collective-permute-start(f32[56,4,1,128]{3,0,2,1:T(8,128)S(1)} %get-tuple-element.45), channel_id=1, source_target_pairs={{0,8},{8,16},{16,24},{24,32},{32,40},{40,48},{48,56},{56,64},{64,7... | collective-permute-start | bytes 344072 | tf_op jit(solution)/shard_map/ppermute | solution.py:78
  18.8 6.3 %collective-permute-start.2 = (f32[56,4,1,128]{3,0,2,1:T(8,128)S(1)}, f32[56,4,1,128]{3,0,2,1:T(8,128)S(1)}, u32[]{:S(2)}, u32[]{:S(2)}) collective-permute-start(f32[56,4,1,128]{3,0,2,1:T(8,128)S(1)} %get-tuple-element.44), channel_id=1, source_target_pairs={{0,120},{8,0},{16,8},{24,16},{32,24},{40,32},{48,40},{56,48},{64,5... | collective-permute-start | bytes 344072 | tf_op jit(solution)/shard_map/ppermute | solution.py:79
  28.8 3.8 %collective-permute-start.3 = (f32[56,4,8,1]{0,2,3,1:T(8,128)S(1)}, f32[56,4,8,1]{0,2,3,1:T(8,128)S(1)}, u32[]{:S(2)}, u32[]{:S(2)}) collective-permute-start(f32[56,4,8,1]{0,2,3,1:T(8,128)S(1)} %copy.91), channel_id=1, source_target_pairs={{0,1},{1,2},{2,3},{3,4},{4,5},{5,6},{6,7},{7,0},{8,9},{9,10},{10,1... | collective-permute-start | bytes 21512 | tf_op jit(solution)/shard_map/ppermute | solution.py:83
  31.1 3.8 %collective-permute-start.4 = (f32[56,4,8,1]{0,2,3,1:T(8,128)S(1)}, f32[56,4,8,1]{0,2,3,1:T(8,128)S(1)}, u32[]{:S(2)}, u32[]{:S(2)}) collective-permute-start(f32[56,4,8,1]{0,2,3,1:T(8,128)S(1)} %copy.93), channel_id=1, source_target_pairs={{0,7},{1,0},{2,1},{3,2},{4,3},{5,4},{6,5},{7,6},{8,15},{9,8},{10,9... | collective-permute-start | bytes 21512 | tf_op jit(solution)/shard_map/ppermute | solution.py:84
  42.1 1.2 %collective-permute-start.5 = (f32[19]{0:T(128)S(1)}, f32[19]{0:T(128)S(1)}, u32[]{:S(2)}, u32[]{:S(2)}) collective-permute-start(f32[19]{0:T(128)S(1)} %broadcast_select_fusion.1), channel_id=1, source_target_pairs={{0,8},{8,0},{16,24},{24,16},{32,40},{40,32},{48,56},{56,48},{64,72... | collective-permute-start | bytes 236 | tf_op jit(solution)/shard_map/ppermute | solution.py:98
  43.3 3.8 %collective-permute-start.6 = (f32[19]{0:T(128)S(1)}, f32[19]{0:T(128)S(1)}, u32[]{:S(2)}, u32[]{:S(2)}) collective-permute-start(f32[19]{0:T(128)S(1)} %add.135), channel_id=1, source_target_pairs={{0,16},{8,24},{16,0},{24,8},{32,48},{40,56},{48,32},{56,40},{64,80... | collective-permute-start | bytes 236 | tf_op jit(solution)/shard_map/ppermute | solution.py:98
  47.1 1.6 %copy-start.17 = (f32[7]{0:T(128)S(1)}, f32[7]{0:T(128)}, u32[]{:S(2)}) copy-start(f32[7]{0:T(128)} %constant.145) | copy-start | bytes 88
  47.1 1.6 %copy-start.11 = (f32[7]{0:T(128)S(1)}, f32[7]{0:T(128)}, u32[]{:S(2)}) copy-start(f32[7]{0:T(128)} %constant.142) | copy-start | bytes 88
  47.1 1.6 %copy-start.13 = (f32[7]{0:T(128)S(1)}, f32[7]{0:T(128)}, u32[]{:S(2)}) copy-start(f32[7]{0:T(128)} %constant.143) | copy-start | bytes 88
  47.1 1.6 %copy-start.15 = (f32[7]{0:T(128)S(1)}, f32[7]{0:T(128)}, u32[]{:S(2)}) copy-start(f32[7]{0:T(128)} %constant.144) | copy-start | bytes 88
  47.1 3.6 %collective-permute-start.7 = (f32[19]{0:T(128)S(1)}, f32[19]{0:T(128)S(1)}, u32[]{:S(2)}, u32[]{:S(2)}) collective-permute-start(f32[19]{0:T(128)S(1)} %add.136), channel_id=1, source_target_pairs={{0,32},{8,40},{16,48},{24,56},{32,0},{40,8},{48,16},{56,24},{64,96... | collective-permute-start | bytes 236 | tf_op jit(solution)/shard_map/ppermute | solution.py:98
  50.8 5.0 %collective-permute-start.8 = (f32[19]{0:T(128)S(1)}, f32[19]{0:T(128)S(1)}, u32[]{:S(2)}, u32[]{:S(2)}) collective-permute-start(f32[19]{0:T(128)S(1)} %add.137), channel_id=1, source_target_pairs={{0,64},{8,72},{16,80},{24,88},{32,96},{40,104},{48,112},{56,120},{... | collective-permute-start | bytes 236 | tf_op jit(solution)/shard_map/ppermute | solution.py:98
  55.8 4.5 %collective-permute-start.9 = (f32[19]{0:T(128)S(1)}, f32[19]{0:T(128)S(1)}, u32[]{:S(2)}, u32[]{:S(2)}) collective-permute-start(f32[19]{0:T(128)S(1)} %add.138), channel_id=1, source_target_pairs={{0,1},{1,0},{2,3},{3,2},{4,5},{5,4},{6,7},{7,6},{8,9},{9,8},{10,11... | collective-permute-start | bytes 236 | tf_op jit(solution)/shard_map/ppermute | solution.py:98
  60.3 6.2 %collective-permute-start.10 = (f32[19]{0:T(128)S(1)}, f32[19]{0:T(128)S(1)}, u32[]{:S(2)}, u32[]{:S(2)}) collective-permute-start(f32[19]{0:T(128)S(1)} %add.139), channel_id=1, source_target_pairs={{0,2},{1,3},{2,0},{3,1},{4,6},{5,7},{6,4},{7,5},{8,10},{9,11},{10,... | collective-permute-start | bytes 236 | tf_op jit(solution)/shard_map/ppermute | solution.py:98
  66.6 7.4 %collective-permute-start.11 = (f32[19]{0:T(128)S(1)}, f32[19]{0:T(128)S(1)}, u32[]{:S(2)}, u32[]{:S(2)}) collective-permute-start(f32[19]{0:T(128)S(1)} %add.140), channel_id=1, source_target_pairs={{0,4},{1,5},{2,6},{3,7},{4,0},{5,1},{6,2},{7,3},{8,12},{9,13},{10,... | collective-permute-start | bytes 236 | tf_op jit(solution)/shard_map/ppermute | solution.py:98
  74.0 5.9 %collective-permute-start.12 = (f32[4,4,8,128]{3,2,1,0:T(8,128)S(1)}, f32[4,4,8,128]{3,2,1,0:T(8,128)S(1)}, u32[]{:S(2)}, u32[]{:S(2)}) collective-permute-start(f32[4,4,8,128]{3,2,1,0:T(8,128)S(1)} %select_maximum_fusion), channel_id=1, source_target_pairs={{0,128},{128,0},{1,129},{129,1},{2,130},{130,2},{3,131},{131,3},{4... | collective-permute-start | bytes 196616 | tf_op jit(solution)/shard_map/ppermute | solution.py:201
  (24 other events, 16.2 us)

commit v3 on v2

--- a/solution.py
+++ b/solution.py
@@ -80,17 +80,23 @@
     from_low = jnp.concatenate([low, field[:, :, : size_y - 1, :]], axis=2)
     from_high = jnp.concatenate([field[:, :, 1:, :], high], axis=2)
     field = jnp.where(move_y > 0, from_low, jnp.where(move_y < 0, from_high, field))
-    low = lax.ppermute(field[:, :, :, size_z - 1 :], "gz", ring("gz", 1))
-    high = lax.ppermute(field[:, :, :, :1], "gz", ring("gz", -1))
-    from_low = jnp.concatenate([low, field[:, :, :, : size_z - 1]], axis=3)
-    from_high = jnp.concatenate([field[:, :, :, 1:], high], axis=3)
+    low = lax.ppermute(field[:, :, :, size_z - 1], "gz", ring("gz", 1))
+    high = lax.ppermute(field[:, :, :, 0], "gz", ring("gz", -1))
+    lane = lax.broadcasted_iota(jnp.int32, field.shape, 3)
+    from_low = jnp.where(lane == 0, low[..., None], jnp.roll(field, 1, axis=3))
+    from_high = jnp.where(lane == size_z - 1, high[..., None], jnp.roll(field, -1, axis=3))
     field = jnp.where(move_z > 0, from_low, jnp.where(move_z < 0, from_high, field))
     from_low = jnp.roll(field, 1, axis=1)
     from_high = jnp.roll(field, -1, axis=1)
     return jnp.where(move_x > 0, from_low, jnp.where(move_x < 0, from_high, field))
 
 
-def butterfly_sum(values, axes):
+def reverse_pairs(rows, opposite):
+    return jnp.concatenate([rows[int(o) : int(o) + 1] for o in opposite])
+
+
+def butterfly_sum(values, axes, deferred):
+    round_index = 0
     for axis in axes:
         count = lax.axis_size(axis)
         step = 1
@@ -99,6 +105,9 @@
                 values, axis, [(i, i ^ step) for i in range(count)]
             )
             step *= 2
+            if round_index < len(deferred):
+                values = deferred[round_index](values)
+            round_index += 1
     return values
 
 
@@ -129,7 +138,7 @@
     species_eq = factor[None] * concentration[:, None]
     species_gap = grouped - species_eq
     species_relaxed = grouped - species_r * species_gap
-    species_bounce = grouped[:, opposite[:7]]
+    species_bounce = jnp.swapaxes(reverse_pairs(jnp.swapaxes(grouped, 0, 1), opposite[:7]), 0, 1)
     species_post = jnp.where(fluid[None], species_relaxed, species_bounce).reshape(populations.shape)
 
     q_table = jnp.asarray(ortho, jnp.float32)
@@ -141,7 +150,7 @@
     equilibrium = density[None] * poly
     moments = jnp.einsum("ji,jxyz->ixyz", q_table, flow - equilibrium, precision=highest)
     flow_relaxed = flow - jnp.einsum("ij,jxyz->ixyz", q_table, relax * moments, precision=highest)
-    flow_post = jnp.where(fluid, flow_relaxed, flow[opposite])
+    flow_post = jnp.where(fluid, flow_relaxed, reverse_pairs(flow, opposite))
     filler = jnp.zeros((rows - 19,) + populations.shape[1:], jnp.float32)
     post = jnp.where(is_flow, jnp.concatenate([flow_post, filler]), species_post)
 
@@ -157,57 +166,70 @@
     moved = jnp.where(is_flow, jnp.concatenate([moved[:19], filler]), moved)
 
     back_species = returned.reshape(grouped.shape)
-    weighted_back = back_species * small_weights[None]
-    species_motion_grad = 4.0 * jnp.sum(
-        species_r * concentration[:, None] * jnp.stack(
-            [jnp.sum(weighted_back * sx, 1), jnp.sum(weighted_back * sy, 1), jnp.sum(weighted_back * sz, 1)], 1
-        ),
-        0,
-    )
-    species_motion_grad = jnp.where(fluid, species_motion_grad, 0.0)
-    species_t = jnp.sum(back_species * factor[None], 1)
-    species_grad_fluid = (1.0 - species_r) * back_species + species_r * species_t[:, None]
-    species_grad = jnp.where(
-        fluid[None], species_grad_fluid, back_species[:, opposite[:7]]
-    ).reshape(populations.shape)
+    back_flow = returned[:19]
     species_rate_grad = -jnp.sum(
         jnp.where(fluid[None], back_species * species_gap, 0.0), axis=(1, 2, 3, 4)
     )
-
-    back_flow = returned[:19]
     back_moments = jnp.einsum("ji,jxyz->ixyz", q_table, back_flow, precision=highest)
-    through_eq = jnp.einsum("ij,jxyz->ixyz", q_table, relax * back_moments, precision=highest)
     flow_rate_grad = -jnp.sum(
         jnp.where(fluid, back_moments * moments, 0.0)[4:], axis=(1, 2, 3)
     )
-    density_grad = jnp.sum(through_eq * poly, 0)
-    hw = through_eq * w
-    hw_sum = jnp.sum(hw, 0)
-    hwp = hw * (3.0 + 9.0 * projected)
-    motion_grad = density[None] * (
-        jnp.stack([jnp.sum(hwp * vx, 0), jnp.sum(hwp * vy, 0), jnp.sum(hwp * vz, 0)])
-        - 3.0 * motion * hw_sum[None]
-    )
-
     local_rates = jnp.where(
         is_flow,
         jnp.concatenate([flow_rate_grad, jnp.zeros((groups,), jnp.float32)]),
         jnp.concatenate([jnp.zeros((15,), jnp.float32), species_rate_grad]),
     )
-    partial_rates = butterfly_sum(local_rates, ("gy", "gz"))
+
+    later = {}
+
+    def flow_adjoint(values):
+        values, (back_flow_, back_moments_) = lax.optimization_barrier(
+            (values, (back_flow, back_moments))
+        )
+        through_eq = jnp.einsum("ij,jxyz->ixyz", q_table, relax * back_moments_, precision=highest)
+        density_grad = jnp.sum(through_eq * poly, 0)
+        hw = through_eq * w
+        hw_sum = jnp.sum(hw, 0)
+        hwp = hw * (3.0 + 9.0 * projected)
+        later["motion_grad"] = density[None] * (
+            jnp.stack([jnp.sum(hwp * vx, 0), jnp.sum(hwp * vy, 0), jnp.sum(hwp * vz, 0)])
+            - 3.0 * motion * hw_sum[None]
+        )
+        later["flow_base"] = back_flow_ - through_eq + density_grad[None]
+        return values
+
+    def species_adjoint(values):
+        values, back = lax.optimization_barrier((values, back_species))
+        weighted_back = back * small_weights[None]
+        species_motion_grad = 4.0 * jnp.sum(
+            species_r * concentration[:, None] * jnp.stack(
+                [jnp.sum(weighted_back * sx, 1), jnp.sum(weighted_back * sy, 1), jnp.sum(weighted_back * sz, 1)], 1
+            ),
+            0,
+        )
+        later["species_motion_grad"] = jnp.where(fluid, species_motion_grad, 0.0)
+        species_t = jnp.sum(back * factor[None], 1)
+        species_grad_fluid = (1.0 - species_r) * back + species_r * species_t[:, None]
+        bounced = jnp.swapaxes(reverse_pairs(jnp.swapaxes(back, 0, 1), opposite[:7]), 0, 1)
+        later["species_grad"] = jnp.where(fluid[None], species_grad_fluid, bounced).reshape(
+            populations.shape
+        )
+        return values
+
+    partial_rates = butterfly_sum(local_rates, ("gy", "gz"), [flow_adjoint, species_adjoint])
     plane = populations.shape[1:]
     rate_plane = jnp.zeros(plane, jnp.float32).at[0, 0, : partial_rates.shape[0]].set(partial_rates)
-    payload = jnp.concatenate([species_motion_grad, rate_plane[None]])
+    payload = jnp.concatenate([later["species_motion_grad"], rate_plane[None]])
     other = lax.ppermute(payload, "sec", [(0, 1), (1, 0)])
     rate_grad = partial_rates + other[3, 0, 0, : partial_rates.shape[0]]
 
-    motion_grad = jnp.where(fluid, motion_grad + other[:3], 0.0)
+    motion_grad = jnp.where(fluid, later["motion_grad"] + other[:3], 0.0)
     along = vx * motion_grad[0][None] + vy * motion_grad[1][None] + vz * motion_grad[2][None]
     extra = (along - jnp.sum(motion * motion_grad, 0)[None]) / density[None]
     flow_grad = jnp.where(
-        fluid, back_flow - through_eq + density_grad[None] + extra, back_flow[opposite]
-    )
-    grad_rows = jnp.where(is_flow, jnp.concatenate([flow_grad, filler]), species_grad)
+        fluid, later["flow_base"] + extra, reverse_pairs(back_flow, opposite)
+    )
+    grad_rows = jnp.where(is_flow, jnp.concatenate([flow_grad, filler]), later["species_grad"])
     return (moved, grad_rows, rate_grad)
 
 

time: 84.9 us -> 71.5 us (0.84)
  local copies, waits for them, and re-layouts: 21.8 us -> 9.47 us
  other arithmetic: 9.84 us -> 6.36 us
  starting transfers between devices: 26.8 us -> 29.9 us
    unnamed x90 -> x58, local copies, waits for them, and re-layouts: 9.87 us -> 6.49 us
    slice x5 -> x4, local copies, waits for them, and re-layouts: 4.34 us -> 1.43 us  [the longest x1 0.81 us: shift_rows(): low = lax.ppermute(field[:, :, :, size_z - 1], 'gz', ring('gz', 1))]
    ppermute x1, starting transfers between devices: 0.09 us -> 2.97 us  [per_device(): other = lax.ppermute(payload, 'sec', [(0, 1), (1, 0)])]
    ppermute x2 -> x0, local copies, waits for them, and re-layouts: 2.66 us -> none  [the longest x1 1.36 us: shift_rows(): low = lax.ppermute(field[:, :, :, size_z - 1:], 'gz', ring('gz', 1))]
    gather x6 -> x0, local copies, waits for them, and re-layouts: 2.35 us -> none  [the longest x2 0.61 us: per_device(): species_bounce = grouped[:, opposite[:7]]]
    ppermute x2, waiting for transfers between devices: 1.05 us -> 3.32 us  [the longest x1 1.92 us: shift_rows(): high = lax.ppermute(field[:, :, :, 0], 'gz', ring('gz', -1))]
    ppermute x1, waiting for transfers between devices: 4.15 us -> 2.74 us  [per_device(): other = lax.ppermute(payload, 'sec', [(0, 1), (1, 0)])]
    mul x4 -> x0, local copies, waits for them, and re-layouts: 1.34 us -> none  [the longest x2 0.67 us: per_device(): (1.0 - species_r) * back_species + species_r * species_t[:, None]]
  transfers between devices with their start and end apart: 13 -> 13, of which waited for: 10 -> 10; matrix products, arithmetic and copies ran while one was open for 13% -> 7% of each run, Pallas kernels for 0% -> 0%
where the time goes in v3:
time: 71.5 us; the launch traced here: 71.2 us
  starting transfers between devices  29.9 us (42%)
  waiting for transfers between devices  21.9 us (31%)
  local copies, waits for them, and re-layouts  9.47 us (13%)
  other arithmetic  6.36 us (9%)
  matrix products  2.34 us (3%)
  between operations  1.27 us (2%)
    ppermute x7, starting transfers between devices, butterfly_sum(): lax.ppermute(values, axis, [(i, i ^ step) for i in range(count)])  15.9 us
    ppermute x7, waiting for transfers between devices, butterfly_sum(): lax.ppermute(values, axis, [(i, i ^ step) for i in range(count)])  13.4 us
    unnamed x58, local copies, waits for them, and re-layouts  6.49 us
    ppermute x1, starting transfers between devices, per_device(): sent_motion = lax.ppermute(own_motion, 'sec', [(0, 1)])  4.93 us
    ppermute x1, starting transfers between devices, shift_rows(): high = lax.ppermute(field[:, :, :1, :], 'gy', ring('gy', -1))  3.84 us
    ppermute x1, starting transfers between devices, per_device(): other = lax.ppermute(payload, 'sec', [(0, 1), (1, 0)])  2.97 us
    ppermute x1, waiting for transfers between devices, per_device(): other = lax.ppermute(payload, 'sec', [(0, 1), (1, 0)])  2.74 us
    ppermute x1, waiting for transfers between devices, shift_rows(): low = lax.ppermute(field[:, :, size_y - 1:, :], 'gy', ring('gy', 1))  2.36 us
  transfers between devices with their start and end apart: 13, of which 10 were waited for; matrix products, arithmetic and copies ran while one was open for 7% of the time, Pallas kernels for 0%

profile of v3, /device:TPU:32, one launch (start us, length us, event | category | flops | bytes accessed | tf_op | source)
XLA Modules:
  0.0 71.2 jit_solution(14677556068627253841)
XLA Ops:
  0.7 1.3 %copy.83 = f32[28,4,8,128]{3,0,2,1:T(8,128)S(1)} copy(f32[28,4,8,128]{3,2,1,0:T(8,128)} %param.22) | data formatting | bytes 917504 | tf_op args[0]
  2.4 4.9 %collective-permute-start = (f32[3,4,8,128]{3,2,1,0:T(8,128)S(1)}, f32[3,4,8,128]{3,2,1,0:T(8,128)S(1)}, u32[]{:S(2)}, u32[]{:S(2)}) collective-permute-start(f32[3,4,8,128]{3,2,1,0:T(8,128)S(1)} %maximum_divide_fusion), channel_id=1, source_target_pairs={{0,128},{1,129},{2,130},{3,131},{4,132},{5,133},{6,134},{7,135},{8... | collective-permute-start | bytes 147464 | tf_op jit(solution)/shard_map/ppermute | solution.py:128
  7.4 0.7 copy-done.3
  10.1 0.7 copy-done.2
  10.7 0.7 fusion.18
  11.5 0.6 fusion.1
  12.9 3.8 %collective-permute-start.2 = (f32[56,4,1,128]{3,0,2,1:T(8,128)S(1)}, f32[56,4,1,128]{3,0,2,1:T(8,128)S(1)}, u32[]{:S(2)}, u32[]{:S(2)}) collective-permute-start(f32[56,4,1,128]{3,0,2,1:T(8,128)S(1)} %get-tuple-element.53), channel_id=1, source_target_pairs={{0,120},{8,0},{16,8},{24,16},{32,24},{40,32},{48,40},{56,48},{64,5... | collective-permute-start | bytes 344072 | tf_op jit(solution)/shard_map/ppermute | solution.py:79
  16.8 2.4 %collective-permute-done.1 = f32[56,4,1,128]{3,0,2,1:T(8,128)S(1)} collective-permute-done((f32[56,4,1,128]{3,0,2,1:T(8,128)S(1)}, f32[56,4,1,128]{3,0,2,1:T(8,128)S(1)}, u32[]{:S(2)}, u32[]{:S(2)}) %collective-permute-start.1) | collective-permute-done | bytes 114720 | tf_op jit(solution)/shard_map/ppermute | solution.py:78
  19.5 0.8 %slice_reduce_fusion.2 = (f32[56,4,8]{0,2,1:T(8,128)S(1)}, f32[56,4,8]{0,2,1:T(8,128)S(1)}, f32[56,4,8,1]{3,0,2,1:T(8,128)S(1)}, f32[56,4,8,1]{3,0,2,1:T(8,128)S(1)}) fusion(f32[56,4,8,128]{3,0,2,1:T(8,128)S(1)} %fusion.3), kind=kLoop, calls=%fused_computation.162 | loop fusion | bytes 43008 | tf_op jit(solution)/shard_map/slice | solution.py:83
  20.3 2.0 %collective-permute-start.3 = (f32[56,4,8]{0,2,1:T(8,128)S(1)}, f32[56,4,8]{0,2,1:T(8,128)S(1)}, u32[]{:S(2)}, u32[]{:S(2)}) collective-permute-start(f32[56,4,8]{0,2,1:T(8,128)S(1)} %get-tuple-element.34), channel_id=1, source_target_pairs={{0,1},{1,2},{2,3},{3,4},{4,5},{5,6},{6,7},{7,0},{8,9},{9,10},{10,1... | collective-permute-start | bytes 21512 | tf_op jit(solution)/shard_map/ppermute | solution.py:83
  22.7 1.4 %collective-permute-done.3 = f32[56,4,8]{0,2,1:T(8,128)S(1)} collective-permute-done((f32[56,4,8]{0,2,1:T(8,128)S(1)}, f32[56,4,8]{0,2,1:T(8,128)S(1)}, u32[]{:S(2)}, u32[]{:S(2)}) %collective-permute-start.3) | collective-permute-done | bytes 7200 | tf_op jit(solution)/shard_map/ppermute | solution.py:83
  24.1 1.9 %collective-permute-done.4 = f32[56,4,8]{0,2,1:T(8,128)S(1)} collective-permute-done((f32[56,4,8]{0,2,1:T(8,128)S(1)}, f32[56,4,8]{0,2,1:T(8,128)S(1)}, u32[]{:S(2)}, u32[]{:S(2)}) %collective-permute-start.4) | collective-permute-done | bytes 7200 | tf_op jit(solution)/shard_map/ppermute | solution.py:84
  26.0 1.2 %fusion.4 = f32[56,4,8,128]{3,0,2,1:T(8,128)S(1)} fusion(f32[56,4,8,127]{3,0,2,1:T(8,128)S(1)} %get-tuple-element.84, f32[56,4,8,1]{3,0,2,1:T(8,128)S(1)} %get-tuple-element.82, f32[56,4,8,128]{3,0,2,1:T(8,128)S(1)} %fusion.3, f32[56,4,8,1]{3,0,2,1:T(8,128)S(1)} %get-tuple-element.81, f32[56,4,8,127]{3,0,2,1:T(8,128)S(1)} %get-tuple-element.83, ...), kind=kLoop, calls=%fused_computation.15 | loop fusion | flops 1376256 | bytes 3684720 | tf_op jit(solution)/shard_map/jit(_where)/select_n | solution.py:88
  28.6 0.6 copy-done.12
  29.2 0.8 %fusion.70 = (f32[28,4,8,128]{3,0,2,1:T(8,128)S(1)}, f32[28]{0:T(128)S(1)}, f32[28,4,8,128]{3,0,2,1:T(8,128)S(1)}) fusion(f32[56,4,8,128]{3,0,2,1:T(8,128)S(1)} %maximum_select_fusion.2, f32[28,4,8,128]{3,2,1,0:T(8,128)S(1)} %bitcast.96, f32[28,4,8,128]{3,2,1,0:T(8,128)S(1)} %copy-done, pred[4,8,128]{2,1,0:T(8,128)(4,1)S(1)} %broadcast_compare_fusion, ...), kind=kLoop, calls=%fused_computation.164 | loop fusion | flops 688100 | bytes 2756749 | tf_op jit(solution)/shard_map/slice | solution.py:165
  30.8 1.0 %copy.111 = f32[28,4,8,128]{3,2,1,0:T(8,128)} copy(f32[28,4,8,128]{3,0,2,1:T(8,128)S(1)} %get-tuple-element.76) | data formatting | bytes 917504
  32.4 0.8 %collective-permute-start.6 = (f32[19]{0:T(128)S(1)}, f32[19]{0:T(128)S(1)}, u32[]{:S(2)}, u32[]{:S(2)}) collective-permute-start(f32[19]{0:T(128)S(1)} %add.117), channel_id=1, source_target_pairs={{0,16},{8,24},{16,0},{24,8},{32,48},{40,56},{48,32},{56,40},{64,80... | collective-permute-start | bytes 236 | tf_op jit(solution)/shard_map/ppermute | solution.py:104
  33.1 0.6 add_multiply_fusion
  34.3 1.6 %collective-permute-done.6 = f32[19]{0:T(128)S(1)} collective-permute-done((f32[19]{0:T(128)S(1)}, f32[19]{0:T(128)S(1)}, u32[]{:S(2)}, u32[]{:S(2)}) %collective-permute-start.6) | collective-permute-done | bytes 108 | tf_op jit(solution)/shard_map/ppermute | solution.py:104
  36.3 1.6 %collective-permute-start.7 = (f32[19]{0:T(128)S(1)}, f32[19]{0:T(128)S(1)}, u32[]{:S(2)}, u32[]{:S(2)}) collective-permute-start(f32[19]{0:T(128)S(1)} %add.121), channel_id=1, source_target_pairs={{0,32},{8,40},{16,48},{24,56},{32,0},{40,8},{48,16},{56,24},{64,96... | collective-permute-start | bytes 236 | tf_op jit(solution)/shard_map/ppermute | solution.py:104
  37.9 2.0 %collective-permute-done.7 = f32[19]{0:T(128)S(1)} collective-permute-done((f32[19]{0:T(128)S(1)}, f32[19]{0:T(128)S(1)}, u32[]{:S(2)}, u32[]{:S(2)}) %collective-permute-start.7) | collective-permute-done | bytes 108 | tf_op jit(solution)/shard_map/ppermute | solution.py:104
  39.9 3.1 %collective-permute-start.8 = (f32[19]{0:T(128)S(1)}, f32[19]{0:T(128)S(1)}, u32[]{:S(2)}, u32[]{:S(2)}) collective-permute-start(f32[19]{0:T(128)S(1)} %add.122), channel_id=1, source_target_pairs={{0,64},{8,72},{16,80},{24,88},{32,96},{40,104},{48,112},{56,120},{... | collective-permute-start | bytes 236 | tf_op jit(solution)/shard_map/ppermute | solution.py:104
  43.0 2.0 %collective-permute-done.8 = f32[19]{0:T(128)S(1)} collective-permute-done((f32[19]{0:T(128)S(1)}, f32[19]{0:T(128)S(1)}, u32[]{:S(2)}, u32[]{:S(2)}) %collective-permute-start.8) | collective-permute-done | bytes 108 | tf_op jit(solution)/shard_map/ppermute | solution.py:104
  45.0 2.0 %collective-permute-start.9 = (f32[19]{0:T(128)S(1)}, f32[19]{0:T(128)S(1)}, u32[]{:S(2)}, u32[]{:S(2)}) collective-permute-start(f32[19]{0:T(128)S(1)} %add.123), channel_id=1, source_target_pairs={{0,1},{1,0},{2,3},{3,2},{4,5},{5,4},{6,7},{7,6},{8,9},{9,8},{10,11... | collective-permute-start | bytes 236 | tf_op jit(solution)/shard_map/ppermute | solution.py:104
  47.0 1.5 %collective-permute-done.9 = f32[19]{0:T(128)S(1)} collective-permute-done((f32[19]{0:T(128)S(1)}, f32[19]{0:T(128)S(1)}, u32[]{:S(2)}, u32[]{:S(2)}) %collective-permute-start.9) | collective-permute-done | bytes 108 | tf_op jit(solution)/shard_map/ppermute | solution.py:104
  48.5 5.7 %collective-permute-start.10 = (f32[19]{0:T(128)S(1)}, f32[19]{0:T(128)S(1)}, u32[]{:S(2)}, u32[]{:S(2)}) collective-permute-start(f32[19]{0:T(128)S(1)} %add.124), channel_id=1, source_target_pairs={{0,2},{1,3},{2,0},{3,1},{4,6},{5,7},{6,4},{7,5},{8,10},{9,11},{10,... | collective-permute-start | bytes 236 | tf_op jit(solution)/shard_map/ppermute | solution.py:104
  54.2 1.5 %collective-permute-done.10 = f32[19]{0:T(128)S(1)} collective-permute-done((f32[19]{0:T(128)S(1)}, f32[19]{0:T(128)S(1)}, u32[]{:S(2)}, u32[]{:S(2)}) %collective-permute-start.10) | collective-permute-done | bytes 108 | tf_op jit(solution)/shard_map/ppermute | solution.py:104
  55.7 2.6 %collective-permute-start.11 = (f32[19]{0:T(128)S(1)}, f32[19]{0:T(128)S(1)}, u32[]{:S(2)}, u32[]{:S(2)}) collective-permute-start(f32[19]{0:T(128)S(1)} %add.125), channel_id=1, source_target_pairs={{0,4},{1,5},{2,6},{3,7},{4,0},{5,1},{6,2},{7,3},{8,12},{9,13},{10,... | collective-permute-start | bytes 236 | tf_op jit(solution)/shard_map/ppermute | solution.py:104
  58.3 4.8 %collective-permute-done.11 = f32[19]{0:T(128)S(1)} collective-permute-done((f32[19]{0:T(128)S(1)}, f32[19]{0:T(128)S(1)}, u32[]{:S(2)}, u32[]{:S(2)}) %collective-permute-start.11) | collective-permute-done | bytes 108 | tf_op jit(solution)/shard_map/ppermute | solution.py:104
  63.2 3.0 %collective-permute-start.12 = (f32[4,4,8,128]{3,2,1,0:T(8,128)S(1)}, f32[4,4,8,128]{3,2,1,0:T(8,128)S(1)}, u32[]{:S(2)}, u32[]{:S(2)}) collective-permute-start(f32[4,4,8,128]{3,2,1,0:T(8,128)S(1)} %select_maximum_fusion), channel_id=1, source_target_pairs={{0,128},{128,0},{1,129},{129,1},{2,130},{130,2},{3,131},{131,3},{4... | collective-permute-start | bytes 196616 | tf_op jit(solution)/shard_map/ppermute | solution.py:223
  66.3 2.7 %collective-permute-done.12 = f32[4,4,8,128]{3,2,1,0:T(8,128)S(1)} collective-permute-done((f32[4,4,8,128]{3,2,1,0:T(8,128)S(1)}, f32[4,4,8,128]{3,2,1,0:T(8,128)S(1)}, u32[]{:S(2)}, u32[]{:S(2)}) %collective-permute-start.12) | collective-permute-done | bytes 65568 | tf_op jit(solution)/shard_map/ppermute | solution.py:223
  69.6 1.0 %copy.112 = f32[28,4,8,128]{3,2,1,0:T(8,128)} copy(f32[28,4,8,128]{3,0,2,1:T(8,128)S(1)} %copy_select_fusion) | data formatting | bytes 917504
  (119 shorter events, 8.6 us)
Async XLA Ops:
  0.6 1.3 %copy-start.4 = (f32[19]{0:T(128)S(1)}, f32[19]{0:T(128)}, u32[]{:S(2)}) copy-start(f32[19]{0:T(128)} %constant.126) | copy-start | bytes 232
  0.6 1.3 %copy-start.5 = (f32[19]{0:T(128)S(1)}, f32[19]{0:T(128)}, u32[]{:S(2)}) copy-start(f32[19]{0:T(128)} %constant.127) | copy-start | bytes 232
  0.7 1.3 %copy-start.6 = (f32[19]{0:T(128)S(1)}, f32[19]{0:T(128)}, u32[]{:S(2)}) copy-start(f32[19]{0:T(128)} %constant.128) | copy-start | bytes 232
  2.0 5.3 %copy-start = (f32[28,4,8,128]{3,2,1,0:T(8,128)S(1)}, f32[28,4,8,128]{3,2,1,0:T(8,128)}, u32[]{:S(2)}) copy-start(f32[28,4,8,128]{3,2,1,0:T(8,128)} %param.22) | copy-start | bytes 1376260
  2.4 7.6 %collective-permute-start = (f32[3,4,8,128]{3,2,1,0:T(8,128)S(1)}, f32[3,4,8,128]{3,2,1,0:T(8,128)S(1)}, u32[]{:S(2)}, u32[]{:S(2)}) collective-permute-start(f32[3,4,8,128]{3,2,1,0:T(8,128)S(1)} %maximum_divide_fusion), channel_id=1, source_target_pairs={{0,128},{1,129},{2,130},{3,131},{4,132},{5,133},{6,134},{7,135},{8... | collective-permute-start | bytes 147464 | tf_op jit(solution)/shard_map/ppermute | solution.py:128
  7.3 0.7 %copy-start.3 = (s32[4,8,128]{2,1,0:T(8,128)S(1)}, s32[4,8,128]{2,1,0:T(8,128)}, u32[]{:S(2)}) copy-start(s32[4,8,128]{2,1,0:T(8,128)} %param.23) | copy-start | bytes 49156
  8.1 0.7 copy-start.17
  8.1 0.7 copy-start.18
  8.1 0.7 %copy-start.13 = (f32[28,1,1,1]{0,3,2,1:T(1,128)S(1)}, f32[28,1,1,1]{0,3,2,1:T(1,128)}, u32[]{:S(2)}) copy-start(f32[28,1,1,1]{0,3,2,1:T(1,128)} %constant.104.clone) | copy-start | bytes 340
  8.1 0.7 %copy-start.14 = (f32[28,1,1,1]{0,3,2,1:T(1,128)S(1)}, f32[28,1,1,1]{0,3,2,1:T(1,128)}, u32[]{:S(2)}) copy-start(f32[28,1,1,1]{0,3,2,1:T(1,128)} %constant.105.clone) | copy-start | bytes 340
  8.1 0.7 %copy-start.15 = (f32[28,1,1,1]{0,3,2,1:T(1,128)S(1)}, f32[28,1,1,1]{0,3,2,1:T(1,128)}, u32[]{:S(2)}) copy-start(f32[28,1,1,1]{0,3,2,1:T(1,128)} %constant.108.clone) | copy-start | bytes 340
  8.2 0.7 %copy-start.16 = (f32[28,1,1,1]{0,3,2,1:T(1,128)S(1)}, f32[28,1,1,1]{0,3,2,1:T(1,128)}, u32[]{:S(2)}) copy-start(f32[28,1,1,1]{0,3,2,1:T(1,128)} %constant.109.clone) | copy-start | bytes 340
  8.2 0.9 %copy-start.19 = (f32[15]{0:T(128)S(1)}, f32[15]{0:T(128)}, u32[]{:S(2)}) copy-start(f32[15]{0:T(128)} %param.24) | copy-start | bytes 184
  8.2 1.0 %copy-start.1 = (f32[28,4,8,128]{3,2,1,0:T(8,128)S(1)}, f32[28,4,8,128]{3,2,1,0:T(8,128)}, u32[]{:S(2)}) copy-start(f32[28,4,8,128]{3,2,1,0:T(8,128)} %param.26) | copy-start | bytes 1376260
  10.0 0.7 copy-start.2
  10.1 0.7 copy-start.20
  11.4 0.7 copy-start.8
  11.5 0.7 copy-start.9
  11.5 0.7 copy-start.10
  11.5 0.7 copy-start.11
  12.8 6.4 %collective-permute-start.1 = (f32[56,4,1,128]{3,0,2,1:T(8,128)S(1)}, f32[56,4,1,128]{3,0,2,1:T(8,128)S(1)}, u32[]{:S(2)}, u32[]{:S(2)}) collective-permute-start(f32[56,4,1,128]{3,0,2,1:T(8,128)S(1)} %get-tuple-element.54), channel_id=1, source_target_pairs={{0,8},{8,16},{16,24},{24,32},{32,40},{40,48},{48,56},{56,64},{64,7... | collective-permute-start | bytes 344072 | tf_op jit(solution)/shard_map/ppermute | solution.py:78
  12.9 6.3 %collective-permute-start.2 = (f32[56,4,1,128]{3,0,2,1:T(8,128)S(1)}, f32[56,4,1,128]{3,0,2,1:T(8,128)S(1)}, u32[]{:S(2)}, u32[]{:S(2)}) collective-permute-start(f32[56,4,1,128]{3,0,2,1:T(8,128)S(1)} %get-tuple-element.53), channel_id=1, source_target_pairs={{0,120},{8,0},{16,8},{24,16},{32,24},{40,32},{48,40},{56,48},{64,5... | collective-permute-start | bytes 344072 | tf_op jit(solution)/shard_map/ppermute | solution.py:79
  20.3 3.8 %collective-permute-start.3 = (f32[56,4,8]{0,2,1:T(8,128)S(1)}, f32[56,4,8]{0,2,1:T(8,128)S(1)}, u32[]{:S(2)}, u32[]{:S(2)}) collective-permute-start(f32[56,4,8]{0,2,1:T(8,128)S(1)} %get-tuple-element.34), channel_id=1, source_target_pairs={{0,1},{1,2},{2,3},{3,4},{4,5},{5,6},{6,7},{7,0},{8,9},{9,10},{10,1... | collective-permute-start | bytes 21512 | tf_op jit(solution)/shard_map/ppermute | solution.py:83
  22.3 3.7 %collective-permute-start.4 = (f32[56,4,8]{0,2,1:T(8,128)S(1)}, f32[56,4,8]{0,2,1:T(8,128)S(1)}, u32[]{:S(2)}, u32[]{:S(2)}) collective-permute-start(f32[56,4,8]{0,2,1:T(8,128)S(1)} %get-tuple-element.35), channel_id=1, source_target_pairs={{0,7},{1,0},{2,1},{3,2},{4,3},{5,4},{6,5},{7,6},{8,15},{9,8},{10,9... | collective-permute-start | bytes 21512 | tf_op jit(solution)/shard_map/ppermute | solution.py:84
  30.3 2.0 %collective-permute-start.5 = (f32[19]{0:T(128)S(1)}, f32[19]{0:T(128)S(1)}, u32[]{:S(2)}, u32[]{:S(2)}) collective-permute-start(f32[19]{0:T(128)S(1)} %broadcast_select_fusion.1), channel_id=1, source_target_pairs={{0,8},{8,0},{16,24},{24,16},{32,40},{40,32},{48,56},{56,48},{64,72... | collective-permute-start | bytes 236 | tf_op jit(solution)/shard_map/ppermute | solution.py:104
  32.4 3.6 %collective-permute-start.6 = (f32[19]{0:T(128)S(1)}, f32[19]{0:T(128)S(1)}, u32[]{:S(2)}, u32[]{:S(2)}) collective-permute-start(f32[19]{0:T(128)S(1)} %add.117), channel_id=1, source_target_pairs={{0,16},{8,24},{16,0},{24,8},{32,48},{40,56},{48,32},{56,40},{64,80... | collective-permute-start | bytes 236 | tf_op jit(solution)/shard_map/ppermute | solution.py:104
  36.3 3.6 %collective-permute-start.7 = (f32[19]{0:T(128)S(1)}, f32[19]{0:T(128)S(1)}, u32[]{:S(2)}, u32[]{:S(2)}) collective-permute-start(f32[19]{0:T(128)S(1)} %add.121), channel_id=1, source_target_pairs={{0,32},{8,40},{16,48},{24,56},{32,0},{40,8},{48,16},{56,24},{64,96... | collective-permute-start | bytes 236 | tf_op jit(solution)/shard_map/ppermute | solution.py:104
  39.9 5.0 %collective-permute-start.8 = (f32[19]{0:T(128)S(1)}, f32[19]{0:T(128)S(1)}, u32[]{:S(2)}, u32[]{:S(2)}) collective-permute-start(f32[19]{0:T(128)S(1)} %add.122), channel_id=1, source_target_pairs={{0,64},{8,72},{16,80},{24,88},{32,96},{40,104},{48,112},{56,120},{... | collective-permute-start | bytes 236 | tf_op jit(solution)/shard_map/ppermute | solution.py:104
  45.0 3.5 %collective-permute-start.9 = (f32[19]{0:T(128)S(1)}, f32[19]{0:T(128)S(1)}, u32[]{:S(2)}, u32[]{:S(2)}) collective-permute-start(f32[19]{0:T(128)S(1)} %add.123), channel_id=1, source_target_pairs={{0,1},{1,0},{2,3},{3,2},{4,5},{5,4},{6,7},{7,6},{8,9},{9,8},{10,11... | collective-permute-start | bytes 236 | tf_op jit(solution)/shard_map/ppermute | solution.py:104
  48.5 7.2 %collective-permute-start.10 = (f32[19]{0:T(128)S(1)}, f32[19]{0:T(128)S(1)}, u32[]{:S(2)}, u32[]{:S(2)}) collective-permute-start(f32[19]{0:T(128)S(1)} %add.124), channel_id=1, source_target_pairs={{0,2},{1,3},{2,0},{3,1},{4,6},{5,7},{6,4},{7,5},{8,10},{9,11},{10,... | collective-permute-start | bytes 236 | tf_op jit(solution)/shard_map/ppermute | solution.py:104
  55.7 7.4 %collective-permute-start.11 = (f32[19]{0:T(128)S(1)}, f32[19]{0:T(128)S(1)}, u32[]{:S(2)}, u32[]{:S(2)}) collective-permute-start(f32[19]{0:T(128)S(1)} %add.125), channel_id=1, source_target_pairs={{0,4},{1,5},{2,6},{3,7},{4,0},{5,1},{6,2},{7,3},{8,12},{9,13},{10,... | collective-permute-start | bytes 236 | tf_op jit(solution)/shard_map/ppermute | solution.py:104
  63.2 5.9 %collective-permute-start.12 = (f32[4,4,8,128]{3,2,1,0:T(8,128)S(1)}, f32[4,4,8,128]{3,2,1,0:T(8,128)S(1)}, u32[]{:S(2)}, u32[]{:S(2)}) collective-permute-start(f32[4,4,8,128]{3,2,1,0:T(8,128)S(1)} %select_maximum_fusion), channel_id=1, source_target_pairs={{0,128},{128,0},{1,129},{129,1},{2,130},{130,2},{3,131},{131,3},{4... | collective-permute-start | bytes 196616 | tf_op jit(solution)/shard_map/ppermute | solution.py:223
  (2 other events, 1.3 us)

commit v4 on v3

--- a/solution.py
+++ b/solution.py
@@ -95,25 +95,55 @@
     return jnp.concatenate([rows[int(o) : int(o) + 1] for o in opposite])
 
 
+NEAR_HALVES = {4: [3, 2, 1, 0], 8: [6, 7, 4, 5, 2, 3, 0, 1]}
+
+
+def butterfly_rounds(count, inner):
+    rounds = []
+    step = 1
+    while step < inner:
+        rounds.append([i ^ step for i in range(count)])
+        step *= 2
+    ring_size = count // inner
+    step = 1
+    while step < ring_size:
+        if 2 * step == ring_size and ring_size in NEAR_HALVES:
+            mirror = NEAR_HALVES[ring_size]
+        else:
+            mirror = [j ^ step for j in range(ring_size)]
+        rounds.append([mirror[i // inner] * inner + i % inner for i in range(count)])
+        step *= 2
+    return rounds
+
+
 def butterfly_sum(values, axes, deferred):
     round_index = 0
-    for axis in axes:
-        count = lax.axis_size(axis)
-        step = 1
-        while step < count:
-            values = values + lax.ppermute(
-                values, axis, [(i, i ^ step) for i in range(count)]
-            )
-            step *= 2
+    for axis, inner in axes:
+        for targets in butterfly_rounds(lax.axis_size(axis), inner):
+            values = values + lax.ppermute(values, axis, list(enumerate(targets)))
             if round_index < len(deferred):
                 values = deferred[round_index](values)
             round_index += 1
     return values
 
 
+def mix(table, field, scale=None):
+    rows = [field[j] if scale is None else field[j] * scale[j] for j in range(table.shape[0])]
+    out = []
+    for k in range(table.shape[1]):
+        total = None
+        for j in range(table.shape[0]):
+            weight = float(table[j, k])
+            if abs(weight) < 1e-12:
+                continue
+            term = rows[j] * weight
+            total = term if total is None else total + term
+        out.append(total if total is not None else jnp.zeros_like(rows[0]))
+    return jnp.stack(out)
+
+
 def per_device(populations, solid_mask, flow_rates, species_rates, cotangents):
     velocity, weights, opposite, ortho = lattice_tables()
-    highest = lax.Precision.HIGHEST
     rows = populations.shape[0]
     groups = rows // 7
     is_flow = lax.axis_index("sec") == 0
@@ -141,15 +171,14 @@
     species_bounce = jnp.swapaxes(reverse_pairs(jnp.swapaxes(grouped, 0, 1), opposite[:7]), 0, 1)
     species_post = jnp.where(fluid[None], species_relaxed, species_bounce).reshape(populations.shape)
 
-    q_table = jnp.asarray(ortho, jnp.float32)
-    relax = jnp.concatenate([jnp.zeros((4,), flow_rates.dtype), flow_rates]).reshape(19, 1, 1, 1)
+    relax_scalars = [0.0] * 4 + [flow_rates[k] for k in range(flow_rates.shape[0])]
     w = column(weights)
     projected = vx * motion[0][None] + vy * motion[1][None] + vz * motion[2][None]
     squared = jnp.sum(motion * motion, 0)
     poly = w * (1.0 + 3.0 * projected + 4.5 * projected * projected - 1.5 * squared[None])
     equilibrium = density[None] * poly
-    moments = jnp.einsum("ji,jxyz->ixyz", q_table, flow - equilibrium, precision=highest)
-    flow_relaxed = flow - jnp.einsum("ij,jxyz->ixyz", q_table, relax * moments, precision=highest)
+    moments = mix(ortho, flow - equilibrium)
+    flow_relaxed = flow - mix(ortho.T, moments, relax_scalars)
     flow_post = jnp.where(fluid, flow_relaxed, reverse_pairs(flow, opposite))
     filler = jnp.zeros((rows - 19,) + populations.shape[1:], jnp.float32)
     post = jnp.where(is_flow, jnp.concatenate([flow_post, filler]), species_post)
@@ -170,7 +199,7 @@
     species_rate_grad = -jnp.sum(
         jnp.where(fluid[None], back_species * species_gap, 0.0), axis=(1, 2, 3, 4)
     )
-    back_moments = jnp.einsum("ji,jxyz->ixyz", q_table, back_flow, precision=highest)
+    back_moments = mix(ortho, back_flow)
     flow_rate_grad = -jnp.sum(
         jnp.where(fluid, back_moments * moments, 0.0)[4:], axis=(1, 2, 3)
     )
@@ -186,7 +215,7 @@
         values, (back_flow_, back_moments_) = lax.optimization_barrier(
             (values, (back_flow, back_moments))
         )
-        through_eq = jnp.einsum("ij,jxyz->ixyz", q_table, relax * back_moments_, precision=highest)
+        through_eq = mix(ortho.T, back_moments_, relax_scalars)
         density_grad = jnp.sum(through_eq * poly, 0)
         hw = through_eq * w
         hw_sum = jnp.sum(hw, 0)
@@ -216,7 +245,7 @@
         )
         return values
 
-    partial_rates = butterfly_sum(local_rates, ("gy", "gz"), [flow_adjoint, species_adjoint])
+    partial_rates = butterfly_sum(local_rates, (("gy", 4), ("gz", 1)), [flow_adjoint, species_adjoint])
     plane = populations.shape[1:]
     rate_plane = jnp.zeros(plane, jnp.float32).at[0, 0, : partial_rates.shape[0]].set(partial_rates)
     payload = jnp.concatenate([later["species_motion_grad"], rate_plane[None]])

time: 71.5 us -> 279 us (3.90); the launches traced: 71.2 us -> 275 us
  other arithmetic: 6.36 us -> 211 us
  local copies, waits for them, and re-layouts: 9.47 us -> 15.8 us
  starting transfers between devices: 29.9 us -> 25.7 us
    unnamed x0 -> x71, other arithmetic: none -> 185 us
    another operation x0 -> x4, other arithmetic: none -> 13.8 us  [mix(): return jnp.stack(out)]
    unnamed x58 -> x147, local copies, waits for them, and re-layouts: 6.49 us -> 11.7 us
    ppermute x1, starting transfers between devices: 2.97 us -> 0.09 us  [per_device(): other = lax.ppermute(payload, 'sec', [(0, 1), (1, 0)])]
  transfers between devices with their start and end apart: 13 -> 13, of which waited for: 10 -> 9; matrix products, arithmetic and copies ran while one was open for 7% -> 38% of each run, Pallas kernels for 0% -> 0%
where the time goes in v4:
time: 279 us; the launch traced here: 275 us
  other arithmetic  211 us (76%)
  starting transfers between devices  25.7 us (9%)
  waiting for transfers between devices  20.5 us (7%)
  local copies, waits for them, and re-layouts  15.8 us (6%)
    unnamed x71, other arithmetic  185 us
    ppermute x7, starting transfers between devices, butterfly_sum(): values = values + lax.ppermute(values, axis, list(enumerate(targets)))  14.7 us
    another operation x4, other arithmetic, mix(): return jnp.stack(out)  13.8 us
    unnamed x147, local copies, waits for them, and re-layouts  11.7 us
    ppermute x7, waiting for transfers between devices, butterfly_sum(): values = values + lax.ppermute(values, axis, list(enumerate(targets)))  11.3 us
  transfers between devices with their start and end apart: 13, of which 9 were waited for; matrix products, arithmetic and copies ran while one was open for 38% of the time, Pallas kernels for 0%

profile of v4, /device:TPU:32, one launch (start us, length us, event | category | flops | bytes accessed | tf_op | source)
XLA Modules:
  0.0 275.3 jit_solution(14582504113095584813)
XLA Ops:
  2.4 4.9 %collective-permute-start = (f32[3,4,8,128]{3,2,1,0:T(8,128)S(1)}, f32[3,4,8,128]{3,2,1,0:T(8,128)S(1)}, u32[]{:S(2)}, u32[]{:S(2)}) collective-permute-start(f32[3,4,8,128]{3,2,1,0:T(8,128)S(1)} %maximum_divide_fusion), channel_id=1, source_target_pairs={{0,128},{1,129},{2,130},{3,131},{4,132},{5,133},{6,134},{7,135},{8... | collective-permute-start | bytes 147464 | tf_op jit(solution)/shard_map/ppermute | solution.py:158
  20.1 4.3 %constant_dynamic-update-slice_fusion.17 = (f32[19,4,8,128]{3,2,1,0:T(8,128)S(1)}, f32[1,4,8,128]{3,2,1,0:T(8,128)S(1)}) fusion(f32[19,4,8,128]{3,2,1,0:T(8,128)S(1)} %constant_dynamic-update-slice_fusion.18, f32[1,4,8,128]{3,2,1,0:T(8,128)S(1)} %get-tuple-element.64, f32[]{:T(128)} %bitcast.19, f32[1,4,8,128]{3,2,1,0:T(8,128)S(1)} %get-tuple-element.66, ...), kind=kLoop, calls=%fused_computation.66 | loop fusion | flops 98304 | bytes 180252
  24.4 4.3 %constant_dynamic-update-slice_fusion.16 = (f32[19,4,8,128]{3,2,1,0:T(8,128)S(1)}, f32[1,4,8,128]{3,2,1,0:T(8,128)S(1)}) fusion(f32[19,4,8,128]{3,2,1,0:T(8,128)S(1)} %get-tuple-element.89, f32[1,4,8,128]{3,2,1,0:T(8,128)S(1)} %get-tuple-element.64, f32[]{:T(128)} %bitcast.19, f32[1,4,8,128]{3,2,1,0:T(8,128)S(1)} %get-tuple-element.66, f32[]{:T(128)} %bitcast.18, ...), kind=kLoop, calls=%fused_computation.65 | loop fusion | flops 98304 | bytes 180252
  28.8 4.8 %constant_dynamic-update-slice_fusion.15 = f32[19,4,8,128]{3,2,1,0:T(8,128)S(1)} fusion(f32[19,4,8,128]{3,2,1,0:T(8,128)S(1)} %get-tuple-element.87, f32[1,4,8,128]{3,2,1,0:T(8,128)S(1)} %get-tuple-element.60, f32[1,4,8,128]{3,2,1,0:T(8,128)S(1)} %get-tuple-element.50, f32[]{:T(128)} %bitcast.21, f32[]{:T(128)} %bitcast.17, ...), kind=kLoop, calls=%fused_computation.64 | loop fusion | flops 110592 | bytes 180256
  33.6 4.8 %constant_dynamic-update-slice_fusion.14 = f32[19,4,8,128]{3,2,1,0:T(8,128)S(1)} fusion(f32[19,4,8,128]{3,2,1,0:T(8,128)S(1)} %constant_dynamic-update-slice_fusion.15, f32[1,4,8,128]{3,2,1,0:T(8,128)S(1)} %get-tuple-element.60, f32[1,4,8,128]{3,2,1,0:T(8,128)S(1)} %get-tuple-element.50, f32[]{:T(128)} %bitcast.21, f32[]{:T(128)} %bitcast.17, ...), kind=kLoop, calls=%fused_computation.63 | loop fusion | flops 110592 | bytes 180256
  38.4 5.0 %constant_dynamic-update-slice_fusion.13 = f32[19,4,8,128]{3,2,1,0:T(8,128)S(1)} fusion(f32[19,4,8,128]{3,2,1,0:T(8,128)S(1)} %constant_dynamic-update-slice_fusion.14, f32[1,4,8,128]{3,2,1,0:T(8,128)S(1)} %get-tuple-element.80, f32[1,4,8,128]{3,2,1,0:T(8,128)S(1)} %get-tuple-element.56, f32[1,4,8,128]{3,2,1,0:T(8,128)S(1)} %get-tuple-element.50, ...), kind=kLoop, calls=%fused_computation.62 | loop fusion | flops 110592 | bytes 180256
  43.4 5.0 %constant_dynamic-update-slice_fusion.12 = f32[19,4,8,128]{3,2,1,0:T(8,128)S(1)} fusion(f32[19,4,8,128]{3,2,1,0:T(8,128)S(1)} %constant_dynamic-update-slice_fusion.13, f32[1,4,8,128]{3,2,1,0:T(8,128)S(1)} %get-tuple-element.80, f32[1,4,8,128]{3,2,1,0:T(8,128)S(1)} %get-tuple-element.56, f32[1,4,8,128]{3,2,1,0:T(8,128)S(1)} %get-tuple-element.50, ...), kind=kLoop, calls=%fused_computation.61 | loop fusion | flops 110592 | bytes 180256
  61.2 4.3 %constant_dynamic-update-slice_fusion.8 = f32[19,4,8,128]{3,2,1,0:T(8,128)S(1)} fusion(f32[19,4,8,128]{3,2,1,0:T(8,128)S(1)} %constant_dynamic-update-slice_fusion.9, f32[1,4,8,128]{3,2,1,0:T(8,128)S(1)} %get-tuple-element.88, f32[1,4,8,128]{3,2,1,0:T(8,128)S(1)} %get-tuple-element.82, f32[1,4,8,128]{3,2,1,0:T(8,128)S(1)} %get-tuple-element.72, f32[]{:T(128)} %bitcast.24, ...), kind=kLoop, calls=%fused_computation.57 | loop fusion | flops 94208 | bytes 163868
  65.5 5.7 %constant_dynamic-update-slice_fusion.7 = f32[19,4,8,128]{3,2,1,0:T(8,128)S(1)} fusion(f32[19,4,8,128]{3,2,1,0:T(8,128)S(1)} %constant_dynamic-update-slice_fusion.8, f32[1,4,8,128]{3,2,1,0:T(8,128)S(1)} %get-tuple-element.90, f32[1,4,8,128]{3,2,1,0:T(8,128)S(1)} %get-tuple-element.68, f32[1,4,8,128]{3,2,1,0:T(8,128)S(1)} %get-tuple-element.80, ...), kind=kLoop, calls=%fused_computation.56 | loop fusion | flops 118784 | bytes 196644
  71.2 5.7 %constant_dynamic-update-slice_fusion.6 = f32[19,4,8,128]{3,2,1,0:T(8,128)S(1)} fusion(f32[19,4,8,128]{3,2,1,0:T(8,128)S(1)} %constant_dynamic-update-slice_fusion.7, f32[1,4,8,128]{3,2,1,0:T(8,128)S(1)} %get-tuple-element.90, f32[1,4,8,128]{3,2,1,0:T(8,128)S(1)} %get-tuple-element.68, f32[1,4,8,128]{3,2,1,0:T(8,128)S(1)} %get-tuple-element.80, ...), kind=kLoop, calls=%fused_computation.55 | loop fusion | flops 118784 | bytes 196644
  76.9 5.7 %constant_dynamic-update-slice_fusion.5 = f32[19,4,8,128]{3,2,1,0:T(8,128)S(1)} fusion(f32[19,4,8,128]{3,2,1,0:T(8,128)S(1)} %constant_dynamic-update-slice_fusion.6, f32[1,4,8,128]{3,2,1,0:T(8,128)S(1)} %get-tuple-element.88, f32[1,4,8,128]{3,2,1,0:T(8,128)S(1)} %get-tuple-element.68, f32[1,4,8,128]{3,2,1,0:T(8,128)S(1)} %get-tuple-element.80, ...), kind=kLoop, calls=%fused_computation.54 | loop fusion | flops 118784 | bytes 196644
  82.5 5.7 %constant_dynamic-update-slice_fusion.4 = f32[19,4,8,128]{3,2,1,0:T(8,128)S(1)} fusion(f32[19,4,8,128]{3,2,1,0:T(8,128)S(1)} %constant_dynamic-update-slice_fusion.5, f32[1,4,8,128]{3,2,1,0:T(8,128)S(1)} %get-tuple-element.88, f32[1,4,8,128]{3,2,1,0:T(8,128)S(1)} %get-tuple-element.68, f32[1,4,8,128]{3,2,1,0:T(8,128)S(1)} %get-tuple-element.80, ...), kind=kLoop, calls=%fused_computation.53 | loop fusion | flops 118784 | bytes 196644
  88.2 6.8 %constant_dynamic-update-slice_fusion.3 = f32[19,4,8,128]{3,2,1,0:T(8,128)S(1)} fusion(f32[19,4,8,128]{3,2,1,0:T(8,128)S(1)} %constant_dynamic-update-slice_fusion.4, f32[1,4,8,128]{3,2,1,0:T(8,128)S(1)} %get-tuple-element.70, f32[1,4,8,128]{3,2,1,0:T(8,128)S(1)} %get-tuple-element.80, f32[1,4,8,128]{3,2,1,0:T(8,128)S(1)} %get-tuple-element.56, ...), kind=kLoop, calls=%fused_computation.52 | loop fusion | flops 155648 | bytes 245804
  95.0 6.8 %constant_dynamic-update-slice_fusion.2 = f32[19,4,8,128]{3,2,1,0:T(8,128)S(1)} fusion(f32[19,4,8,128]{3,2,1,0:T(8,128)S(1)} %constant_dynamic-update-slice_fusion.3, f32[1,4,8,128]{3,2,1,0:T(8,128)S(1)} %get-tuple-element.70, f32[1,4,8,128]{3,2,1,0:T(8,128)S(1)} %get-tuple-element.80, f32[1,4,8,128]{3,2,1,0:T(8,128)S(1)} %get-tuple-element.56, ...), kind=kLoop, calls=%fused_computation.51 | loop fusion | flops 155648 | bytes 245804
  101.9 6.8 %constant_dynamic-update-slice_fusion.1 = f32[19,4,8,128]{3,2,1,0:T(8,128)S(1)} fusion(f32[19,4,8,128]{3,2,1,0:T(8,128)S(1)} %constant_dynamic-update-slice_fusion.2, f32[1,4,8,128]{3,2,1,0:T(8,128)S(1)} %get-tuple-element.70, f32[1,4,8,128]{3,2,1,0:T(8,128)S(1)} %get-tuple-element.80, f32[1,4,8,128]{3,2,1,0:T(8,128)S(1)} %get-tuple-element.56, ...), kind=kLoop, calls=%fused_computation.50 | loop fusion | flops 155648 | bytes 245804
  108.7 6.8 %constant_dynamic-update-slice_fusion = f32[19,4,8,128]{3,2,1,0:T(8,128)S(1)} fusion(f32[19,4,8,128]{3,2,1,0:T(8,128)S(1)} %constant_dynamic-update-slice_fusion.1, f32[1,4,8,128]{3,2,1,0:T(8,128)S(1)} %get-tuple-element.70, f32[1,4,8,128]{3,2,1,0:T(8,128)S(1)} %get-tuple-element.80, f32[1,4,8,128]{3,2,1,0:T(8,128)S(1)} %get-tuple-element.56, ...), kind=kLoop, calls=%fused_computation.49 | loop fusion | flops 155648 | bytes 245804 | tf_op jit(solution)/shard_map/stack | solution.py:142
  145.6 4.3 %constant_dynamic-update-slice_fusion.100 = (f32[19,4,8,128]{3,2,1,0:T(8,128)S(1)}, f32[1,4,8,128]{3,2,1,0:T(8,128)S(1)}) fusion(f32[19,4,8,128]{3,2,1,0:T(8,128)S(1)} %constant_dynamic-update-slice_fusion.101, f32[]{:T(128)} %bitcast.19, f32[19,4,8,128]{3,2,1,0:T(8,128)S(1)} %constant_dynamic-update-slice_fusion.45, f32[]{:T(128)} %bitcast.18, ...), kind=kLoop, calls=%fused_computation.149 | loop fusion | flops 98304 | bytes 180252
  149.9 4.3 %constant_dynamic-update-slice_fusion.99 = (f32[19,4,8,128]{3,2,1,0:T(8,128)S(1)}, f32[1,4,8,128]{3,2,1,0:T(8,128)S(1)}) fusion(f32[19,4,8,128]{3,2,1,0:T(8,128)S(1)} %get-tuple-element.47, f32[]{:T(128)} %bitcast.19, f32[19,4,8,128]{3,2,1,0:T(8,128)S(1)} %constant_dynamic-update-slice_fusion.45, f32[]{:T(128)} %bitcast.18, f32[]{:T(128)} %bitcast.12, ...), kind=kLoop, calls=%fused_computation.148 | loop fusion | flops 98304 | bytes 180252
  154.2 4.8 %constant_dynamic-update-slice_fusion.98 = f32[19,4,8,128]{3,2,1,0:T(8,128)S(1)} fusion(f32[19,4,8,128]{3,2,1,0:T(8,128)S(1)} %get-tuple-element.45, f32[]{:T(128)} %bitcast.21, f32[19,4,8,128]{3,2,1,0:T(8,128)S(1)} %constant_dynamic-update-slice_fusion.45, f32[]{:T(128)} %bitcast.17, f32[]{:T(128)} %bitcast.20, f32[]{:T(128)} %bitcast.12, f32[]{:T(128)} %bitcast.16, ...), kind=kLoop, calls=%fused_computation.147 | loop fusion | flops 110592 | bytes 180256
  159.1 4.8 %constant_dynamic-update-slice_fusion.97 = f32[19,4,8,128]{3,2,1,0:T(8,128)S(1)} fusion(f32[19,4,8,128]{3,2,1,0:T(8,128)S(1)} %constant_dynamic-update-slice_fusion.98, f32[]{:T(128)} %bitcast.21, f32[19,4,8,128]{3,2,1,0:T(8,128)S(1)} %constant_dynamic-update-slice_fusion.45, f32[]{:T(128)} %bitcast.17, f32[]{:T(128)} %bitcast.20, f32[]{:T(128)} %bitcast.12, ...), kind=kLoop, calls=%fused_computation.146 | loop fusion | flops 110592 | bytes 180256
  163.9 5.0 %constant_dynamic-update-slice_fusion.96 = f32[19,4,8,128]{3,2,1,0:T(8,128)S(1)} fusion(f32[19,4,8,128]{3,2,1,0:T(8,128)S(1)} %constant_dynamic-update-slice_fusion.97, f32[19,4,8,128]{3,2,1,0:T(8,128)S(1)} %constant_dynamic-update-slice_fusion.45, f32[]{:T(128)} %bitcast.23, f32[]{:T(128)} %bitcast.17, f32[]{:T(128)} %bitcast.22, f32[]{:T(128)} %bitcast.12, ...), kind=kLoop, calls=%fused_computation.145 | loop fusion | flops 110592 | bytes 180256
  168.9 5.0 %constant_dynamic-update-slice_fusion.95 = f32[19,4,8,128]{3,2,1,0:T(8,128)S(1)} fusion(f32[19,4,8,128]{3,2,1,0:T(8,128)S(1)} %constant_dynamic-update-slice_fusion.96, f32[19,4,8,128]{3,2,1,0:T(8,128)S(1)} %constant_dynamic-update-slice_fusion.45, f32[]{:T(128)} %bitcast.23, f32[]{:T(128)} %bitcast.17, f32[]{:T(128)} %bitcast.22, f32[]{:T(128)} %bitcast.12, ...), kind=kLoop, calls=%fused_computation.144 | loop fusion | flops 110592 | bytes 180256
  191.0 5.7 %constant_dynamic-update-slice_fusion.90 = f32[19,4,8,128]{3,2,1,0:T(8,128)S(1)} fusion(f32[19,4,8,128]{3,2,1,0:T(8,128)S(1)} %constant_dynamic-update-slice_fusion.91, f32[1,4,8,128]{3,2,1,0:T(8,128)S(1)} %get-tuple-element.48, f32[19,4,8,128]{3,2,1,0:T(8,128)S(1)} %constant_dynamic-update-slice_fusion.45, f32[]{:T(128)} %bitcast.25, f32[]{:T(128)} %bitcast.19, ...), kind=kLoop, calls=%fused_computation.139 | loop fusion | flops 118784 | bytes 196644
  196.7 5.7 %constant_dynamic-update-slice_fusion.89 = f32[19,4,8,128]{3,2,1,0:T(8,128)S(1)} fusion(f32[19,4,8,128]{3,2,1,0:T(8,128)S(1)} %constant_dynamic-update-slice_fusion.90, f32[1,4,8,128]{3,2,1,0:T(8,128)S(1)} %get-tuple-element.48, f32[19,4,8,128]{3,2,1,0:T(8,128)S(1)} %constant_dynamic-update-slice_fusion.45, f32[]{:T(128)} %bitcast.25, f32[]{:T(128)} %bitcast.19, ...), kind=kLoop, calls=%fused_computation.138 | loop fusion | flops 118784 | bytes 196644
  202.3 5.7 %constant_dynamic-update-slice_fusion.88 = f32[19,4,8,128]{3,2,1,0:T(8,128)S(1)} fusion(f32[19,4,8,128]{3,2,1,0:T(8,128)S(1)} %constant_dynamic-update-slice_fusion.89, f32[1,4,8,128]{3,2,1,0:T(8,128)S(1)} %get-tuple-element.46, f32[19,4,8,128]{3,2,1,0:T(8,128)S(1)} %constant_dynamic-update-slice_fusion.45, f32[]{:T(128)} %bitcast.25, f32[]{:T(128)} %bitcast.19, ...), kind=kLoop, calls=%fused_computation.137 | loop fusion | flops 118784 | bytes 196644
  208.0 5.7 %constant_dynamic-update-slice_fusion.87 = f32[19,4,8,128]{3,2,1,0:T(8,128)S(1)} fusion(f32[19,4,8,128]{3,2,1,0:T(8,128)S(1)} %constant_dynamic-update-slice_fusion.88, f32[1,4,8,128]{3,2,1,0:T(8,128)S(1)} %get-tuple-element.46, f32[19,4,8,128]{3,2,1,0:T(8,128)S(1)} %constant_dynamic-update-slice_fusion.45, f32[]{:T(128)} %bitcast.25, f32[]{:T(128)} %bitcast.19, ...), kind=kLoop, calls=%fused_computation.136 | loop fusion | flops 118784 | bytes 196644
  213.7 6.8 %constant_dynamic-update-slice_fusion.86 = f32[19,4,8,128]{3,2,1,0:T(8,128)S(1)} fusion(f32[19,4,8,128]{3,2,1,0:T(8,128)S(1)} %constant_dynamic-update-slice_fusion.87, f32[19,4,8,128]{3,2,1,0:T(8,128)S(1)} %constant_dynamic-update-slice_fusion.45, f32[]{:T(128)} %bitcast.26, f32[]{:T(128)} %bitcast.21, f32[]{:T(128)} %bitcast.23, f32[]{:T(128)} %bitcast.17, ...), kind=kLoop, calls=%fused_computation.135 | loop fusion | flops 155648 | bytes 245804
  220.5 6.8 %constant_dynamic-update-slice_fusion.85 = f32[19,4,8,128]{3,2,1,0:T(8,128)S(1)} fusion(f32[19,4,8,128]{3,2,1,0:T(8,128)S(1)} %constant_dynamic-update-slice_fusion.86, f32[19,4,8,128]{3,2,1,0:T(8,128)S(1)} %constant_dynamic-update-slice_fusion.45, f32[]{:T(128)} %bitcast.26, f32[]{:T(128)} %bitcast.21, f32[]{:T(128)} %bitcast.23, f32[]{:T(128)} %bitcast.17, ...), kind=kLoop, calls=%fused_computation.134 | loop fusion | flops 155648 | bytes 245804
  227.4 6.8 %constant_dynamic-update-slice_fusion.84 = f32[19,4,8,128]{3,2,1,0:T(8,128)S(1)} fusion(f32[19,4,8,128]{3,2,1,0:T(8,128)S(1)} %constant_dynamic-update-slice_fusion.85, f32[19,4,8,128]{3,2,1,0:T(8,128)S(1)} %constant_dynamic-update-slice_fusion.45, f32[]{:T(128)} %bitcast.26, f32[]{:T(128)} %bitcast.21, f32[]{:T(128)} %bitcast.23, f32[]{:T(128)} %bitcast.17, ...), kind=kLoop, calls=%fused_computation.133 | loop fusion | flops 155648 | bytes 245804
  234.3 6.9 %constant_dynamic-update-slice_fusion.83 = f32[19,4,8,128]{3,2,1,0:T(8,128)S(1)} fusion(f32[19,4,8,128]{3,2,1,0:T(8,128)S(1)} %constant_dynamic-update-slice_fusion.84, f32[19,4,8,128]{3,2,1,0:T(8,128)S(1)} %constant_dynamic-update-slice_fusion.45, f32[]{:T(128)} %bitcast.26, f32[]{:T(128)} %bitcast.21, f32[]{:T(128)} %bitcast.23, f32[]{:T(128)} %bitcast.17, ...), kind=kLoop, calls=%fused_computation.132 | loop fusion | flops 155648 | bytes 245804 | tf_op jit(solution)/shard_map/stack | solution.py:142
  256.2 4.5 %collective-permute-start.10 = (f32[19]{0:T(128)S(1)}, f32[19]{0:T(128)S(1)}, u32[]{:S(2)}, u32[]{:S(2)}) collective-permute-start(f32[19]{0:T(128)S(1)} %add.6508), channel_id=1, source_target_pairs={{0,2},{1,3},{2,0},{3,1},{4,6},{5,7},{6,4},{7,5},{8,10},{9,11},{10,... | collective-permute-start | bytes 236 | tf_op jit(solution)/shard_map/ppermute | solution.py:123
  268.7 5.0 %collective-permute-done.12 = f32[4,4,8,128]{3,2,1,0:T(8,128)S(1)} collective-permute-done((f32[4,4,8,128]{3,2,1,0:T(8,128)S(1)}, f32[4,4,8,128]{3,2,1,0:T(8,128)S(1)}, u32[]{:S(2)}, u32[]{:S(2)}) %collective-permute-start.12) | collective-permute-done | bytes 65568 | tf_op jit(solution)/shard_map/ppermute | solution.py:252
  (282 shorter events, 97.8 us)
Async XLA Ops:
  0.7 6.7 %copy-start.1 = (f32[28,4,8,128]{3,2,1,0:T(8,128)S(1)}, f32[28,4,8,128]{3,2,1,0:T(8,128)}, u32[]{:S(2)}) copy-start(f32[28,4,8,128]{3,2,1,0:T(8,128)} %param.21) | copy-start | bytes 1376260
  2.4 11.2 %collective-permute-start = (f32[3,4,8,128]{3,2,1,0:T(8,128)S(1)}, f32[3,4,8,128]{3,2,1,0:T(8,128)S(1)}, u32[]{:S(2)}, u32[]{:S(2)}) collective-permute-start(f32[3,4,8,128]{3,2,1,0:T(8,128)S(1)} %maximum_divide_fusion), channel_id=1, source_target_pairs={{0,128},{1,129},{2,130},{3,131},{4,132},{5,133},{6,134},{7,135},{8... | collective-permute-start | bytes 147464 | tf_op jit(solution)/shard_map/ppermute | solution.py:158
  7.4 2.0 copy-start.21
  13.6 102.8 %copy-start.6 = (f32[4,4,8,128]{3,2,1,0:T(8,128)}, f32[4,4,8,128]{3,2,1,0:T(8,128)S(1)}, u32[]{:S(2)}) copy-start(f32[4,4,8,128]{3,2,1,0:T(8,128)S(1)} %reduce_sum.183) | copy-start | bytes 196612
  14.3 101.4 %copy-start.10 = (f32[4,8,128]{2,1,0:T(8,128)}, f32[4,8,128]{2,1,0:T(8,128)S(1)}, u32[]{:S(2)}) copy-start(f32[4,8,128]{2,1,0:T(8,128)S(1)} %get-tuple-element.121) | copy-start | bytes 49156
  14.3 101.4 %copy-start.12 = (f32[4,8,128]{2,1,0:T(8,128)}, f32[4,8,128]{2,1,0:T(8,128)S(1)}, u32[]{:S(2)}) copy-start(f32[4,8,128]{2,1,0:T(8,128)S(1)} %get-tuple-element.122) | copy-start | bytes 49156
  14.3 101.4 %copy-start.14 = (f32[4,8,128]{2,1,0:T(8,128)}, f32[4,8,128]{2,1,0:T(8,128)S(1)}, u32[]{:S(2)}) copy-start(f32[4,8,128]{2,1,0:T(8,128)S(1)} %get-tuple-element.123) | copy-start | bytes 49156
  117.3 1.0 copy-start.2
  118.5 6.4 %collective-permute-start.1 = (f32[56,4,1,128]{3,2,1,0:T(1,128)S(1)}, f32[56,4,1,128]{3,2,1,0:T(1,128)S(1)}, u32[]{:S(2)}, u32[]{:S(2)}) collective-permute-start(f32[56,4,1,128]{3,2,1,0:T(1,128)S(1)} %get-tuple-element.115), channel_id=1, source_target_pairs={{0,8},{8,16},{16,24},{24,32},{32,40},{40,48},{48,56},{56,64},{64,7... | collective-permute-start | bytes 344072 | tf_op jit(solution)/shard_map/ppermute | solution.py:78
  118.5 6.3 %collective-permute-start.2 = (f32[56,4,1,128]{3,2,1,0:T(1,128)S(1)}, f32[56,4,1,128]{3,2,1,0:T(1,128)S(1)}, u32[]{:S(2)}, u32[]{:S(2)}) collective-permute-start(f32[56,4,1,128]{3,2,1,0:T(1,128)S(1)} %get-tuple-element.114), channel_id=1, source_target_pairs={{0,120},{8,0},{16,8},{24,16},{32,24},{40,32},{48,40},{56,48},{64,5... | collective-permute-start | bytes 344072 | tf_op jit(solution)/shard_map/ppermute | solution.py:79
  126.2 4.2 %collective-permute-start.3 = (f32[56,4,8]{0,2,1:T(8,128)S(1)}, f32[56,4,8]{0,2,1:T(8,128)S(1)}, u32[]{:S(2)}, u32[]{:S(2)}) collective-permute-start(f32[56,4,8]{0,2,1:T(8,128)S(1)} %bitcast.106), channel_id=1, source_target_pairs={{0,1},{1,2},{2,3},{3,4},{4,5},{5,6},{6,7},{7,0},{8,9},{9,10},{10,1... | collective-permute-start | bytes 21512 | tf_op jit(solution)/shard_map/ppermute | solution.py:83
  128.7 3.8 %collective-permute-start.4 = (f32[56,4,8]{0,2,1:T(8,128)S(1)}, f32[56,4,8]{0,2,1:T(8,128)S(1)}, u32[]{:S(2)}, u32[]{:S(2)}) collective-permute-start(f32[56,4,8]{0,2,1:T(8,128)S(1)} %bitcast.107), channel_id=1, source_target_pairs={{0,7},{1,0},{2,1},{3,2},{4,3},{5,4},{6,5},{7,6},{8,15},{9,8},{10,9... | collective-permute-start | bytes 21512 | tf_op jit(solution)/shard_map/ppermute | solution.py:84
  128.8 3.8 %copy-start.50 = (pred[128]{0:T(512)(128)(4,1)S(1)}, pred[128]{0:T(512)(128)(4,1)}, u32[]{:S(2)}) copy-start(pred[128]{0:T(512)(128)(4,1)} %get-tuple-element.156) | copy-start | bytes 388
  136.7 3.8 %copy-start = (f32[56,4,8,128]{3,2,1,0:T(8,128)}, f32[56,4,8,128]{3,2,1,0:T(8,128)S(1)}, u32[]{:S(2)}) copy-start(f32[56,4,8,128]{3,2,1,0:T(8,128)S(1)} %maximum_select_fusion.2) | copy-start | bytes 2752516
  137.3 1.0 copy-start.17
  137.3 1.1 copy-start.3
  140.4 1.1 collective-permute-start.5
  141.6 100.0 %collective-permute-start.6 = (f32[19]{0:T(128)S(1)}, f32[19]{0:T(128)S(1)}, u32[]{:S(2)}, u32[]{:S(2)}) collective-permute-start(f32[19]{0:T(128)S(1)} %add.6323), channel_id=1, source_target_pairs={{0,16},{8,24},{16,0},{24,8},{32,48},{40,56},{48,32},{56,40},{64,80... | collective-permute-start | bytes 236 | tf_op jit(solution)/shard_map/ppermute | solution.py:123
  234.2 6.9 %copy-start.11 = (f32[4,8,128]{2,1,0:T(8,128)S(1)}, f32[4,8,128]{2,1,0:T(8,128)}, u32[]{:S(2)}) copy-start(f32[4,8,128]{2,1,0:T(8,128)} %copy-done.10) | copy-start | bytes 49156
  234.2 6.9 %copy-start.13 = (f32[4,8,128]{2,1,0:T(8,128)S(1)}, f32[4,8,128]{2,1,0:T(8,128)}, u32[]{:S(2)}) copy-start(f32[4,8,128]{2,1,0:T(8,128)} %copy-done.12) | copy-start | bytes 49156
  234.2 6.9 %copy-start.15 = (f32[4,8,128]{2,1,0:T(8,128)S(1)}, f32[4,8,128]{2,1,0:T(8,128)}, u32[]{:S(2)}) copy-start(f32[4,8,128]{2,1,0:T(8,128)} %copy-done.14) | copy-start | bytes 49156
  234.2 6.9 %copy-start.19 = (f32[4,8,128]{2,1,0:T(8,128)S(1)}, f32[4,8,128]{2,1,0:T(8,128)}, u32[]{:S(2)}) copy-start(f32[4,8,128]{2,1,0:T(8,128)} %copy-done.18) | copy-start | bytes 49156
  234.2 6.9 %copy-start.38 = (f32[19]{0:T(128)S(1)}, f32[19]{0:T(128)}, u32[]{:S(2)}) copy-start(f32[19]{0:T(128)} %constant.207) | copy-start | bytes 232
  234.3 7.4 %copy-start.36 = (f32[7]{0:T(128)S(1)}, f32[7]{0:T(128)}, u32[]{:S(2)}) copy-start(f32[7]{0:T(128)} %constant.215) | copy-start | bytes 88
  243.2 3.6 %collective-permute-start.7 = (f32[19]{0:T(128)S(1)}, f32[19]{0:T(128)S(1)}, u32[]{:S(2)}, u32[]{:S(2)}) collective-permute-start(f32[19]{0:T(128)S(1)} %add.6505), channel_id=1, source_target_pairs={{0,32},{8,40},{16,48},{24,56},{32,0},{40,8},{48,16},{56,24},{64,96... | collective-permute-start | bytes 236 | tf_op jit(solution)/shard_map/ppermute | solution.py:123
  246.9 4.8 %collective-permute-start.8 = (f32[19]{0:T(128)S(1)}, f32[19]{0:T(128)S(1)}, u32[]{:S(2)}, u32[]{:S(2)}) collective-permute-start(f32[19]{0:T(128)S(1)} %add.6506), channel_id=1, source_target_pairs={{0,96},{8,104},{16,112},{24,120},{32,64},{40,72},{48,80},{56,88},{... | collective-permute-start | bytes 236 | tf_op jit(solution)/shard_map/ppermute | solution.py:123
  251.6 4.5 %collective-permute-start.9 = (f32[19]{0:T(128)S(1)}, f32[19]{0:T(128)S(1)}, u32[]{:S(2)}, u32[]{:S(2)}) collective-permute-start(f32[19]{0:T(128)S(1)} %add.6507), channel_id=1, source_target_pairs={{0,1},{1,0},{2,3},{3,2},{4,5},{5,4},{6,7},{7,6},{8,9},{9,8},{10,11... | collective-permute-start | bytes 236 | tf_op jit(solution)/shard_map/ppermute | solution.py:123
  256.2 6.0 %collective-permute-start.10 = (f32[19]{0:T(128)S(1)}, f32[19]{0:T(128)S(1)}, u32[]{:S(2)}, u32[]{:S(2)}) collective-permute-start(f32[19]{0:T(128)S(1)} %add.6508), channel_id=1, source_target_pairs={{0,2},{1,3},{2,0},{3,1},{4,6},{5,7},{6,4},{7,5},{8,10},{9,11},{10,... | collective-permute-start | bytes 236 | tf_op jit(solution)/shard_map/ppermute | solution.py:123
  262.2 5.7 %collective-permute-start.11 = (f32[19]{0:T(128)S(1)}, f32[19]{0:T(128)S(1)}, u32[]{:S(2)}, u32[]{:S(2)}) collective-permute-start(f32[19]{0:T(128)S(1)} %add.6509), channel_id=1, source_target_pairs={{0,6},{1,7},{2,4},{3,5},{4,2},{5,3},{6,0},{7,1},{8,14},{9,15},{10,... | collective-permute-start | bytes 236 | tf_op jit(solution)/shard_map/ppermute | solution.py:123
  267.9 5.9 %collective-permute-start.12 = (f32[4,4,8,128]{3,2,1,0:T(8,128)S(1)}, f32[4,4,8,128]{3,2,1,0:T(8,128)S(1)}, u32[]{:S(2)}, u32[]{:S(2)}) collective-permute-start(f32[4,4,8,128]{3,2,1,0:T(8,128)S(1)} %select_maximum_fusion), channel_id=1, source_target_pairs={{0,128},{128,0},{1,129},{129,1},{2,130},{130,2},{3,131},{131,3},{4... | collective-permute-start | bytes 196616 | tf_op jit(solution)/shard_map/ppermute | solution.py:252
  268.6 5.2 %copy-start.9 = (f32[3,4,8,128]{3,2,1,0:T(8,128)S(1)}, f32[3,4,8,128]{3,2,1,0:T(8,128)}, u32[]{:S(2)}) copy-start(f32[3,4,8,128]{3,2,1,0:T(8,128)} %copy-done.8) | copy-start | bytes 147460
  268.7 5.1 %slice-start = ((f32[56,4,8,128]{3,2,1,0:T(8,128)}), f32[19,4,8,128]{3,2,1,0:T(8,128)S(1)}, s32[]{:S(2)}) async-start(f32[56,4,8,128]{3,2,1,0:T(8,128)} %copy-done), calls=%async_computation | async-start | bytes 622592 | tf_op jit(solution)/shard_map/slice | solution.py:198
  (33 other events, 22.8 us)

commit v5 on v4

--- a/solution.py
+++ b/solution.py
@@ -127,23 +127,9 @@
     return values
 
 
-def mix(table, field, scale=None):
-    rows = [field[j] if scale is None else field[j] * scale[j] for j in range(table.shape[0])]
-    out = []
-    for k in range(table.shape[1]):
-        total = None
-        for j in range(table.shape[0]):
-            weight = float(table[j, k])
-            if abs(weight) < 1e-12:
-                continue
-            term = rows[j] * weight
-            total = term if total is None else total + term
-        out.append(total if total is not None else jnp.zeros_like(rows[0]))
-    return jnp.stack(out)
-
-
 def per_device(populations, solid_mask, flow_rates, species_rates, cotangents):
     velocity, weights, opposite, ortho = lattice_tables()
+    highest = lax.Precision.HIGHEST
     rows = populations.shape[0]
     groups = rows // 7
     is_flow = lax.axis_index("sec") == 0
@@ -171,14 +157,15 @@
     species_bounce = jnp.swapaxes(reverse_pairs(jnp.swapaxes(grouped, 0, 1), opposite[:7]), 0, 1)
     species_post = jnp.where(fluid[None], species_relaxed, species_bounce).reshape(populations.shape)
 
-    relax_scalars = [0.0] * 4 + [flow_rates[k] for k in range(flow_rates.shape[0])]
+    q_table = jnp.asarray(ortho, jnp.float32)
+    relax = jnp.concatenate([jnp.zeros((4,), flow_rates.dtype), flow_rates]).reshape(19, 1, 1, 1)
     w = column(weights)
     projected = vx * motion[0][None] + vy * motion[1][None] + vz * motion[2][None]
     squared = jnp.sum(motion * motion, 0)
     poly = w * (1.0 + 3.0 * projected + 4.5 * projected * projected - 1.5 * squared[None])
     equilibrium = density[None] * poly
-    moments = mix(ortho, flow - equilibrium)
-    flow_relaxed = flow - mix(ortho.T, moments, relax_scalars)
+    moments = jnp.einsum("ji,jxyz->ixyz", q_table, flow - equilibrium, precision=highest)
+    flow_relaxed = flow - jnp.einsum("ij,jxyz->ixyz", q_table, relax * moments, precision=highest)
     flow_post = jnp.where(fluid, flow_relaxed, reverse_pairs(flow, opposite))
     filler = jnp.zeros((rows - 19,) + populations.shape[1:], jnp.float32)
     post = jnp.where(is_flow, jnp.concatenate([flow_post, filler]), species_post)
@@ -199,7 +186,7 @@
     species_rate_grad = -jnp.sum(
         jnp.where(fluid[None], back_species * species_gap, 0.0), axis=(1, 2, 3, 4)
     )
-    back_moments = mix(ortho, back_flow)
+    back_moments = jnp.einsum("ji,jxyz->ixyz", q_table, back_flow, precision=highest)
     flow_rate_grad = -jnp.sum(
         jnp.where(fluid, back_moments * moments, 0.0)[4:], axis=(1, 2, 3)
     )
@@ -215,7 +202,7 @@
         values, (back_flow_, back_moments_) = lax.optimization_barrier(
             (values, (back_flow, back_moments))
         )
-        through_eq = mix(ortho.T, back_moments_, relax_scalars)
+        through_eq = jnp.einsum("ij,jxyz->ixyz", q_table, relax * back_moments_, precision=highest)
         density_grad = jnp.sum(through_eq * poly, 0)
         hw = through_eq * w
         hw_sum = jnp.sum(hw, 0)

time: 279 us -> 69.4 us (0.25); the launches traced: 275 us -> 69.1 us
  other arithmetic: 211 us -> 6.36 us
  local copies, waits for them, and re-layouts: 15.8 us -> 9.47 us
  starting transfers between devices: 25.7 us -> 29 us
    unnamed x71 -> x0, other arithmetic: 185 us -> none
    another operation x4 -> x0, other arithmetic: 13.8 us -> none  [mix(): return jnp.stack(out)]
    unnamed x147 -> x58, local copies, waits for them, and re-layouts: 11.7 us -> 6.49 us
    ppermute x1, starting transfers between devices: 0.09 us -> 2.97 us  [per_device(): other = lax.ppermute(payload, 'sec', [(0, 1), (1, 0)])]
  transfers between devices with their start and end apart: 13 -> 13, of which waited for: 9 -> 10; matrix products, arithmetic and copies ran while one was open for 38% -> 7% of each run, Pallas kernels for 0% -> 0%
where the time goes in v5:
time: 69.4 us; the launch traced here: 69.1 us
  starting transfers between devices  29 us (42%)
  waiting for transfers between devices  20.6 us (30%)
  local copies, waits for them, and re-layouts  9.47 us (14%)
  other arithmetic  6.36 us (9%)
  matrix products  2.34 us (3%)
  between operations  1.27 us (2%)
    ppermute x7, starting transfers between devices, butterfly_sum(): values = values + lax.ppermute(values, axis, list(enumerate(targets)))  15.1 us
    ppermute x7, waiting for transfers between devices, butterfly_sum(): values = values + lax.ppermute(values, axis, list(enumerate(targets)))  12.2 us
    unnamed x58, local copies, waits for them, and re-layouts  6.49 us
    ppermute x1, starting transfers between devices, per_device(): sent_motion = lax.ppermute(own_motion, 'sec', [(0, 1)])  4.93 us
    ppermute x1, starting transfers between devices, shift_rows(): high = lax.ppermute(field[:, :, :1, :], 'gy', ring('gy', -1))  3.84 us
    ppermute x1, starting transfers between devices, per_device(): other = lax.ppermute(payload, 'sec', [(0, 1), (1, 0)])  2.97 us
    ppermute x1, waiting for transfers between devices, per_device(): other = lax.ppermute(payload, 'sec', [(0, 1), (1, 0)])  2.74 us
    ppermute x1, waiting for transfers between devices, shift_rows(): low = lax.ppermute(field[:, :, size_y - 1:, :], 'gy', ring('gy', 1))  2.36 us
  transfers between devices with their start and end apart: 13, of which 10 were waited for; matrix products, arithmetic and copies ran while one was open for 7% of the time, Pallas kernels for 0%

profile of v5, /device:TPU:32, one launch (start us, length us, event | category | flops | bytes accessed | tf_op | source)
XLA Modules:
  0.0 69.1 jit_solution(12063929339898465384)
XLA Ops:
  0.7 1.3 %copy.83 = f32[28,4,8,128]{3,0,2,1:T(8,128)S(1)} copy(f32[28,4,8,128]{3,2,1,0:T(8,128)} %param.22) | data formatting | bytes 917504 | tf_op args[0]
  2.4 4.9 %collective-permute-start = (f32[3,4,8,128]{3,2,1,0:T(8,128)S(1)}, f32[3,4,8,128]{3,2,1,0:T(8,128)S(1)}, u32[]{:S(2)}, u32[]{:S(2)}) collective-permute-start(f32[3,4,8,128]{3,2,1,0:T(8,128)S(1)} %maximum_divide_fusion), channel_id=1, source_target_pairs={{0,128},{1,129},{2,130},{3,131},{4,132},{5,133},{6,134},{7,135},{8... | collective-permute-start | bytes 147464 | tf_op jit(solution)/shard_map/ppermute | solution.py:144
  7.4 0.7 copy-done.3
  10.1 0.7 copy-done.2
  10.7 0.7 fusion.18
  11.5 0.6 fusion.1
  12.9 3.8 %collective-permute-start.2 = (f32[56,4,1,128]{3,0,2,1:T(8,128)S(1)}, f32[56,4,1,128]{3,0,2,1:T(8,128)S(1)}, u32[]{:S(2)}, u32[]{:S(2)}) collective-permute-start(f32[56,4,1,128]{3,0,2,1:T(8,128)S(1)} %get-tuple-element.53), channel_id=1, source_target_pairs={{0,120},{8,0},{16,8},{24,16},{32,24},{40,32},{48,40},{56,48},{64,5... | collective-permute-start | bytes 344072 | tf_op jit(solution)/shard_map/ppermute | solution.py:79
  16.8 2.4 %collective-permute-done.1 = f32[56,4,1,128]{3,0,2,1:T(8,128)S(1)} collective-permute-done((f32[56,4,1,128]{3,0,2,1:T(8,128)S(1)}, f32[56,4,1,128]{3,0,2,1:T(8,128)S(1)}, u32[]{:S(2)}, u32[]{:S(2)}) %collective-permute-start.1) | collective-permute-done | bytes 114720 | tf_op jit(solution)/shard_map/ppermute | solution.py:78
  19.5 0.8 %slice_reduce_fusion.2 = (f32[56,4,8]{0,2,1:T(8,128)S(1)}, f32[56,4,8]{0,2,1:T(8,128)S(1)}, f32[56,4,8,1]{3,0,2,1:T(8,128)S(1)}, f32[56,4,8,1]{3,0,2,1:T(8,128)S(1)}) fusion(f32[56,4,8,128]{3,0,2,1:T(8,128)S(1)} %fusion.3), kind=kLoop, calls=%fused_computation.162 | loop fusion | bytes 43008 | tf_op jit(solution)/shard_map/slice | solution.py:83
  20.3 2.0 %collective-permute-start.3 = (f32[56,4,8]{0,2,1:T(8,128)S(1)}, f32[56,4,8]{0,2,1:T(8,128)S(1)}, u32[]{:S(2)}, u32[]{:S(2)}) collective-permute-start(f32[56,4,8]{0,2,1:T(8,128)S(1)} %get-tuple-element.34), channel_id=1, source_target_pairs={{0,1},{1,2},{2,3},{3,4},{4,5},{5,6},{6,7},{7,0},{8,9},{9,10},{10,1... | collective-permute-start | bytes 21512 | tf_op jit(solution)/shard_map/ppermute | solution.py:83
  22.7 1.4 %collective-permute-done.3 = f32[56,4,8]{0,2,1:T(8,128)S(1)} collective-permute-done((f32[56,4,8]{0,2,1:T(8,128)S(1)}, f32[56,4,8]{0,2,1:T(8,128)S(1)}, u32[]{:S(2)}, u32[]{:S(2)}) %collective-permute-start.3) | collective-permute-done | bytes 7200 | tf_op jit(solution)/shard_map/ppermute | solution.py:83
  24.1 1.9 %collective-permute-done.4 = f32[56,4,8]{0,2,1:T(8,128)S(1)} collective-permute-done((f32[56,4,8]{0,2,1:T(8,128)S(1)}, f32[56,4,8]{0,2,1:T(8,128)S(1)}, u32[]{:S(2)}, u32[]{:S(2)}) %collective-permute-start.4) | collective-permute-done | bytes 7200 | tf_op jit(solution)/shard_map/ppermute | solution.py:84
  26.0 1.2 %fusion.4 = f32[56,4,8,128]{3,0,2,1:T(8,128)S(1)} fusion(f32[56,4,8,127]{3,0,2,1:T(8,128)S(1)} %get-tuple-element.84, f32[56,4,8,1]{3,0,2,1:T(8,128)S(1)} %get-tuple-element.82, f32[56,4,8,128]{3,0,2,1:T(8,128)S(1)} %fusion.3, f32[56,4,8,1]{3,0,2,1:T(8,128)S(1)} %get-tuple-element.81, f32[56,4,8,127]{3,0,2,1:T(8,128)S(1)} %get-tuple-element.83, ...), kind=kLoop, calls=%fused_computation.15 | loop fusion | flops 1376256 | bytes 3684720 | tf_op jit(solution)/shard_map/jit(_where)/select_n | solution.py:88
  28.6 0.6 copy-done.12
  29.2 0.8 %fusion.70 = (f32[28,4,8,128]{3,0,2,1:T(8,128)S(1)}, f32[28]{0:T(128)S(1)}, f32[28,4,8,128]{3,0,2,1:T(8,128)S(1)}) fusion(f32[56,4,8,128]{3,0,2,1:T(8,128)S(1)} %maximum_select_fusion.2, f32[28,4,8,128]{3,2,1,0:T(8,128)S(1)} %bitcast.96, f32[28,4,8,128]{3,2,1,0:T(8,128)S(1)} %copy-done, pred[4,8,128]{2,1,0:T(8,128)(4,1)S(1)} %broadcast_compare_fusion, ...), kind=kLoop, calls=%fused_computation.164 | loop fusion | flops 688100 | bytes 2756749 | tf_op jit(solution)/shard_map/slice | solution.py:181
  30.8 1.0 %copy.111 = f32[28,4,8,128]{3,2,1,0:T(8,128)} copy(f32[28,4,8,128]{3,0,2,1:T(8,128)S(1)} %get-tuple-element.76) | data formatting | bytes 917504
  32.4 0.8 %collective-permute-start.6 = (f32[19]{0:T(128)S(1)}, f32[19]{0:T(128)S(1)}, u32[]{:S(2)}, u32[]{:S(2)}) collective-permute-start(f32[19]{0:T(128)S(1)} %add.117), channel_id=1, source_target_pairs={{0,16},{8,24},{16,0},{24,8},{32,48},{40,56},{48,32},{56,40},{64,80... | collective-permute-start | bytes 236 | tf_op jit(solution)/shard_map/ppermute | solution.py:123
  33.1 0.6 add_multiply_fusion
  34.3 1.6 %collective-permute-done.6 = f32[19]{0:T(128)S(1)} collective-permute-done((f32[19]{0:T(128)S(1)}, f32[19]{0:T(128)S(1)}, u32[]{:S(2)}, u32[]{:S(2)}) %collective-permute-start.6) | collective-permute-done | bytes 108 | tf_op jit(solution)/shard_map/ppermute | solution.py:123
  36.3 1.6 %collective-permute-start.7 = (f32[19]{0:T(128)S(1)}, f32[19]{0:T(128)S(1)}, u32[]{:S(2)}, u32[]{:S(2)}) collective-permute-start(f32[19]{0:T(128)S(1)} %add.121), channel_id=1, source_target_pairs={{0,32},{8,40},{16,48},{24,56},{32,0},{40,8},{48,16},{56,24},{64,96... | collective-permute-start | bytes 236 | tf_op jit(solution)/shard_map/ppermute | solution.py:123
  37.9 2.0 %collective-permute-done.7 = f32[19]{0:T(128)S(1)} collective-permute-done((f32[19]{0:T(128)S(1)}, f32[19]{0:T(128)S(1)}, u32[]{:S(2)}, u32[]{:S(2)}) %collective-permute-start.7) | collective-permute-done | bytes 108 | tf_op jit(solution)/shard_map/ppermute | solution.py:123
  39.9 2.9 %collective-permute-start.8 = (f32[19]{0:T(128)S(1)}, f32[19]{0:T(128)S(1)}, u32[]{:S(2)}, u32[]{:S(2)}) collective-permute-start(f32[19]{0:T(128)S(1)} %add.122), channel_id=1, source_target_pairs={{0,96},{8,104},{16,112},{24,120},{32,64},{40,72},{48,80},{56,88},{... | collective-permute-start | bytes 236 | tf_op jit(solution)/shard_map/ppermute | solution.py:123
  42.8 1.9 %collective-permute-done.8 = f32[19]{0:T(128)S(1)} collective-permute-done((f32[19]{0:T(128)S(1)}, f32[19]{0:T(128)S(1)}, u32[]{:S(2)}, u32[]{:S(2)}) %collective-permute-start.8) | collective-permute-done | bytes 108 | tf_op jit(solution)/shard_map/ppermute | solution.py:123
  44.7 2.0 %collective-permute-start.9 = (f32[19]{0:T(128)S(1)}, f32[19]{0:T(128)S(1)}, u32[]{:S(2)}, u32[]{:S(2)}) collective-permute-start(f32[19]{0:T(128)S(1)} %add.123), channel_id=1, source_target_pairs={{0,1},{1,0},{2,3},{3,2},{4,5},{5,4},{6,7},{7,6},{8,9},{9,8},{10,11... | collective-permute-start | bytes 236 | tf_op jit(solution)/shard_map/ppermute | solution.py:123
  46.7 1.5 %collective-permute-done.9 = f32[19]{0:T(128)S(1)} collective-permute-done((f32[19]{0:T(128)S(1)}, f32[19]{0:T(128)S(1)}, u32[]{:S(2)}, u32[]{:S(2)}) %collective-permute-start.9) | collective-permute-done | bytes 108 | tf_op jit(solution)/shard_map/ppermute | solution.py:123
  48.2 5.7 %collective-permute-start.10 = (f32[19]{0:T(128)S(1)}, f32[19]{0:T(128)S(1)}, u32[]{:S(2)}, u32[]{:S(2)}) collective-permute-start(f32[19]{0:T(128)S(1)} %add.124), channel_id=1, source_target_pairs={{0,2},{1,3},{2,0},{3,1},{4,6},{5,7},{6,4},{7,5},{8,10},{9,11},{10,... | collective-permute-start | bytes 236 | tf_op jit(solution)/shard_map/ppermute | solution.py:123
  53.9 1.5 %collective-permute-done.10 = f32[19]{0:T(128)S(1)} collective-permute-done((f32[19]{0:T(128)S(1)}, f32[19]{0:T(128)S(1)}, u32[]{:S(2)}, u32[]{:S(2)}) %collective-permute-start.10) | collective-permute-done | bytes 108 | tf_op jit(solution)/shard_map/ppermute | solution.py:123
  55.4 2.0 %collective-permute-start.11 = (f32[19]{0:T(128)S(1)}, f32[19]{0:T(128)S(1)}, u32[]{:S(2)}, u32[]{:S(2)}) collective-permute-start(f32[19]{0:T(128)S(1)} %add.125), channel_id=1, source_target_pairs={{0,6},{1,7},{2,4},{3,5},{4,2},{5,3},{6,0},{7,1},{8,14},{9,15},{10,... | collective-permute-start | bytes 236 | tf_op jit(solution)/shard_map/ppermute | solution.py:123
  57.4 3.6 %collective-permute-done.11 = f32[19]{0:T(128)S(1)} collective-permute-done((f32[19]{0:T(128)S(1)}, f32[19]{0:T(128)S(1)}, u32[]{:S(2)}, u32[]{:S(2)}) %collective-permute-start.11) | collective-permute-done | bytes 108 | tf_op jit(solution)/shard_map/ppermute | solution.py:123
  61.1 3.0 %collective-permute-start.12 = (f32[4,4,8,128]{3,2,1,0:T(8,128)S(1)}, f32[4,4,8,128]{3,2,1,0:T(8,128)S(1)}, u32[]{:S(2)}, u32[]{:S(2)}) collective-permute-start(f32[4,4,8,128]{3,2,1,0:T(8,128)S(1)} %select_maximum_fusion), channel_id=1, source_target_pairs={{0,128},{128,0},{1,129},{129,1},{2,130},{130,2},{3,131},{131,3},{4... | collective-permute-start | bytes 196616 | tf_op jit(solution)/shard_map/ppermute | solution.py:239
  64.2 2.7 %collective-permute-done.12 = f32[4,4,8,128]{3,2,1,0:T(8,128)S(1)} collective-permute-done((f32[4,4,8,128]{3,2,1,0:T(8,128)S(1)}, f32[4,4,8,128]{3,2,1,0:T(8,128)S(1)}, u32[]{:S(2)}, u32[]{:S(2)}) %collective-permute-start.12) | collective-permute-done | bytes 65568 | tf_op jit(solution)/shard_map/ppermute | solution.py:239
  67.5 1.0 %copy.112 = f32[28,4,8,128]{3,2,1,0:T(8,128)} copy(f32[28,4,8,128]{3,0,2,1:T(8,128)S(1)} %copy_select_fusion) | data formatting | bytes 917504
  (119 shorter events, 8.6 us)
Async XLA Ops:
  0.6 1.3 %copy-start.4 = (f32[19]{0:T(128)S(1)}, f32[19]{0:T(128)}, u32[]{:S(2)}) copy-start(f32[19]{0:T(128)} %constant.126) | copy-start | bytes 232
  0.6 1.3 %copy-start.5 = (f32[19]{0:T(128)S(1)}, f32[19]{0:T(128)}, u32[]{:S(2)}) copy-start(f32[19]{0:T(128)} %constant.127) | copy-start | bytes 232
  0.7 1.3 %copy-start.6 = (f32[19]{0:T(128)S(1)}, f32[19]{0:T(128)}, u32[]{:S(2)}) copy-start(f32[19]{0:T(128)} %constant.128) | copy-start | bytes 232
  2.0 5.3 %copy-start = (f32[28,4,8,128]{3,2,1,0:T(8,128)S(1)}, f32[28,4,8,128]{3,2,1,0:T(8,128)}, u32[]{:S(2)}) copy-start(f32[28,4,8,128]{3,2,1,0:T(8,128)} %param.22) | copy-start | bytes 1376260
  2.4 7.6 %collective-permute-start = (f32[3,4,8,128]{3,2,1,0:T(8,128)S(1)}, f32[3,4,8,128]{3,2,1,0:T(8,128)S(1)}, u32[]{:S(2)}, u32[]{:S(2)}) collective-permute-start(f32[3,4,8,128]{3,2,1,0:T(8,128)S(1)} %maximum_divide_fusion), channel_id=1, source_target_pairs={{0,128},{1,129},{2,130},{3,131},{4,132},{5,133},{6,134},{7,135},{8... | collective-permute-start | bytes 147464 | tf_op jit(solution)/shard_map/ppermute | solution.py:144
  7.3 0.7 %copy-start.3 = (s32[4,8,128]{2,1,0:T(8,128)S(1)}, s32[4,8,128]{2,1,0:T(8,128)}, u32[]{:S(2)}) copy-start(s32[4,8,128]{2,1,0:T(8,128)} %param.23) | copy-start | bytes 49156
  8.1 0.7 copy-start.17
  8.1 0.7 copy-start.18
  8.1 0.7 %copy-start.13 = (f32[28,1,1,1]{0,3,2,1:T(1,128)S(1)}, f32[28,1,1,1]{0,3,2,1:T(1,128)}, u32[]{:S(2)}) copy-start(f32[28,1,1,1]{0,3,2,1:T(1,128)} %constant.104.clone) | copy-start | bytes 340
  8.1 0.7 %copy-start.14 = (f32[28,1,1,1]{0,3,2,1:T(1,128)S(1)}, f32[28,1,1,1]{0,3,2,1:T(1,128)}, u32[]{:S(2)}) copy-start(f32[28,1,1,1]{0,3,2,1:T(1,128)} %constant.105.clone) | copy-start | bytes 340
  8.1 0.7 %copy-start.15 = (f32[28,1,1,1]{0,3,2,1:T(1,128)S(1)}, f32[28,1,1,1]{0,3,2,1:T(1,128)}, u32[]{:S(2)}) copy-start(f32[28,1,1,1]{0,3,2,1:T(1,128)} %constant.108.clone) | copy-start | bytes 340
  8.2 0.7 %copy-start.16 = (f32[28,1,1,1]{0,3,2,1:T(1,128)S(1)}, f32[28,1,1,1]{0,3,2,1:T(1,128)}, u32[]{:S(2)}) copy-start(f32[28,1,1,1]{0,3,2,1:T(1,128)} %constant.109.clone) | copy-start | bytes 340
  8.2 0.9 %copy-start.19 = (f32[15]{0:T(128)S(1)}, f32[15]{0:T(128)}, u32[]{:S(2)}) copy-start(f32[15]{0:T(128)} %param.24) | copy-start | bytes 184
  8.2 1.0 %copy-start.1 = (f32[28,4,8,128]{3,2,1,0:T(8,128)S(1)}, f32[28,4,8,128]{3,2,1,0:T(8,128)}, u32[]{:S(2)}) copy-start(f32[28,4,8,128]{3,2,1,0:T(8,128)} %param.26) | copy-start | bytes 1376260
  10.0 0.7 %copy-start.2 = (f32[19,19,1,1]{0,1,3,2:T(8,128)S(1)}, f32[19,19,1,1]{0,1,3,2:T(8,128)}, u32[]{:S(2)}) copy-start(f32[19,19,1,1]{0,1,3,2:T(8,128)} %constant.133) | copy-start | bytes 4336
  10.1 0.7 copy-start.20
  11.4 0.7 copy-start.8
  11.5 0.7 copy-start.9
  11.5 0.7 copy-start.10
  11.5 0.7 copy-start.11
  12.8 6.4 %collective-permute-start.1 = (f32[56,4,1,128]{3,0,2,1:T(8,128)S(1)}, f32[56,4,1,128]{3,0,2,1:T(8,128)S(1)}, u32[]{:S(2)}, u32[]{:S(2)}) collective-permute-start(f32[56,4,1,128]{3,0,2,1:T(8,128)S(1)} %get-tuple-element.54), channel_id=1, source_target_pairs={{0,8},{8,16},{16,24},{24,32},{32,40},{40,48},{48,56},{56,64},{64,7... | collective-permute-start | bytes 344072 | tf_op jit(solution)/shard_map/ppermute | solution.py:78
  12.9 6.3 %collective-permute-start.2 = (f32[56,4,1,128]{3,0,2,1:T(8,128)S(1)}, f32[56,4,1,128]{3,0,2,1:T(8,128)S(1)}, u32[]{:S(2)}, u32[]{:S(2)}) collective-permute-start(f32[56,4,1,128]{3,0,2,1:T(8,128)S(1)} %get-tuple-element.53), channel_id=1, source_target_pairs={{0,120},{8,0},{16,8},{24,16},{32,24},{40,32},{48,40},{56,48},{64,5... | collective-permute-start | bytes 344072 | tf_op jit(solution)/shard_map/ppermute | solution.py:79
  20.3 3.8 %collective-permute-start.3 = (f32[56,4,8]{0,2,1:T(8,128)S(1)}, f32[56,4,8]{0,2,1:T(8,128)S(1)}, u32[]{:S(2)}, u32[]{:S(2)}) collective-permute-start(f32[56,4,8]{0,2,1:T(8,128)S(1)} %get-tuple-element.34), channel_id=1, source_target_pairs={{0,1},{1,2},{2,3},{3,4},{4,5},{5,6},{6,7},{7,0},{8,9},{9,10},{10,1... | collective-permute-start | bytes 21512 | tf_op jit(solution)/shard_map/ppermute | solution.py:83
  22.3 3.7 %collective-permute-start.4 = (f32[56,4,8]{0,2,1:T(8,128)S(1)}, f32[56,4,8]{0,2,1:T(8,128)S(1)}, u32[]{:S(2)}, u32[]{:S(2)}) collective-permute-start(f32[56,4,8]{0,2,1:T(8,128)S(1)} %get-tuple-element.35), channel_id=1, source_target_pairs={{0,7},{1,0},{2,1},{3,2},{4,3},{5,4},{6,5},{7,6},{8,15},{9,8},{10,9... | collective-permute-start | bytes 21512 | tf_op jit(solution)/shard_map/ppermute | solution.py:84
  30.3 2.0 %collective-permute-start.5 = (f32[19]{0:T(128)S(1)}, f32[19]{0:T(128)S(1)}, u32[]{:S(2)}, u32[]{:S(2)}) collective-permute-start(f32[19]{0:T(128)S(1)} %broadcast_select_fusion.1), channel_id=1, source_target_pairs={{0,8},{8,0},{16,24},{24,16},{32,40},{40,32},{48,56},{56,48},{64,72... | collective-permute-start | bytes 236 | tf_op jit(solution)/shard_map/ppermute | solution.py:123
  32.4 3.6 %collective-permute-start.6 = (f32[19]{0:T(128)S(1)}, f32[19]{0:T(128)S(1)}, u32[]{:S(2)}, u32[]{:S(2)}) collective-permute-start(f32[19]{0:T(128)S(1)} %add.117), channel_id=1, source_target_pairs={{0,16},{8,24},{16,0},{24,8},{32,48},{40,56},{48,32},{56,40},{64,80... | collective-permute-start | bytes 236 | tf_op jit(solution)/shard_map/ppermute | solution.py:123
  36.3 3.6 %collective-permute-start.7 = (f32[19]{0:T(128)S(1)}, f32[19]{0:T(128)S(1)}, u32[]{:S(2)}, u32[]{:S(2)}) collective-permute-start(f32[19]{0:T(128)S(1)} %add.121), channel_id=1, source_target_pairs={{0,32},{8,40},{16,48},{24,56},{32,0},{40,8},{48,16},{56,24},{64,96... | collective-permute-start | bytes 236 | tf_op jit(solution)/shard_map/ppermute | solution.py:123
  39.9 4.8 %collective-permute-start.8 = (f32[19]{0:T(128)S(1)}, f32[19]{0:T(128)S(1)}, u32[]{:S(2)}, u32[]{:S(2)}) collective-permute-start(f32[19]{0:T(128)S(1)} %add.122), channel_id=1, source_target_pairs={{0,96},{8,104},{16,112},{24,120},{32,64},{40,72},{48,80},{56,88},{... | collective-permute-start | bytes 236 | tf_op jit(solution)/shard_map/ppermute | solution.py:123
  44.7 3.5 %collective-permute-start.9 = (f32[19]{0:T(128)S(1)}, f32[19]{0:T(128)S(1)}, u32[]{:S(2)}, u32[]{:S(2)}) collective-permute-start(f32[19]{0:T(128)S(1)} %add.123), channel_id=1, source_target_pairs={{0,1},{1,0},{2,3},{3,2},{4,5},{5,4},{6,7},{7,6},{8,9},{9,8},{10,11... | collective-permute-start | bytes 236 | tf_op jit(solution)/shard_map/ppermute | solution.py:123
  48.2 7.2 %collective-permute-start.10 = (f32[19]{0:T(128)S(1)}, f32[19]{0:T(128)S(1)}, u32[]{:S(2)}, u32[]{:S(2)}) collective-permute-start(f32[19]{0:T(128)S(1)} %add.124), channel_id=1, source_target_pairs={{0,2},{1,3},{2,0},{3,1},{4,6},{5,7},{6,4},{7,5},{8,10},{9,11},{10,... | collective-permute-start | bytes 236 | tf_op jit(solution)/shard_map/ppermute | solution.py:123
  55.4 5.7 %collective-permute-start.11 = (f32[19]{0:T(128)S(1)}, f32[19]{0:T(128)S(1)}, u32[]{:S(2)}, u32[]{:S(2)}) collective-permute-start(f32[19]{0:T(128)S(1)} %add.125), channel_id=1, source_target_pairs={{0,6},{1,7},{2,4},{3,5},{4,2},{5,3},{6,0},{7,1},{8,14},{9,15},{10,... | collective-permute-start | bytes 236 | tf_op jit(solution)/shard_map/ppermute | solution.py:123
  61.1 5.9 %collective-permute-start.12 = (f32[4,4,8,128]{3,2,1,0:T(8,128)S(1)}, f32[4,4,8,128]{3,2,1,0:T(8,128)S(1)}, u32[]{:S(2)}, u32[]{:S(2)}) collective-permute-start(f32[4,4,8,128]{3,2,1,0:T(8,128)S(1)} %select_maximum_fusion), channel_id=1, source_target_pairs={{0,128},{128,0},{1,129},{129,1},{2,130},{130,2},{3,131},{131,3},{4... | collective-permute-start | bytes 196616 | tf_op jit(solution)/shard_map/ppermute | solution.py:239
  (2 other events, 1.3 us)

commit v6 on v5

--- a/solution.py
+++ b/solution.py
@@ -142,14 +142,15 @@
         [jnp.sum(flow * vx, 0), jnp.sum(flow * vy, 0), jnp.sum(flow * vz, 0)]
     ) / density[None]
     sent_motion = lax.ppermute(own_motion, "sec", [(0, 1)])
-    motion = jnp.where(is_flow, own_motion, sent_motion)
 
     small_weights = column([0.25] + [0.125] * 6)
     grouped = populations.reshape((groups, 7) + populations.shape[1:])
     species_r = species_rates.reshape((groups, 1, 1, 1, 1))
     concentration = jnp.sum(grouped, 1)
     sx, sy, sz = (column(velocity[:7, d])[None] for d in range(3))
-    projected_small = motion[0][None] * sx[0] + motion[1][None] * sy[0] + motion[2][None] * sz[0]
+    projected_small = (
+        sent_motion[0][None] * sx[0] + sent_motion[1][None] * sy[0] + sent_motion[2][None] * sz[0]
+    )
     factor = small_weights * (1.0 + 4.0 * projected_small)
     species_eq = factor[None] * concentration[:, None]
     species_gap = grouped - species_eq
@@ -160,27 +161,26 @@
     q_table = jnp.asarray(ortho, jnp.float32)
     relax = jnp.concatenate([jnp.zeros((4,), flow_rates.dtype), flow_rates]).reshape(19, 1, 1, 1)
     w = column(weights)
-    projected = vx * motion[0][None] + vy * motion[1][None] + vz * motion[2][None]
-    squared = jnp.sum(motion * motion, 0)
+    projected = vx * own_motion[0][None] + vy * own_motion[1][None] + vz * own_motion[2][None]
+    squared = jnp.sum(own_motion * own_motion, 0)
     poly = w * (1.0 + 3.0 * projected + 4.5 * projected * projected - 1.5 * squared[None])
     equilibrium = density[None] * poly
     moments = jnp.einsum("ji,jxyz->ixyz", q_table, flow - equilibrium, precision=highest)
     flow_relaxed = flow - jnp.einsum("ij,jxyz->ixyz", q_table, relax * moments, precision=highest)
     flow_post = jnp.where(fluid, flow_relaxed, reverse_pairs(flow, opposite))
     filler = jnp.zeros((rows - 19,) + populations.shape[1:], jnp.float32)
-    post = jnp.where(is_flow, jnp.concatenate([flow_post, filler]), species_post)
 
     flow_moves = np.concatenate([velocity, np.zeros((rows - 19, 3))])
     species_moves = np.tile(velocity[:7], (groups, 1))
     both_moves = []
+    species_post_moves = []
     for d in range(3):
         table = jnp.where(is_flow, column(flow_moves[:, d]), column(species_moves[:, d]))
-        both_moves.append(jnp.concatenate([table, -table]))
-    both = shift_rows(jnp.concatenate([post, cotangents]), both_moves)
-    moved = both[:rows]
+        both_moves.append(jnp.concatenate([column(flow_moves[:, d]), -table]))
+        species_post_moves.append(column(species_moves[:, d]))
+    first = jnp.concatenate([jnp.concatenate([flow_post, filler]), cotangents])
+    both = shift_rows(first, both_moves)
     returned = both[rows:]
-    moved = jnp.where(is_flow, jnp.concatenate([moved[:19], filler]), moved)
-
     back_species = returned.reshape(grouped.shape)
     back_flow = returned[:19]
     species_rate_grad = -jnp.sum(
@@ -209,7 +209,7 @@
         hwp = hw * (3.0 + 9.0 * projected)
         later["motion_grad"] = density[None] * (
             jnp.stack([jnp.sum(hwp * vx, 0), jnp.sum(hwp * vy, 0), jnp.sum(hwp * vz, 0)])
-            - 3.0 * motion * hw_sum[None]
+            - 3.0 * own_motion * hw_sum[None]
         )
         later["flow_base"] = back_flow_ - through_eq + density_grad[None]
         return values
@@ -232,7 +232,15 @@
         )
         return values
 
-    partial_rates = butterfly_sum(local_rates, (("gy", 4), ("gz", 1)), [flow_adjoint, species_adjoint])
+    def species_passing(values):
+        values, species_post_ = lax.optimization_barrier((values, species_post))
+        later["species_moved"] = shift_rows(species_post_, species_post_moves)
+        return values
+
+    partial_rates = butterfly_sum(
+        local_rates, (("gy", 4), ("gz", 1)), [species_passing, flow_adjoint, species_adjoint]
+    )
+    moved = jnp.where(is_flow, both[:rows], later["species_moved"])
     plane = populations.shape[1:]
     rate_plane = jnp.zeros(plane, jnp.float32).at[0, 0, : partial_rates.shape[0]].set(partial_rates)
     payload = jnp.concatenate([later["species_motion_grad"], rate_plane[None]])
@@ -241,7 +249,7 @@
 
     motion_grad = jnp.where(fluid, later["motion_grad"] + other[:3], 0.0)
     along = vx * motion_grad[0][None] + vy * motion_grad[1][None] + vz * motion_grad[2][None]
-    extra = (along - jnp.sum(motion * motion_grad, 0)[None]) / density[None]
+    extra = (along - jnp.sum(own_motion * motion_grad, 0)[None]) / density[None]
     flow_grad = jnp.where(
         fluid, later["flow_base"] + extra, reverse_pairs(back_flow, opposite)
     )

time: 69.4 us -> 89.9 us (1.30)
  the two profiles are of different devices: /device:TPU:32 before, /device:TPU:4 now
where the time goes in v6:
time: 89.9 us; the launch traced here: 89 us
  starting transfers between devices  31.5 us (35%)
  local copies, waits for them, and re-layouts  25.1 us (28%)
  waiting for transfers between devices  15.6 us (17%)
  other arithmetic  12.5 us (14%)
  matrix products  2.33 us (3%)
  between operations  1.85 us (2%)
    unnamed x208, local copies, waits for them, and re-layouts  18.7 us
    ppermute x7, waiting for transfers between devices, butterfly_sum(): values = values + lax.ppermute(values, axis, list(enumerate(targets)))  12 us
    ppermute x7, starting transfers between devices, butterfly_sum(): values = values + lax.ppermute(values, axis, list(enumerate(targets)))  8.09 us
    ppermute x2, starting transfers between devices, shift_rows(): high = lax.ppermute(field[:, :, :1, :], 'gy', ring('gy', -1))  7.32 us
    ppermute x2, starting transfers between devices, shift_rows(): high = lax.ppermute(field[:, :, :, 0], 'gz', ring('gz', -1))  5.24 us
    ppermute x1, starting transfers between devices, per_device(): other = lax.ppermute(payload, 'sec', [(0, 1), (1, 0)])  4.83 us
    ppermute x2, starting transfers between devices, shift_rows(): low = lax.ppermute(field[:, :, :, size_z - 1], 'gz', ring('gz', 1))  4.09 us
    ppermute x2, waiting for transfers between devices, shift_rows(): low = lax.ppermute(field[:, :, :, size_z - 1], 'gz', ring('gz', 1))  2.82 us
  transfers between devices with their start and end apart: 17, of which 8 were waited for; matrix products, arithmetic and copies ran while one was open for 16% of the time, Pallas kernels for 0%

profile of v6, /device:TPU:4, one launch (start us, length us, event | category | flops | bytes accessed | tf_op | source)
XLA Modules:
  0.0 89.0 jit_solution(12936177079075418390)
XLA Ops:
  0.7 1.3 %copy.93 = f32[28,4,8,128]{3,0,2,1:T(8,128)S(1)} copy(f32[28,4,8,128]{3,2,1,0:T(8,128)} %param.28) | data formatting | bytes 917504 | tf_op args[0]
  2.4 1.4 %collective-permute-start.4 = (f32[3,4,8,128]{3,2,1,0:T(8,128)S(1)}, f32[3,4,8,128]{3,2,1,0:T(8,128)}, u32[]{:S(2)}, u32[]{:S(2)}) collective-permute-start(f32[3,4,8,128]{3,2,1,0:T(8,128)S(1)} %get-tuple-element.56), channel_id=1, source_target_pairs={{0,128},{1,129},{2,130},{3,131},{4,132},{5,133},{6,134},{7,135},{8... | collective-permute-start | bytes 147464 | tf_op jit(solution)/shard_map/ppermute | solution.py:144
  4.0 0.7 copy-done.36
  8.1 0.7 fusion.74
  8.8 3.9 %collective-permute-start.1 = (f32[56,4,1,128]{3,0,2,1:T(8,128)}, f32[56,4,1,128]{3,0,2,1:T(8,128)}, u32[]{:S(2)}, u32[]{:S(2)}) collective-permute-start(f32[56,4,1,128]{3,0,2,1:T(8,128)} %get-tuple-element.88), channel_id=1, source_target_pairs={{0,120},{8,0},{16,8},{24,16},{32,24},{40,32},{48,40},{56,48},{64,5... | collective-permute-start | bytes 344072 | tf_op jit(solution)/shard_map/ppermute | solution.py:79
  19.3 0.8 slice_bitcast_fusion.5
  21.5 1.3 %bitcast_select_fusion.1 = (f32[4,7,4,8,128]{4,3,2,1,0:T(8,128)S(1)}, f32[4,7,4,8,128]{4,3,2,1,0:T(8,128)S(1)}) fusion(f32[7,4,4,8,128]{4,3,2,0,1:T(8,128)} %copy-done.5, f32[4,7,4,8,128]{4,3,2,1,0:T(8,128)S(1)} %bitcast.86, f32[4]{0:T(128)S(1)} %copy-done.52, pred[4,8,128]{2,1,0:T(8,128)(4,1)S(1)} %copy-done.12, f32[4,4,8,128]{3,2,1,0:T(8,128)S(1)} %reduce_sum.184, ...), kind=kLoop, calls=%fused_computation.28 | loop fusion | flops 573440 | bytes 2019344 | tf_op jit(solution)/shard_map/jit(_where)/select_n | solution.py:159
  23.5 1.2 %maximum_select_fusion = f32[56,4,8,128]{3,0,2,1:T(8,128)S(1)} fusion(f32[56,4,7,128]{3,0,2,1:T(8,128)S(1)} %get-tuple-element.87, f32[56,4,1,128]{3,0,2,1:T(8,128)} %collective-permute-done, f32[56,4,1,128]{3,0,2,1:T(8,128)} %collective-permute-done.1, f32[56,4,7,128]{3,0,2,1:T(8,128)S(1)} %get-tuple-element.86, pred[56]{0:T(512)(128)(4,1)S(1)} %copy-done.60, ...), kind=kLoop, calls=%fused_computation.4 | loop fusion | flops 1376256 | bytes 3522896 | tf_op jit(solution)/shard_map/jit(_where)/select_n | solution.py:82
  24.7 0.8 slice_reduce_fusion.4
  25.5 2.0 %collective-permute-start.2 = (f32[56,4,8]{0,2,1:T(8,128)S(1)}, f32[56,4,8]{0,2,1:T(8,128)S(1)}, u32[]{:S(2)}, u32[]{:S(2)}) collective-permute-start(f32[56,4,8]{0,2,1:T(8,128)S(1)} %get-tuple-element.38), channel_id=1, source_target_pairs={{0,1},{1,2},{2,3},{3,4},{4,5},{5,6},{6,7},{7,0},{8,9},{9,10},{10,1... | collective-permute-start | bytes 21512 | tf_op jit(solution)/shard_map/ppermute | solution.py:83
  27.5 4.0 %collective-permute-start.3 = (f32[56,4,8]{0,2,1:T(8,128)S(1)}, f32[56,4,8]{0,2,1:T(8,128)S(1)}, u32[]{:S(2)}, u32[]{:S(2)}) collective-permute-start(f32[56,4,8]{0,2,1:T(8,128)S(1)} %get-tuple-element.39), channel_id=1, source_target_pairs={{0,7},{1,0},{2,1},{3,2},{4,3},{5,4},{6,5},{7,6},{8,15},{9,8},{10,9... | collective-permute-start | bytes 21512 | tf_op jit(solution)/shard_map/ppermute | solution.py:84
  31.8 1.3 %collective-permute-done.2 = f32[56,4,8]{0,2,1:T(8,128)S(1)} collective-permute-done((f32[56,4,8]{0,2,1:T(8,128)S(1)}, f32[56,4,8]{0,2,1:T(8,128)S(1)}, u32[]{:S(2)}, u32[]{:S(2)}) %collective-permute-start.2) | collective-permute-done | bytes 7200 | tf_op jit(solution)/shard_map/ppermute | solution.py:83
  33.8 1.2 %fusion.2 = f32[56,4,8,128]{3,0,2,1:T(8,128)S(1)} fusion(f32[56,4,8,127]{3,0,2,1:T(8,128)S(1)} %get-tuple-element.85, f32[56,4,8,1]{3,0,2,1:T(8,128)S(1)} %get-tuple-element.83, f32[56,4,8,128]{3,0,2,1:T(8,128)S(1)} %maximum_select_fusion, f32[56,4,8,1]{3,0,2,1:T(8,128)S(1)} %get-tuple-element.82, f32[56,4,8,127]{3,0,2,1:T(8,128)S(1)} %get-tuple-element.84, ...), kind=kLoop, calls=%fused_computation.7 | loop fusion | flops 1376256 | bytes 3684720 | tf_op jit(solution)/shard_map/jit(_where)/select_n | solution.py:88
  37.0 0.9 %fusion.68 = (f32[1,4,8,128]{3,0,2,1:T(1,128)}, f32[1,4,8,128]{3,0,2,1:T(1,128)}, f32[1,4,8,128]{3,0,2,1:T(1,128)}, f32[1,4,8,128]{3,0,2,1:T(1,128)}, f32[1,4,8,...) fusion(f32[56,4,8,128]{3,0,2,1:T(8,128)S(1)} %maximum_select_fu, ...), kind=kLoop, calls=%fused_computation.162 | loop fusion | bytes 622592 | tf_op jit(solution)/shard_map/slice | solution.py:95
  37.9 1.2 %fusion.69 = (f32[28,4,8,128]{3,0,2,1:T(8,128)S(1)}, f32[28]{0:T(128)}) fusion(f32[56,4,8,128]{3,0,2,1:T(8,128)S(1)} %maximum_select_fusion.4, f32[28,4,8,128]{3,2,1,0:T(8,128)S(1)} %bitcast.98, f32[28,4,8,128]{3,2,1,0:T(8,128)S(1)} %copy-done, pred[4,8,128]{2,1,0:T(8,128)(4,1)S(1)} %copy-done.12), kind=kLoop, calls=%fused_computation.163 | loop fusion | flops 458724 | bytes 1839216 | tf_op jit(solution)/shard_map/slice | solution.py:183
  43.3 3.5 %collective-permute-start.7 = (f32[28,4,1,128]{3,0,2,1:T(8,128)S(1)}, f32[28,4,1,128]{3,0,2,1:T(8,128)S(1)}, u32[]{:S(2)}, u32[]{:S(2)}) collective-permute-start(f32[28,4,1,128]{3,0,2,1:T(8,128)S(1)} %get-tuple-element.100), channel_id=1, source_target_pairs={{0,120},{8,0},{16,8},{24,16},{32,24},{40,32},{48,40},{56,48},{64,5... | collective-permute-start | bytes 172040 | tf_op jit(solution)/shard_map/ppermute | solution.py:79
  47.5 0.7 copy-done.38
  48.8 1.5 %collective-permute-done.11 = f32[19]{0:T(128)S(1)} collective-permute-done((f32[19]{0:T(128)S(1)}, f32[19]{0:T(128)S(1)}, u32[]{:S(2)}, u32[]{:S(2)}) %collective-permute-start.11) | collective-permute-done | bytes 108 | tf_op jit(solution)/shard_map/ppermute | solution.py:123
  52.0 1.4 %collective-permute-start.12 = (f32[19]{0:T(128)S(1)}, f32[19]{0:T(128)S(1)}, u32[]{:S(2)}, u32[]{:S(2)}) collective-permute-start(f32[19]{0:T(128)S(1)} %add.120), channel_id=1, source_target_pairs={{0,96},{8,104},{16,112},{24,120},{32,64},{40,72},{48,80},{56,88},{... | collective-permute-start | bytes 236 | tf_op jit(solution)/shard_map/ppermute | solution.py:123
  53.4 3.4 %collective-permute-done.12 = f32[19]{0:T(128)S(1)} collective-permute-done((f32[19]{0:T(128)S(1)}, f32[19]{0:T(128)S(1)}, u32[]{:S(2)}, u32[]{:S(2)}) %collective-permute-start.12) | collective-permute-done | bytes 108 | tf_op jit(solution)/shard_map/ppermute | solution.py:123
  57.6 2.7 %collective-permute-done.13 = f32[19]{0:T(128)S(1)} collective-permute-done((f32[19]{0:T(128)S(1)}, f32[19]{0:T(128)S(1)}, u32[]{:S(2)}, u32[]{:S(2)}) %collective-permute-start.13) | collective-permute-done | bytes 108 | tf_op jit(solution)/shard_map/ppermute | solution.py:123
  60.4 3.7 %collective-permute-start.14 = (f32[19]{0:T(128)S(1)}, f32[19]{0:T(128)S(1)}, u32[]{:S(2)}, u32[]{:S(2)}) collective-permute-start(f32[19]{0:T(128)S(1)} %add.122), channel_id=1, source_target_pairs={{0,2},{1,3},{2,0},{3,1},{4,6},{5,7},{6,4},{7,5},{8,10},{9,11},{10,... | collective-permute-start | bytes 236 | tf_op jit(solution)/shard_map/ppermute | solution.py:123
  64.0 1.5 %collective-permute-done.14 = f32[19]{0:T(128)S(1)} collective-permute-done((f32[19]{0:T(128)S(1)}, f32[19]{0:T(128)S(1)}, u32[]{:S(2)}, u32[]{:S(2)}) %collective-permute-start.14) | collective-permute-done | bytes 108 | tf_op jit(solution)/shard_map/ppermute | solution.py:123
  65.5 2.7 %collective-permute-start.15 = (f32[19]{0:T(128)S(1)}, f32[19]{0:T(128)S(1)}, u32[]{:S(2)}, u32[]{:S(2)}) collective-permute-start(f32[19]{0:T(128)S(1)} %add.123), channel_id=1, source_target_pairs={{0,6},{1,7},{2,4},{3,5},{4,2},{5,3},{6,0},{7,1},{8,14},{9,15},{10,... | collective-permute-start | bytes 236 | tf_op jit(solution)/shard_map/ppermute | solution.py:123
  68.3 2.9 %collective-permute-done.15 = f32[19]{0:T(128)S(1)} collective-permute-done((f32[19]{0:T(128)S(1)}, f32[19]{0:T(128)S(1)}, u32[]{:S(2)}, u32[]{:S(2)}) %collective-permute-start.15) | collective-permute-done | bytes 108 | tf_op jit(solution)/shard_map/ppermute | solution.py:123
  71.2 4.8 %collective-permute-start.16 = (f32[4,4,8,128]{3,2,1,0:T(8,128)S(1)}, f32[4,4,8,128]{3,2,1,0:T(8,128)S(1)}, u32[]{:S(2)}, u32[]{:S(2)}) collective-permute-start(f32[4,4,8,128]{3,2,1,0:T(8,128)S(1)} %select_maximum_fusion), channel_id=1, source_target_pairs={{0,128},{128,0},{1,129},{129,1},{2,130},{130,2},{3,131},{131,3},{4... | collective-permute-start | bytes 196616 | tf_op jit(solution)/shard_map/ppermute | solution.py:247
  77.5 2.1 %collective-permute-start.8 = (f32[28,4,8]{0,2,1:T(8,128)S(1)}, f32[28,4,8]{0,2,1:T(8,128)S(1)}, u32[]{:S(2)}, u32[]{:S(2)}) collective-permute-start(f32[28,4,8]{0,2,1:T(8,128)S(1)} %get-tuple-element.40), channel_id=1, source_target_pairs={{0,1},{1,2},{2,3},{3,4},{4,5},{5,6},{6,7},{7,0},{8,9},{9,10},{10,1... | collective-permute-start | bytes 10760 | tf_op jit(solution)/shard_map/ppermute | solution.py:83
  79.6 1.2 %collective-permute-start.9 = (f32[28,4,8]{0,2,1:T(8,128)S(1)}, f32[28,4,8]{0,2,1:T(8,128)S(1)}, u32[]{:S(2)}, u32[]{:S(2)}) collective-permute-start(f32[28,4,8]{0,2,1:T(8,128)S(1)} %get-tuple-element.41), channel_id=1, source_target_pairs={{0,7},{1,0},{2,1},{3,2},{4,3},{5,4},{6,5},{7,6},{8,15},{9,8},{10,9... | collective-permute-start | bytes 10760 | tf_op jit(solution)/shard_map/ppermute | solution.py:84
  81.1 1.5 %collective-permute-done.8 = f32[28,4,8]{0,2,1:T(8,128)S(1)} collective-permute-done((f32[28,4,8]{0,2,1:T(8,128)S(1)}, f32[28,4,8]{0,2,1:T(8,128)S(1)}, u32[]{:S(2)}, u32[]{:S(2)}) %collective-permute-start.8) | collective-permute-done | bytes 3616 | tf_op jit(solution)/shard_map/ppermute | solution.py:83
  82.6 0.8 collective-permute-done.9
  85.8 1.0 %copy.125 = f32[28,4,8,128]{3,2,1,0:T(8,128)} copy(f32[28,4,8,128]{3,0,2,1:T(8,128)S(1)} %slice_select_fusion) | data formatting | bytes 917504
  87.4 1.0 %copy.126 = f32[28,4,8,128]{3,2,1,0:T(8,128)} copy(f32[28,4,8,128]{3,0,2,1:T(8,128)S(1)} %copy_select_fusion) | data formatting | bytes 917504
  (289 shorter events, 28.1 us)
Async XLA Ops:
  2.4 3.2 %copy-start.13 = (f32[4,8,128]{2,1,0:T(8,128)}, f32[4,8,128]{2,1,0:T(8,128)S(1)}, u32[]{:S(2)}) copy-start(f32[4,8,128]{2,1,0:T(8,128)S(1)} %get-tuple-element.42) | copy-start | bytes 49156
  2.4 2.3 %copy-start.8 = (f32[28,4,8,128]{3,2,1,0:T(8,128)S(1)}, f32[28,4,8,128]{3,2,1,0:T(8,128)}, u32[]{:S(2)}) copy-start(f32[28,4,8,128]{3,2,1,0:T(8,128)} %param.32) | copy-start | bytes 1376260
  2.4 16.9 %collective-permute-start.4 = (f32[3,4,8,128]{3,2,1,0:T(8,128)S(1)}, f32[3,4,8,128]{3,2,1,0:T(8,128)}, u32[]{:S(2)}, u32[]{:S(2)}) collective-permute-start(f32[3,4,8,128]{3,2,1,0:T(8,128)S(1)} %get-tuple-element.56), channel_id=1, source_target_pairs={{0,128},{1,129},{2,130},{3,131},{4,132},{5,133},{6,134},{7,135},{8... | collective-permute-start | bytes 147464 | tf_op jit(solution)/shard_map/ppermute | solution.py:144
  4.7 2.7 %copy-start.11 = (pred[4,8,128]{2,1,0:T(8,128)(4,1)}, pred[4,8,128]{2,1,0:T(8,128)(4,1)S(1)}, u32[]{:S(2)}) copy-start(pred[4,8,128]{2,1,0:T(8,128)(4,1)S(1)} %broadcast_compare_fusion) | copy-start | bytes 12292
  5.5 2.4 %copy-start.73 = (f32[56]{0:T(128)}, f32[56]{0:T(128)S(1)}, u32[]{:S(2)}) copy-start(f32[56]{0:T(128)S(1)} %pad.41.clone) | copy-start | bytes 676
  8.8 14.0 %collective-permute-start = (f32[56,4,1,128]{3,0,2,1:T(8,128)}, f32[56,4,1,128]{3,0,2,1:T(8,128)}, u32[]{:S(2)}, u32[]{:S(2)}) collective-permute-start(f32[56,4,1,128]{3,0,2,1:T(8,128)} %get-tuple-element.89), channel_id=1, source_target_pairs={{0,8},{8,16},{16,24},{24,32},{32,40},{40,48},{48,56},{56,64},{64,7... | collective-permute-start | bytes 344072 | tf_op jit(solution)/shard_map/ppermute | solution.py:78
  8.8 14.0 %collective-permute-start.1 = (f32[56,4,1,128]{3,0,2,1:T(8,128)}, f32[56,4,1,128]{3,0,2,1:T(8,128)}, u32[]{:S(2)}, u32[]{:S(2)}) collective-permute-start(f32[56,4,1,128]{3,0,2,1:T(8,128)} %get-tuple-element.88), channel_id=1, source_target_pairs={{0,120},{8,0},{16,8},{24,16},{32,24},{40,32},{48,40},{56,48},{64,5... | collective-permute-start | bytes 344072 | tf_op jit(solution)/shard_map/ppermute | solution.py:79
  14.1 6.1 %copy-start.5 = (f32[7,4,4,8,128]{4,3,2,0,1:T(8,128)}, f32[7,4,4,8,128]{4,3,2,0,1:T(8,128)S(1)}, u32[]{:S(2)}) copy-start(f32[7,4,4,8,128]{4,3,2,0,1:T(8,128)S(1)} %slice_dynamic-update-slice_fusion.7) | copy-start | bytes 1376260
  25.5 7.7 %collective-permute-start.2 = (f32[56,4,8]{0,2,1:T(8,128)S(1)}, f32[56,4,8]{0,2,1:T(8,128)S(1)}, u32[]{:S(2)}, u32[]{:S(2)}) collective-permute-start(f32[56,4,8]{0,2,1:T(8,128)S(1)} %get-tuple-element.38), channel_id=1, source_target_pairs={{0,1},{1,2},{2,3},{3,4},{4,5},{5,6},{6,7},{7,0},{8,9},{9,10},{10,1... | collective-permute-start | bytes 21512 | tf_op jit(solution)/shard_map/ppermute | solution.py:83
  27.5 5.7 %collective-permute-start.3 = (f32[56,4,8]{0,2,1:T(8,128)S(1)}, f32[56,4,8]{0,2,1:T(8,128)S(1)}, u32[]{:S(2)}, u32[]{:S(2)}) collective-permute-start(f32[56,4,8]{0,2,1:T(8,128)S(1)} %get-tuple-element.39), channel_id=1, source_target_pairs={{0,7},{1,0},{2,1},{3,2},{4,3},{5,4},{6,5},{7,6},{8,15},{9,8},{10,9... | collective-permute-start | bytes 21512 | tf_op jit(solution)/shard_map/ppermute | solution.py:84
  37.9 2.1 %copy-start.2 = (f32[19,4,8,128]{3,0,2,1:T(8,128)S(1)}, f32[19,4,8,128]{3,0,2,1:T(8,128)}, u32[]{:S(2)}) copy-start(f32[19,4,8,128]{3,0,2,1:T(8,128)} %copy-done.1) | copy-start | bytes 933892
  40.3 1.9 %collective-permute-start.5 = (f32[19]{0:T(128)S(1)}, f32[19]{0:T(128)S(1)}, u32[]{:S(2)}, u32[]{:S(2)}) collective-permute-start(f32[19]{0:T(128)S(1)} %broadcast_select_fusion), channel_id=1, source_target_pairs={{0,8},{8,0},{16,24},{24,16},{32,40},{40,32},{48,56},{56,48},{64,72... | collective-permute-start | bytes 236 | tf_op jit(solution)/shard_map/ppermute | solution.py:123
  42.6 4.2 %copy-start.40 = (f32[4,8,128]{2,1,0:T(8,128)S(1)}, f32[4,8,128]{2,1,0:T(8,128)}, u32[]{:S(2)}) copy-start(f32[4,8,128]{2,1,0:T(8,128)} %copy-done.39) | copy-start | bytes 49156
  42.6 4.2 %copy-start.42 = (f32[4,8,128]{2,1,0:T(8,128)S(1)}, f32[4,8,128]{2,1,0:T(8,128)}, u32[]{:S(2)}) copy-start(f32[4,8,128]{2,1,0:T(8,128)} %copy-done.41) | copy-start | bytes 49156
  42.6 4.2 %copy-start.44 = (f32[4,8,128]{2,1,0:T(8,128)S(1)}, f32[4,8,128]{2,1,0:T(8,128)}, u32[]{:S(2)}) copy-start(f32[4,8,128]{2,1,0:T(8,128)} %copy-done.43) | copy-start | bytes 49156
  42.6 4.1 %collective-permute-start.10 = (f32[19]{0:T(128)S(1)}, f32[19]{0:T(128)S(1)}, u32[]{:S(2)}, u32[]{:S(2)}) collective-permute-start(f32[19]{0:T(128)S(1)} %add.115), channel_id=1, source_target_pairs={{0,16},{8,24},{16,0},{24,8},{32,48},{40,56},{48,32},{56,40},{64,80... | collective-permute-start | bytes 236 | tf_op jit(solution)/shard_map/ppermute | solution.py:123
  42.7 33.3 %collective-permute-start.6 = (f32[28,4,1,128]{3,0,2,1:T(8,128)S(1)}, f32[28,4,1,128]{3,0,2,1:T(8,128)S(1)}, u32[]{:S(2)}, u32[]{:S(2)}) collective-permute-start(f32[28,4,1,128]{3,0,2,1:T(8,128)S(1)} %get-tuple-element.101), channel_id=1, source_target_pairs={{0,8},{8,16},{16,24},{24,32},{32,40},{40,48},{48,56},{56,64},{64,7... | collective-permute-start | bytes 172040 | tf_op jit(solution)/shard_map/ppermute | solution.py:78
  43.3 3.5 %copy-start.78 = (f32[19]{0:T(128)S(1)}, f32[19]{0:T(128)}, u32[]{:S(2)}) copy-start(f32[19]{0:T(128)} %copy-done.77) | copy-start | bytes 232
  43.3 3.5 %copy-start.95 = (f32[19]{0:T(128)S(1)}, f32[19]{0:T(128)}, u32[]{:S(2)}) copy-start(f32[19]{0:T(128)} %constant.127) | copy-start | bytes 232
  43.3 3.6 %copy-start.46 = (f32[19]{0:T(128)S(1)}, f32[19]{0:T(128)}, u32[]{:S(2)}) copy-start(f32[19]{0:T(128)} %constant.128) | copy-start | bytes 232
  43.3 3.6 %copy-start.48 = (f32[19]{0:T(128)S(1)}, f32[19]{0:T(128)}, u32[]{:S(2)}) copy-start(f32[19]{0:T(128)} %constant.129) | copy-start | bytes 232
  43.3 3.6 %copy-start.50 = (f32[19]{0:T(128)S(1)}, f32[19]{0:T(128)}, u32[]{:S(2)}) copy-start(f32[19]{0:T(128)} %constant.130) | copy-start | bytes 232
  43.3 32.7 %collective-permute-start.7 = (f32[28,4,1,128]{3,0,2,1:T(8,128)S(1)}, f32[28,4,1,128]{3,0,2,1:T(8,128)S(1)}, u32[]{:S(2)}, u32[]{:S(2)}) collective-permute-start(f32[28,4,1,128]{3,0,2,1:T(8,128)S(1)} %get-tuple-element.100), channel_id=1, source_target_pairs={{0,120},{8,0},{16,8},{24,16},{32,24},{40,32},{48,40},{56,48},{64,5... | collective-permute-start | bytes 172040 | tf_op jit(solution)/shard_map/ppermute | solution.py:79
  46.8 3.5 %collective-permute-start.11 = (f32[19]{0:T(128)S(1)}, f32[19]{0:T(128)S(1)}, u32[]{:S(2)}, u32[]{:S(2)}) collective-permute-start(f32[19]{0:T(128)S(1)} %add.116), channel_id=1, source_target_pairs={{0,32},{8,40},{16,48},{24,56},{32,0},{40,8},{48,16},{56,24},{64,96... | collective-permute-start | bytes 236 | tf_op jit(solution)/shard_map/ppermute | solution.py:123
  52.0 4.8 %collective-permute-start.12 = (f32[19]{0:T(128)S(1)}, f32[19]{0:T(128)S(1)}, u32[]{:S(2)}, u32[]{:S(2)}) collective-permute-start(f32[19]{0:T(128)S(1)} %add.120), channel_id=1, source_target_pairs={{0,96},{8,104},{16,112},{24,120},{32,64},{40,72},{48,80},{56,88},{... | collective-permute-start | bytes 236 | tf_op jit(solution)/shard_map/ppermute | solution.py:123
  56.8 3.5 %collective-permute-start.13 = (f32[19]{0:T(128)S(1)}, f32[19]{0:T(128)S(1)}, u32[]{:S(2)}, u32[]{:S(2)}) collective-permute-start(f32[19]{0:T(128)S(1)} %add.121), channel_id=1, source_target_pairs={{0,1},{1,0},{2,3},{3,2},{4,5},{5,4},{6,7},{7,6},{8,9},{9,8},{10,11... | collective-permute-start | bytes 236 | tf_op jit(solution)/shard_map/ppermute | solution.py:123
  60.4 5.2 %collective-permute-start.14 = (f32[19]{0:T(128)S(1)}, f32[19]{0:T(128)S(1)}, u32[]{:S(2)}, u32[]{:S(2)}) collective-permute-start(f32[19]{0:T(128)S(1)} %add.122), channel_id=1, source_target_pairs={{0,2},{1,3},{2,0},{3,1},{4,6},{5,7},{6,4},{7,5},{8,10},{9,11},{10,... | collective-permute-start | bytes 236 | tf_op jit(solution)/shard_map/ppermute | solution.py:123
  65.5 5.7 %collective-permute-start.15 = (f32[19]{0:T(128)S(1)}, f32[19]{0:T(128)S(1)}, u32[]{:S(2)}, u32[]{:S(2)}) collective-permute-start(f32[19]{0:T(128)S(1)} %add.123), channel_id=1, source_target_pairs={{0,6},{1,7},{2,4},{3,5},{4,2},{5,3},{6,0},{7,1},{8,14},{9,15},{10,... | collective-permute-start | bytes 236 | tf_op jit(solution)/shard_map/ppermute | solution.py:123
  71.2 15.6 %collective-permute-start.16 = (f32[4,4,8,128]{3,2,1,0:T(8,128)S(1)}, f32[4,4,8,128]{3,2,1,0:T(8,128)S(1)}, u32[]{:S(2)}, u32[]{:S(2)}) collective-permute-start(f32[4,4,8,128]{3,2,1,0:T(8,128)S(1)} %select_maximum_fusion), channel_id=1, source_target_pairs={{0,128},{128,0},{1,129},{129,1},{2,130},{130,2},{3,131},{131,3},{4... | collective-permute-start | bytes 196616 | tf_op jit(solution)/shard_map/ppermute | solution.py:247
  77.5 5.0 %collective-permute-start.8 = (f32[28,4,8]{0,2,1:T(8,128)S(1)}, f32[28,4,8]{0,2,1:T(8,128)S(1)}, u32[]{:S(2)}, u32[]{:S(2)}) collective-permute-start(f32[28,4,8]{0,2,1:T(8,128)S(1)} %get-tuple-element.40), channel_id=1, source_target_pairs={{0,1},{1,2},{2,3},{3,4},{4,5},{5,6},{6,7},{7,0},{8,9},{9,10},{10,1... | collective-permute-start | bytes 10760 | tf_op jit(solution)/shard_map/ppermute | solution.py:83
  79.6 3.7 %collective-permute-start.9 = (f32[28,4,8]{0,2,1:T(8,128)S(1)}, f32[28,4,8]{0,2,1:T(8,128)S(1)}, u32[]{:S(2)}, u32[]{:S(2)}) collective-permute-start(f32[28,4,8]{0,2,1:T(8,128)S(1)} %get-tuple-element.41), channel_id=1, source_target_pairs={{0,7},{1,0},{2,1},{3,2},{4,3},{5,4},{6,5},{7,6},{8,15},{9,8},{10,9... | collective-permute-start | bytes 10760 | tf_op jit(solution)/shard_map/ppermute | solution.py:84
  80.9 2.5 %copy-start.92 = (pred[28]{0:T(512)(128)(4,1)S(1)}, pred[28]{0:T(512)(128)(4,1)}, u32[]{:S(2)}) copy-start(pred[28]{0:T(512)(128)(4,1)} %constant.144) | copy-start | bytes 88
  (81 other events, 70.6 us)

commit v7 on v6

--- a/solution.py
+++ b/solution.py
@@ -72,14 +72,17 @@
     return [(i, (i + step) % count) for i in range(count)]
 
 
-def shift_rows(field, moves):
-    move_x, move_y, move_z = moves
-    size_y, size_z = field.shape[2], field.shape[3]
+def shift_y(field, move_y):
+    size_y = field.shape[2]
     low = lax.ppermute(field[:, :, size_y - 1 :, :], "gy", ring("gy", 1))
     high = lax.ppermute(field[:, :, :1, :], "gy", ring("gy", -1))
     from_low = jnp.concatenate([low, field[:, :, : size_y - 1, :]], axis=2)
     from_high = jnp.concatenate([field[:, :, 1:, :], high], axis=2)
-    field = jnp.where(move_y > 0, from_low, jnp.where(move_y < 0, from_high, field))
+    return jnp.where(move_y > 0, from_low, jnp.where(move_y < 0, from_high, field))
+
+
+def shift_zx(field, move_z, move_x):
+    size_z = field.shape[3]
     low = lax.ppermute(field[:, :, :, size_z - 1], "gz", ring("gz", 1))
     high = lax.ppermute(field[:, :, :, 0], "gz", ring("gz", -1))
     lane = lax.broadcasted_iota(jnp.int32, field.shape, 3)
@@ -89,6 +92,10 @@
     from_low = jnp.roll(field, 1, axis=1)
     from_high = jnp.roll(field, -1, axis=1)
     return jnp.where(move_x > 0, from_low, jnp.where(move_x < 0, from_high, field))
+
+
+def shift_rows(field, moves):
+    return shift_zx(shift_y(field, moves[1]), moves[2], moves[0])
 
 
 def reverse_pairs(rows, opposite):
@@ -172,15 +179,10 @@
 
     flow_moves = np.concatenate([velocity, np.zeros((rows - 19, 3))])
     species_moves = np.tile(velocity[:7], (groups, 1))
-    both_moves = []
-    species_post_moves = []
-    for d in range(3):
-        table = jnp.where(is_flow, column(flow_moves[:, d]), column(species_moves[:, d]))
-        both_moves.append(jnp.concatenate([column(flow_moves[:, d]), -table]))
-        species_post_moves.append(column(species_moves[:, d]))
-    first = jnp.concatenate([jnp.concatenate([flow_post, filler]), cotangents])
-    both = shift_rows(first, both_moves)
-    returned = both[rows:]
+    post_moves = [
+        jnp.where(is_flow, column(flow_moves[:, d]), column(species_moves[:, d])) for d in range(3)
+    ]
+    returned = shift_rows(cotangents, [-m for m in post_moves])
     back_species = returned.reshape(grouped.shape)
     back_flow = returned[:19]
     species_rate_grad = -jnp.sum(
@@ -232,15 +234,22 @@
         )
         return values
 
-    def species_passing(values):
-        values, species_post_ = lax.optimization_barrier((values, species_post))
-        later["species_moved"] = shift_rows(species_post_, species_post_moves)
+    def post_passing_y(values):
+        values, post_ = lax.optimization_barrier(
+            (values, jnp.where(is_flow, jnp.concatenate([flow_post, filler]), species_post))
+        )
+        later["post_y"] = shift_y(post_, post_moves[1])
+        return values
+
+    def post_passing_zx(values):
+        values, post_y = lax.optimization_barrier((values, later["post_y"]))
+        later["moved"] = shift_zx(post_y, post_moves[2], post_moves[0])
         return values
 
     partial_rates = butterfly_sum(
-        local_rates, (("gy", 4), ("gz", 1)), [species_passing, flow_adjoint, species_adjoint]
-    )
-    moved = jnp.where(is_flow, both[:rows], later["species_moved"])
+        local_rates, (("gy", 4), ("gz", 1)), [post_passing_y, flow_adjoint, species_adjoint, post_passing_zx]
+    )
+    moved = jnp.where(is_flow, jnp.concatenate([later["moved"][:19], filler]), later["moved"])
     plane = populations.shape[1:]
     rate_plane = jnp.zeros(plane, jnp.float32).at[0, 0, : partial_rates.shape[0]].set(partial_rates)
     payload = jnp.concatenate([later["species_motion_grad"], rate_plane[None]])

time: 89.9 us -> 82.9 us (0.922)
  the two profiles are of different devices: /device:TPU:4 before, /device:TPU:32 now
where the time goes in v7:
time: 82.9 us; the launch traced here: 82.2 us
  starting transfers between devices  27.6 us (33%)
  local copies, waits for them, and re-layouts  23.3 us (28%)
  waiting for transfers between devices  15.4 us (19%)
  other arithmetic  11.4 us (14%)
  matrix products  3.01 us (4%)
  between operations  1.53 us (2%)
    unnamed x129, local copies, waits for them, and re-layouts  17 us
    ppermute x7, starting transfers between devices, butterfly_sum(): values = values + lax.ppermute(values, axis, list(enumerate(targets)))  12.4 us
    ppermute x7, waiting for transfers between devices, butterfly_sum(): values = values + lax.ppermute(values, axis, list(enumerate(targets)))  9.61 us
    ppermute x2, starting transfers between devices, shift_y(): high = lax.ppermute(field[:, :, :1, :], 'gy', ring('gy', -1))  6.64 us
    ppermute x1, starting transfers between devices, per_device(): sent_motion = lax.ppermute(own_motion, 'sec', [(0, 1)])  5.53 us
    ppermute x1, waiting for transfers between devices, per_device(): other = lax.ppermute(payload, 'sec', [(0, 1), (1, 0)])  2.34 us
    ppermute x2, starting transfers between devices, shift_zx(): low = lax.ppermute(field[:, :, :, size_z - 1], 'gz', ring('gz', 1))  2 us
    ppermute x2, waiting for transfers between devices, shift_zx(): high = lax.ppermute(field[:, :, :, 0], 'gz', ring('gz', -1))  1.92 us
  transfers between devices with their start and end apart: 17, of which 10 were waited for; matrix products, arithmetic and copies ran while one was open for 24% of the time, Pallas kernels for 0%

profile of v7, /device:TPU:32, one launch (start us, length us, event | category | flops | bytes accessed | tf_op | source)
XLA Modules:
  0.0 82.2 jit_solution(13776054465899130219)
XLA Ops:
  0.7 1.3 %copy.96 = f32[28,4,8,128]{3,0,2,1:T(8,128)S(1)} copy(f32[28,4,8,128]{3,2,1,0:T(8,128)} %param.22) | data formatting | bytes 917504 | tf_op args[0]
  3.0 5.5 %collective-permute-start.4 = (f32[3,4,8,128]{3,2,1,0:T(8,128)}, f32[3,4,8,128]{3,2,1,0:T(8,128)}, u32[]{:S(2)}, u32[]{:S(2)}) collective-permute-start(f32[3,4,8,128]{3,2,1,0:T(8,128)} %get-tuple-element.60), channel_id=1, source_target_pairs={{0,128},{1,129},{2,130},{3,131},{4,132},{5,133},{6,134},{7,135},{8... | collective-permute-start | bytes 147464 | tf_op jit(solution)/shard_map/ppermute | solution.py:151
  9.9 3.9 %collective-permute-start.1 = (f32[28,4,1,128]{3,0,2,1:T(8,128)}, f32[28,4,1,128]{3,0,2,1:T(8,128)}, u32[]{:S(2)}, u32[]{:S(2)}) collective-permute-start(f32[28,4,1,128]{3,0,2,1:T(8,128)} %copy.143), channel_id=1, source_target_pairs={{0,120},{8,0},{16,8},{24,16},{32,24},{40,32},{48,40},{56,48},{64,5... | collective-permute-start | bytes 172040 | tf_op jit(solution)/shard_map/ppermute | solution.py:78
  13.8 0.8 slice_bitcast_fusion.8
  14.7 0.7 copy-done.5
  22.3 0.7 fusion.16
  23.5 1.2 %fusion.1 = f32[19,4,8,128]{3,0,2,1:T(8,128)S(1)} fusion(f32[19,4,8,128]{3,0,2,1:T(8,128)S(1)} %concatenate.84, f32[19,19,1,1]{0,1,3,2:T(8,128)S(1)} %copy-done.4, f32[19,4,8,128]{3,0,2,1:T(8,128)S(1)} %fusion.16, f32[28,4,8,128]{3,0,2,1:T(8,128)S(1)} %copy.96, f32[19]{0:T(128)} %concatenate.83, pred[4,8,128]{2,1,0:T(8,128)(4,1)S(1)} %broadcast_compare_fusion), kind=kOutput, calls=%fused_computation.2 | convolution fusion | flops 17977344 | bytes 1250800 | tf_op jit(solution)/shard_map/ij,jxyz->ixyz/dot_general | solution.py:176
  26.0 0.8 slice_bitcast_fusion.5
  28.1 1.2 %bitcast_select_fusion.1 = (f32[4,7,4,8,128]{4,3,2,1,0:T(8,128)S(1)}, f32[4,7,4,8,128]{4,3,2,1,0:T(8,128)S(1)}) fusion(f32[7,4,4,8,128]{4,3,2,0,1:T(8,128)} %slice_dynamic-update-slice_fusion.7, f32[4,7,4,8,128]{4,3,2,1,0:T(8,128)S(1)} %bitcast.104, f32[4]{0:T(128)S(1)} %copy-done.21, pred[4,8,128]{2,1,0:T(8,128)(4,1)S(1)} %broadcast_compare_fusion, ...), kind=kLoop, calls=%fused_computation.28 | loop fusion | flops 573440 | bytes 2019344 | tf_op jit(solution)/shard_map/jit(_where)/select_n | solution.py:166
  30.3 1.2 %maximum_select_fusion = f32[28,4,8,128]{3,0,2,1:T(8,128)S(1)} fusion(f32[28,4,7,128]{3,0,2,1:T(8,128)S(1)} %copy.141, f32[28,4,1,128]{3,0,2,1:T(8,128)} %collective-permute-done, f32[28,4,1,128]{3,0,2,1:T(8,128)} %collective-permute-done.1, f32[28,4,7,128]{3,0,2,1:T(8,128)S(1)} %copy.144, pred[28]{0:T(512)(128)(4,1)S(1)} %copy-done.23, ...), kind=kLoop, calls=%fused_computation.5 | loop fusion | flops 458752 | bytes 1835064 | tf_op jit(solution)/shard_map/jit(_where)/select_n | solution.py:81
  32.0 2.0 %collective-permute-start.2 = (f32[28,4,8]{0,2,1:T(8,128)S(1)}, f32[28,4,8]{0,2,1:T(8,128)S(1)}, u32[]{:S(2)}, u32[]{:S(2)}) collective-permute-start(f32[28,4,8]{0,2,1:T(8,128)S(1)} %get-tuple-element.48), channel_id=1, source_target_pairs={{0,1},{1,2},{2,3},{3,4},{4,5},{5,6},{6,7},{7,0},{8,9},{9,10},{10,1... | collective-permute-start | bytes 10760 | tf_op jit(solution)/shard_map/ppermute | solution.py:86
  34.3 1.5 %collective-permute-done.2 = f32[28,4,8]{0,2,1:T(8,128)S(1)} collective-permute-done((f32[28,4,8]{0,2,1:T(8,128)S(1)}, f32[28,4,8]{0,2,1:T(8,128)S(1)}, u32[]{:S(2)}, u32[]{:S(2)}) %collective-permute-start.2) | collective-permute-done | bytes 3616 | tf_op jit(solution)/shard_map/ppermute | solution.py:86
  35.8 1.9 %collective-permute-done.3 = f32[28,4,8]{0,2,1:T(8,128)S(1)} collective-permute-done((f32[28,4,8]{0,2,1:T(8,128)S(1)}, f32[28,4,8]{0,2,1:T(8,128)S(1)}, u32[]{:S(2)}, u32[]{:S(2)}) %collective-permute-start.3) | collective-permute-done | bytes 3616 | tf_op jit(solution)/shard_map/ppermute | solution.py:87
  38.5 0.8 %fusion.8 = (f32[28]{0:T(128)S(1)}, f32[28,4,8,128]{3,0,2,1:T(8,128)S(1)}) fusion(f32[28,4,8,128]{3,2,1,0:T(8,128)S(1)} %bitcast.114, pred[4,8,128]{2,1,0:T(8,128)(4,1)S(1)} %broadcast_compare_fusion, f32[28,4,8,128]{3,2,1,0:T(8,128)S(1)} %copy-done, f32[28,4,8,128]{3,0,2,1:T(8,128)S(1)} %fusion.2, f32[28,1,8,128]{3,0,2,1:T(8,128)S(1)} %get-tuple-element.95, ...), kind=kLoop, calls=%fused_computation.26 | loop fusion | flops 917476 | bytes 2756776 | tf_op jit(solution)/shard_map/reduce_sum | solution.py:188
  42.5 2.8 %collective-permute-start.10 = (f32[28,4,1,128]{3,0,2,1:T(8,128)S(1)}, f32[28,4,1,128]{3,0,2,1:T(8,128)S(1)}, u32[]{:S(2)}, u32[]{:S(2)}) collective-permute-start(f32[28,4,1,128]{3,0,2,1:T(8,128)S(1)} %get-tuple-element.92), channel_id=1, source_target_pairs={{0,120},{8,0},{16,8},{24,16},{32,24},{40,32},{48,40},{56,48},{64,5... | collective-permute-start | bytes 172040 | tf_op jit(solution)/shard_map/ppermute | solution.py:78
  46.5 0.6 add_multiply_fusion
  47.1 0.7 copy-done.7
  48.4 1.2 %collective-permute-done.7 = f32[19]{0:T(128)S(1)} collective-permute-done((f32[19]{0:T(128)S(1)}, f32[19]{0:T(128)S(1)}, u32[]{:S(2)}, u32[]{:S(2)}) %collective-permute-start.7) | collective-permute-done | bytes 108 | tf_op jit(solution)/shard_map/ppermute | solution.py:130
  51.2 1.9 %collective-permute-start.8 = (f32[19]{0:T(128)S(1)}, f32[19]{0:T(128)S(1)}, u32[]{:S(2)}, u32[]{:S(2)}) collective-permute-start(f32[19]{0:T(128)S(1)} %add.119), channel_id=1, source_target_pairs={{0,96},{8,104},{16,112},{24,120},{32,64},{40,72},{48,80},{56,88},{... | collective-permute-start | bytes 236 | tf_op jit(solution)/shard_map/ppermute | solution.py:130
  53.2 0.7 copy-done.44
  54.1 2.0 %collective-permute-done.8 = f32[19]{0:T(128)S(1)} collective-permute-done((f32[19]{0:T(128)S(1)}, f32[19]{0:T(128)S(1)}, u32[]{:S(2)}, u32[]{:S(2)}) %collective-permute-start.8) | collective-permute-done | bytes 108 | tf_op jit(solution)/shard_map/ppermute | solution.py:130
  56.9 2.1 %collective-permute-start.13 = (f32[19]{0:T(128)S(1)}, f32[19]{0:T(128)S(1)}, u32[]{:S(2)}, u32[]{:S(2)}) collective-permute-start(f32[19]{0:T(128)S(1)} %add.120), channel_id=1, source_target_pairs={{0,1},{1,0},{2,3},{3,2},{4,5},{5,4},{6,7},{7,6},{8,9},{9,8},{10,11... | collective-permute-start | bytes 236 | tf_op jit(solution)/shard_map/ppermute | solution.py:130
  59.8 0.8 collective-permute-done.13
  60.6 5.7 %collective-permute-start.14 = (f32[19]{0:T(128)S(1)}, f32[19]{0:T(128)S(1)}, u32[]{:S(2)}, u32[]{:S(2)}) collective-permute-start(f32[19]{0:T(128)S(1)} %add.124), channel_id=1, source_target_pairs={{0,2},{1,3},{2,0},{3,1},{4,6},{5,7},{6,4},{7,5},{8,10},{9,11},{10,... | collective-permute-start | bytes 236 | tf_op jit(solution)/shard_map/ppermute | solution.py:130
  66.2 1.5 %collective-permute-done.14 = f32[19]{0:T(128)S(1)} collective-permute-done((f32[19]{0:T(128)S(1)}, f32[19]{0:T(128)S(1)}, u32[]{:S(2)}, u32[]{:S(2)}) %collective-permute-start.14) | collective-permute-done | bytes 108 | tf_op jit(solution)/shard_map/ppermute | solution.py:130
  67.8 2.0 %collective-permute-start.15 = (f32[19]{0:T(128)S(1)}, f32[19]{0:T(128)S(1)}, u32[]{:S(2)}, u32[]{:S(2)}) collective-permute-start(f32[19]{0:T(128)S(1)} %add.125), channel_id=1, source_target_pairs={{0,6},{1,7},{2,4},{3,5},{4,2},{5,3},{6,0},{7,1},{8,14},{9,15},{10,... | collective-permute-start | bytes 236 | tf_op jit(solution)/shard_map/ppermute | solution.py:130
  69.8 0.7 collective-permute-start.12
  70.5 2.9 %collective-permute-done.15 = f32[19]{0:T(128)S(1)} collective-permute-done((f32[19]{0:T(128)S(1)}, f32[19]{0:T(128)S(1)}, u32[]{:S(2)}, u32[]{:S(2)}) %collective-permute-start.15) | collective-permute-done | bytes 108 | tf_op jit(solution)/shard_map/ppermute | solution.py:130
  75.9 1.0 %copy.123 = f32[28,4,8,128]{3,2,1,0:T(8,128)} copy(f32[28,4,8,128]{3,0,2,1:T(8,128)S(1)} %select_select_fusion) | data formatting | bytes 917504
  76.9 2.3 %collective-permute-done.16 = f32[4,4,8,128]{3,2,1,0:T(8,128)S(1)} collective-permute-done((f32[4,4,8,128]{3,2,1,0:T(8,128)S(1)}, f32[4,4,8,128]{3,2,1,0:T(8,128)S(1)}, u32[]{:S(2)}, u32[]{:S(2)}) %collective-permute-start.16) | collective-permute-done | bytes 65568 | tf_op jit(solution)/shard_map/ppermute | solution.py:256
  79.3 0.8 multiply_reduce_fusion.12
  80.7 1.0 %copy.124 = f32[28,4,8,128]{3,2,1,0:T(8,128)} copy(f32[28,4,8,128]{3,0,2,1:T(8,128)S(1)} %copy_select_fusion) | data formatting | bytes 917504
  (203 shorter events, 26.4 us)
Async XLA Ops:
  0.7 7.9 %copy-start.1 = (f32[28,4,8,128]{3,2,1,0:T(8,128)S(1)}, f32[28,4,8,128]{3,2,1,0:T(8,128)}, u32[]{:S(2)}) copy-start(f32[28,4,8,128]{3,2,1,0:T(8,128)} %param.26) | copy-start | bytes 1376260
  2.1 11.7 %copy-start = (f32[28,4,8,128]{3,2,1,0:T(8,128)S(1)}, f32[28,4,8,128]{3,2,1,0:T(8,128)}, u32[]{:S(2)}) copy-start(f32[28,4,8,128]{3,2,1,0:T(8,128)} %param.22) | copy-start | bytes 1376260
  2.4 19.3 %copy-start.2 = (f32[4,8,128]{2,1,0:T(8,128)}, f32[4,8,128]{2,1,0:T(8,128)S(1)}, u32[]{:S(2)}) copy-start(f32[4,8,128]{2,1,0:T(8,128)S(1)} %get-tuple-element.44) | copy-start | bytes 49156
  3.0 22.9 %collective-permute-start.4 = (f32[3,4,8,128]{3,2,1,0:T(8,128)}, f32[3,4,8,128]{3,2,1,0:T(8,128)}, u32[]{:S(2)}, u32[]{:S(2)}) collective-permute-start(f32[3,4,8,128]{3,2,1,0:T(8,128)} %get-tuple-element.60), channel_id=1, source_target_pairs={{0,128},{1,129},{2,130},{3,131},{4,132},{5,133},{6,134},{7,135},{8... | collective-permute-start | bytes 147464 | tf_op jit(solution)/shard_map/ppermute | solution.py:151
  9.3 20.3 %collective-permute-start = (f32[28,4,1,128]{3,0,2,1:T(8,128)}, f32[28,4,1,128]{3,0,2,1:T(8,128)}, u32[]{:S(2)}, u32[]{:S(2)}) collective-permute-start(f32[28,4,1,128]{3,0,2,1:T(8,128)} %copy.142), channel_id=1, source_target_pairs={{0,8},{8,16},{16,24},{24,32},{32,40},{40,48},{48,56},{56,64},{64,7... | collective-permute-start | bytes 172040 | tf_op jit(solution)/shard_map/ppermute | solution.py:77
  9.9 19.7 %collective-permute-start.1 = (f32[28,4,1,128]{3,0,2,1:T(8,128)}, f32[28,4,1,128]{3,0,2,1:T(8,128)}, u32[]{:S(2)}, u32[]{:S(2)}) collective-permute-start(f32[28,4,1,128]{3,0,2,1:T(8,128)} %copy.143), channel_id=1, source_target_pairs={{0,120},{8,0},{16,8},{24,16},{32,24},{40,32},{48,40},{56,48},{64,5... | collective-permute-start | bytes 172040 | tf_op jit(solution)/shard_map/ppermute | solution.py:78
  14.6 7.1 %copy-start.8 = (f32[4,8,128]{2,1,0:T(8,128)}, f32[4,8,128]{2,1,0:T(8,128)S(1)}, u32[]{:S(2)}) copy-start(f32[4,8,128]{2,1,0:T(8,128)S(1)} %get-tuple-element.132) | copy-start | bytes 49156
  14.6 7.1 %copy-start.10 = (f32[4,8,128]{2,1,0:T(8,128)}, f32[4,8,128]{2,1,0:T(8,128)S(1)}, u32[]{:S(2)}) copy-start(f32[4,8,128]{2,1,0:T(8,128)S(1)} %get-tuple-element.133) | copy-start | bytes 49156
  14.6 7.1 %copy-start.12 = (f32[4,8,128]{2,1,0:T(8,128)}, f32[4,8,128]{2,1,0:T(8,128)S(1)}, u32[]{:S(2)}) copy-start(f32[4,8,128]{2,1,0:T(8,128)S(1)} %get-tuple-element.134) | copy-start | bytes 49156
  15.4 6.3 %copy-start.6 = (f32[4,8,128]{2,1,0:T(8,128)}, f32[4,8,128]{2,1,0:T(8,128)S(1)}, u32[]{:S(2)}) copy-start(f32[4,8,128]{2,1,0:T(8,128)S(1)} %broadcast_multiply_fusion.4) | copy-start | bytes 49156
  19.9 1.8 %copy-start.4 = (f32[19,19,1,1]{0,1,3,2:T(8,128)S(1)}, f32[19,19,1,1]{0,1,3,2:T(8,128)}, u32[]{:S(2)}) copy-start(f32[19,19,1,1]{0,1,3,2:T(8,128)} %constant.133) | copy-start | bytes 4336
  25.4 12.3 %copy-start.39 = (pred[128]{0:T(512)(128)(4,1)}, pred[128]{0:T(512)(128)(4,1)S(1)}, u32[]{:S(2)}) copy-start(pred[128]{0:T(512)(128)(4,1)S(1)} %get-tuple-element.157) | copy-start | bytes 388
  25.4 12.3 %copy-start.41 = (pred[128]{0:T(512)(128)(4,1)}, pred[128]{0:T(512)(128)(4,1)S(1)}, u32[]{:S(2)}) copy-start(pred[128]{0:T(512)(128)(4,1)S(1)} %get-tuple-element.158) | copy-start | bytes 388
  32.0 3.8 %collective-permute-start.2 = (f32[28,4,8]{0,2,1:T(8,128)S(1)}, f32[28,4,8]{0,2,1:T(8,128)S(1)}, u32[]{:S(2)}, u32[]{:S(2)}) collective-permute-start(f32[28,4,8]{0,2,1:T(8,128)S(1)} %get-tuple-element.48), channel_id=1, source_target_pairs={{0,1},{1,2},{2,3},{3,4},{4,5},{5,6},{6,7},{7,0},{8,9},{9,10},{10,1... | collective-permute-start | bytes 10760 | tf_op jit(solution)/shard_map/ppermute | solution.py:86
  34.0 3.7 %collective-permute-start.3 = (f32[28,4,8]{0,2,1:T(8,128)S(1)}, f32[28,4,8]{0,2,1:T(8,128)S(1)}, u32[]{:S(2)}, u32[]{:S(2)}) collective-permute-start(f32[28,4,8]{0,2,1:T(8,128)S(1)} %get-tuple-element.49), channel_id=1, source_target_pairs={{0,7},{1,0},{2,1},{3,2},{4,3},{5,4},{6,5},{7,6},{8,15},{9,8},{10,9... | collective-permute-start | bytes 10760 | tf_op jit(solution)/shard_map/ppermute | solution.py:87
  40.9 1.1 %collective-permute-start.5 = (f32[19]{0:T(128)S(1)}, f32[19]{0:T(128)S(1)}, u32[]{:S(2)}, u32[]{:S(2)}) collective-permute-start(f32[19]{0:T(128)S(1)} %broadcast_select_fusion), channel_id=1, source_target_pairs={{0,8},{8,0},{16,24},{24,16},{32,40},{40,32},{48,56},{56,48},{64,72... | collective-permute-start | bytes 236 | tf_op jit(solution)/shard_map/ppermute | solution.py:130
  42.2 4.2 %copy-start.9 = (f32[4,8,128]{2,1,0:T(8,128)S(1)}, f32[4,8,128]{2,1,0:T(8,128)}, u32[]{:S(2)}) copy-start(f32[4,8,128]{2,1,0:T(8,128)} %copy-done.8) | copy-start | bytes 49156
  42.2 4.2 %copy-start.11 = (f32[4,8,128]{2,1,0:T(8,128)S(1)}, f32[4,8,128]{2,1,0:T(8,128)}, u32[]{:S(2)}) copy-start(f32[4,8,128]{2,1,0:T(8,128)} %copy-done.10) | copy-start | bytes 49156
  42.2 4.2 %copy-start.13 = (f32[4,8,128]{2,1,0:T(8,128)S(1)}, f32[4,8,128]{2,1,0:T(8,128)}, u32[]{:S(2)}) copy-start(f32[4,8,128]{2,1,0:T(8,128)} %copy-done.12) | copy-start | bytes 49156
  42.2 3.8 %collective-permute-start.6 = (f32[19]{0:T(128)S(1)}, f32[19]{0:T(128)S(1)}, u32[]{:S(2)}, u32[]{:S(2)}) collective-permute-start(f32[19]{0:T(128)S(1)} %add.117), channel_id=1, source_target_pairs={{0,16},{8,24},{16,0},{24,8},{32,48},{40,56},{48,32},{56,40},{64,80... | collective-permute-start | bytes 236 | tf_op jit(solution)/shard_map/ppermute | solution.py:130
  42.5 13.6 %collective-permute-start.10 = (f32[28,4,1,128]{3,0,2,1:T(8,128)S(1)}, f32[28,4,1,128]{3,0,2,1:T(8,128)S(1)}, u32[]{:S(2)}, u32[]{:S(2)}) collective-permute-start(f32[28,4,1,128]{3,0,2,1:T(8,128)S(1)} %get-tuple-element.92), channel_id=1, source_target_pairs={{0,120},{8,0},{16,8},{24,16},{32,24},{40,32},{48,40},{56,48},{64,5... | collective-permute-start | bytes 172040 | tf_op jit(solution)/shard_map/ppermute | solution.py:78
  45.3 10.7 %collective-permute-start.9 = (f32[28,4,1,128]{3,0,2,1:T(8,128)S(1)}, f32[28,4,1,128]{3,0,2,1:T(8,128)S(1)}, u32[]{:S(2)}, u32[]{:S(2)}) collective-permute-start(f32[28,4,1,128]{3,0,2,1:T(8,128)S(1)} %get-tuple-element.93), channel_id=1, source_target_pairs={{0,8},{8,16},{16,24},{24,32},{32,40},{40,48},{48,56},{56,64},{64,7... | collective-permute-start | bytes 172040 | tf_op jit(solution)/shard_map/ppermute | solution.py:77
  46.0 3.5 %collective-permute-start.7 = (f32[19]{0:T(128)S(1)}, f32[19]{0:T(128)S(1)}, u32[]{:S(2)}, u32[]{:S(2)}) collective-permute-start(f32[19]{0:T(128)S(1)} %add.118), channel_id=1, source_target_pairs={{0,32},{8,40},{16,48},{24,56},{32,0},{40,8},{48,16},{56,24},{64,96... | collective-permute-start | bytes 236 | tf_op jit(solution)/shard_map/ppermute | solution.py:130
  51.2 4.8 %collective-permute-start.8 = (f32[19]{0:T(128)S(1)}, f32[19]{0:T(128)S(1)}, u32[]{:S(2)}, u32[]{:S(2)}) collective-permute-start(f32[19]{0:T(128)S(1)} %add.119), channel_id=1, source_target_pairs={{0,96},{8,104},{16,112},{24,120},{32,64},{40,72},{48,80},{56,88},{... | collective-permute-start | bytes 236 | tf_op jit(solution)/shard_map/ppermute | solution.py:130
  56.9 3.6 %collective-permute-start.13 = (f32[19]{0:T(128)S(1)}, f32[19]{0:T(128)S(1)}, u32[]{:S(2)}, u32[]{:S(2)}) collective-permute-start(f32[19]{0:T(128)S(1)} %add.120), channel_id=1, source_target_pairs={{0,1},{1,0},{2,3},{3,2},{4,5},{5,4},{6,7},{7,6},{8,9},{9,8},{10,11... | collective-permute-start | bytes 236 | tf_op jit(solution)/shard_map/ppermute | solution.py:130
  59.5 14.0 %copy-start.42 = (pred[128]{0:T(512)(128)(4,1)S(1)}, pred[128]{0:T(512)(128)(4,1)}, u32[]{:S(2)}) copy-start(pred[128]{0:T(512)(128)(4,1)} %copy-done.41) | copy-start | bytes 388
  60.6 7.2 %collective-permute-start.14 = (f32[19]{0:T(128)S(1)}, f32[19]{0:T(128)S(1)}, u32[]{:S(2)}, u32[]{:S(2)}) collective-permute-start(f32[19]{0:T(128)S(1)} %add.124), channel_id=1, source_target_pairs={{0,2},{1,3},{2,0},{3,1},{4,6},{5,7},{6,4},{7,5},{8,10},{9,11},{10,... | collective-permute-start | bytes 236 | tf_op jit(solution)/shard_map/ppermute | solution.py:130
  66.2 7.3 %collective-permute-start.11 = (f32[28,4,8]{0,2,1:T(8,128)S(1)}, f32[28,4,8]{0,2,1:T(8,128)S(1)}, u32[]{:S(2)}, u32[]{:S(2)}) collective-permute-start(f32[28,4,8]{0,2,1:T(8,128)S(1)} %get-tuple-element.42), channel_id=1, source_target_pairs={{0,1},{1,2},{2,3},{3,4},{4,5},{5,6},{6,7},{7,0},{8,9},{9,10},{10,1... | collective-permute-start | bytes 10760 | tf_op jit(solution)/shard_map/ppermute | solution.py:86
  67.8 5.7 %collective-permute-start.15 = (f32[19]{0:T(128)S(1)}, f32[19]{0:T(128)S(1)}, u32[]{:S(2)}, u32[]{:S(2)}) collective-permute-start(f32[19]{0:T(128)S(1)} %add.125), channel_id=1, source_target_pairs={{0,6},{1,7},{2,4},{3,5},{4,2},{5,3},{6,0},{7,1},{8,14},{9,15},{10,... | collective-permute-start | bytes 236 | tf_op jit(solution)/shard_map/ppermute | solution.py:130
  69.8 3.8 %collective-permute-start.12 = (f32[28,4,8]{0,2,1:T(8,128)S(1)}, f32[28,4,8]{0,2,1:T(8,128)S(1)}, u32[]{:S(2)}, u32[]{:S(2)}) collective-permute-start(f32[28,4,8]{0,2,1:T(8,128)S(1)} %get-tuple-element.43), channel_id=1, source_target_pairs={{0,7},{1,0},{2,1},{3,2},{4,3},{5,4},{6,5},{7,6},{8,15},{9,8},{10,9... | collective-permute-start | bytes 10760 | tf_op jit(solution)/shard_map/ppermute | solution.py:87
  73.4 5.9 %collective-permute-start.16 = (f32[4,4,8,128]{3,2,1,0:T(8,128)S(1)}, f32[4,4,8,128]{3,2,1,0:T(8,128)S(1)}, u32[]{:S(2)}, u32[]{:S(2)}) collective-permute-start(f32[4,4,8,128]{3,2,1,0:T(8,128)S(1)} %select_maximum_fusion), channel_id=1, source_target_pairs={{0,128},{128,0},{1,129},{129,1},{2,130},{130,2},{3,131},{131,3},{4... | collective-permute-start | bytes 196616 | tf_op jit(solution)/shard_map/ppermute | solution.py:256
  75.9 3.4 %copy-start.3 = (f32[4,8,128]{2,1,0:T(8,128)S(1)}, f32[4,8,128]{2,1,0:T(8,128)}, u32[]{:S(2)}) copy-start(f32[4,8,128]{2,1,0:T(8,128)} %copy-done.2) | copy-start | bytes 49156
  (40 other events, 37.7 us)

commit v8 on v7

--- a/solution.py
+++ b/solution.py
@@ -161,9 +161,6 @@
     factor = small_weights * (1.0 + 4.0 * projected_small)
     species_eq = factor[None] * concentration[:, None]
     species_gap = grouped - species_eq
-    species_relaxed = grouped - species_r * species_gap
-    species_bounce = jnp.swapaxes(reverse_pairs(jnp.swapaxes(grouped, 0, 1), opposite[:7]), 0, 1)
-    species_post = jnp.where(fluid[None], species_relaxed, species_bounce).reshape(populations.shape)
 
     q_table = jnp.asarray(ortho, jnp.float32)
     relax = jnp.concatenate([jnp.zeros((4,), flow_rates.dtype), flow_rates]).reshape(19, 1, 1, 1)
@@ -173,8 +170,6 @@
     poly = w * (1.0 + 3.0 * projected + 4.5 * projected * projected - 1.5 * squared[None])
     equilibrium = density[None] * poly
     moments = jnp.einsum("ji,jxyz->ixyz", q_table, flow - equilibrium, precision=highest)
-    flow_relaxed = flow - jnp.einsum("ij,jxyz->ixyz", q_table, relax * moments, precision=highest)
-    flow_post = jnp.where(fluid, flow_relaxed, reverse_pairs(flow, opposite))
     filler = jnp.zeros((rows - 19,) + populations.shape[1:], jnp.float32)
 
     flow_moves = np.concatenate([velocity, np.zeros((rows - 19, 3))])
@@ -235,9 +230,15 @@
         return values
 
     def post_passing_y(values):
-        values, post_ = lax.optimization_barrier(
-            (values, jnp.where(is_flow, jnp.concatenate([flow_post, filler]), species_post))
-        )
+        values, (flow_, grouped_, moments_, species_gap_) = lax.optimization_barrier(
+            (values, (flow, grouped, moments, species_gap))
+        )
+        species_relaxed = grouped_ - species_r * species_gap_
+        species_bounce = jnp.swapaxes(reverse_pairs(jnp.swapaxes(grouped_, 0, 1), opposite[:7]), 0, 1)
+        species_post = jnp.where(fluid[None], species_relaxed, species_bounce).reshape(populations.shape)
+        flow_relaxed = flow_ - jnp.einsum("ij,jxyz->ixyz", q_table, relax * moments_, precision=highest)
+        flow_post = jnp.where(fluid, flow_relaxed, reverse_pairs(flow_, opposite))
+        post_ = jnp.where(is_flow, jnp.concatenate([flow_post, filler]), species_post)
         later["post_y"] = shift_y(post_, post_moves[1])
         return values
 

time: 82.9 us -> 82.2 us (level)
  waiting for transfers between devices: 15.4 us -> 18.5 us
  starting transfers between devices: 27.6 us -> 24.9 us
  other arithmetic: 11.4 us -> 9.3 us
    ppermute x2, waiting for transfers between devices: 0.01 us -> 3.69 us  [shift_y(): low = lax.ppermute(field[:, :, size_y - 1:, :], 'gy', ring('gy', 1))]
    unnamed x129 -> x147, local copies, waits for them, and re-layouts: 17 us -> 14.4 us
    ppermute x2, starting transfers between devices: 6.64 us -> 4.84 us  [shift_y(): high = lax.ppermute(field[:, :, :1, :], 'gy', ring('gy', -1))]
    concatenate x4, local copies, waits for them, and re-layouts: 1.59 us -> 3.36 us  [reverse_pairs(): return jnp.concatenate([rows[int(o):int(o) + 1] for o in opposite])]
    slice x2, local copies, waits for them, and re-layouts: 0.08 us -> 1.32 us  [shift_y(): high = lax.ppermute(field[:, :, :1, :], 'gy', ring('gy', -1))]
    select_n x1 -> x0, other arithmetic: 1.21 us -> none  [per_device(): jnp.where(fluid[None], species_relaxed, species_bounce)]
    add x7, other arithmetic: 0.02 us -> 1.18 us  [butterfly_sum(): values = values + lax.ppermute(values, axis, list(enumerate(targets)))]
    slice x2, local copies, waits for them, and re-layouts: 0.3 us -> 1.2 us  [reverse_pairs(): return jnp.concatenate([rows[int(o):int(o) + 1] for o in opposite])]
  transfers between devices with their start and end apart: 17 -> 17, of which waited for: 10 -> 11; matrix products, arithmetic and copies ran while one was open for 24% -> 19% of each run, Pallas kernels for 0% -> 0%
where the time goes in v8:
time: 82.2 us; the launch traced here: 81.3 us
  starting transfers between devices  24.9 us (30%)
  local copies, waits for them, and re-layouts  23.2 us (28%)
  waiting for transfers between devices  18.5 us (23%)
  other arithmetic  9.3 us (11%)
  matrix products  3.7 us (5%)
  between operations  1.74 us (2%)
    unnamed x147, local copies, waits for them, and re-layouts  14.4 us
    ppermute x7, starting transfers between devices, butterfly_sum(): values = values + lax.ppermute(values, axis, list(enumerate(targets)))  12.1 us
    ppermute x7, waiting for transfers between devices, butterfly_sum(): values = values + lax.ppermute(values, axis, list(enumerate(targets)))  8.9 us
    ppermute x1, starting transfers between devices, per_device(): sent_motion = lax.ppermute(own_motion, 'sec', [(0, 1)])  4.93 us
    ppermute x2, starting transfers between devices, shift_y(): high = lax.ppermute(field[:, :, :1, :], 'gy', ring('gy', -1))  4.84 us
    ppermute x2, waiting for transfers between devices, shift_y(): low = lax.ppermute(field[:, :, size_y - 1:, :], 'gy', ring('gy', 1))  3.69 us
    concatenate x4, local copies, waits for them, and re-layouts, reverse_pairs(): return jnp.concatenate([rows[int(o):int(o) + 1] for o in opposite])  3.36 us
    ppermute x1, waiting for transfers between devices, per_device(): other = lax.ppermute(payload, 'sec', [(0, 1), (1, 0)])  2.34 us
  transfers between devices with their start and end apart: 17, of which 11 were waited for; matrix products, arithmetic and copies ran while one was open for 19% of the time, Pallas kernels for 0%

profile of v8, /device:TPU:32, one launch (start us, length us, event | category | flops | bytes accessed | tf_op | source)
XLA Modules:
  0.0 81.3 jit_solution(11035679193434572547)
XLA Ops:
  0.6 1.3 %fusion.73 = (f32[28,4,1,128]{3,2,1,0:T(1,128)S(1)}, f32[28,4,1,128]{3,2,1,0:T(1,128)S(1)}) fusion(f32[28,4,8,128]{3,2,1,0:T(8,128)} %param.26), kind=kLoop, calls=%fused_computation.170 | loop fusion | bytes 229376 | tf_op jit(solution)/shard_map/slice | solution.py:78
  2.7 3.8 %collective-permute-start.1 = (f32[28,4,1,128]{3,0,2,1:T(8,128)}, f32[28,4,1,128]{3,0,2,1:T(8,128)S(1)}, u32[]{:S(2)}, u32[]{:S(2)}) collective-permute-start(f32[28,4,1,128]{3,0,2,1:T(8,128)} %copy.86), channel_id=1, source_target_pairs={{0,120},{8,0},{16,8},{24,16},{32,24},{40,32},{48,40},{56,48},{64,5... | collective-permute-start | bytes 172040 | tf_op jit(solution)/shard_map/ppermute | solution.py:78
  7.2 4.9 %collective-permute-start.4 = (f32[3,4,8,128]{3,2,1,0:T(8,128)S(1)}, f32[3,4,8,128]{3,2,1,0:T(8,128)S(1)}, u32[]{:S(2)}, u32[]{:S(2)}) collective-permute-start(f32[3,4,8,128]{3,2,1,0:T(8,128)S(1)} %get-tuple-element.66), channel_id=1, source_target_pairs={{0,128},{1,129},{2,130},{3,131},{4,132},{5,133},{6,134},{7,135},{8... | collective-permute-start | bytes 147464 | tf_op jit(solution)/shard_map/ppermute | solution.py:151
  12.4 0.6 copy-done.27
  16.1 1.3 %fusion.16 = f32[19,4,8,128]{3,0,2,1:T(8,128)S(1)} fusion(f32[19,19,1,1]{0,1,3,2:T(8,128)S(1)} %copy-done.8, f32[4,8,128]{2,1,0:T(8,128)S(1)} %broadcast_multiply_fusion.4, f32[4,8,128]{2,1,0:T(8,128)S(1)} %get-tuple-element.140, f32[4,8,128]{2,1,0:T(8,128)S(1)} %get-tuple-element.141, f32[4,8,128]{2,1,0:T(8,128)S(1)} %get-tuple-element.139, ...), kind=kOutput, calls=%fused_computation.46 | convolution fusion | flops 18833408 | bytes 800332 | tf_op jit(solution)/shard_map/ji,jxyz->ixyz/dot_general | solution.py:172
  21.8 2.0 %collective-permute-start.2 = (f32[28,4,8]{0,2,1:T(8,128)S(1)}, f32[28,4,8]{0,2,1:T(8,128)S(1)}, u32[]{:S(2)}, u32[]{:S(2)}) collective-permute-start(f32[28,4,8]{0,2,1:T(8,128)S(1)} %get-tuple-element.54), channel_id=1, source_target_pairs={{0,1},{1,2},{2,3},{3,4},{4,5},{5,6},{6,7},{7,0},{8,9},{9,10},{10,1... | collective-permute-start | bytes 10760 | tf_op jit(solution)/shard_map/ppermute | solution.py:86
  24.1 1.5 %collective-permute-done.2 = f32[28,4,8]{0,2,1:T(8,128)S(1)} collective-permute-done((f32[28,4,8]{0,2,1:T(8,128)S(1)}, f32[28,4,8]{0,2,1:T(8,128)S(1)}, u32[]{:S(2)}, u32[]{:S(2)}) %collective-permute-start.2) | collective-permute-done | bytes 3616 | tf_op jit(solution)/shard_map/ppermute | solution.py:86
  25.6 1.9 %collective-permute-done.3 = f32[28,4,8]{0,2,1:T(8,128)S(1)} collective-permute-done((f32[28,4,8]{0,2,1:T(8,128)S(1)}, f32[28,4,8]{0,2,1:T(8,128)S(1)}, u32[]{:S(2)}, u32[]{:S(2)}) %collective-permute-start.3) | collective-permute-done | bytes 3616 | tf_op jit(solution)/shard_map/ppermute | solution.py:87
  27.5 0.7 copy-done.47
  29.6 0.8 %fusion.8 = (f32[28]{0:T(128)S(1)}, f32[28,4,8,128]{3,0,2,1:T(8,128)S(1)}) fusion(f32[28,4,8,128]{3,2,1,0:T(8,128)S(1)} %bitcast.95, pred[4,8,128]{2,1,0:T(8,128)(4,1)S(1)} %broadcast_compare_fusion, f32[28,4,8,128]{3,2,1,0:T(8,128)S(1)} %copy-done, f32[28,4,8,128]{3,0,2,1:T(8,128)S(1)} %fusion.2, f32[28,1,8,128]{3,0,2,1:T(8,128)S(1)} %get-tuple-element.102, ...), kind=kLoop, calls=%fused_computation.26 | loop fusion | flops 917476 | bytes 2756776 | tf_op jit(solution)/shard_map/reduce_sum | solution.py:183
  33.9 0.9 %fusion.74 = (f32[1,4,8,128]{3,0,2,1:T(1,128)}, f32[1,4,8,128]{3,0,2,1:T(1,128)}, f32[1,4,8,128]{3,0,2,1:T(1,128)}, f32[1,4,8,128]{3,0,2,1:T(1,128)}, f32[1,4,8,...) fusion(f32[19,4,8,128]{3,0,2,1:T(8,128)S(1)} %get-tuple-element.30), kind=kLoop, calls=%fused_computation.171 | loop fusion | bytes 622592 | tf_op jit(solution)/shard_map/slice | solution.py:102
  34.9 0.8 copy-done.4
  35.7 2.9 %concatenate.84 = f32[19,4,8,128]{3,0,2,1:T(8,128)S(1)} concatenate(f32[1,4,8,128]{3,0,2,1:T(1,128)} %get-tuple-element.133, f32[1,4,8,128]{3,0,2,1:T(1,128)} %get-tuple-element.132, f32[1,4,8,128]{3,0,2,1:T(1,128)} %get-tuple-element.131, f32[1,4,8,128]{3,0,2,1:T(1,128)} %get-tuple-element.130, f32[1,4,8,128]{3,0,2,1:T(1,128)} %get-tuple-element.129, ...), dimensions={0} | concatenate | bytes 622592 | tf_op jit(solution)/shard_map/concatenate | solution.py:102
  38.6 1.3 %fusion.1 = f32[19,4,8,128]{3,0,2,1:T(8,128)S(1)} fusion(f32[19,4,8,128]{3,0,2,1:T(8,128)S(1)} %concatenate.84, f32[19,4,8,128]{3,0,2,1:T(8,128)S(1)} %get-tuple-element.30, f32[19,19,1,1]{0,1,3,2:T(8,128)S(1)} %copy-done.8, f32[19,4,8,128]{3,0,2,1:T(8,128)S(1)} %fusion.16, f32[19]{0:T(128)} %concatenate.83, pred[4,8,128]{2,1,0:T(8,128)(4,1)S(1)} %broadcast_compare_fusion), kind=kOutput, calls=%fused_computation.2 | convolution fusion | flops 17977344 | bytes 1250800 | tf_op jit(solution)/shard_map/ij,jxyz->ixyz/dot_general | solution.py:239
  41.7 0.7 copy-done.11
  43.0 1.1 %collective-permute-done.7 = f32[19]{0:T(128)S(1)} collective-permute-done((f32[19]{0:T(128)S(1)}, f32[19]{0:T(128)S(1)}, u32[]{:S(2)}, u32[]{:S(2)}) %collective-permute-start.7) | collective-permute-done | bytes 108 | tf_op jit(solution)/shard_map/ppermute | solution.py:130
  45.0 0.6 copy-done.28
  47.2 1.9 %collective-permute-start.8 = (f32[19]{0:T(128)S(1)}, f32[19]{0:T(128)S(1)}, u32[]{:S(2)}, u32[]{:S(2)}) collective-permute-start(f32[19]{0:T(128)S(1)} %add.119), channel_id=1, source_target_pairs={{0,96},{8,104},{16,112},{24,120},{32,64},{40,72},{48,80},{56,88},{... | collective-permute-start | bytes 236 | tf_op jit(solution)/shard_map/ppermute | solution.py:130
  49.1 1.0 %collective-permute-start.10 = (f32[28,4,1,128]{3,0,2,1:T(8,128)S(1)}, f32[28,4,1,128]{3,0,2,1:T(8,128)S(1)}, u32[]{:S(2)}, u32[]{:S(2)}) collective-permute-start(f32[28,4,1,128]{3,0,2,1:T(8,128)S(1)} %get-tuple-element.98), channel_id=1, source_target_pairs={{0,120},{8,0},{16,8},{24,16},{32,24},{40,32},{48,40},{56,48},{64,5... | collective-permute-start | bytes 172040 | tf_op jit(solution)/shard_map/ppermute | solution.py:78
  50.2 1.9 %collective-permute-done.8 = f32[19]{0:T(128)S(1)} collective-permute-done((f32[19]{0:T(128)S(1)}, f32[19]{0:T(128)S(1)}, u32[]{:S(2)}, u32[]{:S(2)}) %collective-permute-start.8) | collective-permute-done | bytes 108 | tf_op jit(solution)/shard_map/ppermute | solution.py:130
  52.2 3.7 %collective-permute-done.9 = f32[28,4,1,128]{3,0,2,1:T(8,128)S(1)} collective-permute-done((f32[28,4,1,128]{3,0,2,1:T(8,128)S(1)}, f32[28,4,1,128]{3,0,2,1:T(8,128)S(1)}, u32[]{:S(2)}, u32[]{:S(2)}) %collective-permute-start.9) | collective-permute-done | bytes 57376 | tf_op jit(solution)/shard_map/ppermute | solution.py:77
  55.9 0.7 copy-done.43
  56.8 2.1 %collective-permute-start.13 = (f32[19]{0:T(128)S(1)}, f32[19]{0:T(128)S(1)}, u32[]{:S(2)}, u32[]{:S(2)}) collective-permute-start(f32[19]{0:T(128)S(1)} %add.120), channel_id=1, source_target_pairs={{0,1},{1,0},{2,3},{3,2},{4,5},{5,4},{6,7},{7,6},{8,9},{9,8},{10,11... | collective-permute-start | bytes 236 | tf_op jit(solution)/shard_map/ppermute | solution.py:130
  59.6 0.8 collective-permute-done.13
  60.4 5.7 %collective-permute-start.14 = (f32[19]{0:T(128)S(1)}, f32[19]{0:T(128)S(1)}, u32[]{:S(2)}, u32[]{:S(2)}) collective-permute-start(f32[19]{0:T(128)S(1)} %add.124), channel_id=1, source_target_pairs={{0,2},{1,3},{2,0},{3,1},{4,6},{5,7},{6,4},{7,5},{8,10},{9,11},{10,... | collective-permute-start | bytes 236 | tf_op jit(solution)/shard_map/ppermute | solution.py:130
  66.1 1.5 %collective-permute-done.14 = f32[19]{0:T(128)S(1)} collective-permute-done((f32[19]{0:T(128)S(1)}, f32[19]{0:T(128)S(1)}, u32[]{:S(2)}, u32[]{:S(2)}) %collective-permute-start.14) | collective-permute-done | bytes 108 | tf_op jit(solution)/shard_map/ppermute | solution.py:130
  67.6 2.0 %collective-permute-start.15 = (f32[19]{0:T(128)S(1)}, f32[19]{0:T(128)S(1)}, u32[]{:S(2)}, u32[]{:S(2)}) collective-permute-start(f32[19]{0:T(128)S(1)} %add.125), channel_id=1, source_target_pairs={{0,6},{1,7},{2,4},{3,5},{4,2},{5,3},{6,0},{7,1},{8,14},{9,15},{10,... | collective-permute-start | bytes 236 | tf_op jit(solution)/shard_map/ppermute | solution.py:130
  69.7 0.7 collective-permute-start.12
  70.4 2.9 %collective-permute-done.15 = f32[19]{0:T(128)S(1)} collective-permute-done((f32[19]{0:T(128)S(1)}, f32[19]{0:T(128)S(1)}, u32[]{:S(2)}, u32[]{:S(2)}) %collective-permute-start.15) | collective-permute-done | bytes 108 | tf_op jit(solution)/shard_map/ppermute | solution.py:130
  75.8 1.0 %copy.66 = f32[28,4,8,128]{3,2,1,0:T(8,128)} copy(f32[28,4,8,128]{3,0,2,1:T(8,128)S(1)} %select_select_fusion) | data formatting | bytes 917504
  76.8 2.3 %collective-permute-done.16 = f32[4,4,8,128]{3,2,1,0:T(8,128)S(1)} collective-permute-done((f32[4,4,8,128]{3,2,1,0:T(8,128)S(1)}, f32[4,4,8,128]{3,2,1,0:T(8,128)S(1)}, u32[]{:S(2)}, u32[]{:S(2)}) %collective-permute-start.16) | collective-permute-done | bytes 65568 | tf_op jit(solution)/shard_map/ppermute | solution.py:257
  79.8 1.0 %copy.67 = f32[28,4,8,128]{3,2,1,0:T(8,128)} copy(f32[28,4,8,128]{3,0,2,1:T(8,128)S(1)} %copy_select_fusion) | data formatting | bytes 917504
  (221 shorter events, 23.0 us)
Async XLA Ops:
  0.6 5.9 %copy-start = (f32[28,4,8,128]{3,2,1,0:T(8,128)S(1)}, f32[28,4,8,128]{3,2,1,0:T(8,128)}, u32[]{:S(2)}) copy-start(f32[28,4,8,128]{3,2,1,0:T(8,128)} %param.22) | copy-start | bytes 1376260
  2.0 18.3 %collective-permute-start = (f32[28,4,1,128]{3,0,2,1:T(8,128)S(1)}, f32[28,4,1,128]{3,0,2,1:T(8,128)S(1)}, u32[]{:S(2)}, u32[]{:S(2)}) collective-permute-start(f32[28,4,1,128]{3,0,2,1:T(8,128)S(1)} %copy.85), channel_id=1, source_target_pairs={{0,8},{8,16},{16,24},{24,32},{32,40},{40,48},{48,56},{56,64},{64,7... | collective-permute-start | bytes 172040 | tf_op jit(solution)/shard_map/ppermute | solution.py:77
  2.7 4.1 %copy-start.18 = (f32[19]{0:T(128)S(1)}, f32[19]{0:T(128)}, u32[]{:S(2)}) copy-start(f32[19]{0:T(128)} %constant.128) | copy-start | bytes 232
  2.7 4.1 %copy-start.21 = (f32[19]{0:T(128)S(1)}, f32[19]{0:T(128)}, u32[]{:S(2)}) copy-start(f32[19]{0:T(128)} %constant.127) | copy-start | bytes 232
  2.7 4.1 %copy-start.24 = (f32[19]{0:T(128)S(1)}, f32[19]{0:T(128)}, u32[]{:S(2)}) copy-start(f32[19]{0:T(128)} %constant.126) | copy-start | bytes 232
  2.7 17.5 %collective-permute-start.1 = (f32[28,4,1,128]{3,0,2,1:T(8,128)}, f32[28,4,1,128]{3,0,2,1:T(8,128)S(1)}, u32[]{:S(2)}, u32[]{:S(2)}) collective-permute-start(f32[28,4,1,128]{3,0,2,1:T(8,128)} %copy.86), channel_id=1, source_target_pairs={{0,120},{8,0},{16,8},{24,16},{32,24},{40,32},{48,40},{56,48},{64,5... | collective-permute-start | bytes 172040 | tf_op jit(solution)/shard_map/ppermute | solution.py:78
  6.8 5.3 %copy-start.1 = (f32[28,4,8,128]{3,2,1,0:T(8,128)S(1)}, f32[28,4,8,128]{3,2,1,0:T(8,128)}, u32[]{:S(2)}) copy-start(f32[28,4,8,128]{3,2,1,0:T(8,128)} %param.26) | copy-start | bytes 1376260
  7.2 5.0 %copy-start.6 = (f32[3,4,8,128]{3,2,1,0:T(8,128)}, f32[3,4,8,128]{3,2,1,0:T(8,128)S(1)}, u32[]{:S(2)}) copy-start(f32[3,4,8,128]{3,2,1,0:T(8,128)S(1)} %get-tuple-element.66) | copy-start | bytes 147460
  7.2 12.1 %collective-permute-start.4 = (f32[3,4,8,128]{3,2,1,0:T(8,128)S(1)}, f32[3,4,8,128]{3,2,1,0:T(8,128)S(1)}, u32[]{:S(2)}, u32[]{:S(2)}) collective-permute-start(f32[3,4,8,128]{3,2,1,0:T(8,128)S(1)} %get-tuple-element.66), channel_id=1, source_target_pairs={{0,128},{1,129},{2,130},{3,131},{4,132},{5,133},{6,134},{7,135},{8... | collective-permute-start | bytes 147464 | tf_op jit(solution)/shard_map/ppermute | solution.py:151
  12.2 3.3 %copy-start.12 = (f32[4,8,128]{2,1,0:T(8,128)}, f32[4,8,128]{2,1,0:T(8,128)S(1)}, u32[]{:S(2)}) copy-start(f32[4,8,128]{2,1,0:T(8,128)S(1)} %get-tuple-element.139) | copy-start | bytes 49156
  12.2 3.3 %copy-start.14 = (f32[4,8,128]{2,1,0:T(8,128)}, f32[4,8,128]{2,1,0:T(8,128)S(1)}, u32[]{:S(2)}) copy-start(f32[4,8,128]{2,1,0:T(8,128)S(1)} %get-tuple-element.140) | copy-start | bytes 49156
  12.2 3.3 %copy-start.16 = (f32[4,8,128]{2,1,0:T(8,128)}, f32[4,8,128]{2,1,0:T(8,128)S(1)}, u32[]{:S(2)}) copy-start(f32[4,8,128]{2,1,0:T(8,128)S(1)} %get-tuple-element.141) | copy-start | bytes 49156
  13.6 3.9 %copy-start.10 = (f32[4,8,128]{2,1,0:T(8,128)}, f32[4,8,128]{2,1,0:T(8,128)S(1)}, u32[]{:S(2)}) copy-start(f32[4,8,128]{2,1,0:T(8,128)S(1)} %broadcast_multiply_fusion.4) | copy-start | bytes 49156
  18.2 9.3 %copy-start.49 = (pred[128]{0:T(512)(128)(4,1)}, pred[128]{0:T(512)(128)(4,1)S(1)}, u32[]{:S(2)}) copy-start(pred[128]{0:T(512)(128)(4,1)S(1)} %get-tuple-element.166) | copy-start | bytes 388
  18.2 9.3 %copy-start.51 = (pred[128]{0:T(512)(128)(4,1)}, pred[128]{0:T(512)(128)(4,1)S(1)}, u32[]{:S(2)}) copy-start(pred[128]{0:T(512)(128)(4,1)S(1)} %get-tuple-element.167) | copy-start | bytes 388
  21.8 3.8 %collective-permute-start.2 = (f32[28,4,8]{0,2,1:T(8,128)S(1)}, f32[28,4,8]{0,2,1:T(8,128)S(1)}, u32[]{:S(2)}, u32[]{:S(2)}) collective-permute-start(f32[28,4,8]{0,2,1:T(8,128)S(1)} %get-tuple-element.54), channel_id=1, source_target_pairs={{0,1},{1,2},{2,3},{3,4},{4,5},{5,6},{6,7},{7,0},{8,9},{9,10},{10,1... | collective-permute-start | bytes 10760 | tf_op jit(solution)/shard_map/ppermute | solution.py:86
  23.7 3.7 %collective-permute-start.3 = (f32[28,4,8]{0,2,1:T(8,128)S(1)}, f32[28,4,8]{0,2,1:T(8,128)S(1)}, u32[]{:S(2)}, u32[]{:S(2)}) collective-permute-start(f32[28,4,8]{0,2,1:T(8,128)S(1)} %get-tuple-element.55), channel_id=1, source_target_pairs={{0,7},{1,0},{2,1},{3,2},{4,3},{5,4},{6,5},{7,6},{8,15},{9,8},{10,9... | collective-permute-start | bytes 10760 | tf_op jit(solution)/shard_map/ppermute | solution.py:87
  32.2 1.1 %collective-permute-start.5 = (f32[19]{0:T(128)S(1)}, f32[19]{0:T(128)S(1)}, u32[]{:S(2)}, u32[]{:S(2)}) collective-permute-start(f32[19]{0:T(128)S(1)} %broadcast_select_fusion), channel_id=1, source_target_pairs={{0,8},{8,0},{16,24},{24,16},{32,40},{40,32},{48,56},{56,48},{64,72... | collective-permute-start | bytes 236 | tf_op jit(solution)/shard_map/ppermute | solution.py:130
  33.9 6.1 %collective-permute-start.6 = (f32[19]{0:T(128)}, f32[19]{0:T(128)}, u32[]{:S(2)}, u32[]{:S(2)}) collective-permute-start(f32[19]{0:T(128)} %add.117), channel_id=1, source_target_pairs={{0,16},{8,24},{16,0},{24,8},{32,48},{40,56},{48,32},{56,40},{64,80... | collective-permute-start | bytes 236 | tf_op jit(solution)/shard_map/ppermute | solution.py:130
  38.6 2.4 %copy-start.3 = (f32[19,4,8,128]{3,0,2,1:T(8,128)S(1)}, f32[19,4,8,128]{3,0,2,1:T(8,128)}, u32[]{:S(2)}) copy-start(f32[19,4,8,128]{3,0,2,1:T(8,128)} %copy-done.2) | copy-start | bytes 933892
  40.6 3.5 %collective-permute-start.7 = (f32[19]{0:T(128)S(1)}, f32[19]{0:T(128)S(1)}, u32[]{:S(2)}, u32[]{:S(2)}) collective-permute-start(f32[19]{0:T(128)S(1)} %add.118), channel_id=1, source_target_pairs={{0,32},{8,40},{16,48},{24,56},{32,0},{40,8},{48,16},{56,24},{64,96... | collective-permute-start | bytes 236 | tf_op jit(solution)/shard_map/ppermute | solution.py:130
  47.2 4.8 %collective-permute-start.8 = (f32[19]{0:T(128)S(1)}, f32[19]{0:T(128)S(1)}, u32[]{:S(2)}, u32[]{:S(2)}) collective-permute-start(f32[19]{0:T(128)S(1)} %add.119), channel_id=1, source_target_pairs={{0,96},{8,104},{16,112},{24,120},{32,64},{40,72},{48,80},{56,88},{... | collective-permute-start | bytes 236 | tf_op jit(solution)/shard_map/ppermute | solution.py:130
  49.1 3.1 %collective-permute-start.10 = (f32[28,4,1,128]{3,0,2,1:T(8,128)S(1)}, f32[28,4,1,128]{3,0,2,1:T(8,128)S(1)}, u32[]{:S(2)}, u32[]{:S(2)}) collective-permute-start(f32[28,4,1,128]{3,0,2,1:T(8,128)S(1)} %get-tuple-element.98), channel_id=1, source_target_pairs={{0,120},{8,0},{16,8},{24,16},{32,24},{40,32},{48,40},{56,48},{64,5... | collective-permute-start | bytes 172040 | tf_op jit(solution)/shard_map/ppermute | solution.py:78
  50.1 5.8 %collective-permute-start.9 = (f32[28,4,1,128]{3,0,2,1:T(8,128)S(1)}, f32[28,4,1,128]{3,0,2,1:T(8,128)S(1)}, u32[]{:S(2)}, u32[]{:S(2)}) collective-permute-start(f32[28,4,1,128]{3,0,2,1:T(8,128)S(1)} %get-tuple-element.99), channel_id=1, source_target_pairs={{0,8},{8,16},{16,24},{24,32},{32,40},{40,48},{48,56},{56,64},{64,7... | collective-permute-start | bytes 172040 | tf_op jit(solution)/shard_map/ppermute | solution.py:77
  56.8 3.6 %collective-permute-start.13 = (f32[19]{0:T(128)S(1)}, f32[19]{0:T(128)S(1)}, u32[]{:S(2)}, u32[]{:S(2)}) collective-permute-start(f32[19]{0:T(128)S(1)} %add.120), channel_id=1, source_target_pairs={{0,1},{1,0},{2,3},{3,2},{4,5},{5,4},{6,7},{7,6},{8,9},{9,8},{10,11... | collective-permute-start | bytes 236 | tf_op jit(solution)/shard_map/ppermute | solution.py:130
  59.1 14.3 %copy-start.52 = (pred[128]{0:T(512)(128)(4,1)S(1)}, pred[128]{0:T(512)(128)(4,1)}, u32[]{:S(2)}) copy-start(pred[128]{0:T(512)(128)(4,1)} %copy-done.51) | copy-start | bytes 388
  60.4 7.2 %collective-permute-start.14 = (f32[19]{0:T(128)S(1)}, f32[19]{0:T(128)S(1)}, u32[]{:S(2)}, u32[]{:S(2)}) collective-permute-start(f32[19]{0:T(128)S(1)} %add.124), channel_id=1, source_target_pairs={{0,2},{1,3},{2,0},{3,1},{4,6},{5,7},{6,4},{7,5},{8,10},{9,11},{10,... | collective-permute-start | bytes 236 | tf_op jit(solution)/shard_map/ppermute | solution.py:130
  66.1 7.3 %collective-permute-start.11 = (f32[28,4,8]{0,2,1:T(8,128)S(1)}, f32[28,4,8]{0,2,1:T(8,128)S(1)}, u32[]{:S(2)}, u32[]{:S(2)}) collective-permute-start(f32[28,4,8]{0,2,1:T(8,128)S(1)} %get-tuple-element.48), channel_id=1, source_target_pairs={{0,1},{1,2},{2,3},{3,4},{4,5},{5,6},{6,7},{7,0},{8,9},{9,10},{10,1... | collective-permute-start | bytes 10760 | tf_op jit(solution)/shard_map/ppermute | solution.py:86
  67.6 5.7 %collective-permute-start.15 = (f32[19]{0:T(128)S(1)}, f32[19]{0:T(128)S(1)}, u32[]{:S(2)}, u32[]{:S(2)}) collective-permute-start(f32[19]{0:T(128)S(1)} %add.125), channel_id=1, source_target_pairs={{0,6},{1,7},{2,4},{3,5},{4,2},{5,3},{6,0},{7,1},{8,14},{9,15},{10,... | collective-permute-start | bytes 236 | tf_op jit(solution)/shard_map/ppermute | solution.py:130
  69.7 3.8 %collective-permute-start.12 = (f32[28,4,8]{0,2,1:T(8,128)S(1)}, f32[28,4,8]{0,2,1:T(8,128)S(1)}, u32[]{:S(2)}, u32[]{:S(2)}) collective-permute-start(f32[28,4,8]{0,2,1:T(8,128)S(1)} %get-tuple-element.49), channel_id=1, source_target_pairs={{0,7},{1,0},{2,1},{3,2},{4,3},{5,4},{6,5},{7,6},{8,15},{9,8},{10,9... | collective-permute-start | bytes 10760 | tf_op jit(solution)/shard_map/ppermute | solution.py:87
  73.3 5.9 %collective-permute-start.16 = (f32[4,4,8,128]{3,2,1,0:T(8,128)S(1)}, f32[4,4,8,128]{3,2,1,0:T(8,128)S(1)}, u32[]{:S(2)}, u32[]{:S(2)}) collective-permute-start(f32[4,4,8,128]{3,2,1,0:T(8,128)S(1)} %select_maximum_fusion), channel_id=1, source_target_pairs={{0,128},{128,0},{1,129},{129,1},{2,130},{130,2},{3,131},{131,3},{4... | collective-permute-start | bytes 196616 | tf_op jit(solution)/shard_map/ppermute | solution.py:257
  75.8 3.4 %copy-start.7 = (f32[3,4,8,128]{3,2,1,0:T(8,128)S(1)}, f32[3,4,8,128]{3,2,1,0:T(8,128)}, u32[]{:S(2)}) copy-start(f32[3,4,8,128]{3,2,1,0:T(8,128)} %copy-done.6) | copy-start | bytes 147460
  (49 other events, 41.7 us)

commit v9 on v5

--- a/solution.py
+++ b/solution.py
@@ -127,9 +127,13 @@
     return values
 
 
+def mix(table, field):
+    weights = jnp.asarray(np.asarray(table, np.float32)).reshape(table.shape + (1,) * (field.ndim - 1))
+    return jnp.sum(weights * field[:, None], axis=0)
+
+
 def per_device(populations, solid_mask, flow_rates, species_rates, cotangents):
     velocity, weights, opposite, ortho = lattice_tables()
-    highest = lax.Precision.HIGHEST
     rows = populations.shape[0]
     groups = rows // 7
     is_flow = lax.axis_index("sec") == 0
@@ -157,15 +161,14 @@
     species_bounce = jnp.swapaxes(reverse_pairs(jnp.swapaxes(grouped, 0, 1), opposite[:7]), 0, 1)
     species_post = jnp.where(fluid[None], species_relaxed, species_bounce).reshape(populations.shape)
 
-    q_table = jnp.asarray(ortho, jnp.float32)
     relax = jnp.concatenate([jnp.zeros((4,), flow_rates.dtype), flow_rates]).reshape(19, 1, 1, 1)
     w = column(weights)
     projected = vx * motion[0][None] + vy * motion[1][None] + vz * motion[2][None]
     squared = jnp.sum(motion * motion, 0)
     poly = w * (1.0 + 3.0 * projected + 4.5 * projected * projected - 1.5 * squared[None])
     equilibrium = density[None] * poly
-    moments = jnp.einsum("ji,jxyz->ixyz", q_table, flow - equilibrium, precision=highest)
-    flow_relaxed = flow - jnp.einsum("ij,jxyz->ixyz", q_table, relax * moments, precision=highest)
+    moments = mix(ortho, flow - equilibrium)
+    flow_relaxed = flow - mix(ortho.T, relax * moments)
     flow_post = jnp.where(fluid, flow_relaxed, reverse_pairs(flow, opposite))
     filler = jnp.zeros((rows - 19,) + populations.shape[1:], jnp.float32)
     post = jnp.where(is_flow, jnp.concatenate([flow_post, filler]), species_post)
@@ -186,7 +189,7 @@
     species_rate_grad = -jnp.sum(
         jnp.where(fluid[None], back_species * species_gap, 0.0), axis=(1, 2, 3, 4)
     )
-    back_moments = jnp.einsum("ji,jxyz->ixyz", q_table, back_flow, precision=highest)
+    back_moments = mix(ortho, back_flow)
     flow_rate_grad = -jnp.sum(
         jnp.where(fluid, back_moments * moments, 0.0)[4:], axis=(1, 2, 3)
     )
@@ -202,7 +205,7 @@
         values, (back_flow_, back_moments_) = lax.optimization_barrier(
             (values, (back_flow, back_moments))
         )
-        through_eq = jnp.einsum("ij,jxyz->ixyz", q_table, relax * back_moments_, precision=highest)
+        through_eq = mix(ortho.T, relax * back_moments_)
         density_grad = jnp.sum(through_eq * poly, 0)
         hw = through_eq * w
         hw_sum = jnp.sum(hw, 0)

time: 69.4 us -> 85 us (1.22); the launches traced: 69.1 us -> 83.4 us
  local copies, waits for them, and re-layouts: 9.47 us -> 18.6 us
  other arithmetic: 6.36 us -> 15.1 us
  starting transfers between devices: 29 us -> 25.5 us
  matrix products: 2.34 us -> 0 us
  waiting for transfers between devices: 20.6 us -> 22.3 us
    unnamed x58 -> x152, local copies, waits for them, and re-layouts: 6.49 us -> 11.2 us
    ppermute x0 -> x2, local copies, waits for them, and re-layouts: none -> 2.91 us  [the longest x1 1.46 us: shift_rows(): high = lax.ppermute(field[:, :, :, 0], 'gz', ring('gz', -1))]
    ppermute x1, starting transfers between devices: 2.97 us -> 0.09 us  [per_device(): other = lax.ppermute(payload, 'sec', [(0, 1), (1, 0)])]
    ppermute x1, waiting for transfers between devices: 2.74 us -> 5.59 us  [per_device(): other = lax.ppermute(payload, 'sec', [(0, 1), (1, 0)])]
    dot_general x4 -> x0, matrix products: 2.34 us -> none  [the longest x1 0.69 us: per_device(): jnp.einsum('ji,jxyz->ixyz', q_table, flow - equilibrium, precision=highest)]
    reduce_sum x0 -> x4, other arithmetic: none -> 1.89 us  [mix(): return jnp.sum(weights * field[:, None], axis=0)]
    ppermute x1, waiting for transfers between devices: 1.41 us -> 0.01 us  [shift_rows(): low = lax.ppermute(field[:, :, :, size_z - 1], 'gz', ring('gz', 1))]
    ppermute x7, waiting for transfers between devices: 12.2 us -> 13.6 us  [butterfly_sum(): values = values + lax.ppermute(values, axis, list(enumerate(targets)))]
  transfers between devices with their start and end apart: 13 -> 13, of which waited for: 10 -> 10; matrix products, arithmetic and copies ran while one was open for 7% -> 21% of each run, Pallas kernels for 0% -> 0%
where the time goes in v9:
time: 85 us; the launch traced here: 83.4 us
  starting transfers between devices  25.5 us (30%)
  waiting for transfers between devices  22.3 us (26%)
  local copies, waits for them, and re-layouts  18.6 us (22%)
  other arithmetic  15.1 us (18%)
  between operations  1.83 us (2%)
    ppermute x7, starting transfers between devices, butterfly_sum(): values = values + lax.ppermute(values, axis, list(enumerate(targets)))  14.5 us
    ppermute x7, waiting for transfers between devices, butterfly_sum(): values = values + lax.ppermute(values, axis, list(enumerate(targets)))  13.6 us
    unnamed x152, local copies, waits for them, and re-layouts  11.2 us
    ppermute x1, waiting for transfers between devices, per_device(): other = lax.ppermute(payload, 'sec', [(0, 1), (1, 0)])  5.59 us
    ppermute x1, starting transfers between devices, per_device(): sent_motion = lax.ppermute(own_motion, 'sec', [(0, 1)])  4.93 us
    ppermute x1, starting transfers between devices, shift_rows(): high = lax.ppermute(field[:, :, :1, :], 'gy', ring('gy', -1))  3.84 us
    select_n x1, other arithmetic, shift_rows(): jnp.where(move_z > 0, from_low, jnp.where(move_z < 0, from_high, field))  2.45 us
    ppermute x1, waiting for transfers between devices, shift_rows(): low = lax.ppermute(field[:, :, size_y - 1:, :], 'gy', ring('gy', 1))  2.22 us
  transfers between devices with their start and end apart: 13, of which 10 were waited for; matrix products, arithmetic and copies ran while one was open for 21% of the time, Pallas kernels for 0%

profile of v9, /device:TPU:32, one launch (start us, length us, event | category | flops | bytes accessed | tf_op | source)
XLA Modules:
  0.0 83.4 jit_solution(17023514047941223578)
XLA Ops:
  0.6 1.2 %slice_reduce_fusion = (f32[4,8,128]{2,1,0:T(8,128)S(1)}, f32[4,8,128]{2,1,0:T(8,128)S(1)}, f32[4,8,128]{2,1,0:T(8,128)S(1)}, f32[4,8,128]{2,1,0:T(8,128)S(1)}) fusion(f32[28,4,8,128]{3,2,1,0:T(8,128)} %param.25, f32[19]{0:T(128)} %constant.129, f32[19]{0:T(128)} %constant.130, f32[19]{0:T(128)} %constant.131), kind=kLoop, calls=%fused_computation.57 | loop fusion | flops 528384 | bytes 377060 | tf_op jit(solution)/shard_map/reduce_sum | solution.py:144
  1.9 4.9 %collective-permute-start = (f32[3,4,8,128]{3,2,1,0:T(8,128)S(1)}, f32[3,4,8,128]{3,2,1,0:T(8,128)S(1)}, u32[]{:S(2)}, u32[]{:S(2)}) collective-permute-start(f32[3,4,8,128]{3,2,1,0:T(8,128)S(1)} %maximum_divide_fusion), channel_id=1, source_target_pairs={{0,128},{1,129},{2,130},{3,131},{4,132},{5,133},{6,134},{7,135},{8... | collective-permute-start | bytes 147464 | tf_op jit(solution)/shard_map/ppermute | solution.py:148
  6.9 0.7 constant_dynamic-update-slice_fusion.18
  8.2 0.7 broadcast_compare_fusion
  10.4 0.7 constant_dynamic-update-slice_fusion.15
  21.0 0.9 %broadcast_multiply_fusion = (f32[4,7,4,8,128]{4,3,2,1,0:T(8,128)}, f32[4,7,4,8,128]{4,3,2,1,0:T(8,128)S(1)}) fusion(f32[4,4,8,128]{3,2,1,0:T(8,128)S(1)} %reduce_sum.221, f32[7,4,8,128]{3,2,1,0:T(8,128)S(1)} %add_multiply_fusion.1, f32[7,4,4,8,128]{4,3,2,0,1:T(8,128)S(1)} %constant_dynamic-update-slice_fusion.19, f32[4,7,4,8,128]{4,3,2,1,0:T(8,128)S(1)} %bitcast.69, ...), kind=kLoop, calls=%fused_computation.56 | loop fusion | flops 573440 | bytes 2019344 | tf_op jit(solution)/shard_map/mul | solution.py:158
  21.9 1.0 %copy-done.1 = f32[28,4,8,128]{3,2,1,0:T(8,128)S(1)} copy-done((f32[28,4,8,128]{3,2,1,0:T(8,128)S(1)}, f32[28,4,8,128]{3,2,1,0:T(8,128)}, u32[]{:S(2)}) %copy-start.1) | copy-done | bytes 458776
  23.1 3.8 %collective-permute-start.2 = (f32[56,4,1,128]{3,2,1,0:T(1,128)S(1)}, f32[56,4,1,128]{3,2,1,0:T(1,128)S(1)}, u32[]{:S(2)}, u32[]{:S(2)}) collective-permute-start(f32[56,4,1,128]{3,2,1,0:T(1,128)S(1)} %get-tuple-element.60), channel_id=1, source_target_pairs={{0,120},{8,0},{16,8},{24,16},{32,24},{40,32},{48,40},{56,48},{64,5... | collective-permute-start | bytes 344072 | tf_op jit(solution)/shard_map/ppermute | solution.py:79
  27.2 2.2 %collective-permute-done.1 = f32[56,4,1,128]{3,2,1,0:T(1,128)S(1)} collective-permute-done((f32[56,4,1,128]{3,2,1,0:T(1,128)S(1)}, f32[56,4,1,128]{3,2,1,0:T(1,128)S(1)}, u32[]{:S(2)}, u32[]{:S(2)}) %collective-permute-start.1) | collective-permute-done | bytes 114720 | tf_op jit(solution)/shard_map/ppermute | solution.py:78
  30.2 1.1 %copy.75 = f32[56,4,8,1]{0,2,3,1:T(8,128)} copy(f32[56,4,8,1]{3,2,1,0:T(8,128)S(1)} %get-tuple-element.57) | data formatting | bytes 14336 | tf_op jit(solution)/shard_map/slice | solution.py:83
  31.3 1.9 %collective-permute-start.3 = (f32[56,4,8]{0,2,1:T(8,128)}, f32[56,4,8]{0,2,1:T(8,128)}, u32[]{:S(2)}, u32[]{:S(2)}) collective-permute-start(f32[56,4,8]{0,2,1:T(8,128)} %bitcast.91), channel_id=1, source_target_pairs={{0,1},{1,2},{2,3},{3,4},{4,5},{5,6},{6,7},{7,0},{8,9},{9,10},{10,1... | collective-permute-start | bytes 21512 | tf_op jit(solution)/shard_map/ppermute | solution.py:83
  33.3 1.1 %copy.77 = f32[56,4,8,1]{0,2,3,1:T(8,128)} copy(f32[56,4,8,1]{3,2,1,0:T(8,128)S(1)} %get-tuple-element.56) | data formatting | bytes 14336 | tf_op jit(solution)/shard_map/slice | solution.py:84
  34.5 1.5 %fusion.27 = (f32[56,4,8,127]{3,2,1,0:T(8,128)}, f32[56,4,8,127]{3,2,1,0:T(8,128)}) fusion(f32[56,4,8,128]{3,2,1,0:T(8,128)S(1)} %fusion.3), kind=kLoop, calls=%fused_computation.166 | loop fusion | bytes 3641344 | tf_op jit(solution)/shard_map/jit(_roll_static)/slice | solution.py:87
  36.1 1.5 %copy.76 = f32[56,4,8]{2,1,0:T(4,128)} copy(f32[56,4,8]{0,2,1:T(8,128)} %collective-permute-done.3) | data formatting | bytes 14336 | tf_op jit(solution)/shard_map/ppermute | solution.py:83
  37.5 0.9 %collective-permute-done.4 = f32[56,4,8]{0,2,1:T(8,128)} collective-permute-done((f32[56,4,8]{0,2,1:T(8,128)}, f32[56,4,8]{0,2,1:T(8,128)}, u32[]{:S(2)}, u32[]{:S(2)}) %collective-permute-start.4) | collective-permute-done | bytes 7200 | tf_op jit(solution)/shard_map/ppermute | solution.py:84
  38.5 1.5 %copy.78 = f32[56,4,8]{2,1,0:T(4,128)} copy(f32[56,4,8]{0,2,1:T(8,128)} %collective-permute-done.4) | data formatting | bytes 14336 | tf_op jit(solution)/shard_map/ppermute | solution.py:84
  39.9 2.4 %fusion.4 = f32[56,4,8,128]{3,2,1,0:T(8,128)S(1)} fusion(f32[56,4,8,127]{3,2,1,0:T(8,128)} %get-tuple-element.55, f32[56,4,8,1]{3,2,1,0:T(8,128)S(1)} %get-tuple-element.57, f32[56,4,8,128]{3,2,1,0:T(8,128)S(1)} %fusion.3, f32[56,4,8,1]{3,2,1,0:T(8,128)S(1)} %get-tuple-element.56, f32[56,4,8,127]{3,2,1,0:T(8,128)} %get-tuple-element.54, ...), kind=kLoop, calls=%fused_computation.18 | loop fusion | flops 1376256 | bytes 3684720 | tf_op jit(solution)/shard_map/jit(_where)/select_n | solution.py:88
  44.7 1.0 %fusion.24 = (f32[28,4,8,128]{3,2,1,0:T(8,128)S(1)}, f32[28]{0:T(128)S(1)}, f32[28,4,8,128]{3,2,1,0:T(8,128)}) fusion(f32[56,4,8,128]{3,2,1,0:T(8,128)S(1)} %maximum_select_fusion.2, f32[28,4,8,128]{3,2,1,0:T(8,128)S(1)} %copy-done, f32[4,7,4,8,128]{4,3,2,1,0:T(8,128)S(1)} %copy-done.2, pred[4,8,128]{2,1,0:T(8,128)(4,1)S(1)} %broadcast_compare_fusion, ...), kind=kLoop, calls=%fused_computation.163 | loop fusion | flops 688100 | bytes 2756749 | tf_op jit(solution)/shard_map/slice | solution.py:184
  46.4 0.8 collective-permute-done.5
  48.7 2.1 %collective-permute-done.6 = f32[19]{0:T(128)S(1)} collective-permute-done((f32[19]{0:T(128)S(1)}, f32[19]{0:T(128)S(1)}, u32[]{:S(2)}, u32[]{:S(2)}) %collective-permute-start.6) | collective-permute-done | bytes 108 | tf_op jit(solution)/shard_map/ppermute | solution.py:123
  51.2 1.6 %collective-permute-start.7 = (f32[19]{0:T(128)S(1)}, f32[19]{0:T(128)S(1)}, u32[]{:S(2)}, u32[]{:S(2)}) collective-permute-start(f32[19]{0:T(128)S(1)} %add.121), channel_id=1, source_target_pairs={{0,32},{8,40},{16,48},{24,56},{32,0},{40,8},{48,16},{56,24},{64,96... | collective-permute-start | bytes 236 | tf_op jit(solution)/shard_map/ppermute | solution.py:123
  52.8 2.0 %collective-permute-done.7 = f32[19]{0:T(128)S(1)} collective-permute-done((f32[19]{0:T(128)S(1)}, f32[19]{0:T(128)S(1)}, u32[]{:S(2)}, u32[]{:S(2)}) %collective-permute-start.7) | collective-permute-done | bytes 108 | tf_op jit(solution)/shard_map/ppermute | solution.py:123
  54.8 2.9 %collective-permute-start.8 = (f32[19]{0:T(128)S(1)}, f32[19]{0:T(128)S(1)}, u32[]{:S(2)}, u32[]{:S(2)}) collective-permute-start(f32[19]{0:T(128)S(1)} %add.122), channel_id=1, source_target_pairs={{0,96},{8,104},{16,112},{24,120},{32,64},{40,72},{48,80},{56,88},{... | collective-permute-start | bytes 236 | tf_op jit(solution)/shard_map/ppermute | solution.py:123
  57.7 1.9 %collective-permute-done.8 = f32[19]{0:T(128)S(1)} collective-permute-done((f32[19]{0:T(128)S(1)}, f32[19]{0:T(128)S(1)}, u32[]{:S(2)}, u32[]{:S(2)}) %collective-permute-start.8) | collective-permute-done | bytes 108 | tf_op jit(solution)/shard_map/ppermute | solution.py:123
  59.6 3.0 %collective-permute-start.9 = (f32[19]{0:T(128)S(1)}, f32[19]{0:T(128)S(1)}, u32[]{:S(2)}, u32[]{:S(2)}) collective-permute-start(f32[19]{0:T(128)S(1)} %add.123), channel_id=1, source_target_pairs={{0,1},{1,0},{2,3},{3,2},{4,5},{5,4},{6,7},{7,6},{8,9},{9,8},{10,11... | collective-permute-start | bytes 236 | tf_op jit(solution)/shard_map/ppermute | solution.py:123
  62.6 1.5 %collective-permute-done.9 = f32[19]{0:T(128)S(1)} collective-permute-done((f32[19]{0:T(128)S(1)}, f32[19]{0:T(128)S(1)}, u32[]{:S(2)}, u32[]{:S(2)}) %collective-permute-start.9) | collective-permute-done | bytes 108 | tf_op jit(solution)/shard_map/ppermute | solution.py:123
  64.1 4.7 %collective-permute-start.10 = (f32[19]{0:T(128)S(1)}, f32[19]{0:T(128)S(1)}, u32[]{:S(2)}, u32[]{:S(2)}) collective-permute-start(f32[19]{0:T(128)S(1)} %add.124), channel_id=1, source_target_pairs={{0,2},{1,3},{2,0},{3,1},{4,6},{5,7},{6,4},{7,5},{8,10},{9,11},{10,... | collective-permute-start | bytes 236 | tf_op jit(solution)/shard_map/ppermute | solution.py:123
  68.8 1.5 %collective-permute-done.10 = f32[19]{0:T(128)S(1)} collective-permute-done((f32[19]{0:T(128)S(1)}, f32[19]{0:T(128)S(1)}, u32[]{:S(2)}, u32[]{:S(2)}) %collective-permute-start.10) | collective-permute-done | bytes 108 | tf_op jit(solution)/shard_map/ppermute | solution.py:123
  70.3 1.9 %collective-permute-start.11 = (f32[19]{0:T(128)S(1)}, f32[19]{0:T(128)S(1)}, u32[]{:S(2)}, u32[]{:S(2)}) collective-permute-start(f32[19]{0:T(128)S(1)} %add.125), channel_id=1, source_target_pairs={{0,6},{1,7},{2,4},{3,5},{4,2},{5,3},{6,0},{7,1},{8,14},{9,15},{10,... | collective-permute-start | bytes 236 | tf_op jit(solution)/shard_map/ppermute | solution.py:123
  72.2 3.7 %collective-permute-done.11 = f32[19]{0:T(128)S(1)} collective-permute-done((f32[19]{0:T(128)S(1)}, f32[19]{0:T(128)S(1)}, u32[]{:S(2)}, u32[]{:S(2)}) %collective-permute-start.11) | collective-permute-done | bytes 108 | tf_op jit(solution)/shard_map/ppermute | solution.py:123
  76.2 5.6 %collective-permute-done.12 = f32[4,4,8,128]{3,2,1,0:T(8,128)S(1)} collective-permute-done((f32[4,4,8,128]{3,2,1,0:T(8,128)S(1)}, f32[4,4,8,128]{3,2,1,0:T(8,128)S(1)}, u32[]{:S(2)}, u32[]{:S(2)}) %collective-permute-start.12) | collective-permute-done | bytes 65568 | tf_op jit(solution)/shard_map/ppermute | solution.py:242
  82.1 0.8 bitcast_select_fusion
  (217 shorter events, 18.3 us)
Async XLA Ops:
  0.6 16.2 %copy-start = (f32[28,4,8,128]{3,2,1,0:T(8,128)S(1)}, f32[28,4,8,128]{3,2,1,0:T(8,128)}, u32[]{:S(2)}) copy-start(f32[28,4,8,128]{3,2,1,0:T(8,128)} %param.25) | copy-start | bytes 1376260
  1.8 15.2 %copy-start.27 = (f32[4]{0:T(128)S(1)}, f32[4]{0:T(128)}, u32[]{:S(2)}) copy-start(f32[4]{0:T(128)} %param.28) | copy-start | bytes 52
  1.8 15.8 %copy-start.48 = (f32[28,1,1,1]{0,3,2,1:T(1,128)S(1)}, f32[28,1,1,1]{0,3,2,1:T(1,128)}, u32[]{:S(2)}) copy-start(f32[28,1,1,1]{0,3,2,1:T(1,128)} %constant.109.clone) | copy-start | bytes 340
  1.9 15.8 %copy-start.49 = (f32[28,1,1,1]{0,3,2,1:T(1,128)S(1)}, f32[28,1,1,1]{0,3,2,1:T(1,128)}, u32[]{:S(2)}) copy-start(f32[28,1,1,1]{0,3,2,1:T(1,128)} %constant.110.clone) | copy-start | bytes 340
  1.9 15.8 %copy-start.44 = (f32[28,1,1,1]{0,3,2,1:T(1,128)S(1)}, f32[28,1,1,1]{0,3,2,1:T(1,128)}, u32[]{:S(2)}) copy-start(f32[28,1,1,1]{0,3,2,1:T(1,128)} %constant.107.clone) | copy-start | bytes 340
  1.9 15.8 %copy-start.45 = (f32[28,1,1,1]{0,3,2,1:T(1,128)S(1)}, f32[28,1,1,1]{0,3,2,1:T(1,128)}, u32[]{:S(2)}) copy-start(f32[28,1,1,1]{0,3,2,1:T(1,128)} %constant.108.clone) | copy-start | bytes 340
  1.9 15.8 %copy-start.46 = (f32[28,1,1,1]{0,3,2,1:T(1,128)S(1)}, f32[28,1,1,1]{0,3,2,1:T(1,128)}, u32[]{:S(2)}) copy-start(f32[28,1,1,1]{0,3,2,1:T(1,128)} %constant.111.clone) | copy-start | bytes 340
  1.9 15.8 %copy-start.47 = (f32[28,1,1,1]{0,3,2,1:T(1,128)S(1)}, f32[28,1,1,1]{0,3,2,1:T(1,128)}, u32[]{:S(2)}) copy-start(f32[28,1,1,1]{0,3,2,1:T(1,128)} %constant.112.clone) | copy-start | bytes 340
  1.9 17.1 %copy-start.51 = (f32[15]{0:T(128)S(1)}, f32[15]{0:T(128)}, u32[]{:S(2)}) copy-start(f32[15]{0:T(128)} %param.27) | copy-start | bytes 184
  1.9 17.2 %collective-permute-start = (f32[3,4,8,128]{3,2,1,0:T(8,128)S(1)}, f32[3,4,8,128]{3,2,1,0:T(8,128)S(1)}, u32[]{:S(2)}, u32[]{:S(2)}) collective-permute-start(f32[3,4,8,128]{3,2,1,0:T(8,128)S(1)} %maximum_divide_fusion), channel_id=1, source_target_pairs={{0,128},{1,129},{2,130},{3,131},{4,132},{5,133},{6,134},{7,135},{8... | collective-permute-start | bytes 147464 | tf_op jit(solution)/shard_map/ppermute | solution.py:148
  23.0 6.4 %collective-permute-start.1 = (f32[56,4,1,128]{3,2,1,0:T(1,128)S(1)}, f32[56,4,1,128]{3,2,1,0:T(1,128)S(1)}, u32[]{:S(2)}, u32[]{:S(2)}) collective-permute-start(f32[56,4,1,128]{3,2,1,0:T(1,128)S(1)} %get-tuple-element.61), channel_id=1, source_target_pairs={{0,8},{8,16},{16,24},{24,32},{32,40},{40,48},{48,56},{56,64},{64,7... | collective-permute-start | bytes 344072 | tf_op jit(solution)/shard_map/ppermute | solution.py:78
  23.1 6.3 %collective-permute-start.2 = (f32[56,4,1,128]{3,2,1,0:T(1,128)S(1)}, f32[56,4,1,128]{3,2,1,0:T(1,128)S(1)}, u32[]{:S(2)}, u32[]{:S(2)}) collective-permute-start(f32[56,4,1,128]{3,2,1,0:T(1,128)S(1)} %get-tuple-element.60), channel_id=1, source_target_pairs={{0,120},{8,0},{16,8},{24,16},{32,24},{40,32},{48,40},{56,48},{64,5... | collective-permute-start | bytes 344072 | tf_op jit(solution)/shard_map/ppermute | solution.py:79
  31.3 4.7 %collective-permute-start.3 = (f32[56,4,8]{0,2,1:T(8,128)}, f32[56,4,8]{0,2,1:T(8,128)}, u32[]{:S(2)}, u32[]{:S(2)}) collective-permute-start(f32[56,4,8]{0,2,1:T(8,128)} %bitcast.91), channel_id=1, source_target_pairs={{0,1},{1,2},{2,3},{3,4},{4,5},{5,6},{6,7},{7,0},{8,9},{9,10},{10,1... | collective-permute-start | bytes 21512 | tf_op jit(solution)/shard_map/ppermute | solution.py:83
  34.4 4.1 %collective-permute-start.4 = (f32[56,4,8]{0,2,1:T(8,128)}, f32[56,4,8]{0,2,1:T(8,128)}, u32[]{:S(2)}, u32[]{:S(2)}) collective-permute-start(f32[56,4,8]{0,2,1:T(8,128)} %bitcast.92), channel_id=1, source_target_pairs={{0,7},{1,0},{2,1},{3,2},{4,3},{5,4},{6,5},{7,6},{8,15},{9,8},{10,9... | collective-permute-start | bytes 21512 | tf_op jit(solution)/shard_map/ppermute | solution.py:84
  44.7 3.0 %copy-start.42 = (f32[19]{0:T(128)S(1)}, f32[19]{0:T(128)}, u32[]{:S(2)}) copy-start(f32[19]{0:T(128)} %copy-done.41) | copy-start | bytes 232
  46.0 1.2 %collective-permute-start.5 = (f32[19]{0:T(128)S(1)}, f32[19]{0:T(128)S(1)}, u32[]{:S(2)}, u32[]{:S(2)}) collective-permute-start(f32[19]{0:T(128)S(1)} %broadcast_select_fusion.1), channel_id=1, source_target_pairs={{0,8},{8,0},{16,24},{24,16},{32,40},{40,32},{48,56},{56,48},{64,72... | collective-permute-start | bytes 236 | tf_op jit(solution)/shard_map/ppermute | solution.py:123
  46.3 4.5 %copy-start.4 = (f32[7,4,8,128]{3,2,1,0:T(8,128)S(1)}, f32[7,4,8,128]{3,2,1,0:T(8,128)}, u32[]{:S(2)}) copy-start(f32[7,4,8,128]{3,2,1,0:T(8,128)} %copy-done.3) | copy-start | bytes 344068
  46.4 4.5 %copy-start.32 = (f32[7]{0:T(128)S(1)}, f32[7]{0:T(128)}, u32[]{:S(2)}) copy-start(f32[7]{0:T(128)} %constant.132) | copy-start | bytes 88
  46.4 4.4 %copy-start.34 = (f32[7]{0:T(128)S(1)}, f32[7]{0:T(128)}, u32[]{:S(2)}) copy-start(f32[7]{0:T(128)} %constant.133) | copy-start | bytes 88
  46.4 4.4 %copy-start.36 = (f32[7]{0:T(128)S(1)}, f32[7]{0:T(128)}, u32[]{:S(2)}) copy-start(f32[7]{0:T(128)} %constant.134) | copy-start | bytes 88
  46.4 4.4 %copy-start.38 = (f32[7]{0:T(128)S(1)}, f32[7]{0:T(128)}, u32[]{:S(2)}) copy-start(f32[7]{0:T(128)} %constant.135) | copy-start | bytes 88
  47.3 3.5 %collective-permute-start.6 = (f32[19]{0:T(128)S(1)}, f32[19]{0:T(128)S(1)}, u32[]{:S(2)}, u32[]{:S(2)}) collective-permute-start(f32[19]{0:T(128)S(1)} %add.117), channel_id=1, source_target_pairs={{0,16},{8,24},{16,0},{24,8},{32,48},{40,56},{48,32},{56,40},{64,80... | collective-permute-start | bytes 236 | tf_op jit(solution)/shard_map/ppermute | solution.py:123
  47.7 3.3 %copy-start.6 = (f32[4,4,8,128]{3,2,1,0:T(8,128)S(1)}, f32[4,4,8,128]{3,2,1,0:T(8,128)}, u32[]{:S(2)}) copy-start(f32[4,4,8,128]{3,2,1,0:T(8,128)} %copy-done.5) | copy-start | bytes 196612
  47.8 3.3 %copy-start.28 = (f32[4]{0:T(128)S(1)}, f32[4]{0:T(128)}, u32[]{:S(2)}) copy-start(f32[4]{0:T(128)} %param.28) | copy-start | bytes 52
  51.1 25.0 %copy-start.43 = (f32[4]{0:T(128)S(1)}, f32[4]{0:T(128)}, u32[]{:S(2)}) copy-start(f32[4]{0:T(128)} %broadcast_subtract_fusion) | copy-start | bytes 52
  51.2 3.6 %collective-permute-start.7 = (f32[19]{0:T(128)S(1)}, f32[19]{0:T(128)S(1)}, u32[]{:S(2)}, u32[]{:S(2)}) collective-permute-start(f32[19]{0:T(128)S(1)} %add.121), channel_id=1, source_target_pairs={{0,32},{8,40},{16,48},{24,56},{32,0},{40,8},{48,16},{56,24},{64,96... | collective-permute-start | bytes 236 | tf_op jit(solution)/shard_map/ppermute | solution.py:123
  54.8 4.8 %collective-permute-start.8 = (f32[19]{0:T(128)S(1)}, f32[19]{0:T(128)S(1)}, u32[]{:S(2)}, u32[]{:S(2)}) collective-permute-start(f32[19]{0:T(128)S(1)} %add.122), channel_id=1, source_target_pairs={{0,96},{8,104},{16,112},{24,120},{32,64},{40,72},{48,80},{56,88},{... | collective-permute-start | bytes 236 | tf_op jit(solution)/shard_map/ppermute | solution.py:123
  59.6 4.5 %collective-permute-start.9 = (f32[19]{0:T(128)S(1)}, f32[19]{0:T(128)S(1)}, u32[]{:S(2)}, u32[]{:S(2)}) collective-permute-start(f32[19]{0:T(128)S(1)} %add.123), channel_id=1, source_target_pairs={{0,1},{1,0},{2,3},{3,2},{4,5},{5,4},{6,7},{7,6},{8,9},{9,8},{10,11... | collective-permute-start | bytes 236 | tf_op jit(solution)/shard_map/ppermute | solution.py:123
  64.1 6.2 %collective-permute-start.10 = (f32[19]{0:T(128)S(1)}, f32[19]{0:T(128)S(1)}, u32[]{:S(2)}, u32[]{:S(2)}) collective-permute-start(f32[19]{0:T(128)S(1)} %add.124), channel_id=1, source_target_pairs={{0,2},{1,3},{2,0},{3,1},{4,6},{5,7},{6,4},{7,5},{8,10},{9,11},{10,... | collective-permute-start | bytes 236 | tf_op jit(solution)/shard_map/ppermute | solution.py:123
  68.8 13.0 %copy-start.8 = (f32[3,4,8,128]{3,2,1,0:T(8,128)S(1)}, f32[3,4,8,128]{3,2,1,0:T(8,128)}, u32[]{:S(2)}) copy-start(f32[3,4,8,128]{3,2,1,0:T(8,128)} %copy-done.7) | copy-start | bytes 147460
  70.3 5.7 %collective-permute-start.11 = (f32[19]{0:T(128)S(1)}, f32[19]{0:T(128)S(1)}, u32[]{:S(2)}, u32[]{:S(2)}) collective-permute-start(f32[19]{0:T(128)S(1)} %add.125), channel_id=1, source_target_pairs={{0,6},{1,7},{2,4},{3,5},{4,2},{5,3},{6,0},{7,1},{8,14},{9,15},{10,... | collective-permute-start | bytes 236 | tf_op jit(solution)/shard_map/ppermute | solution.py:123
  76.0 5.9 %collective-permute-start.12 = (f32[4,4,8,128]{3,2,1,0:T(8,128)S(1)}, f32[4,4,8,128]{3,2,1,0:T(8,128)S(1)}, u32[]{:S(2)}, u32[]{:S(2)}) collective-permute-start(f32[4,4,8,128]{3,2,1,0:T(8,128)S(1)} %select_maximum_fusion), channel_id=1, source_target_pairs={{0,128},{128,0},{1,129},{129,1},{2,130},{130,2},{3,131},{131,3},{4... | collective-permute-start | bytes 196616 | tf_op jit(solution)/shard_map/ppermute | solution.py:242
  (33 other events, 51.2 us)

commit v10 on v5

--- a/solution.py
+++ b/solution.py
@@ -143,6 +143,8 @@
     ) / density[None]
     sent_motion = lax.ppermute(own_motion, "sec", [(0, 1)])
     motion = jnp.where(is_flow, own_motion, sent_motion)
+    populations, motion = lax.optimization_barrier((populations, motion))
+    flow = populations[:19]
 
     small_weights = column([0.25] + [0.125] * 6)
     grouped = populations.reshape((groups, 7) + populations.shape[1:])

time: 69.4 us -> 71.2 us (1.026)
  other arithmetic: 6.36 us -> 7.41 us
  local copies, waits for them, and re-layouts: 9.47 us -> 10.3 us
    reduce_sum x1, other arithmetic: 0.33 us -> 1.06 us  [per_device(): density = jnp.sum(flow, 0)]
    unnamed x58 -> x57, local copies, waits for them, and re-layouts: 6.49 us -> 7.09 us
  transfers between devices with their start and end apart: 13 -> 13, of which waited for: 10 -> 10; matrix products, arithmetic and copies ran while one was open for 7% -> 6% of each run, Pallas kernels for 0% -> 0%
where the time goes in v10:
time: 71.2 us; the launch traced here: 70.9 us
  starting transfers between devices  28.5 us (40%)
  waiting for transfers between devices  21.2 us (30%)
  local copies, waits for them, and re-layouts  10.3 us (14%)
  other arithmetic  7.41 us (10%)
  matrix products  2.34 us (3%)
  between operations  1.21 us (2%)
    ppermute x7, starting transfers between devices, butterfly_sum(): values = values + lax.ppermute(values, axis, list(enumerate(targets)))  15.1 us
    ppermute x7, waiting for transfers between devices, butterfly_sum(): values = values + lax.ppermute(values, axis, list(enumerate(targets)))  12.2 us
    unnamed x57, local copies, waits for them, and re-layouts  7.09 us
    ppermute x1, starting transfers between devices, per_device(): sent_motion = lax.ppermute(own_motion, 'sec', [(0, 1)])  4.93 us
    ppermute x1, starting transfers between devices, shift_rows(): high = lax.ppermute(field[:, :, :1, :], 'gy', ring('gy', -1))  3.84 us
    ppermute x1, waiting for transfers between devices, per_device(): other = lax.ppermute(payload, 'sec', [(0, 1), (1, 0)])  3.29 us
    ppermute x1, starting transfers between devices, per_device(): other = lax.ppermute(payload, 'sec', [(0, 1), (1, 0)])  2.42 us
    ppermute x1, waiting for transfers between devices, shift_rows(): low = lax.ppermute(field[:, :, size_y - 1:, :], 'gy', ring('gy', 1))  2.36 us
  transfers between devices with their start and end apart: 13, of which 10 were waited for; matrix products, arithmetic and copies ran while one was open for 6% of the time, Pallas kernels for 0%

profile of v10, /device:TPU:32, one launch (start us, length us, event | category | flops | bytes accessed | tf_op | source)
XLA Modules:
  0.0 70.9 jit_solution(2599128262906630045)
XLA Ops:
  0.6 1.1 %slice_reduce_fusion = (f32[4,8,128]{2,1,0:T(8,128)S(1)}, f32[19,4,8,128]{3,2,1,0:T(8,128)S(1)}) fusion(f32[28,4,8,128]{3,2,1,0:T(8,128)} %param.22), kind=kLoop, calls=%fused_computation.161 | loop fusion | flops 73728 | bytes 638976 | tf_op jit(solution)/shard_map/reduce_sum | solution.py:140
  2.8 4.9 %collective-permute-start = (f32[3,4,8,128]{3,2,1,0:T(8,128)S(1)}, f32[3,4,8,128]{3,2,1,0:T(8,128)S(1)}, u32[]{:S(2)}, u32[]{:S(2)}) collective-permute-start(f32[3,4,8,128]{3,2,1,0:T(8,128)S(1)} %maximum_divide_fusion), channel_id=1, source_target_pairs={{0,128},{1,129},{2,130},{3,131},{4,132},{5,133},{6,134},{7,135},{8... | collective-permute-start | bytes 147464 | tf_op jit(solution)/shard_map/ppermute | solution.py:144
  7.8 0.6 copy-done.7
  8.4 0.7 copy-done.17
  11.5 0.6 copy-done.2
  12.1 0.7 fusion.21
  14.8 3.8 %collective-permute-start.2 = (f32[56,4,1,128]{3,0,2,1:T(8,128)S(1)}, f32[56,4,1,128]{3,0,2,1:T(8,128)S(1)}, u32[]{:S(2)}, u32[]{:S(2)}) collective-permute-start(f32[56,4,1,128]{3,0,2,1:T(8,128)S(1)} %get-tuple-element.54), channel_id=1, source_target_pairs={{0,120},{8,0},{16,8},{24,16},{32,24},{40,32},{48,40},{56,48},{64,5... | collective-permute-start | bytes 344072 | tf_op jit(solution)/shard_map/ppermute | solution.py:79
  18.7 2.4 %collective-permute-done.1 = f32[56,4,1,128]{3,0,2,1:T(8,128)S(1)} collective-permute-done((f32[56,4,1,128]{3,0,2,1:T(8,128)S(1)}, f32[56,4,1,128]{3,0,2,1:T(8,128)S(1)}, u32[]{:S(2)}, u32[]{:S(2)}) %collective-permute-start.1) | collective-permute-done | bytes 114720 | tf_op jit(solution)/shard_map/ppermute | solution.py:78
  21.3 0.8 %slice_reduce_fusion.2 = (f32[56,4,8]{0,2,1:T(8,128)S(1)}, f32[56,4,8]{0,2,1:T(8,128)S(1)}, f32[56,4,8,1]{3,0,2,1:T(8,128)S(1)}, f32[56,4,8,1]{3,0,2,1:T(8,128)S(1)}) fusion(f32[56,4,8,128]{3,0,2,1:T(8,128)S(1)} %fusion.3), kind=kLoop, calls=%fused_computation.165 | loop fusion | bytes 43008 | tf_op jit(solution)/shard_map/slice | solution.py:83
  22.1 2.0 %collective-permute-start.3 = (f32[56,4,8]{0,2,1:T(8,128)S(1)}, f32[56,4,8]{0,2,1:T(8,128)S(1)}, u32[]{:S(2)}, u32[]{:S(2)}) collective-permute-start(f32[56,4,8]{0,2,1:T(8,128)S(1)} %get-tuple-element.38), channel_id=1, source_target_pairs={{0,1},{1,2},{2,3},{3,4},{4,5},{5,6},{6,7},{7,0},{8,9},{9,10},{10,1... | collective-permute-start | bytes 21512 | tf_op jit(solution)/shard_map/ppermute | solution.py:83
  24.6 1.4 %collective-permute-done.3 = f32[56,4,8]{0,2,1:T(8,128)S(1)} collective-permute-done((f32[56,4,8]{0,2,1:T(8,128)S(1)}, f32[56,4,8]{0,2,1:T(8,128)S(1)}, u32[]{:S(2)}, u32[]{:S(2)}) %collective-permute-start.3) | collective-permute-done | bytes 7200 | tf_op jit(solution)/shard_map/ppermute | solution.py:83
  26.0 1.9 %collective-permute-done.4 = f32[56,4,8]{0,2,1:T(8,128)S(1)} collective-permute-done((f32[56,4,8]{0,2,1:T(8,128)S(1)}, f32[56,4,8]{0,2,1:T(8,128)S(1)}, u32[]{:S(2)}, u32[]{:S(2)}) %collective-permute-start.4) | collective-permute-done | bytes 7200 | tf_op jit(solution)/shard_map/ppermute | solution.py:84
  27.9 1.2 %fusion.4 = f32[56,4,8,128]{3,0,2,1:T(8,128)S(1)} fusion(f32[56,4,8,127]{3,0,2,1:T(8,128)S(1)} %get-tuple-element.85, f32[56,4,8,1]{3,0,2,1:T(8,128)S(1)} %get-tuple-element.83, f32[56,4,8,128]{3,0,2,1:T(8,128)S(1)} %fusion.3, f32[56,4,8,1]{3,0,2,1:T(8,128)S(1)} %get-tuple-element.82, f32[56,4,8,127]{3,0,2,1:T(8,128)S(1)} %get-tuple-element.84, ...), kind=kLoop, calls=%fused_computation.15 | loop fusion | flops 1376256 | bytes 3684720 | tf_op jit(solution)/shard_map/jit(_where)/select_n | solution.py:88
  30.4 0.6 copy-done.12
  31.1 0.8 %fusion.73 = (f32[28,4,8,128]{3,0,2,1:T(8,128)S(1)}, f32[28]{0:T(128)S(1)}, f32[28,4,8,128]{3,0,2,1:T(8,128)S(1)}) fusion(f32[56,4,8,128]{3,0,2,1:T(8,128)S(1)} %maximum_select_fusion.2, f32[28,4,8,128]{3,2,1,0:T(8,128)S(1)} %bitcast.96, f32[28,4,8,128]{3,2,1,0:T(8,128)S(1)} %copy-done, pred[4,8,128]{2,1,0:T(8,128)(4,1)S(1)} %broadcast_compare_fusion, ...), kind=kLoop, calls=%fused_computation.167 | loop fusion | flops 688100 | bytes 2756749 | tf_op jit(solution)/shard_map/slice | solution.py:183
  32.7 1.0 %copy.114 = f32[28,4,8,128]{3,2,1,0:T(8,128)} copy(f32[28,4,8,128]{3,0,2,1:T(8,128)S(1)} %get-tuple-element.77) | data formatting | bytes 917504
  34.2 0.7 %collective-permute-start.6 = (f32[19]{0:T(128)S(1)}, f32[19]{0:T(128)S(1)}, u32[]{:S(2)}, u32[]{:S(2)}) collective-permute-start(f32[19]{0:T(128)S(1)} %add.117), channel_id=1, source_target_pairs={{0,16},{8,24},{16,0},{24,8},{32,48},{40,56},{48,32},{56,40},{64,80... | collective-permute-start | bytes 236 | tf_op jit(solution)/shard_map/ppermute | solution.py:123
  35.0 0.6 add_multiply_fusion
  36.2 1.6 %collective-permute-done.6 = f32[19]{0:T(128)S(1)} collective-permute-done((f32[19]{0:T(128)S(1)}, f32[19]{0:T(128)S(1)}, u32[]{:S(2)}, u32[]{:S(2)}) %collective-permute-start.6) | collective-permute-done | bytes 108 | tf_op jit(solution)/shard_map/ppermute | solution.py:123
  38.1 1.6 %collective-permute-start.7 = (f32[19]{0:T(128)S(1)}, f32[19]{0:T(128)S(1)}, u32[]{:S(2)}, u32[]{:S(2)}) collective-permute-start(f32[19]{0:T(128)S(1)} %add.121), channel_id=1, source_target_pairs={{0,32},{8,40},{16,48},{24,56},{32,0},{40,8},{48,16},{56,24},{64,96... | collective-permute-start | bytes 236 | tf_op jit(solution)/shard_map/ppermute | solution.py:123
  39.8 2.0 %collective-permute-done.7 = f32[19]{0:T(128)S(1)} collective-permute-done((f32[19]{0:T(128)S(1)}, f32[19]{0:T(128)S(1)}, u32[]{:S(2)}, u32[]{:S(2)}) %collective-permute-start.7) | collective-permute-done | bytes 108 | tf_op jit(solution)/shard_map/ppermute | solution.py:123
  41.8 2.9 %collective-permute-start.8 = (f32[19]{0:T(128)S(1)}, f32[19]{0:T(128)S(1)}, u32[]{:S(2)}, u32[]{:S(2)}) collective-permute-start(f32[19]{0:T(128)S(1)} %add.122), channel_id=1, source_target_pairs={{0,96},{8,104},{16,112},{24,120},{32,64},{40,72},{48,80},{56,88},{... | collective-permute-start | bytes 236 | tf_op jit(solution)/shard_map/ppermute | solution.py:123
  44.6 1.9 %collective-permute-done.8 = f32[19]{0:T(128)S(1)} collective-permute-done((f32[19]{0:T(128)S(1)}, f32[19]{0:T(128)S(1)}, u32[]{:S(2)}, u32[]{:S(2)}) %collective-permute-start.8) | collective-permute-done | bytes 108 | tf_op jit(solution)/shard_map/ppermute | solution.py:123
  46.5 2.0 %collective-permute-start.9 = (f32[19]{0:T(128)S(1)}, f32[19]{0:T(128)S(1)}, u32[]{:S(2)}, u32[]{:S(2)}) collective-permute-start(f32[19]{0:T(128)S(1)} %add.123), channel_id=1, source_target_pairs={{0,1},{1,0},{2,3},{3,2},{4,5},{5,4},{6,7},{7,6},{8,9},{9,8},{10,11... | collective-permute-start | bytes 236 | tf_op jit(solution)/shard_map/ppermute | solution.py:123
  48.6 1.5 %collective-permute-done.9 = f32[19]{0:T(128)S(1)} collective-permute-done((f32[19]{0:T(128)S(1)}, f32[19]{0:T(128)S(1)}, u32[]{:S(2)}, u32[]{:S(2)}) %collective-permute-start.9) | collective-permute-done | bytes 108 | tf_op jit(solution)/shard_map/ppermute | solution.py:123
  50.1 5.7 %collective-permute-start.10 = (f32[19]{0:T(128)S(1)}, f32[19]{0:T(128)S(1)}, u32[]{:S(2)}, u32[]{:S(2)}) collective-permute-start(f32[19]{0:T(128)S(1)} %add.124), channel_id=1, source_target_pairs={{0,2},{1,3},{2,0},{3,1},{4,6},{5,7},{6,4},{7,5},{8,10},{9,11},{10,... | collective-permute-start | bytes 236 | tf_op jit(solution)/shard_map/ppermute | solution.py:123
  55.8 1.5 %collective-permute-done.10 = f32[19]{0:T(128)S(1)} collective-permute-done((f32[19]{0:T(128)S(1)}, f32[19]{0:T(128)S(1)}, u32[]{:S(2)}, u32[]{:S(2)}) %collective-permute-start.10) | collective-permute-done | bytes 108 | tf_op jit(solution)/shard_map/ppermute | solution.py:123
  57.3 2.0 %collective-permute-start.11 = (f32[19]{0:T(128)S(1)}, f32[19]{0:T(128)S(1)}, u32[]{:S(2)}, u32[]{:S(2)}) collective-permute-start(f32[19]{0:T(128)S(1)} %add.125), channel_id=1, source_target_pairs={{0,6},{1,7},{2,4},{3,5},{4,2},{5,3},{6,0},{7,1},{8,14},{9,15},{10,... | collective-permute-start | bytes 236 | tf_op jit(solution)/shard_map/ppermute | solution.py:123
  59.3 3.6 %collective-permute-done.11 = f32[19]{0:T(128)S(1)} collective-permute-done((f32[19]{0:T(128)S(1)}, f32[19]{0:T(128)S(1)}, u32[]{:S(2)}, u32[]{:S(2)}) %collective-permute-start.11) | collective-permute-done | bytes 108 | tf_op jit(solution)/shard_map/ppermute | solution.py:123
  62.9 2.4 %collective-permute-start.12 = (f32[4,4,8,128]{3,2,1,0:T(8,128)S(1)}, f32[4,4,8,128]{3,2,1,0:T(8,128)S(1)}, u32[]{:S(2)}, u32[]{:S(2)}) collective-permute-start(f32[4,4,8,128]{3,2,1,0:T(8,128)S(1)} %select_maximum_fusion), channel_id=1, source_target_pairs={{0,128},{128,0},{1,129},{129,1},{2,130},{130,2},{3,131},{131,3},{4... | collective-permute-start | bytes 196616 | tf_op jit(solution)/shard_map/ppermute | solution.py:241
  65.5 3.3 %collective-permute-done.12 = f32[4,4,8,128]{3,2,1,0:T(8,128)S(1)} collective-permute-done((f32[4,4,8,128]{3,2,1,0:T(8,128)S(1)}, f32[4,4,8,128]{3,2,1,0:T(8,128)S(1)}, u32[]{:S(2)}, u32[]{:S(2)}) %collective-permute-start.12) | collective-permute-done | bytes 65568 | tf_op jit(solution)/shard_map/ppermute | solution.py:241
  69.4 1.0 %copy.115 = f32[28,4,8,128]{3,2,1,0:T(8,128)} copy(f32[28,4,8,128]{3,0,2,1:T(8,128)S(1)} %copy_select_fusion) | data formatting | bytes 917504
  (121 shorter events, 10.7 us)
Async XLA Ops:
  0.6 9.3 %copy-start.1 = (f32[28,4,8,128]{3,2,1,0:T(8,128)S(1)}, f32[28,4,8,128]{3,2,1,0:T(8,128)}, u32[]{:S(2)}) copy-start(f32[28,4,8,128]{3,2,1,0:T(8,128)} %param.26) | copy-start | bytes 1376260
  1.7 0.7 copy-start.4
  1.7 0.7 copy-start.5
  1.7 0.7 copy-start.6
  2.7 5.0 %copy-start.3 = (s32[4,8,128]{2,1,0:T(8,128)S(1)}, s32[4,8,128]{2,1,0:T(8,128)}, u32[]{:S(2)}) copy-start(s32[4,8,128]{2,1,0:T(8,128)} %param.23) | copy-start | bytes 49156
  2.8 7.9 %collective-permute-start = (f32[3,4,8,128]{3,2,1,0:T(8,128)S(1)}, f32[3,4,8,128]{3,2,1,0:T(8,128)S(1)}, u32[]{:S(2)}, u32[]{:S(2)}) collective-permute-start(f32[3,4,8,128]{3,2,1,0:T(8,128)S(1)} %maximum_divide_fusion), channel_id=1, source_target_pairs={{0,128},{1,129},{2,130},{3,131},{4,132},{5,133},{6,134},{7,135},{8... | collective-permute-start | bytes 147464 | tf_op jit(solution)/shard_map/ppermute | solution.py:144
  7.7 0.7 copy-start.7
  8.4 0.7 copy-start.18
  9.1 0.7 copy-start.14
  9.1 0.7 copy-start.15
  9.1 0.7 copy-start.16
  9.9 0.7 copy-start.19
  9.9 1.0 %copy-start = (f32[28,4,8,128]{3,2,1,0:T(8,128)S(1)}, f32[28,4,8,128]{3,2,1,0:T(8,128)}, u32[]{:S(2)}) copy-start(f32[28,4,8,128]{3,2,1,0:T(8,128)} %param.22) | copy-start | bytes 1376260
  11.4 0.7 %copy-start.2 = (f32[19,19,1,1]{0,1,3,2:T(8,128)S(1)}, f32[19,19,1,1]{0,1,3,2:T(8,128)}, u32[]{:S(2)}) copy-start(f32[19,19,1,1]{0,1,3,2:T(8,128)} %constant.133) | copy-start | bytes 4336
  11.5 0.7 copy-start.20
  13.3 0.7 copy-start.8
  13.3 0.7 copy-start.9
  13.3 0.7 copy-start.10
  13.4 0.7 copy-start.11
  14.7 6.4 %collective-permute-start.1 = (f32[56,4,1,128]{3,0,2,1:T(8,128)S(1)}, f32[56,4,1,128]{3,0,2,1:T(8,128)S(1)}, u32[]{:S(2)}, u32[]{:S(2)}) collective-permute-start(f32[56,4,1,128]{3,0,2,1:T(8,128)S(1)} %get-tuple-element.55), channel_id=1, source_target_pairs={{0,8},{8,16},{16,24},{24,32},{32,40},{40,48},{48,56},{56,64},{64,7... | collective-permute-start | bytes 344072 | tf_op jit(solution)/shard_map/ppermute | solution.py:78
  14.8 6.3 %collective-permute-start.2 = (f32[56,4,1,128]{3,0,2,1:T(8,128)S(1)}, f32[56,4,1,128]{3,0,2,1:T(8,128)S(1)}, u32[]{:S(2)}, u32[]{:S(2)}) collective-permute-start(f32[56,4,1,128]{3,0,2,1:T(8,128)S(1)} %get-tuple-element.54), channel_id=1, source_target_pairs={{0,120},{8,0},{16,8},{24,16},{32,24},{40,32},{48,40},{56,48},{64,5... | collective-permute-start | bytes 344072 | tf_op jit(solution)/shard_map/ppermute | solution.py:79
  22.1 3.8 %collective-permute-start.3 = (f32[56,4,8]{0,2,1:T(8,128)S(1)}, f32[56,4,8]{0,2,1:T(8,128)S(1)}, u32[]{:S(2)}, u32[]{:S(2)}) collective-permute-start(f32[56,4,8]{0,2,1:T(8,128)S(1)} %get-tuple-element.38), channel_id=1, source_target_pairs={{0,1},{1,2},{2,3},{3,4},{4,5},{5,6},{6,7},{7,0},{8,9},{9,10},{10,1... | collective-permute-start | bytes 21512 | tf_op jit(solution)/shard_map/ppermute | solution.py:83
  24.1 3.7 %collective-permute-start.4 = (f32[56,4,8]{0,2,1:T(8,128)S(1)}, f32[56,4,8]{0,2,1:T(8,128)S(1)}, u32[]{:S(2)}, u32[]{:S(2)}) collective-permute-start(f32[56,4,8]{0,2,1:T(8,128)S(1)} %get-tuple-element.39), channel_id=1, source_target_pairs={{0,7},{1,0},{2,1},{3,2},{4,3},{5,4},{6,5},{7,6},{8,15},{9,8},{10,9... | collective-permute-start | bytes 21512 | tf_op jit(solution)/shard_map/ppermute | solution.py:84
  30.4 0.7 copy-start.12
  32.2 2.0 %collective-permute-start.5 = (f32[19]{0:T(128)S(1)}, f32[19]{0:T(128)S(1)}, u32[]{:S(2)}, u32[]{:S(2)}) collective-permute-start(f32[19]{0:T(128)S(1)} %broadcast_select_fusion.1), channel_id=1, source_target_pairs={{0,8},{8,0},{16,24},{24,16},{32,40},{40,32},{48,56},{56,48},{64,72... | collective-permute-start | bytes 236 | tf_op jit(solution)/shard_map/ppermute | solution.py:123
  34.2 3.6 %collective-permute-start.6 = (f32[19]{0:T(128)S(1)}, f32[19]{0:T(128)S(1)}, u32[]{:S(2)}, u32[]{:S(2)}) collective-permute-start(f32[19]{0:T(128)S(1)} %add.117), channel_id=1, source_target_pairs={{0,16},{8,24},{16,0},{24,8},{32,48},{40,56},{48,32},{56,40},{64,80... | collective-permute-start | bytes 236 | tf_op jit(solution)/shard_map/ppermute | solution.py:123
  38.1 3.6 %collective-permute-start.7 = (f32[19]{0:T(128)S(1)}, f32[19]{0:T(128)S(1)}, u32[]{:S(2)}, u32[]{:S(2)}) collective-permute-start(f32[19]{0:T(128)S(1)} %add.121), channel_id=1, source_target_pairs={{0,32},{8,40},{16,48},{24,56},{32,0},{40,8},{48,16},{56,24},{64,96... | collective-permute-start | bytes 236 | tf_op jit(solution)/shard_map/ppermute | solution.py:123
  41.8 4.8 %collective-permute-start.8 = (f32[19]{0:T(128)S(1)}, f32[19]{0:T(128)S(1)}, u32[]{:S(2)}, u32[]{:S(2)}) collective-permute-start(f32[19]{0:T(128)S(1)} %add.122), channel_id=1, source_target_pairs={{0,96},{8,104},{16,112},{24,120},{32,64},{40,72},{48,80},{56,88},{... | collective-permute-start | bytes 236 | tf_op jit(solution)/shard_map/ppermute | solution.py:123
  46.5 3.5 %collective-permute-start.9 = (f32[19]{0:T(128)S(1)}, f32[19]{0:T(128)S(1)}, u32[]{:S(2)}, u32[]{:S(2)}) collective-permute-start(f32[19]{0:T(128)S(1)} %add.123), channel_id=1, source_target_pairs={{0,1},{1,0},{2,3},{3,2},{4,5},{5,4},{6,7},{7,6},{8,9},{9,8},{10,11... | collective-permute-start | bytes 236 | tf_op jit(solution)/shard_map/ppermute | solution.py:123
  50.1 7.2 %collective-permute-start.10 = (f32[19]{0:T(128)S(1)}, f32[19]{0:T(128)S(1)}, u32[]{:S(2)}, u32[]{:S(2)}) collective-permute-start(f32[19]{0:T(128)S(1)} %add.124), channel_id=1, source_target_pairs={{0,2},{1,3},{2,0},{3,1},{4,6},{5,7},{6,4},{7,5},{8,10},{9,11},{10,... | collective-permute-start | bytes 236 | tf_op jit(solution)/shard_map/ppermute | solution.py:123
  57.3 5.7 %collective-permute-start.11 = (f32[19]{0:T(128)S(1)}, f32[19]{0:T(128)S(1)}, u32[]{:S(2)}, u32[]{:S(2)}) collective-permute-start(f32[19]{0:T(128)S(1)} %add.125), channel_id=1, source_target_pairs={{0,6},{1,7},{2,4},{3,5},{4,2},{5,3},{6,0},{7,1},{8,14},{9,15},{10,... | collective-permute-start | bytes 236 | tf_op jit(solution)/shard_map/ppermute | solution.py:123
  62.9 5.9 %collective-permute-start.12 = (f32[4,4,8,128]{3,2,1,0:T(8,128)S(1)}, f32[4,4,8,128]{3,2,1,0:T(8,128)S(1)}, u32[]{:S(2)}, u32[]{:S(2)}) collective-permute-start(f32[4,4,8,128]{3,2,1,0:T(8,128)S(1)} %select_maximum_fusion), channel_id=1, source_target_pairs={{0,128},{128,0},{1,129},{129,1},{2,130},{130,2},{3,131},{131,3},{4... | collective-permute-start | bytes 196616 | tf_op jit(solution)/shard_map/ppermute | solution.py:241
  (2 other events, 1.3 us)

commit v11 on v5

--- a/solution.py
+++ b/solution.py
@@ -232,20 +232,28 @@
         )
         return values
 
-    partial_rates = butterfly_sum(local_rates, (("gy", 4), ("gz", 1)), [flow_adjoint, species_adjoint])
+    partial_rates = butterfly_sum(local_rates, (("gy", 4),), [flow_adjoint, species_adjoint])
     plane = populations.shape[1:]
     rate_plane = jnp.zeros(plane, jnp.float32).at[0, 0, : partial_rates.shape[0]].set(partial_rates)
     payload = jnp.concatenate([later["species_motion_grad"], rate_plane[None]])
     other = lax.ppermute(payload, "sec", [(0, 1), (1, 0)])
-    rate_grad = partial_rates + other[3, 0, 0, : partial_rates.shape[0]]
-
-    motion_grad = jnp.where(fluid, later["motion_grad"] + other[:3], 0.0)
-    along = vx * motion_grad[0][None] + vy * motion_grad[1][None] + vz * motion_grad[2][None]
-    extra = (along - jnp.sum(motion * motion_grad, 0)[None]) / density[None]
-    flow_grad = jnp.where(
-        fluid, later["flow_base"] + extra, reverse_pairs(back_flow, opposite)
-    )
-    grad_rows = jnp.where(is_flow, jnp.concatenate([flow_grad, filler]), later["species_grad"])
+    partial_rates = partial_rates + other[3, 0, 0, : partial_rates.shape[0]]
+
+    def flow_gradient(values):
+        values, received = lax.optimization_barrier((values, other[:3]))
+        motion_grad = jnp.where(fluid, later["motion_grad"] + received, 0.0)
+        along = vx * motion_grad[0][None] + vy * motion_grad[1][None] + vz * motion_grad[2][None]
+        extra = (along - jnp.sum(motion * motion_grad, 0)[None]) / density[None]
+        flow_grad = jnp.where(
+            fluid, later["flow_base"] + extra, reverse_pairs(back_flow, opposite)
+        )
+        later["grad_rows"] = jnp.where(
+            is_flow, jnp.concatenate([flow_grad, filler]), later["species_grad"]
+        )
+        return values
+
+    rate_grad = butterfly_sum(partial_rates, (("gz", 1),), [flow_gradient])
+    grad_rows = later["grad_rows"]
     return (moved, grad_rows, rate_grad)
 
 

time: 69.4 us -> 67.7 us (0.976)
  waiting for transfers between devices: 20.6 us -> 19 us
    ppermute x7, waiting for transfers between devices: 12.2 us -> 10.5 us  [butterfly_sum(): values = values + lax.ppermute(values, axis, list(enumerate(targets)))]
  transfers between devices with their start and end apart: 13 -> 13, of which waited for: 10 -> 10; matrix products, arithmetic and copies ran while one was open for 7% -> 10% of each run, Pallas kernels for 0% -> 0%
where the time goes in v11:
time: 67.7 us; the launch traced here: 67.5 us
  starting transfers between devices  29 us (43%)
  waiting for transfers between devices  19 us (28%)
  local copies, waits for them, and re-layouts  9.48 us (14%)
  other arithmetic  6.36 us (9%)
  matrix products  2.34 us (3%)
  between operations  1.29 us (2%)
    ppermute x7, starting transfers between devices, butterfly_sum(): values = values + lax.ppermute(values, axis, list(enumerate(targets)))  15.1 us
    ppermute x7, waiting for transfers between devices, butterfly_sum(): values = values + lax.ppermute(values, axis, list(enumerate(targets)))  10.5 us
    unnamed x58, local copies, waits for them, and re-layouts  6.49 us
    ppermute x1, starting transfers between devices, per_device(): sent_motion = lax.ppermute(own_motion, 'sec', [(0, 1)])  4.93 us
    ppermute x1, starting transfers between devices, shift_rows(): high = lax.ppermute(field[:, :, :1, :], 'gy', ring('gy', -1))  3.84 us
    ppermute x1, starting transfers between devices, per_device(): other = lax.ppermute(payload, 'sec', [(0, 1), (1, 0)])  2.97 us
    ppermute x1, waiting for transfers between devices, per_device(): other = lax.ppermute(payload, 'sec', [(0, 1), (1, 0)])  2.74 us
    ppermute x1, waiting for transfers between devices, shift_rows(): low = lax.ppermute(field[:, :, size_y - 1:, :], 'gy', ring('gy', 1))  2.36 us
  transfers between devices with their start and end apart: 13, of which 10 were waited for; matrix products, arithmetic and copies ran while one was open for 10% of the time, Pallas kernels for 0%

profile of v11, /device:TPU:32, one launch (start us, length us, event | category | flops | bytes accessed | tf_op | source)
XLA Modules:
  0.0 67.5 jit_solution(14354088304482080132)
XLA Ops:
  0.7 1.3 %copy.83 = f32[28,4,8,128]{3,0,2,1:T(8,128)S(1)} copy(f32[28,4,8,128]{3,2,1,0:T(8,128)} %param.22) | data formatting | bytes 917504 | tf_op args[0]
  2.4 4.9 %collective-permute-start = (f32[3,4,8,128]{3,2,1,0:T(8,128)S(1)}, f32[3,4,8,128]{3,2,1,0:T(8,128)S(1)}, u32[]{:S(2)}, u32[]{:S(2)}) collective-permute-start(f32[3,4,8,128]{3,2,1,0:T(8,128)S(1)} %maximum_divide_fusion), channel_id=1, source_target_pairs={{0,128},{1,129},{2,130},{3,131},{4,132},{5,133},{6,134},{7,135},{8... | collective-permute-start | bytes 147464 | tf_op jit(solution)/shard_map/ppermute | solution.py:144
  7.4 0.7 copy-done.3
  10.1 0.7 copy-done.2
  10.7 0.7 %fusion.18 = f32[19,4,8,128]{3,0,2,1:T(8,128)S(1)} fusion(f32[19,19,1,1]{0,1,3,2:T(8,128)S(1)} %copy-done.2, f32[28,4,8,128]{3,0,2,1:T(8,128)S(1)} %copy.83, f32[4,8,128]{2,1,0:T(8,128)S(1)} %broadcast_multiply_fusion.4, f32[4,8,128]{2,1,0:T(8,128)S(1)} %get-tuple-element.116, f32[4,8,128]{2,1,0:T(8,128)S(1)} %get-tuple-element.117, ...), kind=kOutput, calls=%fused_computation.49 | convolution fusion | flops 18833408 | bytes 800768 | tf_op jit(solution)/shard_map/ji,jxyz->ixyz/dot_general | solution.py:167
  11.5 0.6 fusion.1
  12.9 3.8 %collective-permute-start.2 = (f32[56,4,1,128]{3,0,2,1:T(8,128)S(1)}, f32[56,4,1,128]{3,0,2,1:T(8,128)S(1)}, u32[]{:S(2)}, u32[]{:S(2)}) collective-permute-start(f32[56,4,1,128]{3,0,2,1:T(8,128)S(1)} %get-tuple-element.57), channel_id=1, source_target_pairs={{0,120},{8,0},{16,8},{24,16},{32,24},{40,32},{48,40},{56,48},{64,5... | collective-permute-start | bytes 344072 | tf_op jit(solution)/shard_map/ppermute | solution.py:79
  16.8 2.4 %collective-permute-done.1 = f32[56,4,1,128]{3,0,2,1:T(8,128)S(1)} collective-permute-done((f32[56,4,1,128]{3,0,2,1:T(8,128)S(1)}, f32[56,4,1,128]{3,0,2,1:T(8,128)S(1)}, u32[]{:S(2)}, u32[]{:S(2)}) %collective-permute-start.1) | collective-permute-done | bytes 114720 | tf_op jit(solution)/shard_map/ppermute | solution.py:78
  19.5 0.8 %slice_reduce_fusion.2 = (f32[56,4,8]{0,2,1:T(8,128)S(1)}, f32[56,4,8]{0,2,1:T(8,128)S(1)}, f32[56,4,8,1]{3,0,2,1:T(8,128)S(1)}, f32[56,4,8,1]{3,0,2,1:T(8,128)S(1)}) fusion(f32[56,4,8,128]{3,0,2,1:T(8,128)S(1)} %fusion.3), kind=kLoop, calls=%fused_computation.162 | loop fusion | bytes 43008 | tf_op jit(solution)/shard_map/slice | solution.py:83
  20.3 2.0 %collective-permute-start.3 = (f32[56,4,8]{0,2,1:T(8,128)S(1)}, f32[56,4,8]{0,2,1:T(8,128)S(1)}, u32[]{:S(2)}, u32[]{:S(2)}) collective-permute-start(f32[56,4,8]{0,2,1:T(8,128)S(1)} %get-tuple-element.38), channel_id=1, source_target_pairs={{0,1},{1,2},{2,3},{3,4},{4,5},{5,6},{6,7},{7,0},{8,9},{9,10},{10,1... | collective-permute-start | bytes 21512 | tf_op jit(solution)/shard_map/ppermute | solution.py:83
  22.7 1.4 %collective-permute-done.3 = f32[56,4,8]{0,2,1:T(8,128)S(1)} collective-permute-done((f32[56,4,8]{0,2,1:T(8,128)S(1)}, f32[56,4,8]{0,2,1:T(8,128)S(1)}, u32[]{:S(2)}, u32[]{:S(2)}) %collective-permute-start.3) | collective-permute-done | bytes 7200 | tf_op jit(solution)/shard_map/ppermute | solution.py:83
  24.1 1.9 %collective-permute-done.4 = f32[56,4,8]{0,2,1:T(8,128)S(1)} collective-permute-done((f32[56,4,8]{0,2,1:T(8,128)S(1)}, f32[56,4,8]{0,2,1:T(8,128)S(1)}, u32[]{:S(2)}, u32[]{:S(2)}) %collective-permute-start.4) | collective-permute-done | bytes 7200 | tf_op jit(solution)/shard_map/ppermute | solution.py:84
  26.0 1.2 %fusion.4 = f32[56,4,8,128]{3,0,2,1:T(8,128)S(1)} fusion(f32[56,4,8,127]{3,0,2,1:T(8,128)S(1)} %get-tuple-element.88, f32[56,4,8,1]{3,0,2,1:T(8,128)S(1)} %get-tuple-element.86, f32[56,4,8,128]{3,0,2,1:T(8,128)S(1)} %fusion.3, f32[56,4,8,1]{3,0,2,1:T(8,128)S(1)} %get-tuple-element.85, f32[56,4,8,127]{3,0,2,1:T(8,128)S(1)} %get-tuple-element.87, ...), kind=kLoop, calls=%fused_computation.15 | loop fusion | flops 1376256 | bytes 3684720 | tf_op jit(solution)/shard_map/jit(_where)/select_n | solution.py:88
  28.6 0.6 copy-done.12
  29.2 0.8 %fusion.71 = (f32[28,4,8,128]{3,0,2,1:T(8,128)S(1)}, f32[28]{0:T(128)S(1)}, f32[28,4,8,128]{3,0,2,1:T(8,128)S(1)}) fusion(f32[56,4,8,128]{3,0,2,1:T(8,128)S(1)} %maximum_select_fusion.2, f32[28,4,8,128]{3,2,1,0:T(8,128)S(1)} %bitcast.96, f32[28,4,8,128]{3,2,1,0:T(8,128)S(1)} %copy-done, pred[4,8,128]{2,1,0:T(8,128)(4,1)S(1)} %broadcast_compare_fusion, ...), kind=kLoop, calls=%fused_computation.164 | loop fusion | flops 688100 | bytes 2756749 | tf_op jit(solution)/shard_map/slice | solution.py:181
  30.8 1.0 %copy.111 = f32[28,4,8,128]{3,2,1,0:T(8,128)} copy(f32[28,4,8,128]{3,0,2,1:T(8,128)S(1)} %get-tuple-element.80) | data formatting | bytes 917504
  32.4 0.8 %collective-permute-start.6 = (f32[19]{0:T(128)S(1)}, f32[19]{0:T(128)S(1)}, u32[]{:S(2)}, u32[]{:S(2)}) collective-permute-start(f32[19]{0:T(128)S(1)} %add.117), channel_id=1, source_target_pairs={{0,16},{8,24},{16,0},{24,8},{32,48},{40,56},{48,32},{56,40},{64,80... | collective-permute-start | bytes 236 | tf_op jit(solution)/shard_map/ppermute | solution.py:123
  33.1 0.6 add_multiply_fusion
  34.3 1.6 %collective-permute-done.6 = f32[19]{0:T(128)S(1)} collective-permute-done((f32[19]{0:T(128)S(1)}, f32[19]{0:T(128)S(1)}, u32[]{:S(2)}, u32[]{:S(2)}) %collective-permute-start.6) | collective-permute-done | bytes 108 | tf_op jit(solution)/shard_map/ppermute | solution.py:123
  36.3 1.6 %collective-permute-start.7 = (f32[19]{0:T(128)S(1)}, f32[19]{0:T(128)S(1)}, u32[]{:S(2)}, u32[]{:S(2)}) collective-permute-start(f32[19]{0:T(128)S(1)} %add.121), channel_id=1, source_target_pairs={{0,32},{8,40},{16,48},{24,56},{32,0},{40,8},{48,16},{56,24},{64,96... | collective-permute-start | bytes 236 | tf_op jit(solution)/shard_map/ppermute | solution.py:123
  37.9 2.0 %collective-permute-done.7 = f32[19]{0:T(128)S(1)} collective-permute-done((f32[19]{0:T(128)S(1)}, f32[19]{0:T(128)S(1)}, u32[]{:S(2)}, u32[]{:S(2)}) %collective-permute-start.7) | collective-permute-done | bytes 108 | tf_op jit(solution)/shard_map/ppermute | solution.py:123
  39.9 2.9 %collective-permute-start.8 = (f32[19]{0:T(128)S(1)}, f32[19]{0:T(128)S(1)}, u32[]{:S(2)}, u32[]{:S(2)}) collective-permute-start(f32[19]{0:T(128)S(1)} %add.122), channel_id=1, source_target_pairs={{0,96},{8,104},{16,112},{24,120},{32,64},{40,72},{48,80},{56,88},{... | collective-permute-start | bytes 236 | tf_op jit(solution)/shard_map/ppermute | solution.py:123
  42.8 1.9 %collective-permute-done.8 = f32[19]{0:T(128)S(1)} collective-permute-done((f32[19]{0:T(128)S(1)}, f32[19]{0:T(128)S(1)}, u32[]{:S(2)}, u32[]{:S(2)}) %collective-permute-start.8) | collective-permute-done | bytes 108 | tf_op jit(solution)/shard_map/ppermute | solution.py:123
  44.7 3.0 %collective-permute-start.9 = (f32[4,4,8,128]{3,2,1,0:T(8,128)S(1)}, f32[4,4,8,128]{3,2,1,0:T(8,128)S(1)}, u32[]{:S(2)}, u32[]{:S(2)}) collective-permute-start(f32[4,4,8,128]{3,2,1,0:T(8,128)S(1)} %select_maximum_fusion), channel_id=1, source_target_pairs={{0,128},{128,0},{1,129},{129,1},{2,130},{130,2},{3,131},{131,3},{4... | collective-permute-start | bytes 196616 | tf_op jit(solution)/shard_map/ppermute | solution.py:239
  47.8 2.7 %collective-permute-done.9 = f32[4,4,8,128]{3,2,1,0:T(8,128)S(1)} collective-permute-done((f32[4,4,8,128]{3,2,1,0:T(8,128)S(1)}, f32[4,4,8,128]{3,2,1,0:T(8,128)S(1)}, u32[]{:S(2)}, u32[]{:S(2)}) %collective-permute-start.9) | collective-permute-done | bytes 65568 | tf_op jit(solution)/shard_map/ppermute | solution.py:239
  50.5 2.0 %collective-permute-start.10 = (f32[19]{0:T(128)S(1)}, f32[19]{0:T(128)S(1)}, u32[]{:S(2)}, u32[]{:S(2)}) collective-permute-start(f32[19]{0:T(128)S(1)} %fusion.57), channel_id=1, source_target_pairs={{0,1},{1,0},{2,3},{3,2},{4,5},{5,4},{6,7},{7,6},{8,9},{9,8},{10,11... | collective-permute-start | bytes 236 | tf_op jit(solution)/shard_map/ppermute | solution.py:123
  52.6 1.5 %collective-permute-done.10 = f32[19]{0:T(128)S(1)} collective-permute-done((f32[19]{0:T(128)S(1)}, f32[19]{0:T(128)S(1)}, u32[]{:S(2)}, u32[]{:S(2)}) %collective-permute-start.10) | collective-permute-done | bytes 108 | tf_op jit(solution)/shard_map/ppermute | solution.py:123
  54.1 5.7 %collective-permute-start.11 = (f32[19]{0:T(128)S(1)}, f32[19]{0:T(128)S(1)}, u32[]{:S(2)}, u32[]{:S(2)}) collective-permute-start(f32[19]{0:T(128)S(1)} %add.125), channel_id=1, source_target_pairs={{0,2},{1,3},{2,0},{3,1},{4,6},{5,7},{6,4},{7,5},{8,10},{9,11},{10,... | collective-permute-start | bytes 236 | tf_op jit(solution)/shard_map/ppermute | solution.py:123
  60.3 0.9 %collective-permute-done.11 = f32[19]{0:T(128)S(1)} collective-permute-done((f32[19]{0:T(128)S(1)}, f32[19]{0:T(128)S(1)}, u32[]{:S(2)}, u32[]{:S(2)}) %collective-permute-start.11) | collective-permute-done | bytes 108 | tf_op jit(solution)/shard_map/ppermute | solution.py:123
  61.3 2.0 %collective-permute-start.12 = (f32[19]{0:T(128)S(1)}, f32[19]{0:T(128)S(1)}, u32[]{:S(2)}, u32[]{:S(2)}) collective-permute-start(f32[19]{0:T(128)S(1)} %add.132), channel_id=1, source_target_pairs={{0,6},{1,7},{2,4},{3,5},{4,2},{5,3},{6,0},{7,1},{8,14},{9,15},{10,... | collective-permute-start | bytes 236 | tf_op jit(solution)/shard_map/ppermute | solution.py:123
  63.3 1.0 %copy.112 = f32[28,4,8,128]{3,2,1,0:T(8,128)} copy(f32[28,4,8,128]{3,0,2,1:T(8,128)S(1)} %copy_select_fusion) | data formatting | bytes 917504
  64.3 2.6 %collective-permute-done.12 = f32[19]{0:T(128)S(1)} collective-permute-done((f32[19]{0:T(128)S(1)}, f32[19]{0:T(128)S(1)}, u32[]{:S(2)}, u32[]{:S(2)}) %collective-permute-start.12) | collective-permute-done | bytes 108 | tf_op jit(solution)/shard_map/ppermute | solution.py:123
  (120 shorter events, 8.6 us)
Async XLA Ops:
  0.6 1.3 %copy-start.4 = (f32[19]{0:T(128)S(1)}, f32[19]{0:T(128)}, u32[]{:S(2)}) copy-start(f32[19]{0:T(128)} %constant.126) | copy-start | bytes 232
  0.6 1.3 %copy-start.5 = (f32[19]{0:T(128)S(1)}, f32[19]{0:T(128)}, u32[]{:S(2)}) copy-start(f32[19]{0:T(128)} %constant.127) | copy-start | bytes 232
  0.7 1.3 %copy-start.6 = (f32[19]{0:T(128)S(1)}, f32[19]{0:T(128)}, u32[]{:S(2)}) copy-start(f32[19]{0:T(128)} %constant.128) | copy-start | bytes 232
  2.0 5.3 %copy-start = (f32[28,4,8,128]{3,2,1,0:T(8,128)S(1)}, f32[28,4,8,128]{3,2,1,0:T(8,128)}, u32[]{:S(2)}) copy-start(f32[28,4,8,128]{3,2,1,0:T(8,128)} %param.22) | copy-start | bytes 1376260
  2.4 7.6 %collective-permute-start = (f32[3,4,8,128]{3,2,1,0:T(8,128)S(1)}, f32[3,4,8,128]{3,2,1,0:T(8,128)S(1)}, u32[]{:S(2)}, u32[]{:S(2)}) collective-permute-start(f32[3,4,8,128]{3,2,1,0:T(8,128)S(1)} %maximum_divide_fusion), channel_id=1, source_target_pairs={{0,128},{1,129},{2,130},{3,131},{4,132},{5,133},{6,134},{7,135},{8... | collective-permute-start | bytes 147464 | tf_op jit(solution)/shard_map/ppermute | solution.py:144
  7.3 0.7 %copy-start.3 = (s32[4,8,128]{2,1,0:T(8,128)S(1)}, s32[4,8,128]{2,1,0:T(8,128)}, u32[]{:S(2)}) copy-start(s32[4,8,128]{2,1,0:T(8,128)} %param.23) | copy-start | bytes 49156
  8.1 0.7 copy-start.17
  8.1 0.7 copy-start.18
  8.1 0.7 %copy-start.13 = (f32[28,1,1,1]{0,3,2,1:T(1,128)S(1)}, f32[28,1,1,1]{0,3,2,1:T(1,128)}, u32[]{:S(2)}) copy-start(f32[28,1,1,1]{0,3,2,1:T(1,128)} %constant.104.clone) | copy-start | bytes 340
  8.1 0.7 %copy-start.14 = (f32[28,1,1,1]{0,3,2,1:T(1,128)S(1)}, f32[28,1,1,1]{0,3,2,1:T(1,128)}, u32[]{:S(2)}) copy-start(f32[28,1,1,1]{0,3,2,1:T(1,128)} %constant.105.clone) | copy-start | bytes 340
  8.1 0.7 %copy-start.15 = (f32[28,1,1,1]{0,3,2,1:T(1,128)S(1)}, f32[28,1,1,1]{0,3,2,1:T(1,128)}, u32[]{:S(2)}) copy-start(f32[28,1,1,1]{0,3,2,1:T(1,128)} %constant.108.clone) | copy-start | bytes 340
  8.2 0.7 %copy-start.16 = (f32[28,1,1,1]{0,3,2,1:T(1,128)S(1)}, f32[28,1,1,1]{0,3,2,1:T(1,128)}, u32[]{:S(2)}) copy-start(f32[28,1,1,1]{0,3,2,1:T(1,128)} %constant.109.clone) | copy-start | bytes 340
  8.2 0.9 %copy-start.19 = (f32[15]{0:T(128)S(1)}, f32[15]{0:T(128)}, u32[]{:S(2)}) copy-start(f32[15]{0:T(128)} %param.24) | copy-start | bytes 184
  8.2 1.0 %copy-start.1 = (f32[28,4,8,128]{3,2,1,0:T(8,128)S(1)}, f32[28,4,8,128]{3,2,1,0:T(8,128)}, u32[]{:S(2)}) copy-start(f32[28,4,8,128]{3,2,1,0:T(8,128)} %param.26) | copy-start | bytes 1376260
  10.0 0.7 %copy-start.2 = (f32[19,19,1,1]{0,1,3,2:T(8,128)S(1)}, f32[19,19,1,1]{0,1,3,2:T(8,128)}, u32[]{:S(2)}) copy-start(f32[19,19,1,1]{0,1,3,2:T(8,128)} %constant.133) | copy-start | bytes 4336
  10.1 0.7 %copy-start.20 = (f32[19]{0:T(128)S(1)}, f32[19]{0:T(128)}, u32[]{:S(2)}) copy-start(f32[19]{0:T(128)} %constant.125) | copy-start | bytes 232
  11.4 0.7 copy-start.8
  11.5 0.7 copy-start.9
  11.5 0.7 copy-start.10
  11.5 0.7 copy-start.11
  12.8 6.4 %collective-permute-start.1 = (f32[56,4,1,128]{3,0,2,1:T(8,128)S(1)}, f32[56,4,1,128]{3,0,2,1:T(8,128)S(1)}, u32[]{:S(2)}, u32[]{:S(2)}) collective-permute-start(f32[56,4,1,128]{3,0,2,1:T(8,128)S(1)} %get-tuple-element.58), channel_id=1, source_target_pairs={{0,8},{8,16},{16,24},{24,32},{32,40},{40,48},{48,56},{56,64},{64,7... | collective-permute-start | bytes 344072 | tf_op jit(solution)/shard_map/ppermute | solution.py:78
  12.9 6.3 %collective-permute-start.2 = (f32[56,4,1,128]{3,0,2,1:T(8,128)S(1)}, f32[56,4,1,128]{3,0,2,1:T(8,128)S(1)}, u32[]{:S(2)}, u32[]{:S(2)}) collective-permute-start(f32[56,4,1,128]{3,0,2,1:T(8,128)S(1)} %get-tuple-element.57), channel_id=1, source_target_pairs={{0,120},{8,0},{16,8},{24,16},{32,24},{40,32},{48,40},{56,48},{64,5... | collective-permute-start | bytes 344072 | tf_op jit(solution)/shard_map/ppermute | solution.py:79
  20.3 3.8 %collective-permute-start.3 = (f32[56,4,8]{0,2,1:T(8,128)S(1)}, f32[56,4,8]{0,2,1:T(8,128)S(1)}, u32[]{:S(2)}, u32[]{:S(2)}) collective-permute-start(f32[56,4,8]{0,2,1:T(8,128)S(1)} %get-tuple-element.38), channel_id=1, source_target_pairs={{0,1},{1,2},{2,3},{3,4},{4,5},{5,6},{6,7},{7,0},{8,9},{9,10},{10,1... | collective-permute-start | bytes 21512 | tf_op jit(solution)/shard_map/ppermute | solution.py:83
  22.3 3.7 %collective-permute-start.4 = (f32[56,4,8]{0,2,1:T(8,128)S(1)}, f32[56,4,8]{0,2,1:T(8,128)S(1)}, u32[]{:S(2)}, u32[]{:S(2)}) collective-permute-start(f32[56,4,8]{0,2,1:T(8,128)S(1)} %get-tuple-element.39), channel_id=1, source_target_pairs={{0,7},{1,0},{2,1},{3,2},{4,3},{5,4},{6,5},{7,6},{8,15},{9,8},{10,9... | collective-permute-start | bytes 21512 | tf_op jit(solution)/shard_map/ppermute | solution.py:84
  30.3 2.0 %collective-permute-start.5 = (f32[19]{0:T(128)S(1)}, f32[19]{0:T(128)S(1)}, u32[]{:S(2)}, u32[]{:S(2)}) collective-permute-start(f32[19]{0:T(128)S(1)} %broadcast_select_fusion.1), channel_id=1, source_target_pairs={{0,8},{8,0},{16,24},{24,16},{32,40},{40,32},{48,56},{56,48},{64,72... | collective-permute-start | bytes 236 | tf_op jit(solution)/shard_map/ppermute | solution.py:123
  32.4 3.6 %collective-permute-start.6 = (f32[19]{0:T(128)S(1)}, f32[19]{0:T(128)S(1)}, u32[]{:S(2)}, u32[]{:S(2)}) collective-permute-start(f32[19]{0:T(128)S(1)} %add.117), channel_id=1, source_target_pairs={{0,16},{8,24},{16,0},{24,8},{32,48},{40,56},{48,32},{56,40},{64,80... | collective-permute-start | bytes 236 | tf_op jit(solution)/shard_map/ppermute | solution.py:123
  36.3 3.6 %collective-permute-start.7 = (f32[19]{0:T(128)S(1)}, f32[19]{0:T(128)S(1)}, u32[]{:S(2)}, u32[]{:S(2)}) collective-permute-start(f32[19]{0:T(128)S(1)} %add.121), channel_id=1, source_target_pairs={{0,32},{8,40},{16,48},{24,56},{32,0},{40,8},{48,16},{56,24},{64,96... | collective-permute-start | bytes 236 | tf_op jit(solution)/shard_map/ppermute | solution.py:123
  39.9 4.8 %collective-permute-start.8 = (f32[19]{0:T(128)S(1)}, f32[19]{0:T(128)S(1)}, u32[]{:S(2)}, u32[]{:S(2)}) collective-permute-start(f32[19]{0:T(128)S(1)} %add.122), channel_id=1, source_target_pairs={{0,96},{8,104},{16,112},{24,120},{32,64},{40,72},{48,80},{56,88},{... | collective-permute-start | bytes 236 | tf_op jit(solution)/shard_map/ppermute | solution.py:123
  44.7 5.9 %collective-permute-start.9 = (f32[4,4,8,128]{3,2,1,0:T(8,128)S(1)}, f32[4,4,8,128]{3,2,1,0:T(8,128)S(1)}, u32[]{:S(2)}, u32[]{:S(2)}) collective-permute-start(f32[4,4,8,128]{3,2,1,0:T(8,128)S(1)} %select_maximum_fusion), channel_id=1, source_target_pairs={{0,128},{128,0},{1,129},{129,1},{2,130},{130,2},{3,131},{131,3},{4... | collective-permute-start | bytes 196616 | tf_op jit(solution)/shard_map/ppermute | solution.py:239
  50.5 3.5 %collective-permute-start.10 = (f32[19]{0:T(128)S(1)}, f32[19]{0:T(128)S(1)}, u32[]{:S(2)}, u32[]{:S(2)}) collective-permute-start(f32[19]{0:T(128)S(1)} %fusion.57), channel_id=1, source_target_pairs={{0,1},{1,0},{2,3},{3,2},{4,5},{5,4},{6,7},{7,6},{8,9},{9,8},{10,11... | collective-permute-start | bytes 236 | tf_op jit(solution)/shard_map/ppermute | solution.py:123
  54.1 7.2 %collective-permute-start.11 = (f32[19]{0:T(128)S(1)}, f32[19]{0:T(128)S(1)}, u32[]{:S(2)}, u32[]{:S(2)}) collective-permute-start(f32[19]{0:T(128)S(1)} %add.125), channel_id=1, source_target_pairs={{0,2},{1,3},{2,0},{3,1},{4,6},{5,7},{6,4},{7,5},{8,10},{9,11},{10,... | collective-permute-start | bytes 236 | tf_op jit(solution)/shard_map/ppermute | solution.py:123
  61.3 5.7 %collective-permute-start.12 = (f32[19]{0:T(128)S(1)}, f32[19]{0:T(128)S(1)}, u32[]{:S(2)}, u32[]{:S(2)}) collective-permute-start(f32[19]{0:T(128)S(1)} %add.132), channel_id=1, source_target_pairs={{0,6},{1,7},{2,4},{3,5},{4,2},{5,3},{6,0},{7,1},{8,14},{9,15},{10,... | collective-permute-start | bytes 236 | tf_op jit(solution)/shard_map/ppermute | solution.py:123
  (2 other events, 1.3 us)

commit v12 on v11

--- a/solution.py
+++ b/solution.py
@@ -165,6 +165,7 @@
     poly = w * (1.0 + 3.0 * projected + 4.5 * projected * projected - 1.5 * squared[None])
     equilibrium = density[None] * poly
     moments = jnp.einsum("ji,jxyz->ixyz", q_table, flow - equilibrium, precision=highest)
+    fluid_moments = jnp.where(fluid, moments, 0.0)
     flow_relaxed = flow - jnp.einsum("ij,jxyz->ixyz", q_table, relax * moments, precision=highest)
     flow_post = jnp.where(fluid, flow_relaxed, reverse_pairs(flow, opposite))
     filler = jnp.zeros((rows - 19,) + populations.shape[1:], jnp.float32)
@@ -186,10 +187,8 @@
     species_rate_grad = -jnp.sum(
         jnp.where(fluid[None], back_species * species_gap, 0.0), axis=(1, 2, 3, 4)
     )
-    back_moments = jnp.einsum("ji,jxyz->ixyz", q_table, back_flow, precision=highest)
-    flow_rate_grad = -jnp.sum(
-        jnp.where(fluid, back_moments * moments, 0.0)[4:], axis=(1, 2, 3)
-    )
+    pairs = jnp.einsum("ixyz,kxyz->ik", back_flow, fluid_moments, precision=highest)
+    flow_rate_grad = -jnp.sum(q_table * pairs, axis=0)[4:]
     local_rates = jnp.where(
         is_flow,
         jnp.concatenate([flow_rate_grad, jnp.zeros((groups,), jnp.float32)]),
@@ -199,9 +198,8 @@
     later = {}
 
     def flow_adjoint(values):
-        values, (back_flow_, back_moments_) = lax.optimization_barrier(
-            (values, (back_flow, back_moments))
-        )
+        values, back_flow_ = lax.optimization_barrier((values, back_flow))
+        back_moments_ = jnp.einsum("ji,jxyz->ixyz", q_table, back_flow_, precision=highest)
         through_eq = jnp.einsum("ij,jxyz->ixyz", q_table, relax * back_moments_, precision=highest)
         density_grad = jnp.sum(through_eq * poly, 0)
         hw = through_eq * w

time: 67.7 us -> 68.3 us (level)
    unnamed x58 -> x60, local copies, waits for them, and re-layouts: 6.49 us -> 6.91 us
where the time goes in v12:
time: 68.3 us; the launch traced here: 67.9 us
  starting transfers between devices  29.1 us (43%)
  waiting for transfers between devices  18.5 us (27%)
  local copies, waits for them, and re-layouts  9.9 us (14%)
  other arithmetic  6.21 us (9%)
  matrix products  3.02 us (4%)
  between operations  1.29 us (2%)
    ppermute x7, starting transfers between devices, butterfly_sum(): values = values + lax.ppermute(values, axis, list(enumerate(targets)))  15.1 us
    ppermute x7, waiting for transfers between devices, butterfly_sum(): values = values + lax.ppermute(values, axis, list(enumerate(targets)))  10.1 us
    unnamed x60, local copies, waits for them, and re-layouts  6.91 us
    ppermute x1, starting transfers between devices, per_device(): sent_motion = lax.ppermute(own_motion, 'sec', [(0, 1)])  4.93 us
    ppermute x1, starting transfers between devices, shift_rows(): high = lax.ppermute(field[:, :, :1, :], 'gy', ring('gy', -1))  3.84 us
    ppermute x1, starting transfers between devices, per_device(): other = lax.ppermute(payload, 'sec', [(0, 1), (1, 0)])  2.99 us
    ppermute x1, waiting for transfers between devices, per_device(): other = lax.ppermute(payload, 'sec', [(0, 1), (1, 0)])  2.71 us
    ppermute x1, waiting for transfers between devices, shift_rows(): low = lax.ppermute(field[:, :, size_y - 1:, :], 'gy', ring('gy', 1))  2.36 us
  transfers between devices with their start and end apart: 13, of which 10 were waited for; matrix products, arithmetic and copies ran while one was open for 10% of the time, Pallas kernels for 0%

profile of v12, /device:TPU:32, one launch (start us, length us, event | category | flops | bytes accessed | tf_op | source)
XLA Modules:
  0.0 67.9 jit_solution(15529174110433614346)
XLA Ops:
  0.7 1.3 %copy.85 = f32[28,4,8,128]{3,0,2,1:T(8,128)S(1)} copy(f32[28,4,8,128]{3,2,1,0:T(8,128)} %param.22) | data formatting | bytes 917504 | tf_op args[0]
  2.4 4.9 %collective-permute-start = (f32[3,4,8,128]{3,2,1,0:T(8,128)S(1)}, f32[3,4,8,128]{3,2,1,0:T(8,128)S(1)}, u32[]{:S(2)}, u32[]{:S(2)}) collective-permute-start(f32[3,4,8,128]{3,2,1,0:T(8,128)S(1)} %maximum_divide_fusion), channel_id=1, source_target_pairs={{0,128},{1,129},{2,130},{3,131},{4,132},{5,133},{6,134},{7,135},{8... | collective-permute-start | bytes 147464 | tf_op jit(solution)/shard_map/ppermute | solution.py:144
  7.4 0.7 copy-done.3
  10.1 0.7 copy-done.2
  10.7 0.8 %fusion.22 = f32[4,8,128,19]{2,3,1,0:T(8,128)S(1)} fusion(f32[19,19,1,1]{0,1,3,2:T(8,128)S(1)} %copy-done.2, f32[28,4,8,128]{3,0,2,1:T(8,128)S(1)} %copy.85, f32[4,8,128]{2,1,0:T(8,128)S(1)} %broadcast_multiply_fusion.4, f32[4,8,128]{2,1,0:T(8,128)S(1)} %get-tuple-element.114, f32[4,8,128]{2,1,0:T(8,128)S(1)} %get-tuple-element.115, ...), kind=kOutput, calls=%fused_computation.55 | convolution fusion | flops 18833408 | bytes 800768 | tf_op jit(solution)/shard_map/ji,jxyz->ixyz/dot_general | solution.py:167
  12.9 3.8 %collective-permute-start.2 = (f32[56,4,1,128]{3,0,2,1:T(8,128)S(1)}, f32[56,4,1,128]{3,0,2,1:T(8,128)S(1)}, u32[]{:S(2)}, u32[]{:S(2)}) collective-permute-start(f32[56,4,1,128]{3,0,2,1:T(8,128)S(1)} %get-tuple-element.55), channel_id=1, source_target_pairs={{0,120},{8,0},{16,8},{24,16},{32,24},{40,32},{48,40},{56,48},{64,5... | collective-permute-start | bytes 344072 | tf_op jit(solution)/shard_map/ppermute | solution.py:79
  16.9 2.4 %collective-permute-done.1 = f32[56,4,1,128]{3,0,2,1:T(8,128)S(1)} collective-permute-done((f32[56,4,1,128]{3,0,2,1:T(8,128)S(1)}, f32[56,4,1,128]{3,0,2,1:T(8,128)S(1)}, u32[]{:S(2)}, u32[]{:S(2)}) %collective-permute-start.1) | collective-permute-done | bytes 114720 | tf_op jit(solution)/shard_map/ppermute | solution.py:78
  19.5 0.8 %slice_reduce_fusion.2 = (f32[56,4,8]{0,2,1:T(8,128)S(1)}, f32[56,4,8]{0,2,1:T(8,128)S(1)}, f32[56,4,8,1]{3,0,2,1:T(8,128)S(1)}, f32[56,4,8,1]{3,0,2,1:T(8,128)S(1)}) fusion(f32[56,4,8,128]{3,0,2,1:T(8,128)S(1)} %fusion.6), kind=kLoop, calls=%fused_computation.167 | loop fusion | bytes 43008 | tf_op jit(solution)/shard_map/slice | solution.py:83
  20.3 2.0 %collective-permute-start.3 = (f32[56,4,8]{0,2,1:T(8,128)S(1)}, f32[56,4,8]{0,2,1:T(8,128)S(1)}, u32[]{:S(2)}, u32[]{:S(2)}) collective-permute-start(f32[56,4,8]{0,2,1:T(8,128)S(1)} %get-tuple-element.36), channel_id=1, source_target_pairs={{0,1},{1,2},{2,3},{3,4},{4,5},{5,6},{6,7},{7,0},{8,9},{9,10},{10,1... | collective-permute-start | bytes 21512 | tf_op jit(solution)/shard_map/ppermute | solution.py:83
  22.7 1.4 %collective-permute-done.3 = f32[56,4,8]{0,2,1:T(8,128)S(1)} collective-permute-done((f32[56,4,8]{0,2,1:T(8,128)S(1)}, f32[56,4,8]{0,2,1:T(8,128)S(1)}, u32[]{:S(2)}, u32[]{:S(2)}) %collective-permute-start.3) | collective-permute-done | bytes 7200 | tf_op jit(solution)/shard_map/ppermute | solution.py:83
  24.1 1.9 %collective-permute-done.4 = f32[56,4,8]{0,2,1:T(8,128)S(1)} collective-permute-done((f32[56,4,8]{0,2,1:T(8,128)S(1)}, f32[56,4,8]{0,2,1:T(8,128)S(1)}, u32[]{:S(2)}, u32[]{:S(2)}) %collective-permute-start.4) | collective-permute-done | bytes 7200 | tf_op jit(solution)/shard_map/ppermute | solution.py:84
  26.1 1.1 %fusion.7 = f32[56,4,8,128]{3,0,2,1:T(8,128)S(1)} fusion(f32[56,4,8,127]{3,0,2,1:T(8,128)S(1)} %get-tuple-element.86, f32[56,4,8,1]{3,0,2,1:T(8,128)S(1)} %get-tuple-element.84, f32[56,4,8,128]{3,0,2,1:T(8,128)S(1)} %fusion.6, f32[56,4,8,1]{3,0,2,1:T(8,128)S(1)} %get-tuple-element.83, f32[56,4,8,127]{3,0,2,1:T(8,128)S(1)} %get-tuple-element.85, ...), kind=kLoop, calls=%fused_computation.20 | loop fusion | flops 1376256 | bytes 3684720 | tf_op jit(solution)/shard_map/jit(_where)/select_n | solution.py:88
  28.3 0.6 fusion.4
  29.1 0.7 copy-done.14
  29.7 0.8 %fusion.74 = (f32[28,4,8,128]{3,0,2,1:T(8,128)S(1)}, f32[28]{0:T(128)S(1)}, f32[28,4,8,128]{3,0,2,1:T(8,128)S(1)}) fusion(f32[56,4,8,128]{3,0,2,1:T(8,128)S(1)} %maximum_select_fusion.2, f32[28,4,8,128]{3,2,1,0:T(8,128)S(1)} %bitcast.112, f32[28,4,8,128]{3,2,1,0:T(8,128)S(1)} %copy-done, pred[4,8,128]{2,1,0:T(8,128)(4,1)S(1)} %broadcast_compare_fusion, ...), kind=kLoop, calls=%fused_computation.169 | loop fusion | flops 688100 | bytes 2756749 | tf_op jit(solution)/shard_map/slice | solution.py:182
  31.3 1.0 %copy.114 = f32[28,4,8,128]{3,2,1,0:T(8,128)} copy(f32[28,4,8,128]{3,0,2,1:T(8,128)S(1)} %get-tuple-element.78) | data formatting | bytes 917504
  32.8 0.8 %collective-permute-start.6 = (f32[19]{0:T(128)S(1)}, f32[19]{0:T(128)S(1)}, u32[]{:S(2)}, u32[]{:S(2)}) collective-permute-start(f32[19]{0:T(128)S(1)} %add.117), channel_id=1, source_target_pairs={{0,16},{8,24},{16,0},{24,8},{32,48},{40,56},{48,32},{56,40},{64,80... | collective-permute-start | bytes 236 | tf_op jit(solution)/shard_map/ppermute | solution.py:123
  34.1 0.6 add_multiply_fusion
  35.3 1.2 %collective-permute-done.6 = f32[19]{0:T(128)S(1)} collective-permute-done((f32[19]{0:T(128)S(1)}, f32[19]{0:T(128)S(1)}, u32[]{:S(2)}, u32[]{:S(2)}) %collective-permute-start.6) | collective-permute-done | bytes 108 | tf_op jit(solution)/shard_map/ppermute | solution.py:123
  36.8 1.6 %collective-permute-start.7 = (f32[19]{0:T(128)S(1)}, f32[19]{0:T(128)S(1)}, u32[]{:S(2)}, u32[]{:S(2)}) collective-permute-start(f32[19]{0:T(128)S(1)} %add.121), channel_id=1, source_target_pairs={{0,32},{8,40},{16,48},{24,56},{32,0},{40,8},{48,16},{56,24},{64,96... | collective-permute-start | bytes 236 | tf_op jit(solution)/shard_map/ppermute | solution.py:123
  38.4 2.0 %collective-permute-done.7 = f32[19]{0:T(128)S(1)} collective-permute-done((f32[19]{0:T(128)S(1)}, f32[19]{0:T(128)S(1)}, u32[]{:S(2)}, u32[]{:S(2)}) %collective-permute-start.7) | collective-permute-done | bytes 108 | tf_op jit(solution)/shard_map/ppermute | solution.py:123
  40.4 2.9 %collective-permute-start.8 = (f32[19]{0:T(128)S(1)}, f32[19]{0:T(128)S(1)}, u32[]{:S(2)}, u32[]{:S(2)}) collective-permute-start(f32[19]{0:T(128)S(1)} %add.122), channel_id=1, source_target_pairs={{0,96},{8,104},{16,112},{24,120},{32,64},{40,72},{48,80},{56,88},{... | collective-permute-start | bytes 236 | tf_op jit(solution)/shard_map/ppermute | solution.py:123
  43.3 1.9 %collective-permute-done.8 = f32[19]{0:T(128)S(1)} collective-permute-done((f32[19]{0:T(128)S(1)}, f32[19]{0:T(128)S(1)}, u32[]{:S(2)}, u32[]{:S(2)}) %collective-permute-start.8) | collective-permute-done | bytes 108 | tf_op jit(solution)/shard_map/ppermute | solution.py:123
  45.2 3.0 %collective-permute-start.9 = (f32[4,4,8,128]{3,2,1,0:T(8,128)S(1)}, f32[4,4,8,128]{3,2,1,0:T(8,128)S(1)}, u32[]{:S(2)}, u32[]{:S(2)}) collective-permute-start(f32[4,4,8,128]{3,2,1,0:T(8,128)S(1)} %select_maximum_fusion), channel_id=1, source_target_pairs={{0,128},{128,0},{1,129},{129,1},{2,130},{130,2},{3,131},{131,3},{4... | collective-permute-start | bytes 196616 | tf_op jit(solution)/shard_map/ppermute | solution.py:237
  48.3 2.7 %collective-permute-done.9 = f32[4,4,8,128]{3,2,1,0:T(8,128)S(1)} collective-permute-done((f32[4,4,8,128]{3,2,1,0:T(8,128)S(1)}, f32[4,4,8,128]{3,2,1,0:T(8,128)S(1)}, u32[]{:S(2)}, u32[]{:S(2)}) %collective-permute-start.9) | collective-permute-done | bytes 65568 | tf_op jit(solution)/shard_map/ppermute | solution.py:237
  51.0 2.0 %collective-permute-start.10 = (f32[19]{0:T(128)S(1)}, f32[19]{0:T(128)S(1)}, u32[]{:S(2)}, u32[]{:S(2)}) collective-permute-start(f32[19]{0:T(128)S(1)} %fusion.60), channel_id=1, source_target_pairs={{0,1},{1,0},{2,3},{3,2},{4,5},{5,4},{6,7},{7,6},{8,9},{9,8},{10,11... | collective-permute-start | bytes 236 | tf_op jit(solution)/shard_map/ppermute | solution.py:123
  53.1 1.5 %collective-permute-done.10 = f32[19]{0:T(128)S(1)} collective-permute-done((f32[19]{0:T(128)S(1)}, f32[19]{0:T(128)S(1)}, u32[]{:S(2)}, u32[]{:S(2)}) %collective-permute-start.10) | collective-permute-done | bytes 108 | tf_op jit(solution)/shard_map/ppermute | solution.py:123
  54.6 5.7 %collective-permute-start.11 = (f32[19]{0:T(128)S(1)}, f32[19]{0:T(128)S(1)}, u32[]{:S(2)}, u32[]{:S(2)}) collective-permute-start(f32[19]{0:T(128)S(1)} %add.125), channel_id=1, source_target_pairs={{0,2},{1,3},{2,0},{3,1},{4,6},{5,7},{6,4},{7,5},{8,10},{9,11},{10,... | collective-permute-start | bytes 236 | tf_op jit(solution)/shard_map/ppermute | solution.py:123
  60.8 0.9 %collective-permute-done.11 = f32[19]{0:T(128)S(1)} collective-permute-done((f32[19]{0:T(128)S(1)}, f32[19]{0:T(128)S(1)}, u32[]{:S(2)}, u32[]{:S(2)}) %collective-permute-start.11) | collective-permute-done | bytes 108 | tf_op jit(solution)/shard_map/ppermute | solution.py:123
  61.8 2.0 %collective-permute-start.12 = (f32[19]{0:T(128)S(1)}, f32[19]{0:T(128)S(1)}, u32[]{:S(2)}, u32[]{:S(2)}) collective-permute-start(f32[19]{0:T(128)S(1)} %add.132), channel_id=1, source_target_pairs={{0,6},{1,7},{2,4},{3,5},{4,2},{5,3},{6,0},{7,1},{8,14},{9,15},{10,... | collective-permute-start | bytes 236 | tf_op jit(solution)/shard_map/ppermute | solution.py:123
  63.8 1.0 %copy.115 = f32[28,4,8,128]{3,2,1,0:T(8,128)} copy(f32[28,4,8,128]{3,0,2,1:T(8,128)S(1)} %copy_select_fusion) | data formatting | bytes 917504
  64.8 2.6 %collective-permute-done.12 = f32[19]{0:T(128)S(1)} collective-permute-done((f32[19]{0:T(128)S(1)}, f32[19]{0:T(128)S(1)}, u32[]{:S(2)}, u32[]{:S(2)}) %collective-permute-start.12) | collective-permute-done | bytes 108 | tf_op jit(solution)/shard_map/ppermute | solution.py:123
  (122 shorter events, 9.4 us)
Async XLA Ops:
  0.6 1.3 %copy-start.5 = (f32[19]{0:T(128)S(1)}, f32[19]{0:T(128)}, u32[]{:S(2)}) copy-start(f32[19]{0:T(128)} %constant.126) | copy-start | bytes 232
  0.6 1.3 %copy-start.6 = (f32[19]{0:T(128)S(1)}, f32[19]{0:T(128)}, u32[]{:S(2)}) copy-start(f32[19]{0:T(128)} %constant.127) | copy-start | bytes 232
  0.7 1.3 %copy-start.7 = (f32[19]{0:T(128)S(1)}, f32[19]{0:T(128)}, u32[]{:S(2)}) copy-start(f32[19]{0:T(128)} %constant.128) | copy-start | bytes 232
  2.0 5.3 %copy-start = (f32[28,4,8,128]{3,2,1,0:T(8,128)S(1)}, f32[28,4,8,128]{3,2,1,0:T(8,128)}, u32[]{:S(2)}) copy-start(f32[28,4,8,128]{3,2,1,0:T(8,128)} %param.22) | copy-start | bytes 1376260
  2.4 7.6 %collective-permute-start = (f32[3,4,8,128]{3,2,1,0:T(8,128)S(1)}, f32[3,4,8,128]{3,2,1,0:T(8,128)S(1)}, u32[]{:S(2)}, u32[]{:S(2)}) collective-permute-start(f32[3,4,8,128]{3,2,1,0:T(8,128)S(1)} %maximum_divide_fusion), channel_id=1, source_target_pairs={{0,128},{1,129},{2,130},{3,131},{4,132},{5,133},{6,134},{7,135},{8... | collective-permute-start | bytes 147464 | tf_op jit(solution)/shard_map/ppermute | solution.py:144
  7.3 0.7 %copy-start.3 = (s32[4,8,128]{2,1,0:T(8,128)S(1)}, s32[4,8,128]{2,1,0:T(8,128)}, u32[]{:S(2)}) copy-start(s32[4,8,128]{2,1,0:T(8,128)} %param.23) | copy-start | bytes 49156
  8.1 0.7 copy-start.19
  8.1 0.7 copy-start.20
  8.1 0.7 %copy-start.15 = (f32[28,1,1,1]{0,3,2,1:T(1,128)S(1)}, f32[28,1,1,1]{0,3,2,1:T(1,128)}, u32[]{:S(2)}) copy-start(f32[28,1,1,1]{0,3,2,1:T(1,128)} %constant.104.clone) | copy-start | bytes 340
  8.1 0.7 %copy-start.16 = (f32[28,1,1,1]{0,3,2,1:T(1,128)S(1)}, f32[28,1,1,1]{0,3,2,1:T(1,128)}, u32[]{:S(2)}) copy-start(f32[28,1,1,1]{0,3,2,1:T(1,128)} %constant.105.clone) | copy-start | bytes 340
  8.1 0.7 %copy-start.17 = (f32[28,1,1,1]{0,3,2,1:T(1,128)S(1)}, f32[28,1,1,1]{0,3,2,1:T(1,128)}, u32[]{:S(2)}) copy-start(f32[28,1,1,1]{0,3,2,1:T(1,128)} %constant.108.clone) | copy-start | bytes 340
  8.2 0.7 %copy-start.18 = (f32[28,1,1,1]{0,3,2,1:T(1,128)S(1)}, f32[28,1,1,1]{0,3,2,1:T(1,128)}, u32[]{:S(2)}) copy-start(f32[28,1,1,1]{0,3,2,1:T(1,128)} %constant.109.clone) | copy-start | bytes 340
  8.2 0.9 %copy-start.21 = (f32[15]{0:T(128)S(1)}, f32[15]{0:T(128)}, u32[]{:S(2)}) copy-start(f32[15]{0:T(128)} %param.24) | copy-start | bytes 184
  8.2 1.0 %copy-start.1 = (f32[28,4,8,128]{3,2,1,0:T(8,128)S(1)}, f32[28,4,8,128]{3,2,1,0:T(8,128)}, u32[]{:S(2)}) copy-start(f32[28,4,8,128]{3,2,1,0:T(8,128)} %param.26) | copy-start | bytes 1376260
  10.0 0.7 %copy-start.2 = (f32[19,19,1,1]{0,1,3,2:T(8,128)S(1)}, f32[19,19,1,1]{0,1,3,2:T(8,128)}, u32[]{:S(2)}) copy-start(f32[19,19,1,1]{0,1,3,2:T(8,128)} %constant.133) | copy-start | bytes 4336
  10.1 0.7 %copy-start.13 = (f32[19]{0:T(128)S(1)}, f32[19]{0:T(128)}, u32[]{:S(2)}) copy-start(f32[19]{0:T(128)} %constant.125) | copy-start | bytes 232
  11.5 0.7 copy-start.11
  11.5 0.7 copy-start.12
  12.9 6.4 %collective-permute-start.1 = (f32[56,4,1,128]{3,0,2,1:T(8,128)S(1)}, f32[56,4,1,128]{3,0,2,1:T(8,128)S(1)}, u32[]{:S(2)}, u32[]{:S(2)}) collective-permute-start(f32[56,4,1,128]{3,0,2,1:T(8,128)S(1)} %get-tuple-element.56), channel_id=1, source_target_pairs={{0,8},{8,16},{16,24},{24,32},{32,40},{40,48},{48,56},{56,64},{64,7... | collective-permute-start | bytes 344072 | tf_op jit(solution)/shard_map/ppermute | solution.py:78
  12.9 6.3 %collective-permute-start.2 = (f32[56,4,1,128]{3,0,2,1:T(8,128)S(1)}, f32[56,4,1,128]{3,0,2,1:T(8,128)S(1)}, u32[]{:S(2)}, u32[]{:S(2)}) collective-permute-start(f32[56,4,1,128]{3,0,2,1:T(8,128)S(1)} %get-tuple-element.55), channel_id=1, source_target_pairs={{0,120},{8,0},{16,8},{24,16},{32,24},{40,32},{48,40},{56,48},{64,5... | collective-permute-start | bytes 344072 | tf_op jit(solution)/shard_map/ppermute | solution.py:79
  20.3 3.8 %collective-permute-start.3 = (f32[56,4,8]{0,2,1:T(8,128)S(1)}, f32[56,4,8]{0,2,1:T(8,128)S(1)}, u32[]{:S(2)}, u32[]{:S(2)}) collective-permute-start(f32[56,4,8]{0,2,1:T(8,128)S(1)} %get-tuple-element.36), channel_id=1, source_target_pairs={{0,1},{1,2},{2,3},{3,4},{4,5},{5,6},{6,7},{7,0},{8,9},{9,10},{10,1... | collective-permute-start | bytes 21512 | tf_op jit(solution)/shard_map/ppermute | solution.py:83
  22.3 3.7 %collective-permute-start.4 = (f32[56,4,8]{0,2,1:T(8,128)S(1)}, f32[56,4,8]{0,2,1:T(8,128)S(1)}, u32[]{:S(2)}, u32[]{:S(2)}) collective-permute-start(f32[56,4,8]{0,2,1:T(8,128)S(1)} %get-tuple-element.37), channel_id=1, source_target_pairs={{0,7},{1,0},{2,1},{3,2},{4,3},{5,4},{6,5},{7,6},{8,15},{9,8},{10,9... | collective-permute-start | bytes 21512 | tf_op jit(solution)/shard_map/ppermute | solution.py:84
  27.6 0.7 %copy-start.4 = (f32[19,19]{0,1:T(8,128)S(1)}, f32[19,19]{0,1:T(8,128)}, u32[]{:S(2)}) copy-start(f32[19,19]{0,1:T(8,128)} %constant.102.clone) | copy-start | bytes 4336
  29.1 0.7 copy-start.14
  30.8 2.0 %collective-permute-start.5 = (f32[19]{0:T(128)S(1)}, f32[19]{0:T(128)S(1)}, u32[]{:S(2)}, u32[]{:S(2)}) collective-permute-start(f32[19]{0:T(128)S(1)} %broadcast_select_fusion.1), channel_id=1, source_target_pairs={{0,8},{8,0},{16,24},{24,16},{32,40},{40,32},{48,56},{56,48},{64,72... | collective-permute-start | bytes 236 | tf_op jit(solution)/shard_map/ppermute | solution.py:123
  32.8 3.6 %collective-permute-start.6 = (f32[19]{0:T(128)S(1)}, f32[19]{0:T(128)S(1)}, u32[]{:S(2)}, u32[]{:S(2)}) collective-permute-start(f32[19]{0:T(128)S(1)} %add.117), channel_id=1, source_target_pairs={{0,16},{8,24},{16,0},{24,8},{32,48},{40,56},{48,32},{56,40},{64,80... | collective-permute-start | bytes 236 | tf_op jit(solution)/shard_map/ppermute | solution.py:123
  36.8 3.6 %collective-permute-start.7 = (f32[19]{0:T(128)S(1)}, f32[19]{0:T(128)S(1)}, u32[]{:S(2)}, u32[]{:S(2)}) collective-permute-start(f32[19]{0:T(128)S(1)} %add.121), channel_id=1, source_target_pairs={{0,32},{8,40},{16,48},{24,56},{32,0},{40,8},{48,16},{56,24},{64,96... | collective-permute-start | bytes 236 | tf_op jit(solution)/shard_map/ppermute | solution.py:123
  40.4 4.8 %collective-permute-start.8 = (f32[19]{0:T(128)S(1)}, f32[19]{0:T(128)S(1)}, u32[]{:S(2)}, u32[]{:S(2)}) collective-permute-start(f32[19]{0:T(128)S(1)} %add.122), channel_id=1, source_target_pairs={{0,96},{8,104},{16,112},{24,120},{32,64},{40,72},{48,80},{56,88},{... | collective-permute-start | bytes 236 | tf_op jit(solution)/shard_map/ppermute | solution.py:123
  45.2 5.9 %collective-permute-start.9 = (f32[4,4,8,128]{3,2,1,0:T(8,128)S(1)}, f32[4,4,8,128]{3,2,1,0:T(8,128)S(1)}, u32[]{:S(2)}, u32[]{:S(2)}) collective-permute-start(f32[4,4,8,128]{3,2,1,0:T(8,128)S(1)} %select_maximum_fusion), channel_id=1, source_target_pairs={{0,128},{128,0},{1,129},{129,1},{2,130},{130,2},{3,131},{131,3},{4... | collective-permute-start | bytes 196616 | tf_op jit(solution)/shard_map/ppermute | solution.py:237
  51.0 3.5 %collective-permute-start.10 = (f32[19]{0:T(128)S(1)}, f32[19]{0:T(128)S(1)}, u32[]{:S(2)}, u32[]{:S(2)}) collective-permute-start(f32[19]{0:T(128)S(1)} %fusion.60), channel_id=1, source_target_pairs={{0,1},{1,0},{2,3},{3,2},{4,5},{5,4},{6,7},{7,6},{8,9},{9,8},{10,11... | collective-permute-start | bytes 236 | tf_op jit(solution)/shard_map/ppermute | solution.py:123
  54.6 7.2 %collective-permute-start.11 = (f32[19]{0:T(128)S(1)}, f32[19]{0:T(128)S(1)}, u32[]{:S(2)}, u32[]{:S(2)}) collective-permute-start(f32[19]{0:T(128)S(1)} %add.125), channel_id=1, source_target_pairs={{0,2},{1,3},{2,0},{3,1},{4,6},{5,7},{6,4},{7,5},{8,10},{9,11},{10,... | collective-permute-start | bytes 236 | tf_op jit(solution)/shard_map/ppermute | solution.py:123
  61.8 5.7 %collective-permute-start.12 = (f32[19]{0:T(128)S(1)}, f32[19]{0:T(128)S(1)}, u32[]{:S(2)}, u32[]{:S(2)}) collective-permute-start(f32[19]{0:T(128)S(1)} %add.132), channel_id=1, source_target_pairs={{0,6},{1,7},{2,4},{3,5},{4,2},{5,3},{6,0},{7,1},{8,14},{9,15},{10,... | collective-permute-start | bytes 236 | tf_op jit(solution)/shard_map/ppermute | solution.py:123
  (3 other events, 2.0 us)

commit v13 on v11

--- a/solution.py
+++ b/solution.py
@@ -72,7 +72,7 @@
     return [(i, (i + step) % count) for i in range(count)]
 
 
-def shift_rows(field, moves):
+def exchange_rows(field, moves):
     move_x, move_y, move_z = moves
     size_y, size_z = field.shape[2], field.shape[3]
     low = lax.ppermute(field[:, :, size_y - 1 :, :], "gy", ring("gy", 1))
@@ -82,6 +82,11 @@
     field = jnp.where(move_y > 0, from_low, jnp.where(move_y < 0, from_high, field))
     low = lax.ppermute(field[:, :, :, size_z - 1], "gz", ring("gz", 1))
     high = lax.ppermute(field[:, :, :, 0], "gz", ring("gz", -1))
+    return field, low, high
+
+
+def finish_rows(field, low, high, move_z, move_x):
+    size_z = field.shape[3]
     lane = lax.broadcasted_iota(jnp.int32, field.shape, 3)
     from_low = jnp.where(lane == 0, low[..., None], jnp.roll(field, 1, axis=3))
     from_high = jnp.where(lane == size_z - 1, high[..., None], jnp.roll(field, -1, axis=3))
@@ -176,10 +181,10 @@
     for d in range(3):
         table = jnp.where(is_flow, column(flow_moves[:, d]), column(species_moves[:, d]))
         both_moves.append(jnp.concatenate([table, -table]))
-    both = shift_rows(jnp.concatenate([post, cotangents]), both_moves)
-    moved = both[:rows]
-    returned = both[rows:]
-    moved = jnp.where(is_flow, jnp.concatenate([moved[:19], filler]), moved)
+    both, low_z, high_z = exchange_rows(jnp.concatenate([post, cotangents]), both_moves)
+    returned = finish_rows(
+        both[rows:], low_z[rows:], high_z[rows:], both_moves[2][rows:], both_moves[0][rows:]
+    )
 
     back_species = returned.reshape(grouped.shape)
     back_flow = returned[:19]
@@ -197,6 +202,14 @@
     )
 
     later = {}
+
+    def post_passing(values):
+        values, (field_, low_, high_) = lax.optimization_barrier(
+            (values, (both[:rows], low_z[:rows], high_z[:rows]))
+        )
+        moved_ = finish_rows(field_, low_, high_, both_moves[2][:rows], both_moves[0][:rows])
+        later["moved"] = jnp.where(is_flow, jnp.concatenate([moved_[:19], filler]), moved_)
+        return values
 
     def flow_adjoint(values):
         values, (back_flow_, back_moments_) = lax.optimization_barrier(
@@ -232,7 +245,7 @@
         )
         return values
 
-    partial_rates = butterfly_sum(local_rates, (("gy", 4),), [flow_adjoint, species_adjoint])
+    partial_rates = butterfly_sum(local_rates, (("gy", 4),), [flow_adjoint, species_adjoint, post_passing])
     plane = populations.shape[1:]
     rate_plane = jnp.zeros(plane, jnp.float32).at[0, 0, : partial_rates.shape[0]].set(partial_rates)
     payload = jnp.concatenate([later["species_motion_grad"], rate_plane[None]])
@@ -254,7 +267,7 @@
 
     rate_grad = butterfly_sum(partial_rates, (("gz", 1),), [flow_gradient])
     grad_rows = later["grad_rows"]
-    return (moved, grad_rows, rate_grad)
+    return (later["moved"], grad_rows, rate_grad)
 
 
 def solution(mesh):

time: 67.7 us -> 71.2 us (1.052)
  the two profiles are of different devices: /device:TPU:32 before, /device:TPU:24 now
where the time goes in v13:
time: 71.2 us; the launch traced here: 70.9 us
  waiting for transfers between devices  32.6 us (46%)
  starting transfers between devices  15.6 us (22%)
  local copies, waits for them, and re-layouts  12.8 us (18%)
  other arithmetic  6.23 us (9%)
  matrix products  2.35 us (3%)
  between operations  1.31 us (2%)
    ppermute x7, waiting for transfers between devices, butterfly_sum(): values = values + lax.ppermute(values, axis, list(enumerate(targets)))  18.6 us
    unnamed x58, local copies, waits for them, and re-layouts  9.03 us
    ppermute x1, starting transfers between devices, exchange_rows(): high = lax.ppermute(field[:, :, :, 0], 'gz', ring('gz', -1))  5.94 us
    ppermute x1, waiting for transfers between devices, per_device(): other = lax.ppermute(payload, 'sec', [(0, 1), (1, 0)])  5.73 us
    ppermute x1, starting transfers between devices, per_device(): sent_motion = lax.ppermute(own_motion, 'sec', [(0, 1)])  4.93 us
    ppermute x1, waiting for transfers between devices, exchange_rows(): low = lax.ppermute(field[:, :, :, size_z - 1], 'gz', ring('gz', 1))  3.74 us
    ppermute x1, waiting for transfers between devices, exchange_rows(): low = lax.ppermute(field[:, :, size_y - 1:, :], 'gy', ring('gy', 1))  3.42 us
    ppermute x1, starting transfers between devices, exchange_rows(): high = lax.ppermute(field[:, :, :1, :], 'gy', ring('gy', -1))  2.63 us
  transfers between devices with their start and end apart: 13, of which 11 were waited for; matrix products, arithmetic and copies ran while one was open for 10% of the time, Pallas kernels for 0%

profile of v13, /device:TPU:24, one launch (start us, length us, event | category | flops | bytes accessed | tf_op | source)
XLA Modules:
  0.0 70.9 jit_solution(11030892556902233178)
XLA Ops:
  0.7 1.3 %copy.83 = f32[28,4,8,128]{3,0,2,1:T(8,128)S(1)} copy(f32[28,4,8,128]{3,2,1,0:T(8,128)} %param.22) | data formatting | bytes 917504 | tf_op args[0]
  2.4 4.9 %collective-permute-start = (f32[3,4,8,128]{3,2,1,0:T(8,128)S(1)}, f32[3,4,8,128]{3,2,1,0:T(8,128)S(1)}, u32[]{:S(2)}, u32[]{:S(2)}) collective-permute-start(f32[3,4,8,128]{3,2,1,0:T(8,128)S(1)} %maximum_divide_fusion), channel_id=1, source_target_pairs={{0,128},{1,129},{2,130},{3,131},{4,132},{5,133},{6,134},{7,135},{8... | collective-permute-start | bytes 147464 | tf_op jit(solution)/shard_map/ppermute | solution.py:149
  7.5 0.7 %copy-done.3 = s32[4,8,128]{2,1,0:T(8,128)S(1)} copy-done((s32[4,8,128]{2,1,0:T(8,128)S(1)}, s32[4,8,128]{2,1,0:T(8,128)}, u32[]{:S(2)}) %copy-start.3) | copy-done | bytes 16408
  8.2 0.6 copy-done.4
  8.9 0.7 copy-done.17
  9.7 0.6 copy-done.15
  10.3 0.6 copy-done.13
  11.3 0.6 copy-done.19
  12.5 0.7 copy-done.2
  13.2 0.7 fusion.19
  15.2 2.6 %collective-permute-start.2 = (f32[56,4,1,128]{3,0,2,1:T(8,128)S(1)}, f32[56,4,1,128]{3,0,2,1:T(8,128)S(1)}, u32[]{:S(2)}, u32[]{:S(2)}) collective-permute-start(f32[56,4,1,128]{3,0,2,1:T(8,128)S(1)} %get-tuple-element.67), channel_id=1, source_target_pairs={{0,120},{8,0},{16,8},{24,16},{32,24},{40,32},{48,40},{56,48},{64,5... | collective-permute-start | bytes 344072 | tf_op jit(solution)/shard_map/ppermute | solution.py:79
  18.0 3.4 %collective-permute-done.1 = f32[56,4,1,128]{3,0,2,1:T(8,128)S(1)} collective-permute-done((f32[56,4,1,128]{3,0,2,1:T(8,128)S(1)}, f32[56,4,1,128]{3,0,2,1:T(8,128)S(1)}, u32[]{:S(2)}, u32[]{:S(2)}) %collective-permute-start.1) | collective-permute-done | bytes 114720 | tf_op jit(solution)/shard_map/ppermute | solution.py:78
  21.9 0.8 %slice_reduce_fusion.1 = (f32[56,4,8]{0,2,1:T(8,128)S(1)}, f32[56,4,8]{0,2,1:T(8,128)S(1)}) fusion(f32[56,4,8,128]{3,0,2,1:T(8,128)S(1)} %fusion.3), kind=kLoop, calls=%fused_computation.15 | loop fusion | bytes 28672 | tf_op jit(solution)/shard_map/slice | solution.py:83
  22.7 5.9 %collective-permute-start.4 = (f32[56,4,8]{0,2,1:T(8,128)S(1)}, f32[56,4,8]{0,2,1:T(8,128)S(1)}, u32[]{:S(2)}, u32[]{:S(2)}) collective-permute-start(f32[56,4,8]{0,2,1:T(8,128)S(1)} %get-tuple-element.47), channel_id=1, source_target_pairs={{0,7},{1,0},{2,1},{3,2},{4,3},{5,4},{6,5},{7,6},{8,15},{9,8},{10,9... | collective-permute-start | bytes 21512 | tf_op jit(solution)/shard_map/ppermute | solution.py:84
  29.0 1.1 %collective-permute-done.4 = f32[56,4,8]{0,2,1:T(8,128)S(1)} collective-permute-done((f32[56,4,8]{0,2,1:T(8,128)S(1)}, f32[56,4,8]{0,2,1:T(8,128)S(1)}, u32[]{:S(2)}, u32[]{:S(2)}) %collective-permute-start.4) | collective-permute-done | bytes 7200 | tf_op jit(solution)/shard_map/ppermute | solution.py:84
  30.2 3.7 %collective-permute-done.3 = f32[56,4,8]{0,2,1:T(8,128)S(1)} collective-permute-done((f32[56,4,8]{0,2,1:T(8,128)S(1)}, f32[56,4,8]{0,2,1:T(8,128)S(1)}, u32[]{:S(2)}, u32[]{:S(2)}) %collective-permute-start.3) | collective-permute-done | bytes 7200 | tf_op jit(solution)/shard_map/ppermute | solution.py:83
  34.0 0.7 fusion.69
  34.8 0.8 %fusion.11 = (f32[28]{0:T(128)S(1)}, f32[28,4,8,128]{3,0,2,1:T(8,128)S(1)}) fusion(f32[28,4,8,128]{3,2,1,0:T(8,128)S(1)} %bitcast.104, pred[4,8,128]{2,1,0:T(8,128)(4,1)S(1)} %broadcast_compare_fusion, f32[28,4,8,128]{3,2,1,0:T(8,128)S(1)} %copy-done, f32[28,4,8,128]{3,0,2,1:T(8,128)S(1)} %get-tuple-element.70, f32[28,1,8,128]{3,0,2,1:T(8,128)S(1)} %get-tuple-element.103, ...), kind=kLoop, calls=%fused_computation.36 | loop fusion | flops 917476 | bytes 2756776 | tf_op jit(solution)/shard_map/reduce_sum | solution.py:191
  37.7 0.6 collective-permute-done.5
  38.6 0.6 add_multiply_fusion
  39.5 2.4 %collective-permute-done.6 = f32[19]{0:T(128)S(1)} collective-permute-done((f32[19]{0:T(128)S(1)}, f32[19]{0:T(128)S(1)}, u32[]{:S(2)}, u32[]{:S(2)}) %collective-permute-start.6) | collective-permute-done | bytes 108 | tf_op jit(solution)/shard_map/ppermute | solution.py:128
  41.9 0.8 %collective-permute-start.7 = (f32[19]{0:T(128)S(1)}, f32[19]{0:T(128)S(1)}, u32[]{:S(2)}, u32[]{:S(2)}) collective-permute-start(f32[19]{0:T(128)S(1)} %add.118), channel_id=1, source_target_pairs={{0,32},{8,40},{16,48},{24,56},{32,0},{40,8},{48,16},{56,24},{64,96... | collective-permute-start | bytes 236 | tf_op jit(solution)/shard_map/ppermute | solution.py:128
  43.3 2.1 %collective-permute-done.7 = f32[19]{0:T(128)S(1)} collective-permute-done((f32[19]{0:T(128)S(1)}, f32[19]{0:T(128)S(1)}, u32[]{:S(2)}, u32[]{:S(2)}) %collective-permute-start.7) | collective-permute-done | bytes 108 | tf_op jit(solution)/shard_map/ppermute | solution.py:128
  46.3 0.6 fusion.7
  47.1 3.6 %collective-permute-done.8 = f32[19]{0:T(128)S(1)} collective-permute-done((f32[19]{0:T(128)S(1)}, f32[19]{0:T(128)S(1)}, u32[]{:S(2)}, u32[]{:S(2)}) %collective-permute-start.8) | collective-permute-done | bytes 108 | tf_op jit(solution)/shard_map/ppermute | solution.py:128
  50.9 5.7 %collective-permute-done.9 = f32[4,4,8,128]{3,2,1,0:T(8,128)S(1)} collective-permute-done((f32[4,4,8,128]{3,2,1,0:T(8,128)S(1)}, f32[4,4,8,128]{3,2,1,0:T(8,128)S(1)}, u32[]{:S(2)}, u32[]{:S(2)}) %collective-permute-start.9) | collective-permute-done | bytes 65568 | tf_op jit(solution)/shard_map/ppermute | solution.py:252
  56.6 3.5 %collective-permute-done.10 = f32[19]{0:T(128)S(1)} collective-permute-done((f32[19]{0:T(128)S(1)}, f32[19]{0:T(128)S(1)}, u32[]{:S(2)}, u32[]{:S(2)}) %collective-permute-start.10) | collective-permute-done | bytes 108 | tf_op jit(solution)/shard_map/ppermute | solution.py:128
  60.7 0.6 copy-done.12
  61.8 1.0 %copy.111 = f32[28,4,8,128]{3,2,1,0:T(8,128)} copy(f32[28,4,8,128]{3,0,2,1:T(8,128)S(1)} %get-tuple-element.154) | data formatting | bytes 917504
  62.8 1.9 %collective-permute-done.11 = f32[19]{0:T(128)S(1)} collective-permute-done((f32[19]{0:T(128)S(1)}, f32[19]{0:T(128)S(1)}, u32[]{:S(2)}, u32[]{:S(2)}) %collective-permute-start.11) | collective-permute-done | bytes 108 | tf_op jit(solution)/shard_map/ppermute | solution.py:128
  64.9 1.0 %copy.112 = f32[28,4,8,128]{3,2,1,0:T(8,128)} copy(f32[28,4,8,128]{3,0,2,1:T(8,128)S(1)} %get-tuple-element.155) | data formatting | bytes 917504
  66.0 4.4 %collective-permute-done.12 = f32[19]{0:T(128)S(1)} collective-permute-done((f32[19]{0:T(128)S(1)}, f32[19]{0:T(128)S(1)}, u32[]{:S(2)}, u32[]{:S(2)}) %collective-permute-start.12) | collective-permute-done | bytes 108 | tf_op jit(solution)/shard_map/ppermute | solution.py:128
  (126 shorter events, 9.9 us)
Async XLA Ops:
  0.6 1.3 %copy-start.9 = (f32[19]{0:T(128)S(1)}, f32[19]{0:T(128)}, u32[]{:S(2)}) copy-start(f32[19]{0:T(128)} %constant.128) | copy-start | bytes 232
  0.6 1.3 %copy-start.10 = (f32[19]{0:T(128)S(1)}, f32[19]{0:T(128)}, u32[]{:S(2)}) copy-start(f32[19]{0:T(128)} %constant.129) | copy-start | bytes 232
  0.7 1.3 %copy-start.11 = (f32[19]{0:T(128)S(1)}, f32[19]{0:T(128)}, u32[]{:S(2)}) copy-start(f32[19]{0:T(128)} %constant.127) | copy-start | bytes 232
  2.0 5.3 %copy-start = (f32[28,4,8,128]{3,2,1,0:T(8,128)S(1)}, f32[28,4,8,128]{3,2,1,0:T(8,128)}, u32[]{:S(2)}) copy-start(f32[28,4,8,128]{3,2,1,0:T(8,128)} %param.22) | copy-start | bytes 1376260
  2.4 10.1 %collective-permute-start = (f32[3,4,8,128]{3,2,1,0:T(8,128)S(1)}, f32[3,4,8,128]{3,2,1,0:T(8,128)S(1)}, u32[]{:S(2)}, u32[]{:S(2)}) collective-permute-start(f32[3,4,8,128]{3,2,1,0:T(8,128)S(1)} %maximum_divide_fusion), channel_id=1, source_target_pairs={{0,128},{1,129},{2,130},{3,131},{4,132},{5,133},{6,134},{7,135},{8... | collective-permute-start | bytes 147464 | tf_op jit(solution)/shard_map/ppermute | solution.py:149
  7.4 3.6 %copy-start.1 = (f32[28,4,8,128]{3,2,1,0:T(8,128)S(1)}, f32[28,4,8,128]{3,2,1,0:T(8,128)}, u32[]{:S(2)}) copy-start(f32[28,4,8,128]{3,2,1,0:T(8,128)} %param.26) | copy-start | bytes 1376260
  7.5 0.8 %copy-start.3 = (s32[4,8,128]{2,1,0:T(8,128)S(1)}, s32[4,8,128]{2,1,0:T(8,128)}, u32[]{:S(2)}) copy-start(s32[4,8,128]{2,1,0:T(8,128)} %param.23) | copy-start | bytes 49156
  8.2 0.7 copy-start.4
  8.9 0.7 copy-start.17
  8.9 0.7 copy-start.18
  9.6 0.7 copy-start.16
  10.2 0.7 copy-start.14
  11.2 0.7 copy-start.19
  12.5 0.7 %copy-start.2 = (f32[19,19,1,1]{0,1,3,2:T(8,128)S(1)}, f32[19,19,1,1]{0,1,3,2:T(8,128)}, u32[]{:S(2)}) copy-start(f32[19,19,1,1]{0,1,3,2:T(8,128)} %constant.134) | copy-start | bytes 4336
  12.5 0.7 copy-start.20
  13.2 0.7 %copy-start.5 = (f32[7]{0:T(128)S(1)}, f32[7]{0:T(128)}, u32[]{:S(2)}) copy-start(f32[7]{0:T(128)} %constant.133) | copy-start | bytes 88
  13.2 0.7 %copy-start.6 = (f32[7]{0:T(128)S(1)}, f32[7]{0:T(128)}, u32[]{:S(2)}) copy-start(f32[7]{0:T(128)} %constant.132) | copy-start | bytes 88
  13.2 0.7 %copy-start.7 = (f32[7]{0:T(128)S(1)}, f32[7]{0:T(128)}, u32[]{:S(2)}) copy-start(f32[7]{0:T(128)} %constant.131) | copy-start | bytes 88
  13.2 0.7 %copy-start.8 = (f32[7]{0:T(128)S(1)}, f32[7]{0:T(128)}, u32[]{:S(2)}) copy-start(f32[7]{0:T(128)} %constant.130) | copy-start | bytes 88
  15.2 6.2 %collective-permute-start.1 = (f32[56,4,1,128]{3,0,2,1:T(8,128)S(1)}, f32[56,4,1,128]{3,0,2,1:T(8,128)S(1)}, u32[]{:S(2)}, u32[]{:S(2)}) collective-permute-start(f32[56,4,1,128]{3,0,2,1:T(8,128)S(1)} %get-tuple-element.68), channel_id=1, source_target_pairs={{0,8},{8,16},{16,24},{24,32},{32,40},{40,48},{48,56},{56,64},{64,7... | collective-permute-start | bytes 344072 | tf_op jit(solution)/shard_map/ppermute | solution.py:78
  15.2 6.2 %collective-permute-start.2 = (f32[56,4,1,128]{3,0,2,1:T(8,128)S(1)}, f32[56,4,1,128]{3,0,2,1:T(8,128)S(1)}, u32[]{:S(2)}, u32[]{:S(2)}) collective-permute-start(f32[56,4,1,128]{3,0,2,1:T(8,128)S(1)} %get-tuple-element.67), channel_id=1, source_target_pairs={{0,120},{8,0},{16,8},{24,16},{32,24},{40,32},{48,40},{56,48},{64,5... | collective-permute-start | bytes 344072 | tf_op jit(solution)/shard_map/ppermute | solution.py:79
  22.7 7.4 %collective-permute-start.4 = (f32[56,4,8]{0,2,1:T(8,128)S(1)}, f32[56,4,8]{0,2,1:T(8,128)S(1)}, u32[]{:S(2)}, u32[]{:S(2)}) collective-permute-start(f32[56,4,8]{0,2,1:T(8,128)S(1)} %get-tuple-element.47), channel_id=1, source_target_pairs={{0,7},{1,0},{2,1},{3,2},{4,3},{5,4},{6,5},{7,6},{8,15},{9,8},{10,9... | collective-permute-start | bytes 21512 | tf_op jit(solution)/shard_map/ppermute | solution.py:84
  28.9 5.0 %collective-permute-start.3 = (f32[56,4,8]{0,2,1:T(8,128)S(1)}, f32[56,4,8]{0,2,1:T(8,128)S(1)}, u32[]{:S(2)}, u32[]{:S(2)}) collective-permute-start(f32[56,4,8]{0,2,1:T(8,128)S(1)} %get-tuple-element.46), channel_id=1, source_target_pairs={{0,1},{1,2},{2,3},{3,4},{4,5},{5,6},{6,7},{7,0},{8,9},{9,10},{10,1... | collective-permute-start | bytes 21512 | tf_op jit(solution)/shard_map/ppermute | solution.py:83
  37.2 1.1 %collective-permute-start.5 = (f32[19]{0:T(128)S(1)}, f32[19]{0:T(128)S(1)}, u32[]{:S(2)}, u32[]{:S(2)}) collective-permute-start(f32[19]{0:T(128)S(1)} %broadcast_select_fusion.1), channel_id=1, source_target_pairs={{0,8},{8,0},{16,24},{24,16},{32,40},{40,32},{48,56},{56,48},{64,72... | collective-permute-start | bytes 236 | tf_op jit(solution)/shard_map/ppermute | solution.py:128
  38.4 3.5 %collective-permute-start.6 = (f32[19]{0:T(128)S(1)}, f32[19]{0:T(128)S(1)}, u32[]{:S(2)}, u32[]{:S(2)}) collective-permute-start(f32[19]{0:T(128)S(1)} %add.117), channel_id=1, source_target_pairs={{0,16},{8,24},{16,0},{24,8},{32,48},{40,56},{48,32},{56,40},{64,80... | collective-permute-start | bytes 236 | tf_op jit(solution)/shard_map/ppermute | solution.py:128
  41.9 3.5 %collective-permute-start.7 = (f32[19]{0:T(128)S(1)}, f32[19]{0:T(128)S(1)}, u32[]{:S(2)}, u32[]{:S(2)}) collective-permute-start(f32[19]{0:T(128)S(1)} %add.118), channel_id=1, source_target_pairs={{0,32},{8,40},{16,48},{24,56},{32,0},{40,8},{48,16},{56,24},{64,96... | collective-permute-start | bytes 236 | tf_op jit(solution)/shard_map/ppermute | solution.py:128
  45.9 4.8 %collective-permute-start.8 = (f32[19]{0:T(128)S(1)}, f32[19]{0:T(128)S(1)}, u32[]{:S(2)}, u32[]{:S(2)}) collective-permute-start(f32[19]{0:T(128)S(1)} %add.119), channel_id=1, source_target_pairs={{0,96},{8,104},{16,112},{24,120},{32,64},{40,72},{48,80},{56,88},{... | collective-permute-start | bytes 236 | tf_op jit(solution)/shard_map/ppermute | solution.py:128
  50.7 5.9 %collective-permute-start.9 = (f32[4,4,8,128]{3,2,1,0:T(8,128)S(1)}, f32[4,4,8,128]{3,2,1,0:T(8,128)S(1)}, u32[]{:S(2)}, u32[]{:S(2)}) collective-permute-start(f32[4,4,8,128]{3,2,1,0:T(8,128)S(1)} %select_maximum_fusion), channel_id=1, source_target_pairs={{0,128},{128,0},{1,129},{129,1},{2,130},{130,2},{3,131},{131,3},{4... | collective-permute-start | bytes 196616 | tf_op jit(solution)/shard_map/ppermute | solution.py:252
  56.6 3.5 %collective-permute-start.10 = (f32[19]{0:T(128)S(1)}, f32[19]{0:T(128)S(1)}, u32[]{:S(2)}, u32[]{:S(2)}) collective-permute-start(f32[19]{0:T(128)S(1)} %fusion.58), channel_id=1, source_target_pairs={{0,1},{1,0},{2,3},{3,2},{4,5},{5,4},{6,7},{7,6},{8,9},{9,8},{10,11... | collective-permute-start | bytes 236 | tf_op jit(solution)/shard_map/ppermute | solution.py:128
  60.2 4.5 %collective-permute-start.11 = (f32[19]{0:T(128)S(1)}, f32[19]{0:T(128)S(1)}, u32[]{:S(2)}, u32[]{:S(2)}) collective-permute-start(f32[19]{0:T(128)S(1)} %add.125), channel_id=1, source_target_pairs={{0,2},{1,3},{2,0},{3,1},{4,6},{5,7},{6,4},{7,5},{8,10},{9,11},{10,... | collective-permute-start | bytes 236 | tf_op jit(solution)/shard_map/ppermute | solution.py:128
  60.7 0.7 copy-start.12
  64.7 5.7 %collective-permute-start.12 = (f32[19]{0:T(128)S(1)}, f32[19]{0:T(128)S(1)}, u32[]{:S(2)}, u32[]{:S(2)}) collective-permute-start(f32[19]{0:T(128)S(1)} %add.132), channel_id=1, source_target_pairs={{0,6},{1,7},{2,4},{3,5},{4,2},{5,3},{6,0},{7,1},{8,14},{9,15},{10,... | collective-permute-start | bytes 236 | tf_op jit(solution)/shard_map/ppermute | solution.py:128
  (2 other events, 1.3 us)

commit v14 on v11

--- a/solution.py
+++ b/solution.py
@@ -142,14 +142,15 @@
         [jnp.sum(flow * vx, 0), jnp.sum(flow * vy, 0), jnp.sum(flow * vz, 0)]
     ) / density[None]
     sent_motion = lax.ppermute(own_motion, "sec", [(0, 1)])
-    motion = jnp.where(is_flow, own_motion, sent_motion)
 
     small_weights = column([0.25] + [0.125] * 6)
     grouped = populations.reshape((groups, 7) + populations.shape[1:])
     species_r = species_rates.reshape((groups, 1, 1, 1, 1))
     concentration = jnp.sum(grouped, 1)
     sx, sy, sz = (column(velocity[:7, d])[None] for d in range(3))
-    projected_small = motion[0][None] * sx[0] + motion[1][None] * sy[0] + motion[2][None] * sz[0]
+    projected_small = (
+        sent_motion[0][None] * sx[0] + sent_motion[1][None] * sy[0] + sent_motion[2][None] * sz[0]
+    )
     factor = small_weights * (1.0 + 4.0 * projected_small)
     species_eq = factor[None] * concentration[:, None]
     species_gap = grouped - species_eq
@@ -160,8 +161,8 @@
     q_table = jnp.asarray(ortho, jnp.float32)
     relax = jnp.concatenate([jnp.zeros((4,), flow_rates.dtype), flow_rates]).reshape(19, 1, 1, 1)
     w = column(weights)
-    projected = vx * motion[0][None] + vy * motion[1][None] + vz * motion[2][None]
-    squared = jnp.sum(motion * motion, 0)
+    projected = vx * own_motion[0][None] + vy * own_motion[1][None] + vz * own_motion[2][None]
+    squared = jnp.sum(own_motion * own_motion, 0)
     poly = w * (1.0 + 3.0 * projected + 4.5 * projected * projected - 1.5 * squared[None])
     equilibrium = density[None] * poly
     moments = jnp.einsum("ji,jxyz->ixyz", q_table, flow - equilibrium, precision=highest)
@@ -209,7 +210,7 @@
         hwp = hw * (3.0 + 9.0 * projected)
         later["motion_grad"] = density[None] * (
             jnp.stack([jnp.sum(hwp * vx, 0), jnp.sum(hwp * vy, 0), jnp.sum(hwp * vz, 0)])
-            - 3.0 * motion * hw_sum[None]
+            - 3.0 * own_motion * hw_sum[None]
         )
         later["flow_base"] = back_flow_ - through_eq + density_grad[None]
         return values
@@ -243,7 +244,7 @@
         values, received = lax.optimization_barrier((values, other[:3]))
         motion_grad = jnp.where(fluid, later["motion_grad"] + received, 0.0)
         along = vx * motion_grad[0][None] + vy * motion_grad[1][None] + vz * motion_grad[2][None]
-        extra = (along - jnp.sum(motion * motion_grad, 0)[None]) / density[None]
+        extra = (along - jnp.sum(own_motion * motion_grad, 0)[None]) / density[None]
         flow_grad = jnp.where(
             fluid, later["flow_base"] + extra, reverse_pairs(back_flow, opposite)
         )

time: 67.7 us -> 70.6 us (1.043)
  starting transfers between devices: 29 us -> 26.1 us
  local copies, waits for them, and re-layouts: 9.48 us -> 12.3 us
  waiting for transfers between devices: 19 us -> 21.8 us
    ppermute x1, starting transfers between devices: 2.97 us -> 0.09 us  [per_device(): other = lax.ppermute(payload, 'sec', [(0, 1), (1, 0)])]
    ppermute x1, waiting for transfers between devices: 2.74 us -> 5.6 us  [per_device(): other = lax.ppermute(payload, 'sec', [(0, 1), (1, 0)])]
    unnamed x58, local copies, waits for them, and re-layouts: 6.49 us -> 9.33 us
  transfers between devices with their start and end apart: 13 -> 13, of which waited for: 10 -> 10; matrix products, arithmetic and copies ran while one was open for 10% -> 11% of each run, Pallas kernels for 0% -> 0%
where the time goes in v14:
time: 70.6 us; the launch traced here: 70.2 us
  starting transfers between devices  26.1 us (37%)
  waiting for transfers between devices  21.8 us (31%)
  local copies, waits for them, and re-layouts  12.3 us (17%)
  other arithmetic  6.33 us (9%)
  matrix products  2.33 us (3%)
  between operations  1.26 us (2%)
    ppermute x7, starting transfers between devices, butterfly_sum(): values = values + lax.ppermute(values, axis, list(enumerate(targets)))  15.1 us
    ppermute x7, waiting for transfers between devices, butterfly_sum(): values = values + lax.ppermute(values, axis, list(enumerate(targets)))  10.5 us
    unnamed x58, local copies, waits for them, and re-layouts  9.33 us
    ppermute x1, waiting for transfers between devices, per_device(): other = lax.ppermute(payload, 'sec', [(0, 1), (1, 0)])  5.6 us
    ppermute x1, starting transfers between devices, per_device(): sent_motion = lax.ppermute(own_motion, 'sec', [(0, 1)])  4.93 us
    ppermute x1, starting transfers between devices, shift_rows(): high = lax.ppermute(field[:, :, :1, :], 'gy', ring('gy', -1))  3.84 us
    ppermute x1, waiting for transfers between devices, shift_rows(): low = lax.ppermute(field[:, :, size_y - 1:, :], 'gy', ring('gy', 1))  2.36 us
    ppermute x1, starting transfers between devices, shift_rows(): low = lax.ppermute(field[:, :, :, size_z - 1], 'gz', ring('gz', 1))  1.99 us
  transfers between devices with their start and end apart: 13, of which 10 were waited for; matrix products, arithmetic and copies ran while one was open for 11% of the time, Pallas kernels for 0%

profile of v14, /device:TPU:32, one launch (start us, length us, event | category | flops | bytes accessed | tf_op | source)
XLA Modules:
  0.0 70.2 jit_solution(1737912179402392600)
XLA Ops:
  0.7 1.3 %copy.83 = f32[28,4,8,128]{3,0,2,1:T(8,128)S(1)} copy(f32[28,4,8,128]{3,2,1,0:T(8,128)} %param.22) | data formatting | bytes 917504 | tf_op args[0]
  2.4 4.9 %collective-permute-start = (f32[3,4,8,128]{3,2,1,0:T(8,128)S(1)}, f32[3,4,8,128]{3,2,1,0:T(8,128)S(1)}, u32[]{:S(2)}, u32[]{:S(2)}) collective-permute-start(f32[3,4,8,128]{3,2,1,0:T(8,128)S(1)} %get-tuple-element.54), channel_id=1, source_target_pairs={{0,128},{1,129},{2,130},{3,131},{4,132},{5,133},{6,134},{7,135},{8... | collective-permute-start | bytes 147464 | tf_op jit(solution)/shard_map/ppermute | solution.py:144
  7.4 0.7 copy-done.3
  8.3 0.6 copy-done.7
  8.9 0.7 copy-done.19
  9.7 0.7 copy-done.17
  11.2 0.7 fusion.18
  13.0 0.9 %copy-done.1 = f32[28,4,8,128]{3,2,1,0:T(8,128)S(1)} copy-done((f32[28,4,8,128]{3,2,1,0:T(8,128)S(1)}, f32[28,4,8,128]{3,2,1,0:T(8,128)}, u32[]{:S(2)}) %copy-start.1) | copy-done | bytes 458776
  15.7 3.8 %collective-permute-start.2 = (f32[56,4,1,128]{3,0,2,1:T(8,128)S(1)}, f32[56,4,1,128]{3,0,2,1:T(8,128)S(1)}, u32[]{:S(2)}, u32[]{:S(2)}) collective-permute-start(f32[56,4,1,128]{3,0,2,1:T(8,128)S(1)} %get-tuple-element.57), channel_id=1, source_target_pairs={{0,120},{8,0},{16,8},{24,16},{32,24},{40,32},{48,40},{56,48},{64,5... | collective-permute-start | bytes 344072 | tf_op jit(solution)/shard_map/ppermute | solution.py:79
  19.6 2.4 %collective-permute-done.1 = f32[56,4,1,128]{3,0,2,1:T(8,128)S(1)} collective-permute-done((f32[56,4,1,128]{3,0,2,1:T(8,128)S(1)}, f32[56,4,1,128]{3,0,2,1:T(8,128)S(1)}, u32[]{:S(2)}, u32[]{:S(2)}) %collective-permute-start.1) | collective-permute-done | bytes 114720 | tf_op jit(solution)/shard_map/ppermute | solution.py:78
  22.2 0.8 %slice_reduce_fusion.2 = (f32[56,4,8]{0,2,1:T(8,128)S(1)}, f32[56,4,8]{0,2,1:T(8,128)S(1)}, f32[56,4,8,1]{3,0,2,1:T(8,128)S(1)}, f32[56,4,8,1]{3,0,2,1:T(8,128)S(1)}) fusion(f32[56,4,8,128]{3,0,2,1:T(8,128)S(1)} %fusion.3), kind=kLoop, calls=%fused_computation.164 | loop fusion | bytes 43008 | tf_op jit(solution)/shard_map/slice | solution.py:83
  23.1 2.0 %collective-permute-start.3 = (f32[56,4,8]{0,2,1:T(8,128)S(1)}, f32[56,4,8]{0,2,1:T(8,128)S(1)}, u32[]{:S(2)}, u32[]{:S(2)}) collective-permute-start(f32[56,4,8]{0,2,1:T(8,128)S(1)} %get-tuple-element.38), channel_id=1, source_target_pairs={{0,1},{1,2},{2,3},{3,4},{4,5},{5,6},{6,7},{7,0},{8,9},{9,10},{10,1... | collective-permute-start | bytes 21512 | tf_op jit(solution)/shard_map/ppermute | solution.py:83
  25.5 1.4 %collective-permute-done.3 = f32[56,4,8]{0,2,1:T(8,128)S(1)} collective-permute-done((f32[56,4,8]{0,2,1:T(8,128)S(1)}, f32[56,4,8]{0,2,1:T(8,128)S(1)}, u32[]{:S(2)}, u32[]{:S(2)}) %collective-permute-start.3) | collective-permute-done | bytes 7200 | tf_op jit(solution)/shard_map/ppermute | solution.py:83
  26.9 1.9 %collective-permute-done.4 = f32[56,4,8]{0,2,1:T(8,128)S(1)} collective-permute-done((f32[56,4,8]{0,2,1:T(8,128)S(1)}, f32[56,4,8]{0,2,1:T(8,128)S(1)}, u32[]{:S(2)}, u32[]{:S(2)}) %collective-permute-start.4) | collective-permute-done | bytes 7200 | tf_op jit(solution)/shard_map/ppermute | solution.py:84
  28.8 1.2 %fusion.4 = f32[56,4,8,128]{3,0,2,1:T(8,128)S(1)} fusion(f32[56,4,8,127]{3,0,2,1:T(8,128)S(1)} %get-tuple-element.88, f32[56,4,8,1]{3,0,2,1:T(8,128)S(1)} %get-tuple-element.86, f32[56,4,8,128]{3,0,2,1:T(8,128)S(1)} %fusion.3, f32[56,4,8,1]{3,0,2,1:T(8,128)S(1)} %get-tuple-element.85, f32[56,4,8,127]{3,0,2,1:T(8,128)S(1)} %get-tuple-element.87, ...), kind=kLoop, calls=%fused_computation.15 | loop fusion | flops 1376256 | bytes 3684720 | tf_op jit(solution)/shard_map/jit(_where)/select_n | solution.py:88
  31.4 0.6 copy-done.12
  32.0 0.8 %fusion.71 = (f32[28,4,8,128]{3,0,2,1:T(8,128)S(1)}, f32[28]{0:T(128)S(1)}, f32[28,4,8,128]{3,0,2,1:T(8,128)S(1)}) fusion(f32[56,4,8,128]{3,0,2,1:T(8,128)S(1)} %maximum_select_fusion.2, f32[28,4,8,128]{3,2,1,0:T(8,128)S(1)} %bitcast.102, f32[28,4,8,128]{3,2,1,0:T(8,128)S(1)} %copy-done, pred[4,8,128]{2,1,0:T(8,128)(4,1)S(1)} %broadcast_compare_fusion, ...), kind=kLoop, calls=%fused_computation.166 | loop fusion | flops 688100 | bytes 2756749 | tf_op jit(solution)/shard_map/slice | solution.py:182
  33.6 1.0 %copy.111 = f32[28,4,8,128]{3,2,1,0:T(8,128)} copy(f32[28,4,8,128]{3,0,2,1:T(8,128)S(1)} %get-tuple-element.80) | data formatting | bytes 917504
  35.1 0.7 %collective-permute-start.6 = (f32[19]{0:T(128)S(1)}, f32[19]{0:T(128)S(1)}, u32[]{:S(2)}, u32[]{:S(2)}) collective-permute-start(f32[19]{0:T(128)S(1)} %add.117), channel_id=1, source_target_pairs={{0,16},{8,24},{16,0},{24,8},{32,48},{40,56},{48,32},{56,40},{64,80... | collective-permute-start | bytes 236 | tf_op jit(solution)/shard_map/ppermute | solution.py:123
  37.1 1.6 %collective-permute-done.6 = f32[19]{0:T(128)S(1)} collective-permute-done((f32[19]{0:T(128)S(1)}, f32[19]{0:T(128)S(1)}, u32[]{:S(2)}, u32[]{:S(2)}) %collective-permute-start.6) | collective-permute-done | bytes 108 | tf_op jit(solution)/shard_map/ppermute | solution.py:123
  39.0 1.6 %collective-permute-start.7 = (f32[19]{0:T(128)S(1)}, f32[19]{0:T(128)S(1)}, u32[]{:S(2)}, u32[]{:S(2)}) collective-permute-start(f32[19]{0:T(128)S(1)} %add.121), channel_id=1, source_target_pairs={{0,32},{8,40},{16,48},{24,56},{32,0},{40,8},{48,16},{56,24},{64,96... | collective-permute-start | bytes 236 | tf_op jit(solution)/shard_map/ppermute | solution.py:123
  40.7 2.0 %collective-permute-done.7 = f32[19]{0:T(128)S(1)} collective-permute-done((f32[19]{0:T(128)S(1)}, f32[19]{0:T(128)S(1)}, u32[]{:S(2)}, u32[]{:S(2)}) %collective-permute-start.7) | collective-permute-done | bytes 108 | tf_op jit(solution)/shard_map/ppermute | solution.py:123
  42.7 2.9 %collective-permute-start.8 = (f32[19]{0:T(128)S(1)}, f32[19]{0:T(128)S(1)}, u32[]{:S(2)}, u32[]{:S(2)}) collective-permute-start(f32[19]{0:T(128)S(1)} %add.122), channel_id=1, source_target_pairs={{0,96},{8,104},{16,112},{24,120},{32,64},{40,72},{48,80},{56,88},{... | collective-permute-start | bytes 236 | tf_op jit(solution)/shard_map/ppermute | solution.py:123
  45.5 1.9 %collective-permute-done.8 = f32[19]{0:T(128)S(1)} collective-permute-done((f32[19]{0:T(128)S(1)}, f32[19]{0:T(128)S(1)}, u32[]{:S(2)}, u32[]{:S(2)}) %collective-permute-start.8) | collective-permute-done | bytes 108 | tf_op jit(solution)/shard_map/ppermute | solution.py:123
  47.7 5.6 %collective-permute-done.9 = f32[4,4,8,128]{3,2,1,0:T(8,128)S(1)} collective-permute-done((f32[4,4,8,128]{3,2,1,0:T(8,128)S(1)}, f32[4,4,8,128]{3,2,1,0:T(8,128)S(1)}, u32[]{:S(2)}, u32[]{:S(2)}) %collective-permute-start.9) | collective-permute-done | bytes 65568 | tf_op jit(solution)/shard_map/ppermute | solution.py:240
  53.3 2.0 %collective-permute-start.10 = (f32[19]{0:T(128)S(1)}, f32[19]{0:T(128)S(1)}, u32[]{:S(2)}, u32[]{:S(2)}) collective-permute-start(f32[19]{0:T(128)S(1)} %fusion.57), channel_id=1, source_target_pairs={{0,1},{1,0},{2,3},{3,2},{4,5},{5,4},{6,7},{7,6},{8,9},{9,8},{10,11... | collective-permute-start | bytes 236 | tf_op jit(solution)/shard_map/ppermute | solution.py:123
  55.3 1.5 %collective-permute-done.10 = f32[19]{0:T(128)S(1)} collective-permute-done((f32[19]{0:T(128)S(1)}, f32[19]{0:T(128)S(1)}, u32[]{:S(2)}, u32[]{:S(2)}) %collective-permute-start.10) | collective-permute-done | bytes 108 | tf_op jit(solution)/shard_map/ppermute | solution.py:123
  56.9 5.7 %collective-permute-start.11 = (f32[19]{0:T(128)S(1)}, f32[19]{0:T(128)S(1)}, u32[]{:S(2)}, u32[]{:S(2)}) collective-permute-start(f32[19]{0:T(128)S(1)} %add.125), channel_id=1, source_target_pairs={{0,2},{1,3},{2,0},{3,1},{4,6},{5,7},{6,4},{7,5},{8,10},{9,11},{10,... | collective-permute-start | bytes 236 | tf_op jit(solution)/shard_map/ppermute | solution.py:123
  63.1 0.9 %collective-permute-done.11 = f32[19]{0:T(128)S(1)} collective-permute-done((f32[19]{0:T(128)S(1)}, f32[19]{0:T(128)S(1)}, u32[]{:S(2)}, u32[]{:S(2)}) %collective-permute-start.11) | collective-permute-done | bytes 108 | tf_op jit(solution)/shard_map/ppermute | solution.py:123
  64.1 2.0 %collective-permute-start.12 = (f32[19]{0:T(128)S(1)}, f32[19]{0:T(128)S(1)}, u32[]{:S(2)}, u32[]{:S(2)}) collective-permute-start(f32[19]{0:T(128)S(1)} %add.132), channel_id=1, source_target_pairs={{0,6},{1,7},{2,4},{3,5},{4,2},{5,3},{6,0},{7,1},{8,14},{9,15},{10,... | collective-permute-start | bytes 236 | tf_op jit(solution)/shard_map/ppermute | solution.py:123
  66.1 1.0 %copy.112 = f32[28,4,8,128]{3,2,1,0:T(8,128)} copy(f32[28,4,8,128]{3,0,2,1:T(8,128)S(1)} %copy_select_fusion) | data formatting | bytes 917504
  67.1 2.6 %collective-permute-done.12 = f32[19]{0:T(128)S(1)} collective-permute-done((f32[19]{0:T(128)S(1)}, f32[19]{0:T(128)S(1)}, u32[]{:S(2)}, u32[]{:S(2)}) %collective-permute-start.12) | collective-permute-done | bytes 108 | tf_op jit(solution)/shard_map/ppermute | solution.py:123
  (120 shorter events, 10.5 us)
Async XLA Ops:
  0.6 1.3 %copy-start.4 = (f32[19]{0:T(128)S(1)}, f32[19]{0:T(128)}, u32[]{:S(2)}) copy-start(f32[19]{0:T(128)} %constant.126) | copy-start | bytes 232
  0.6 1.3 %copy-start.5 = (f32[19]{0:T(128)S(1)}, f32[19]{0:T(128)}, u32[]{:S(2)}) copy-start(f32[19]{0:T(128)} %constant.127) | copy-start | bytes 232
  0.7 1.3 %copy-start.6 = (f32[19]{0:T(128)S(1)}, f32[19]{0:T(128)}, u32[]{:S(2)}) copy-start(f32[19]{0:T(128)} %constant.128) | copy-start | bytes 232
  2.0 5.3 %copy-start = (f32[28,4,8,128]{3,2,1,0:T(8,128)S(1)}, f32[28,4,8,128]{3,2,1,0:T(8,128)}, u32[]{:S(2)}) copy-start(f32[28,4,8,128]{3,2,1,0:T(8,128)} %param.22) | copy-start | bytes 1376260
  2.4 11.8 %collective-permute-start = (f32[3,4,8,128]{3,2,1,0:T(8,128)S(1)}, f32[3,4,8,128]{3,2,1,0:T(8,128)S(1)}, u32[]{:S(2)}, u32[]{:S(2)}) collective-permute-start(f32[3,4,8,128]{3,2,1,0:T(8,128)S(1)} %get-tuple-element.54), channel_id=1, source_target_pairs={{0,128},{1,129},{2,130},{3,131},{4,132},{5,133},{6,134},{7,135},{8... | collective-permute-start | bytes 147464 | tf_op jit(solution)/shard_map/ppermute | solution.py:144
  7.4 0.7 %copy-start.3 = (s32[4,8,128]{2,1,0:T(8,128)S(1)}, s32[4,8,128]{2,1,0:T(8,128)}, u32[]{:S(2)}) copy-start(s32[4,8,128]{2,1,0:T(8,128)} %param.23) | copy-start | bytes 49156
  8.2 2.2 %copy-start.13 = (f32[28,1,1,1]{0,3,2,1:T(1,128)S(1)}, f32[28,1,1,1]{0,3,2,1:T(1,128)}, u32[]{:S(2)}) copy-start(f32[28,1,1,1]{0,3,2,1:T(1,128)} %constant.104.clone) | copy-start | bytes 340
  8.2 2.2 %copy-start.14 = (f32[28,1,1,1]{0,3,2,1:T(1,128)S(1)}, f32[28,1,1,1]{0,3,2,1:T(1,128)}, u32[]{:S(2)}) copy-start(f32[28,1,1,1]{0,3,2,1:T(1,128)} %constant.105.clone) | copy-start | bytes 340
  8.2 2.2 %copy-start.15 = (f32[28,1,1,1]{0,3,2,1:T(1,128)S(1)}, f32[28,1,1,1]{0,3,2,1:T(1,128)}, u32[]{:S(2)}) copy-start(f32[28,1,1,1]{0,3,2,1:T(1,128)} %constant.108.clone) | copy-start | bytes 340
  8.2 2.2 %copy-start.16 = (f32[28,1,1,1]{0,3,2,1:T(1,128)S(1)}, f32[28,1,1,1]{0,3,2,1:T(1,128)}, u32[]{:S(2)}) copy-start(f32[28,1,1,1]{0,3,2,1:T(1,128)} %constant.109.clone) | copy-start | bytes 340
  8.3 0.7 copy-start.7
  9.7 0.7 copy-start.18
  10.3 0.7 %copy-start.2 = (f32[19,19,1,1]{0,1,3,2:T(8,128)S(1)}, f32[19,19,1,1]{0,1,3,2:T(8,128)}, u32[]{:S(2)}) copy-start(f32[19,19,1,1]{0,1,3,2:T(8,128)} %constant.133) | copy-start | bytes 4336
  10.5 0.7 copy-start.20
  12.9 1.0 %copy-start.1 = (f32[28,4,8,128]{3,2,1,0:T(8,128)S(1)}, f32[28,4,8,128]{3,2,1,0:T(8,128)}, u32[]{:S(2)}) copy-start(f32[28,4,8,128]{3,2,1,0:T(8,128)} %param.26) | copy-start | bytes 1376260
  14.2 0.7 copy-start.11
  14.2 0.7 copy-start.8
  14.3 0.7 copy-start.9
  14.3 0.7 copy-start.10
  15.6 6.4 %collective-permute-start.1 = (f32[56,4,1,128]{3,0,2,1:T(8,128)S(1)}, f32[56,4,1,128]{3,0,2,1:T(8,128)S(1)}, u32[]{:S(2)}, u32[]{:S(2)}) collective-permute-start(f32[56,4,1,128]{3,0,2,1:T(8,128)S(1)} %get-tuple-element.58), channel_id=1, source_target_pairs={{0,8},{8,16},{16,24},{24,32},{32,40},{40,48},{48,56},{56,64},{64,7... | collective-permute-start | bytes 344072 | tf_op jit(solution)/shard_map/ppermute | solution.py:78
  15.7 6.3 %collective-permute-start.2 = (f32[56,4,1,128]{3,0,2,1:T(8,128)S(1)}, f32[56,4,1,128]{3,0,2,1:T(8,128)S(1)}, u32[]{:S(2)}, u32[]{:S(2)}) collective-permute-start(f32[56,4,1,128]{3,0,2,1:T(8,128)S(1)} %get-tuple-element.57), channel_id=1, source_target_pairs={{0,120},{8,0},{16,8},{24,16},{32,24},{40,32},{48,40},{56,48},{64,5... | collective-permute-start | bytes 344072 | tf_op jit(solution)/shard_map/ppermute | solution.py:79
  23.1 3.8 %collective-permute-start.3 = (f32[56,4,8]{0,2,1:T(8,128)S(1)}, f32[56,4,8]{0,2,1:T(8,128)S(1)}, u32[]{:S(2)}, u32[]{:S(2)}) collective-permute-start(f32[56,4,8]{0,2,1:T(8,128)S(1)} %get-tuple-element.38), channel_id=1, source_target_pairs={{0,1},{1,2},{2,3},{3,4},{4,5},{5,6},{6,7},{7,0},{8,9},{9,10},{10,1... | collective-permute-start | bytes 21512 | tf_op jit(solution)/shard_map/ppermute | solution.py:83
  25.1 3.7 %collective-permute-start.4 = (f32[56,4,8]{0,2,1:T(8,128)S(1)}, f32[56,4,8]{0,2,1:T(8,128)S(1)}, u32[]{:S(2)}, u32[]{:S(2)}) collective-permute-start(f32[56,4,8]{0,2,1:T(8,128)S(1)} %get-tuple-element.39), channel_id=1, source_target_pairs={{0,7},{1,0},{2,1},{3,2},{4,3},{5,4},{6,5},{7,6},{8,15},{9,8},{10,9... | collective-permute-start | bytes 21512 | tf_op jit(solution)/shard_map/ppermute | solution.py:84
  31.3 0.7 copy-start.12
  33.1 2.0 %collective-permute-start.5 = (f32[19]{0:T(128)S(1)}, f32[19]{0:T(128)S(1)}, u32[]{:S(2)}, u32[]{:S(2)}) collective-permute-start(f32[19]{0:T(128)S(1)} %broadcast_select_fusion), channel_id=1, source_target_pairs={{0,8},{8,0},{16,24},{24,16},{32,40},{40,32},{48,56},{56,48},{64,72... | collective-permute-start | bytes 236 | tf_op jit(solution)/shard_map/ppermute | solution.py:123
  35.1 3.6 %collective-permute-start.6 = (f32[19]{0:T(128)S(1)}, f32[19]{0:T(128)S(1)}, u32[]{:S(2)}, u32[]{:S(2)}) collective-permute-start(f32[19]{0:T(128)S(1)} %add.117), channel_id=1, source_target_pairs={{0,16},{8,24},{16,0},{24,8},{32,48},{40,56},{48,32},{56,40},{64,80... | collective-permute-start | bytes 236 | tf_op jit(solution)/shard_map/ppermute | solution.py:123
  39.0 3.6 %collective-permute-start.7 = (f32[19]{0:T(128)S(1)}, f32[19]{0:T(128)S(1)}, u32[]{:S(2)}, u32[]{:S(2)}) collective-permute-start(f32[19]{0:T(128)S(1)} %add.121), channel_id=1, source_target_pairs={{0,32},{8,40},{16,48},{24,56},{32,0},{40,8},{48,16},{56,24},{64,96... | collective-permute-start | bytes 236 | tf_op jit(solution)/shard_map/ppermute | solution.py:123
  42.7 4.8 %collective-permute-start.8 = (f32[19]{0:T(128)S(1)}, f32[19]{0:T(128)S(1)}, u32[]{:S(2)}, u32[]{:S(2)}) collective-permute-start(f32[19]{0:T(128)S(1)} %add.122), channel_id=1, source_target_pairs={{0,96},{8,104},{16,112},{24,120},{32,64},{40,72},{48,80},{56,88},{... | collective-permute-start | bytes 236 | tf_op jit(solution)/shard_map/ppermute | solution.py:123
  47.4 5.9 %collective-permute-start.9 = (f32[4,4,8,128]{3,2,1,0:T(8,128)S(1)}, f32[4,4,8,128]{3,2,1,0:T(8,128)S(1)}, u32[]{:S(2)}, u32[]{:S(2)}) collective-permute-start(f32[4,4,8,128]{3,2,1,0:T(8,128)S(1)} %select_maximum_fusion), channel_id=1, source_target_pairs={{0,128},{128,0},{1,129},{129,1},{2,130},{130,2},{3,131},{131,3},{4... | collective-permute-start | bytes 196616 | tf_op jit(solution)/shard_map/ppermute | solution.py:240
  53.3 3.5 %collective-permute-start.10 = (f32[19]{0:T(128)S(1)}, f32[19]{0:T(128)S(1)}, u32[]{:S(2)}, u32[]{:S(2)}) collective-permute-start(f32[19]{0:T(128)S(1)} %fusion.57), channel_id=1, source_target_pairs={{0,1},{1,0},{2,3},{3,2},{4,5},{5,4},{6,7},{7,6},{8,9},{9,8},{10,11... | collective-permute-start | bytes 236 | tf_op jit(solution)/shard_map/ppermute | solution.py:123
  56.9 7.2 %collective-permute-start.11 = (f32[19]{0:T(128)S(1)}, f32[19]{0:T(128)S(1)}, u32[]{:S(2)}, u32[]{:S(2)}) collective-permute-start(f32[19]{0:T(128)S(1)} %add.125), channel_id=1, source_target_pairs={{0,2},{1,3},{2,0},{3,1},{4,6},{5,7},{6,4},{7,5},{8,10},{9,11},{10,... | collective-permute-start | bytes 236 | tf_op jit(solution)/shard_map/ppermute | solution.py:123
  64.1 5.7 %collective-permute-start.12 = (f32[19]{0:T(128)S(1)}, f32[19]{0:T(128)S(1)}, u32[]{:S(2)}, u32[]{:S(2)}) collective-permute-start(f32[19]{0:T(128)S(1)} %add.132), channel_id=1, source_target_pairs={{0,6},{1,7},{2,4},{3,5},{4,2},{5,3},{6,0},{7,1},{8,14},{9,15},{10,... | collective-permute-start | bytes 236 | tf_op jit(solution)/shard_map/ppermute | solution.py:123
  (2 other events, 1.3 us)

commit v15 on v11

--- a/solution.py
+++ b/solution.py
@@ -232,12 +232,24 @@
         )
         return values
 
-    partial_rates = butterfly_sum(local_rates, (("gy", 4),), [flow_adjoint, species_adjoint])
+    gy_rounds = butterfly_rounds(lax.axis_size("gy"), 4)
+    partial_rates = local_rates
+    for index, targets in enumerate(gy_rounds[:-1]):
+        partial_rates = partial_rates + lax.ppermute(partial_rates, "gy", list(enumerate(targets)))
+        partial_rates = [flow_adjoint, species_adjoint][index](partial_rates) if index < 2 else partial_rates
+    mirror = gy_rounds[-1]
+    count = lax.axis_size("gy")
     plane = populations.shape[1:]
     rate_plane = jnp.zeros(plane, jnp.float32).at[0, 0, : partial_rates.shape[0]].set(partial_rates)
     payload = jnp.concatenate([later["species_motion_grad"], rate_plane[None]])
     other = lax.ppermute(payload, "sec", [(0, 1), (1, 0)])
-    partial_rates = partial_rates + other[3, 0, 0, : partial_rates.shape[0]]
+    across_y = lax.ppermute(partial_rates, "gy", list(enumerate(mirror)))
+    diagonal = lax.ppermute(
+        partial_rates,
+        ("sec", "gy"),
+        [(sec * count + i, (1 - sec) * count + mirror[i]) for sec in range(2) for i in range(count)],
+    )
+    partial_rates = partial_rates + other[3, 0, 0, : partial_rates.shape[0]] + across_y + diagonal
 
     def flow_gradient(values):
         values, received = lax.optimization_barrier((values, other[:3]))

time: 67.7 us -> 68.1 us (level)
  starting transfers between devices: 29 us -> 29.7 us
    ppermute x0 -> x5, waiting for transfers between devices: none -> 7.95 us  [the longest x1 3.83 us: per_device(): lax.ppermute(partial_rates, ('sec', 'gy'), [(sec * count + i, (1 - sec) *...]
    ppermute x0 -> x5, starting transfers between devices: none -> 5.93 us  [the longest x1 3.04 us: per_device(): lax.ppermute(partial_rates, ('sec', 'gy'), [(sec * count + i, (1 - sec) *...]
    ppermute x7 -> x3, waiting for transfers between devices: 10.5 us -> 5.04 us  [butterfly_sum(): values = values + lax.ppermute(values, axis, list(enumerate(targets)))]
    ppermute x7 -> x3, starting transfers between devices: 15.1 us -> 9.81 us  [butterfly_sum(): values = values + lax.ppermute(values, axis, list(enumerate(targets)))]
    ppermute x1, waiting for transfers between devices: 2.74 us -> 0.01 us  [per_device(): other = lax.ppermute(payload, 'sec', [(0, 1), (1, 0)])]
  transfers between devices with their start and end apart: 13 -> 14, of which waited for: 10 -> 10; matrix products, arithmetic and copies ran while one was open for 10% -> 9% of each run, Pallas kernels for 0% -> 0%
where the time goes in v15:
time: 68.1 us; the launch traced here: 67.8 us
  starting transfers between devices  29.7 us (44%)
  waiting for transfers between devices  18.7 us (27%)
  local copies, waits for them, and re-layouts  9.48 us (14%)
  other arithmetic  6.36 us (9%)
  matrix products  2.34 us (3%)
  between operations  1.3 us (2%)
    ppermute x3, starting transfers between devices, butterfly_sum(): values = values + lax.ppermute(values, axis, list(enumerate(targets)))  9.81 us
    unnamed x58, local copies, waits for them, and re-layouts  6.49 us
    ppermute x3, waiting for transfers between devices, butterfly_sum(): values = values + lax.ppermute(values, axis, list(enumerate(targets)))  5.04 us
    ppermute x1, starting transfers between devices, per_device(): sent_motion = lax.ppermute(own_motion, 'sec', [(0, 1)])  4.93 us
    ppermute x1, starting transfers between devices, shift_rows(): high = lax.ppermute(field[:, :, :1, :], 'gy', ring('gy', -1))  3.84 us
    ppermute x1, waiting for transfers between devices, per_device(): lax.ppermute(partial_rates, ('sec', 'gy'), [(sec * count + i, (1 - sec) *...  3.83 us
    ppermute x3, waiting for transfers between devices, per_device(): lax.ppermute(partial_rates, 'gy', list(enumerate(targets)))  3.58 us
    ppermute x1, starting transfers between devices, per_device(): lax.ppermute(partial_rates, ('sec', 'gy'), [(sec * count + i, (1 - sec) *...  3.04 us
  transfers between devices with their start and end apart: 14, of which 10 were waited for; matrix products, arithmetic and copies ran while one was open for 9% of the time, Pallas kernels for 0%

profile of v15, /device:TPU:32, one launch (start us, length us, event | category | flops | bytes accessed | tf_op | source)
XLA Modules:
  0.0 67.8 jit_solution(10777274188267026261)
XLA Ops:
  0.7 1.3 %copy.83 = f32[28,4,8,128]{3,0,2,1:T(8,128)S(1)} copy(f32[28,4,8,128]{3,2,1,0:T(8,128)} %param.22) | data formatting | bytes 917504 | tf_op args[0]
  2.4 4.9 %collective-permute-start = (f32[3,4,8,128]{3,2,1,0:T(8,128)S(1)}, f32[3,4,8,128]{3,2,1,0:T(8,128)S(1)}, u32[]{:S(2)}, u32[]{:S(2)}) collective-permute-start(f32[3,4,8,128]{3,2,1,0:T(8,128)S(1)} %maximum_divide_fusion), channel_id=1, source_target_pairs={{0,128},{1,129},{2,130},{3,131},{4,132},{5,133},{6,134},{7,135},{8... | collective-permute-start | bytes 147464 | tf_op jit(solution)/shard_map/ppermute | solution.py:144
  7.4 0.7 copy-done.3
  10.1 0.7 copy-done.2
  10.7 0.7 %fusion.18 = f32[19,4,8,128]{3,0,2,1:T(8,128)S(1)} fusion(f32[19,19,1,1]{0,1,3,2:T(8,128)S(1)} %copy-done.2, f32[28,4,8,128]{3,0,2,1:T(8,128)S(1)} %copy.83, f32[4,8,128]{2,1,0:T(8,128)S(1)} %broadcast_multiply_fusion.4, f32[4,8,128]{2,1,0:T(8,128)S(1)} %get-tuple-element.116, f32[4,8,128]{2,1,0:T(8,128)S(1)} %get-tuple-element.117, ...), kind=kOutput, calls=%fused_computation.49 | convolution fusion | flops 18833408 | bytes 800768 | tf_op jit(solution)/shard_map/ji,jxyz->ixyz/dot_general | solution.py:167
  11.5 0.6 fusion.1
  12.9 3.8 %collective-permute-start.2 = (f32[56,4,1,128]{3,0,2,1:T(8,128)S(1)}, f32[56,4,1,128]{3,0,2,1:T(8,128)S(1)}, u32[]{:S(2)}, u32[]{:S(2)}) collective-permute-start(f32[56,4,1,128]{3,0,2,1:T(8,128)S(1)} %get-tuple-element.57), channel_id=1, source_target_pairs={{0,120},{8,0},{16,8},{24,16},{32,24},{40,32},{48,40},{56,48},{64,5... | collective-permute-start | bytes 344072 | tf_op jit(solution)/shard_map/ppermute | solution.py:79
  16.8 2.4 %collective-permute-done.1 = f32[56,4,1,128]{3,0,2,1:T(8,128)S(1)} collective-permute-done((f32[56,4,1,128]{3,0,2,1:T(8,128)S(1)}, f32[56,4,1,128]{3,0,2,1:T(8,128)S(1)}, u32[]{:S(2)}, u32[]{:S(2)}) %collective-permute-start.1) | collective-permute-done | bytes 114720 | tf_op jit(solution)/shard_map/ppermute | solution.py:78
  19.5 0.8 %slice_reduce_fusion.2 = (f32[56,4,8]{0,2,1:T(8,128)S(1)}, f32[56,4,8]{0,2,1:T(8,128)S(1)}, f32[56,4,8,1]{3,0,2,1:T(8,128)S(1)}, f32[56,4,8,1]{3,0,2,1:T(8,128)S(1)}) fusion(f32[56,4,8,128]{3,0,2,1:T(8,128)S(1)} %fusion.3), kind=kLoop, calls=%fused_computation.164 | loop fusion | bytes 43008 | tf_op jit(solution)/shard_map/slice | solution.py:83
  20.3 2.0 %collective-permute-start.3 = (f32[56,4,8]{0,2,1:T(8,128)S(1)}, f32[56,4,8]{0,2,1:T(8,128)S(1)}, u32[]{:S(2)}, u32[]{:S(2)}) collective-permute-start(f32[56,4,8]{0,2,1:T(8,128)S(1)} %get-tuple-element.38), channel_id=1, source_target_pairs={{0,1},{1,2},{2,3},{3,4},{4,5},{5,6},{6,7},{7,0},{8,9},{9,10},{10,1... | collective-permute-start | bytes 21512 | tf_op jit(solution)/shard_map/ppermute | solution.py:83
  22.7 1.4 %collective-permute-done.3 = f32[56,4,8]{0,2,1:T(8,128)S(1)} collective-permute-done((f32[56,4,8]{0,2,1:T(8,128)S(1)}, f32[56,4,8]{0,2,1:T(8,128)S(1)}, u32[]{:S(2)}, u32[]{:S(2)}) %collective-permute-start.3) | collective-permute-done | bytes 7200 | tf_op jit(solution)/shard_map/ppermute | solution.py:83
  24.1 1.9 %collective-permute-done.4 = f32[56,4,8]{0,2,1:T(8,128)S(1)} collective-permute-done((f32[56,4,8]{0,2,1:T(8,128)S(1)}, f32[56,4,8]{0,2,1:T(8,128)S(1)}, u32[]{:S(2)}, u32[]{:S(2)}) %collective-permute-start.4) | collective-permute-done | bytes 7200 | tf_op jit(solution)/shard_map/ppermute | solution.py:84
  26.0 1.2 %fusion.4 = f32[56,4,8,128]{3,0,2,1:T(8,128)S(1)} fusion(f32[56,4,8,127]{3,0,2,1:T(8,128)S(1)} %get-tuple-element.88, f32[56,4,8,1]{3,0,2,1:T(8,128)S(1)} %get-tuple-element.86, f32[56,4,8,128]{3,0,2,1:T(8,128)S(1)} %fusion.3, f32[56,4,8,1]{3,0,2,1:T(8,128)S(1)} %get-tuple-element.85, f32[56,4,8,127]{3,0,2,1:T(8,128)S(1)} %get-tuple-element.87, ...), kind=kLoop, calls=%fused_computation.15 | loop fusion | flops 1376256 | bytes 3684720 | tf_op jit(solution)/shard_map/jit(_where)/select_n | solution.py:88
  28.6 0.6 copy-done.12
  29.2 0.8 %fusion.73 = (f32[28,4,8,128]{3,0,2,1:T(8,128)S(1)}, f32[28]{0:T(128)S(1)}, f32[28,4,8,128]{3,0,2,1:T(8,128)S(1)}) fusion(f32[56,4,8,128]{3,0,2,1:T(8,128)S(1)} %maximum_select_fusion.2, f32[28,4,8,128]{3,2,1,0:T(8,128)S(1)} %bitcast.100, f32[28,4,8,128]{3,2,1,0:T(8,128)S(1)} %copy-done, pred[4,8,128]{2,1,0:T(8,128)(4,1)S(1)} %broadcast_compare_fusion, ...), kind=kLoop, calls=%fused_computation.166 | loop fusion | flops 688100 | bytes 2756749 | tf_op jit(solution)/shard_map/slice | solution.py:181
  30.8 1.0 %copy.111 = f32[28,4,8,128]{3,2,1,0:T(8,128)} copy(f32[28,4,8,128]{3,0,2,1:T(8,128)S(1)} %get-tuple-element.80) | data formatting | bytes 917504
  32.4 0.8 %collective-permute-start.6 = (f32[19]{0:T(128)S(1)}, f32[19]{0:T(128)S(1)}, u32[]{:S(2)}, u32[]{:S(2)}) collective-permute-start(f32[19]{0:T(128)S(1)} %add.120), channel_id=1, source_target_pairs={{0,16},{8,24},{16,0},{24,8},{32,48},{40,56},{48,32},{56,40},{64,80... | collective-permute-start | bytes 236 | tf_op jit(solution)/shard_map/ppermute | solution.py:238
  33.1 0.6 add_multiply_fusion
  34.3 1.6 %collective-permute-done.6 = f32[19]{0:T(128)S(1)} collective-permute-done((f32[19]{0:T(128)S(1)}, f32[19]{0:T(128)S(1)}, u32[]{:S(2)}, u32[]{:S(2)}) %collective-permute-start.6) | collective-permute-done | bytes 108 | tf_op jit(solution)/shard_map/ppermute | solution.py:238
  36.3 1.6 %collective-permute-start.7 = (f32[19]{0:T(128)S(1)}, f32[19]{0:T(128)S(1)}, u32[]{:S(2)}, u32[]{:S(2)}) collective-permute-start(f32[19]{0:T(128)S(1)} %add.124), channel_id=1, source_target_pairs={{0,32},{8,40},{16,48},{24,56},{32,0},{40,8},{48,16},{56,24},{64,96... | collective-permute-start | bytes 236 | tf_op jit(solution)/shard_map/ppermute | solution.py:238
  38.0 1.9 %collective-permute-done.7 = f32[19]{0:T(128)S(1)} collective-permute-done((f32[19]{0:T(128)S(1)}, f32[19]{0:T(128)S(1)}, u32[]{:S(2)}, u32[]{:S(2)}) %collective-permute-start.7) | collective-permute-done | bytes 108 | tf_op jit(solution)/shard_map/ppermute | solution.py:238
  39.9 3.0 %collective-permute-start.8 = (f32[4,4,8,128]{3,2,1,0:T(8,128)S(1)}, f32[4,4,8,128]{3,2,1,0:T(8,128)S(1)}, u32[]{:S(2)}, u32[]{:S(2)}) collective-permute-start(f32[4,4,8,128]{3,2,1,0:T(8,128)S(1)} %select_maximum_fusion), channel_id=1, source_target_pairs={{0,128},{128,0},{1,129},{129,1},{2,130},{130,2},{3,131},{131,3},{4... | collective-permute-start | bytes 196616 | tf_op jit(solution)/shard_map/ppermute | solution.py:245
  43.0 3.0 %collective-permute-start.10 = (f32[19]{0:T(128)S(1)}, f32[19]{0:T(128)S(1)}, u32[]{:S(2)}, u32[]{:S(2)}) collective-permute-start(f32[19]{0:T(128)S(1)} %add.125), channel_id=1, source_target_pairs={{0,224},{8,232},{16,240},{24,248},{32,192},{40,200},{48,208},{56,2... | collective-permute-start | bytes 236 | tf_op jit(solution)/shard_map/ppermute | solution.py:247
  46.4 3.8 %collective-permute-done.10 = f32[19]{0:T(128)S(1)} collective-permute-done((f32[19]{0:T(128)S(1)}, f32[19]{0:T(128)S(1)}, u32[]{:S(2)}, u32[]{:S(2)}) %collective-permute-start.10) | collective-permute-done | bytes 108 | tf_op jit(solution)/shard_map/ppermute | solution.py:247
  50.3 0.5 collective-permute-done.9
  50.8 2.1 %collective-permute-start.11 = (f32[19]{0:T(128)S(1)}, f32[19]{0:T(128)S(1)}, u32[]{:S(2)}, u32[]{:S(2)}) collective-permute-start(f32[19]{0:T(128)S(1)} %fusion.59), channel_id=1, source_target_pairs={{0,1},{1,0},{2,3},{3,2},{4,5},{5,4},{6,7},{7,6},{8,9},{9,8},{10,11... | collective-permute-start | bytes 236 | tf_op jit(solution)/shard_map/ppermute | solution.py:123
  53.0 1.5 %collective-permute-done.11 = f32[19]{0:T(128)S(1)} collective-permute-done((f32[19]{0:T(128)S(1)}, f32[19]{0:T(128)S(1)}, u32[]{:S(2)}, u32[]{:S(2)}) %collective-permute-start.11) | collective-permute-done | bytes 108 | tf_op jit(solution)/shard_map/ppermute | solution.py:123
  54.5 5.7 %collective-permute-start.12 = (f32[19]{0:T(128)S(1)}, f32[19]{0:T(128)S(1)}, u32[]{:S(2)}, u32[]{:S(2)}) collective-permute-start(f32[19]{0:T(128)S(1)} %add.129), channel_id=1, source_target_pairs={{0,2},{1,3},{2,0},{3,1},{4,6},{5,7},{6,4},{7,5},{8,10},{9,11},{10,... | collective-permute-start | bytes 236 | tf_op jit(solution)/shard_map/ppermute | solution.py:123
  60.7 0.9 %collective-permute-done.12 = f32[19]{0:T(128)S(1)} collective-permute-done((f32[19]{0:T(128)S(1)}, f32[19]{0:T(128)S(1)}, u32[]{:S(2)}, u32[]{:S(2)}) %collective-permute-start.12) | collective-permute-done | bytes 108 | tf_op jit(solution)/shard_map/ppermute | solution.py:123
  61.7 2.0 %collective-permute-start.13 = (f32[19]{0:T(128)S(1)}, f32[19]{0:T(128)S(1)}, u32[]{:S(2)}, u32[]{:S(2)}) collective-permute-start(f32[19]{0:T(128)S(1)} %add.136), channel_id=1, source_target_pairs={{0,6},{1,7},{2,4},{3,5},{4,2},{5,3},{6,0},{7,1},{8,14},{9,15},{10,... | collective-permute-start | bytes 236 | tf_op jit(solution)/shard_map/ppermute | solution.py:123
  63.7 1.0 %copy.112 = f32[28,4,8,128]{3,2,1,0:T(8,128)} copy(f32[28,4,8,128]{3,0,2,1:T(8,128)S(1)} %copy_select_fusion) | data formatting | bytes 917504
  64.7 2.6 %collective-permute-done.13 = f32[19]{0:T(128)S(1)} collective-permute-done((f32[19]{0:T(128)S(1)}, f32[19]{0:T(128)S(1)}, u32[]{:S(2)}, u32[]{:S(2)}) %collective-permute-start.13) | collective-permute-done | bytes 108 | tf_op jit(solution)/shard_map/ppermute | solution.py:123
  (121 shorter events, 9.0 us)
Async XLA Ops:
  0.6 1.3 %copy-start.4 = (f32[19]{0:T(128)S(1)}, f32[19]{0:T(128)}, u32[]{:S(2)}) copy-start(f32[19]{0:T(128)} %constant.126) | copy-start | bytes 232
  0.6 1.3 %copy-start.5 = (f32[19]{0:T(128)S(1)}, f32[19]{0:T(128)}, u32[]{:S(2)}) copy-start(f32[19]{0:T(128)} %constant.127) | copy-start | bytes 232
  0.7 1.3 %copy-start.6 = (f32[19]{0:T(128)S(1)}, f32[19]{0:T(128)}, u32[]{:S(2)}) copy-start(f32[19]{0:T(128)} %constant.128) | copy-start | bytes 232
  2.0 5.3 %copy-start = (f32[28,4,8,128]{3,2,1,0:T(8,128)S(1)}, f32[28,4,8,128]{3,2,1,0:T(8,128)}, u32[]{:S(2)}) copy-start(f32[28,4,8,128]{3,2,1,0:T(8,128)} %param.22) | copy-start | bytes 1376260
  2.4 7.6 %collective-permute-start = (f32[3,4,8,128]{3,2,1,0:T(8,128)S(1)}, f32[3,4,8,128]{3,2,1,0:T(8,128)S(1)}, u32[]{:S(2)}, u32[]{:S(2)}) collective-permute-start(f32[3,4,8,128]{3,2,1,0:T(8,128)S(1)} %maximum_divide_fusion), channel_id=1, source_target_pairs={{0,128},{1,129},{2,130},{3,131},{4,132},{5,133},{6,134},{7,135},{8... | collective-permute-start | bytes 147464 | tf_op jit(solution)/shard_map/ppermute | solution.py:144
  7.3 0.7 %copy-start.3 = (s32[4,8,128]{2,1,0:T(8,128)S(1)}, s32[4,8,128]{2,1,0:T(8,128)}, u32[]{:S(2)}) copy-start(s32[4,8,128]{2,1,0:T(8,128)} %param.23) | copy-start | bytes 49156
  8.1 0.7 copy-start.17
  8.1 0.7 copy-start.18
  8.1 0.7 %copy-start.13 = (f32[28,1,1,1]{0,3,2,1:T(1,128)S(1)}, f32[28,1,1,1]{0,3,2,1:T(1,128)}, u32[]{:S(2)}) copy-start(f32[28,1,1,1]{0,3,2,1:T(1,128)} %constant.104.clone) | copy-start | bytes 340
  8.1 0.7 %copy-start.14 = (f32[28,1,1,1]{0,3,2,1:T(1,128)S(1)}, f32[28,1,1,1]{0,3,2,1:T(1,128)}, u32[]{:S(2)}) copy-start(f32[28,1,1,1]{0,3,2,1:T(1,128)} %constant.105.clone) | copy-start | bytes 340
  8.1 0.7 %copy-start.15 = (f32[28,1,1,1]{0,3,2,1:T(1,128)S(1)}, f32[28,1,1,1]{0,3,2,1:T(1,128)}, u32[]{:S(2)}) copy-start(f32[28,1,1,1]{0,3,2,1:T(1,128)} %constant.108.clone) | copy-start | bytes 340
  8.2 0.7 %copy-start.16 = (f32[28,1,1,1]{0,3,2,1:T(1,128)S(1)}, f32[28,1,1,1]{0,3,2,1:T(1,128)}, u32[]{:S(2)}) copy-start(f32[28,1,1,1]{0,3,2,1:T(1,128)} %constant.109.clone) | copy-start | bytes 340
  8.2 0.9 %copy-start.19 = (f32[15]{0:T(128)S(1)}, f32[15]{0:T(128)}, u32[]{:S(2)}) copy-start(f32[15]{0:T(128)} %param.24) | copy-start | bytes 184
  8.2 1.0 %copy-start.1 = (f32[28,4,8,128]{3,2,1,0:T(8,128)S(1)}, f32[28,4,8,128]{3,2,1,0:T(8,128)}, u32[]{:S(2)}) copy-start(f32[28,4,8,128]{3,2,1,0:T(8,128)} %param.26) | copy-start | bytes 1376260
  10.0 0.7 %copy-start.2 = (f32[19,19,1,1]{0,1,3,2:T(8,128)S(1)}, f32[19,19,1,1]{0,1,3,2:T(8,128)}, u32[]{:S(2)}) copy-start(f32[19,19,1,1]{0,1,3,2:T(8,128)} %constant.133) | copy-start | bytes 4336
  10.1 0.7 %copy-start.20 = (f32[19]{0:T(128)S(1)}, f32[19]{0:T(128)}, u32[]{:S(2)}) copy-start(f32[19]{0:T(128)} %constant.125) | copy-start | bytes 232
  11.5 0.7 copy-start.9
  11.5 0.7 copy-start.10
  11.5 0.7 copy-start.11
  12.8 6.4 %collective-permute-start.1 = (f32[56,4,1,128]{3,0,2,1:T(8,128)S(1)}, f32[56,4,1,128]{3,0,2,1:T(8,128)S(1)}, u32[]{:S(2)}, u32[]{:S(2)}) collective-permute-start(f32[56,4,1,128]{3,0,2,1:T(8,128)S(1)} %get-tuple-element.58), channel_id=1, source_target_pairs={{0,8},{8,16},{16,24},{24,32},{32,40},{40,48},{48,56},{56,64},{64,7... | collective-permute-start | bytes 344072 | tf_op jit(solution)/shard_map/ppermute | solution.py:78
  12.9 6.3 %collective-permute-start.2 = (f32[56,4,1,128]{3,0,2,1:T(8,128)S(1)}, f32[56,4,1,128]{3,0,2,1:T(8,128)S(1)}, u32[]{:S(2)}, u32[]{:S(2)}) collective-permute-start(f32[56,4,1,128]{3,0,2,1:T(8,128)S(1)} %get-tuple-element.57), channel_id=1, source_target_pairs={{0,120},{8,0},{16,8},{24,16},{32,24},{40,32},{48,40},{56,48},{64,5... | collective-permute-start | bytes 344072 | tf_op jit(solution)/shard_map/ppermute | solution.py:79
  20.3 3.8 %collective-permute-start.3 = (f32[56,4,8]{0,2,1:T(8,128)S(1)}, f32[56,4,8]{0,2,1:T(8,128)S(1)}, u32[]{:S(2)}, u32[]{:S(2)}) collective-permute-start(f32[56,4,8]{0,2,1:T(8,128)S(1)} %get-tuple-element.38), channel_id=1, source_target_pairs={{0,1},{1,2},{2,3},{3,4},{4,5},{5,6},{6,7},{7,0},{8,9},{9,10},{10,1... | collective-permute-start | bytes 21512 | tf_op jit(solution)/shard_map/ppermute | solution.py:83
  22.3 3.7 %collective-permute-start.4 = (f32[56,4,8]{0,2,1:T(8,128)S(1)}, f32[56,4,8]{0,2,1:T(8,128)S(1)}, u32[]{:S(2)}, u32[]{:S(2)}) collective-permute-start(f32[56,4,8]{0,2,1:T(8,128)S(1)} %get-tuple-element.39), channel_id=1, source_target_pairs={{0,7},{1,0},{2,1},{3,2},{4,3},{5,4},{6,5},{7,6},{8,15},{9,8},{10,9... | collective-permute-start | bytes 21512 | tf_op jit(solution)/shard_map/ppermute | solution.py:84
  30.3 2.0 %collective-permute-start.5 = (f32[19]{0:T(128)S(1)}, f32[19]{0:T(128)S(1)}, u32[]{:S(2)}, u32[]{:S(2)}) collective-permute-start(f32[19]{0:T(128)S(1)} %broadcast_select_fusion.1), channel_id=1, source_target_pairs={{0,8},{8,0},{16,24},{24,16},{32,40},{40,32},{48,56},{56,48},{64,72... | collective-permute-start | bytes 236 | tf_op jit(solution)/shard_map/ppermute | solution.py:238
  32.4 3.6 %collective-permute-start.6 = (f32[19]{0:T(128)S(1)}, f32[19]{0:T(128)S(1)}, u32[]{:S(2)}, u32[]{:S(2)}) collective-permute-start(f32[19]{0:T(128)S(1)} %add.120), channel_id=1, source_target_pairs={{0,16},{8,24},{16,0},{24,8},{32,48},{40,56},{48,32},{56,40},{64,80... | collective-permute-start | bytes 236 | tf_op jit(solution)/shard_map/ppermute | solution.py:238
  36.3 3.6 %collective-permute-start.7 = (f32[19]{0:T(128)S(1)}, f32[19]{0:T(128)S(1)}, u32[]{:S(2)}, u32[]{:S(2)}) collective-permute-start(f32[19]{0:T(128)S(1)} %add.124), channel_id=1, source_target_pairs={{0,32},{8,40},{16,48},{24,56},{32,0},{40,8},{48,16},{56,24},{64,96... | collective-permute-start | bytes 236 | tf_op jit(solution)/shard_map/ppermute | solution.py:238
  39.9 10.9 %collective-permute-start.8 = (f32[4,4,8,128]{3,2,1,0:T(8,128)S(1)}, f32[4,4,8,128]{3,2,1,0:T(8,128)S(1)}, u32[]{:S(2)}, u32[]{:S(2)}) collective-permute-start(f32[4,4,8,128]{3,2,1,0:T(8,128)S(1)} %select_maximum_fusion), channel_id=1, source_target_pairs={{0,128},{128,0},{1,129},{129,1},{2,130},{130,2},{3,131},{131,3},{4... | collective-permute-start | bytes 196616 | tf_op jit(solution)/shard_map/ppermute | solution.py:245
  43.0 7.2 %collective-permute-start.10 = (f32[19]{0:T(128)S(1)}, f32[19]{0:T(128)S(1)}, u32[]{:S(2)}, u32[]{:S(2)}) collective-permute-start(f32[19]{0:T(128)S(1)} %add.125), channel_id=1, source_target_pairs={{0,224},{8,232},{16,240},{24,248},{32,192},{40,200},{48,208},{56,2... | collective-permute-start | bytes 236 | tf_op jit(solution)/shard_map/ppermute | solution.py:247
  46.1 4.8 %collective-permute-start.9 = (f32[19]{0:T(128)S(1)}, f32[19]{0:T(128)S(1)}, u32[]{:S(2)}, u32[]{:S(2)}) collective-permute-start(f32[19]{0:T(128)S(1)} %add.125), channel_id=1, source_target_pairs={{0,96},{8,104},{16,112},{24,120},{32,64},{40,72},{48,80},{56,88},{... | collective-permute-start | bytes 236 | tf_op jit(solution)/shard_map/ppermute | solution.py:246
  50.8 3.6 %collective-permute-start.11 = (f32[19]{0:T(128)S(1)}, f32[19]{0:T(128)S(1)}, u32[]{:S(2)}, u32[]{:S(2)}) collective-permute-start(f32[19]{0:T(128)S(1)} %fusion.59), channel_id=1, source_target_pairs={{0,1},{1,0},{2,3},{3,2},{4,5},{5,4},{6,7},{7,6},{8,9},{9,8},{10,11... | collective-permute-start | bytes 236 | tf_op jit(solution)/shard_map/ppermute | solution.py:123
  54.5 7.2 %collective-permute-start.12 = (f32[19]{0:T(128)S(1)}, f32[19]{0:T(128)S(1)}, u32[]{:S(2)}, u32[]{:S(2)}) collective-permute-start(f32[19]{0:T(128)S(1)} %add.129), channel_id=1, source_target_pairs={{0,2},{1,3},{2,0},{3,1},{4,6},{5,7},{6,4},{7,5},{8,10},{9,11},{10,... | collective-permute-start | bytes 236 | tf_op jit(solution)/shard_map/ppermute | solution.py:123
  61.7 5.7 %collective-permute-start.13 = (f32[19]{0:T(128)S(1)}, f32[19]{0:T(128)S(1)}, u32[]{:S(2)}, u32[]{:S(2)}) collective-permute-start(f32[19]{0:T(128)S(1)} %add.136), channel_id=1, source_target_pairs={{0,6},{1,7},{2,4},{3,5},{4,2},{5,3},{6,0},{7,1},{8,14},{9,15},{10,... | collective-permute-start | bytes 236 | tf_op jit(solution)/shard_map/ppermute | solution.py:123
  (3 other events, 2.0 us)

commit v16 on v11

--- a/solution.py
+++ b/solution.py
@@ -80,9 +80,11 @@
     from_low = jnp.concatenate([low, field[:, :, : size_y - 1, :]], axis=2)
     from_high = jnp.concatenate([field[:, :, 1:, :], high], axis=2)
     field = jnp.where(move_y > 0, from_low, jnp.where(move_y < 0, from_high, field))
-    low = lax.ppermute(field[:, :, :, size_z - 1], "gz", ring("gz", 1))
-    high = lax.ppermute(field[:, :, :, 0], "gz", ring("gz", -1))
     lane = lax.broadcasted_iota(jnp.int32, field.shape, 3)
+    last = jnp.sum(jnp.where(lane == size_z - 1, field, 0.0), axis=3)
+    first = jnp.sum(jnp.where(lane == 0, field, 0.0), axis=3)
+    low = lax.ppermute(last, "gz", ring("gz", 1))
+    high = lax.ppermute(first, "gz", ring("gz", -1))
     from_low = jnp.where(lane == 0, low[..., None], jnp.roll(field, 1, axis=3))
     from_high = jnp.where(lane == size_z - 1, high[..., None], jnp.roll(field, -1, axis=3))
     field = jnp.where(move_z > 0, from_low, jnp.where(move_z < 0, from_high, field))

time: 67.7 us -> 67.7 us (level)
    slice x1 -> x0, local copies, waits for them, and re-layouts: 0.81 us -> none  [shift_rows(): low = lax.ppermute(field[:, :, :, size_z - 1], 'gz', ring('gz', 1))]
    reduce_sum x0 -> x1, other arithmetic: none -> 0.69 us  [shift_rows(): last = jnp.sum(jnp.where(lane == size_z - 1, field, 0.0), axis=3)]
where the time goes in v16:
time: 67.7 us; the launch traced here: 67.4 us
  starting transfers between devices  29 us (43%)
  waiting for transfers between devices  19 us (28%)
  local copies, waits for them, and re-layouts  8.98 us (13%)
  other arithmetic  6.83 us (10%)
  matrix products  2.34 us (3%)
  between operations  1.28 us (2%)
    ppermute x7, starting transfers between devices, butterfly_sum(): values = values + lax.ppermute(values, axis, list(enumerate(targets)))  15.1 us
    ppermute x7, waiting for transfers between devices, butterfly_sum(): values = values + lax.ppermute(values, axis, list(enumerate(targets)))  10.5 us
    unnamed x58, local copies, waits for them, and re-layouts  6.49 us
    ppermute x1, starting transfers between devices, per_device(): sent_motion = lax.ppermute(own_motion, 'sec', [(0, 1)])  4.93 us
    ppermute x1, starting transfers between devices, shift_rows(): high = lax.ppermute(field[:, :, :1, :], 'gy', ring('gy', -1))  3.84 us
    ppermute x1, starting transfers between devices, per_device(): other = lax.ppermute(payload, 'sec', [(0, 1), (1, 0)])  2.96 us
    ppermute x1, waiting for transfers between devices, per_device(): other = lax.ppermute(payload, 'sec', [(0, 1), (1, 0)])  2.74 us
    ppermute x1, waiting for transfers between devices, shift_rows(): low = lax.ppermute(field[:, :, size_y - 1:, :], 'gy', ring('gy', 1))  2.36 us
  transfers between devices with their start and end apart: 13, of which 10 were waited for; matrix products, arithmetic and copies ran while one was open for 10% of the time, Pallas kernels for 0%

profile of v16, /device:TPU:32, one launch (start us, length us, event | category | flops | bytes accessed | tf_op | source)
XLA Modules:
  0.0 67.4 jit_solution(11322032637156616013)
XLA Ops:
  0.7 1.3 %copy.83 = f32[28,4,8,128]{3,0,2,1:T(8,128)S(1)} copy(f32[28,4,8,128]{3,2,1,0:T(8,128)} %param.22) | data formatting | bytes 917504 | tf_op args[0]
  2.4 4.9 %collective-permute-start = (f32[3,4,8,128]{3,2,1,0:T(8,128)S(1)}, f32[3,4,8,128]{3,2,1,0:T(8,128)S(1)}, u32[]{:S(2)}, u32[]{:S(2)}) collective-permute-start(f32[3,4,8,128]{3,2,1,0:T(8,128)S(1)} %maximum_divide_fusion), channel_id=1, source_target_pairs={{0,128},{1,129},{2,130},{3,131},{4,132},{5,133},{6,134},{7,135},{8... | collective-permute-start | bytes 147464 | tf_op jit(solution)/shard_map/ppermute | solution.py:146
  7.4 0.7 copy-done.3
  10.1 0.7 copy-done.2
  10.7 0.7 %fusion.18 = f32[19,4,8,128]{3,0,2,1:T(8,128)S(1)} fusion(f32[19,19,1,1]{0,1,3,2:T(8,128)S(1)} %copy-done.2, f32[28,4,8,128]{3,0,2,1:T(8,128)S(1)} %copy.83, f32[4,8,128]{2,1,0:T(8,128)S(1)} %broadcast_multiply_fusion.4, f32[4,8,128]{2,1,0:T(8,128)S(1)} %get-tuple-element.117, f32[4,8,128]{2,1,0:T(8,128)S(1)} %get-tuple-element.118, ...), kind=kOutput, calls=%fused_computation.51 | convolution fusion | flops 18833408 | bytes 800768 | tf_op jit(solution)/shard_map/ji,jxyz->ixyz/dot_general | solution.py:169
  11.5 0.6 fusion.1
  12.9 3.8 %collective-permute-start.2 = (f32[56,4,1,128]{3,0,2,1:T(8,128)S(1)}, f32[56,4,1,128]{3,0,2,1:T(8,128)S(1)}, u32[]{:S(2)}, u32[]{:S(2)}) collective-permute-start(f32[56,4,1,128]{3,0,2,1:T(8,128)S(1)} %get-tuple-element.57), channel_id=1, source_target_pairs={{0,120},{8,0},{16,8},{24,16},{32,24},{40,32},{48,40},{56,48},{64,5... | collective-permute-start | bytes 344072 | tf_op jit(solution)/shard_map/ppermute | solution.py:79
  16.8 2.4 %collective-permute-done.1 = f32[56,4,1,128]{3,0,2,1:T(8,128)S(1)} collective-permute-done((f32[56,4,1,128]{3,0,2,1:T(8,128)S(1)}, f32[56,4,1,128]{3,0,2,1:T(8,128)S(1)}, u32[]{:S(2)}, u32[]{:S(2)}) %collective-permute-start.1) | collective-permute-done | bytes 114720 | tf_op jit(solution)/shard_map/ppermute | solution.py:78
  19.2 0.7 %select_reduce_fusion.1 = (f32[56,4,8]{0,2,1:T(8,128)S(1)}, f32[56,4,8]{0,2,1:T(8,128)S(1)}, f32[56,4,8,128]{3,0,2,1:T(8,128)S(1)}) fusion(pred[128]{0:T(512)(128)(4,1)S(1)} %get-tuple-element.136, pred[128]{0:T(512)(128)(4,1)S(1)} %get-tuple-element.137, f32[28,4,8,128]{3,0,2,1:T(8,128)S(1)} %copy.105, f32[28,4,8,128]{3,0,2,1:T(8,128)S(1)} %copy_select_fusion.1, ...), kind=kLoop, calls=%fused_computation.21 | loop fusion | flops 2060800 | bytes 3684720 | tf_op jit(solution)/shard_map/reduce_sum | solution.py:84
  20.2 2.0 %collective-permute-start.3 = (f32[56,4,8]{0,2,1:T(8,128)S(1)}, f32[56,4,8]{0,2,1:T(8,128)S(1)}, u32[]{:S(2)}, u32[]{:S(2)}) collective-permute-start(f32[56,4,8]{0,2,1:T(8,128)S(1)} %get-tuple-element.38), channel_id=1, source_target_pairs={{0,1},{1,2},{2,3},{3,4},{4,5},{5,6},{6,7},{7,0},{8,9},{9,10},{10,1... | collective-permute-start | bytes 21512 | tf_op jit(solution)/shard_map/ppermute | solution.py:86
  22.6 1.4 %collective-permute-done.3 = f32[56,4,8]{0,2,1:T(8,128)S(1)} collective-permute-done((f32[56,4,8]{0,2,1:T(8,128)S(1)}, f32[56,4,8]{0,2,1:T(8,128)S(1)}, u32[]{:S(2)}, u32[]{:S(2)}) %collective-permute-start.3) | collective-permute-done | bytes 7200 | tf_op jit(solution)/shard_map/ppermute | solution.py:86
  24.0 1.9 %collective-permute-done.4 = f32[56,4,8]{0,2,1:T(8,128)S(1)} collective-permute-done((f32[56,4,8]{0,2,1:T(8,128)S(1)}, f32[56,4,8]{0,2,1:T(8,128)S(1)}, u32[]{:S(2)}, u32[]{:S(2)}) %collective-permute-start.4) | collective-permute-done | bytes 7200 | tf_op jit(solution)/shard_map/ppermute | solution.py:87
  25.9 1.2 %fusion.4 = f32[56,4,8,128]{3,0,2,1:T(8,128)S(1)} fusion(f32[56,4,8,127]{3,0,2,1:T(8,128)S(1)} %get-tuple-element.87, f32[56,4,8,1]{3,0,2,1:T(8,128)S(1)} %get-tuple-element.89, f32[56,4,8,128]{3,0,2,1:T(8,128)S(1)} %get-tuple-element.53, f32[56,4,8,1]{3,0,2,1:T(8,128)S(1)} %get-tuple-element.88, f32[56,4,8,127]{3,0,2,1:T(8,128)S(1)} %get-tuple-element.86, ...), kind=kLoop, calls=%fused_computation.15 | loop fusion | flops 1376256 | bytes 3684720 | tf_op jit(solution)/shard_map/jit(_where)/select_n | solution.py:90
  28.5 0.6 copy-done.12
  29.2 0.8 %fusion.72 = (f32[28,4,8,128]{3,0,2,1:T(8,128)S(1)}, f32[28]{0:T(128)S(1)}, f32[28,4,8,128]{3,0,2,1:T(8,128)S(1)}) fusion(f32[56,4,8,128]{3,0,2,1:T(8,128)S(1)} %maximum_select_fusion.2, f32[28,4,8,128]{3,2,1,0:T(8,128)S(1)} %bitcast.96, f32[28,4,8,128]{3,2,1,0:T(8,128)S(1)} %copy-done, pred[4,8,128]{2,1,0:T(8,128)(4,1)S(1)} %broadcast_compare_fusion, ...), kind=kLoop, calls=%fused_computation.164 | loop fusion | flops 688100 | bytes 2756749 | tf_op jit(solution)/shard_map/slice | solution.py:183
  30.8 1.0 %copy.111 = f32[28,4,8,128]{3,2,1,0:T(8,128)} copy(f32[28,4,8,128]{3,0,2,1:T(8,128)S(1)} %get-tuple-element.81) | data formatting | bytes 917504
  32.3 0.8 %collective-permute-start.6 = (f32[19]{0:T(128)S(1)}, f32[19]{0:T(128)S(1)}, u32[]{:S(2)}, u32[]{:S(2)}) collective-permute-start(f32[19]{0:T(128)S(1)} %add.117), channel_id=1, source_target_pairs={{0,16},{8,24},{16,0},{24,8},{32,48},{40,56},{48,32},{56,40},{64,80... | collective-permute-start | bytes 236 | tf_op jit(solution)/shard_map/ppermute | solution.py:125
  33.1 0.6 add_multiply_fusion
  34.3 1.6 %collective-permute-done.6 = f32[19]{0:T(128)S(1)} collective-permute-done((f32[19]{0:T(128)S(1)}, f32[19]{0:T(128)S(1)}, u32[]{:S(2)}, u32[]{:S(2)}) %collective-permute-start.6) | collective-permute-done | bytes 108 | tf_op jit(solution)/shard_map/ppermute | solution.py:125
  36.2 1.6 %collective-permute-start.7 = (f32[19]{0:T(128)S(1)}, f32[19]{0:T(128)S(1)}, u32[]{:S(2)}, u32[]{:S(2)}) collective-permute-start(f32[19]{0:T(128)S(1)} %add.121), channel_id=1, source_target_pairs={{0,32},{8,40},{16,48},{24,56},{32,0},{40,8},{48,16},{56,24},{64,96... | collective-permute-start | bytes 236 | tf_op jit(solution)/shard_map/ppermute | solution.py:125
  37.9 2.0 %collective-permute-done.7 = f32[19]{0:T(128)S(1)} collective-permute-done((f32[19]{0:T(128)S(1)}, f32[19]{0:T(128)S(1)}, u32[]{:S(2)}, u32[]{:S(2)}) %collective-permute-start.7) | collective-permute-done | bytes 108 | tf_op jit(solution)/shard_map/ppermute | solution.py:125
  39.9 2.9 %collective-permute-start.8 = (f32[19]{0:T(128)S(1)}, f32[19]{0:T(128)S(1)}, u32[]{:S(2)}, u32[]{:S(2)}) collective-permute-start(f32[19]{0:T(128)S(1)} %add.122), channel_id=1, source_target_pairs={{0,96},{8,104},{16,112},{24,120},{32,64},{40,72},{48,80},{56,88},{... | collective-permute-start | bytes 236 | tf_op jit(solution)/shard_map/ppermute | solution.py:125
  42.7 1.9 %collective-permute-done.8 = f32[19]{0:T(128)S(1)} collective-permute-done((f32[19]{0:T(128)S(1)}, f32[19]{0:T(128)S(1)}, u32[]{:S(2)}, u32[]{:S(2)}) %collective-permute-start.8) | collective-permute-done | bytes 108 | tf_op jit(solution)/shard_map/ppermute | solution.py:125
  44.6 3.0 %collective-permute-start.9 = (f32[4,4,8,128]{3,2,1,0:T(8,128)S(1)}, f32[4,4,8,128]{3,2,1,0:T(8,128)S(1)}, u32[]{:S(2)}, u32[]{:S(2)}) collective-permute-start(f32[4,4,8,128]{3,2,1,0:T(8,128)S(1)} %select_maximum_fusion), channel_id=1, source_target_pairs={{0,128},{128,0},{1,129},{129,1},{2,130},{130,2},{3,131},{131,3},{4... | collective-permute-start | bytes 196616 | tf_op jit(solution)/shard_map/ppermute | solution.py:241
  47.7 2.7 %collective-permute-done.9 = f32[4,4,8,128]{3,2,1,0:T(8,128)S(1)} collective-permute-done((f32[4,4,8,128]{3,2,1,0:T(8,128)S(1)}, f32[4,4,8,128]{3,2,1,0:T(8,128)S(1)}, u32[]{:S(2)}, u32[]{:S(2)}) %collective-permute-start.9) | collective-permute-done | bytes 65568 | tf_op jit(solution)/shard_map/ppermute | solution.py:241
  50.5 2.0 %collective-permute-start.10 = (f32[19]{0:T(128)S(1)}, f32[19]{0:T(128)S(1)}, u32[]{:S(2)}, u32[]{:S(2)}) collective-permute-start(f32[19]{0:T(128)S(1)} %fusion.57), channel_id=1, source_target_pairs={{0,1},{1,0},{2,3},{3,2},{4,5},{5,4},{6,7},{7,6},{8,9},{9,8},{10,11... | collective-permute-start | bytes 236 | tf_op jit(solution)/shard_map/ppermute | solution.py:125
  52.5 1.5 %collective-permute-done.10 = f32[19]{0:T(128)S(1)} collective-permute-done((f32[19]{0:T(128)S(1)}, f32[19]{0:T(128)S(1)}, u32[]{:S(2)}, u32[]{:S(2)}) %collective-permute-start.10) | collective-permute-done | bytes 108 | tf_op jit(solution)/shard_map/ppermute | solution.py:125
  54.0 5.7 %collective-permute-start.11 = (f32[19]{0:T(128)S(1)}, f32[19]{0:T(128)S(1)}, u32[]{:S(2)}, u32[]{:S(2)}) collective-permute-start(f32[19]{0:T(128)S(1)} %add.125), channel_id=1, source_target_pairs={{0,2},{1,3},{2,0},{3,1},{4,6},{5,7},{6,4},{7,5},{8,10},{9,11},{10,... | collective-permute-start | bytes 236 | tf_op jit(solution)/shard_map/ppermute | solution.py:125
  60.3 0.9 %collective-permute-done.11 = f32[19]{0:T(128)S(1)} collective-permute-done((f32[19]{0:T(128)S(1)}, f32[19]{0:T(128)S(1)}, u32[]{:S(2)}, u32[]{:S(2)}) %collective-permute-start.11) | collective-permute-done | bytes 108 | tf_op jit(solution)/shard_map/ppermute | solution.py:125
  61.2 2.0 %collective-permute-start.12 = (f32[19]{0:T(128)S(1)}, f32[19]{0:T(128)S(1)}, u32[]{:S(2)}, u32[]{:S(2)}) collective-permute-start(f32[19]{0:T(128)S(1)} %add.132), channel_id=1, source_target_pairs={{0,6},{1,7},{2,4},{3,5},{4,2},{5,3},{6,0},{7,1},{8,14},{9,15},{10,... | collective-permute-start | bytes 236 | tf_op jit(solution)/shard_map/ppermute | solution.py:125
  63.2 1.0 %copy.112 = f32[28,4,8,128]{3,2,1,0:T(8,128)} copy(f32[28,4,8,128]{3,0,2,1:T(8,128)S(1)} %copy_select_fusion) | data formatting | bytes 917504
  64.3 2.6 %collective-permute-done.12 = f32[19]{0:T(128)S(1)} collective-permute-done((f32[19]{0:T(128)S(1)}, f32[19]{0:T(128)S(1)}, u32[]{:S(2)}, u32[]{:S(2)}) %collective-permute-start.12) | collective-permute-done | bytes 108 | tf_op jit(solution)/shard_map/ppermute | solution.py:125
  (120 shorter events, 8.7 us)
Async XLA Ops:
  0.6 1.3 %copy-start.4 = (f32[19]{0:T(128)S(1)}, f32[19]{0:T(128)}, u32[]{:S(2)}) copy-start(f32[19]{0:T(128)} %constant.126) | copy-start | bytes 232
  0.6 1.3 %copy-start.5 = (f32[19]{0:T(128)S(1)}, f32[19]{0:T(128)}, u32[]{:S(2)}) copy-start(f32[19]{0:T(128)} %constant.127) | copy-start | bytes 232
  0.7 1.3 %copy-start.6 = (f32[19]{0:T(128)S(1)}, f32[19]{0:T(128)}, u32[]{:S(2)}) copy-start(f32[19]{0:T(128)} %constant.128) | copy-start | bytes 232
  2.0 5.3 %copy-start = (f32[28,4,8,128]{3,2,1,0:T(8,128)S(1)}, f32[28,4,8,128]{3,2,1,0:T(8,128)}, u32[]{:S(2)}) copy-start(f32[28,4,8,128]{3,2,1,0:T(8,128)} %param.22) | copy-start | bytes 1376260
  2.4 7.6 %collective-permute-start = (f32[3,4,8,128]{3,2,1,0:T(8,128)S(1)}, f32[3,4,8,128]{3,2,1,0:T(8,128)S(1)}, u32[]{:S(2)}, u32[]{:S(2)}) collective-permute-start(f32[3,4,8,128]{3,2,1,0:T(8,128)S(1)} %maximum_divide_fusion), channel_id=1, source_target_pairs={{0,128},{1,129},{2,130},{3,131},{4,132},{5,133},{6,134},{7,135},{8... | collective-permute-start | bytes 147464 | tf_op jit(solution)/shard_map/ppermute | solution.py:146
  7.3 0.7 %copy-start.3 = (s32[4,8,128]{2,1,0:T(8,128)S(1)}, s32[4,8,128]{2,1,0:T(8,128)}, u32[]{:S(2)}) copy-start(s32[4,8,128]{2,1,0:T(8,128)} %param.23) | copy-start | bytes 49156
  8.1 0.7 copy-start.17
  8.1 0.7 copy-start.18
  8.1 0.7 %copy-start.13 = (f32[28,1,1,1]{0,3,2,1:T(1,128)S(1)}, f32[28,1,1,1]{0,3,2,1:T(1,128)}, u32[]{:S(2)}) copy-start(f32[28,1,1,1]{0,3,2,1:T(1,128)} %constant.104.clone) | copy-start | bytes 340
  8.1 0.7 %copy-start.14 = (f32[28,1,1,1]{0,3,2,1:T(1,128)S(1)}, f32[28,1,1,1]{0,3,2,1:T(1,128)}, u32[]{:S(2)}) copy-start(f32[28,1,1,1]{0,3,2,1:T(1,128)} %constant.105.clone) | copy-start | bytes 340
  8.1 0.7 %copy-start.15 = (f32[28,1,1,1]{0,3,2,1:T(1,128)S(1)}, f32[28,1,1,1]{0,3,2,1:T(1,128)}, u32[]{:S(2)}) copy-start(f32[28,1,1,1]{0,3,2,1:T(1,128)} %constant.108.clone) | copy-start | bytes 340
  8.2 0.7 %copy-start.16 = (f32[28,1,1,1]{0,3,2,1:T(1,128)S(1)}, f32[28,1,1,1]{0,3,2,1:T(1,128)}, u32[]{:S(2)}) copy-start(f32[28,1,1,1]{0,3,2,1:T(1,128)} %constant.109.clone) | copy-start | bytes 340
  8.2 0.9 %copy-start.19 = (f32[15]{0:T(128)S(1)}, f32[15]{0:T(128)}, u32[]{:S(2)}) copy-start(f32[15]{0:T(128)} %param.24) | copy-start | bytes 184
  8.2 1.0 %copy-start.1 = (f32[28,4,8,128]{3,2,1,0:T(8,128)S(1)}, f32[28,4,8,128]{3,2,1,0:T(8,128)}, u32[]{:S(2)}) copy-start(f32[28,4,8,128]{3,2,1,0:T(8,128)} %param.26) | copy-start | bytes 1376260
  10.0 0.7 %copy-start.2 = (f32[19,19,1,1]{0,1,3,2:T(8,128)S(1)}, f32[19,19,1,1]{0,1,3,2:T(8,128)}, u32[]{:S(2)}) copy-start(f32[19,19,1,1]{0,1,3,2:T(8,128)} %constant.133) | copy-start | bytes 4336
  10.1 0.7 %copy-start.20 = (f32[19]{0:T(128)S(1)}, f32[19]{0:T(128)}, u32[]{:S(2)}) copy-start(f32[19]{0:T(128)} %constant.125) | copy-start | bytes 232
  11.4 0.7 copy-start.8
  11.5 0.7 copy-start.9
  11.5 0.7 copy-start.10
  11.5 0.7 copy-start.11
  12.8 6.4 %collective-permute-start.1 = (f32[56,4,1,128]{3,0,2,1:T(8,128)S(1)}, f32[56,4,1,128]{3,0,2,1:T(8,128)S(1)}, u32[]{:S(2)}, u32[]{:S(2)}) collective-permute-start(f32[56,4,1,128]{3,0,2,1:T(8,128)S(1)} %get-tuple-element.56), channel_id=1, source_target_pairs={{0,8},{8,16},{16,24},{24,32},{32,40},{40,48},{48,56},{56,64},{64,7... | collective-permute-start | bytes 344072 | tf_op jit(solution)/shard_map/ppermute | solution.py:78
  12.9 6.3 %collective-permute-start.2 = (f32[56,4,1,128]{3,0,2,1:T(8,128)S(1)}, f32[56,4,1,128]{3,0,2,1:T(8,128)S(1)}, u32[]{:S(2)}, u32[]{:S(2)}) collective-permute-start(f32[56,4,1,128]{3,0,2,1:T(8,128)S(1)} %get-tuple-element.57), channel_id=1, source_target_pairs={{0,120},{8,0},{16,8},{24,16},{32,24},{40,32},{48,40},{56,48},{64,5... | collective-permute-start | bytes 344072 | tf_op jit(solution)/shard_map/ppermute | solution.py:79
  20.2 3.8 %collective-permute-start.3 = (f32[56,4,8]{0,2,1:T(8,128)S(1)}, f32[56,4,8]{0,2,1:T(8,128)S(1)}, u32[]{:S(2)}, u32[]{:S(2)}) collective-permute-start(f32[56,4,8]{0,2,1:T(8,128)S(1)} %get-tuple-element.38), channel_id=1, source_target_pairs={{0,1},{1,2},{2,3},{3,4},{4,5},{5,6},{6,7},{7,0},{8,9},{9,10},{10,1... | collective-permute-start | bytes 21512 | tf_op jit(solution)/shard_map/ppermute | solution.py:86
  22.2 3.7 %collective-permute-start.4 = (f32[56,4,8]{0,2,1:T(8,128)S(1)}, f32[56,4,8]{0,2,1:T(8,128)S(1)}, u32[]{:S(2)}, u32[]{:S(2)}) collective-permute-start(f32[56,4,8]{0,2,1:T(8,128)S(1)} %get-tuple-element.39), channel_id=1, source_target_pairs={{0,7},{1,0},{2,1},{3,2},{4,3},{5,4},{6,5},{7,6},{8,15},{9,8},{10,9... | collective-permute-start | bytes 21512 | tf_op jit(solution)/shard_map/ppermute | solution.py:87
  30.3 2.0 %collective-permute-start.5 = (f32[19]{0:T(128)S(1)}, f32[19]{0:T(128)S(1)}, u32[]{:S(2)}, u32[]{:S(2)}) collective-permute-start(f32[19]{0:T(128)S(1)} %broadcast_select_fusion.1), channel_id=1, source_target_pairs={{0,8},{8,0},{16,24},{24,16},{32,40},{40,32},{48,56},{56,48},{64,72... | collective-permute-start | bytes 236 | tf_op jit(solution)/shard_map/ppermute | solution.py:125
  32.3 3.6 %collective-permute-start.6 = (f32[19]{0:T(128)S(1)}, f32[19]{0:T(128)S(1)}, u32[]{:S(2)}, u32[]{:S(2)}) collective-permute-start(f32[19]{0:T(128)S(1)} %add.117), channel_id=1, source_target_pairs={{0,16},{8,24},{16,0},{24,8},{32,48},{40,56},{48,32},{56,40},{64,80... | collective-permute-start | bytes 236 | tf_op jit(solution)/shard_map/ppermute | solution.py:125
  36.2 3.6 %collective-permute-start.7 = (f32[19]{0:T(128)S(1)}, f32[19]{0:T(128)S(1)}, u32[]{:S(2)}, u32[]{:S(2)}) collective-permute-start(f32[19]{0:T(128)S(1)} %add.121), channel_id=1, source_target_pairs={{0,32},{8,40},{16,48},{24,56},{32,0},{40,8},{48,16},{56,24},{64,96... | collective-permute-start | bytes 236 | tf_op jit(solution)/shard_map/ppermute | solution.py:125
  39.9 4.8 %collective-permute-start.8 = (f32[19]{0:T(128)S(1)}, f32[19]{0:T(128)S(1)}, u32[]{:S(2)}, u32[]{:S(2)}) collective-permute-start(f32[19]{0:T(128)S(1)} %add.122), channel_id=1, source_target_pairs={{0,96},{8,104},{16,112},{24,120},{32,64},{40,72},{48,80},{56,88},{... | collective-permute-start | bytes 236 | tf_op jit(solution)/shard_map/ppermute | solution.py:125
  44.6 5.9 %collective-permute-start.9 = (f32[4,4,8,128]{3,2,1,0:T(8,128)S(1)}, f32[4,4,8,128]{3,2,1,0:T(8,128)S(1)}, u32[]{:S(2)}, u32[]{:S(2)}) collective-permute-start(f32[4,4,8,128]{3,2,1,0:T(8,128)S(1)} %select_maximum_fusion), channel_id=1, source_target_pairs={{0,128},{128,0},{1,129},{129,1},{2,130},{130,2},{3,131},{131,3},{4... | collective-permute-start | bytes 196616 | tf_op jit(solution)/shard_map/ppermute | solution.py:241
  50.5 3.5 %collective-permute-start.10 = (f32[19]{0:T(128)S(1)}, f32[19]{0:T(128)S(1)}, u32[]{:S(2)}, u32[]{:S(2)}) collective-permute-start(f32[19]{0:T(128)S(1)} %fusion.57), channel_id=1, source_target_pairs={{0,1},{1,0},{2,3},{3,2},{4,5},{5,4},{6,7},{7,6},{8,9},{9,8},{10,11... | collective-permute-start | bytes 236 | tf_op jit(solution)/shard_map/ppermute | solution.py:125
  54.0 7.2 %collective-permute-start.11 = (f32[19]{0:T(128)S(1)}, f32[19]{0:T(128)S(1)}, u32[]{:S(2)}, u32[]{:S(2)}) collective-permute-start(f32[19]{0:T(128)S(1)} %add.125), channel_id=1, source_target_pairs={{0,2},{1,3},{2,0},{3,1},{4,6},{5,7},{6,4},{7,5},{8,10},{9,11},{10,... | collective-permute-start | bytes 236 | tf_op jit(solution)/shard_map/ppermute | solution.py:125
  61.2 5.7 %collective-permute-start.12 = (f32[19]{0:T(128)S(1)}, f32[19]{0:T(128)S(1)}, u32[]{:S(2)}, u32[]{:S(2)}) collective-permute-start(f32[19]{0:T(128)S(1)} %add.132), channel_id=1, source_target_pairs={{0,6},{1,7},{2,4},{3,5},{4,2},{5,3},{6,0},{7,1},{8,14},{9,15},{10,... | collective-permute-start | bytes 236 | tf_op jit(solution)/shard_map/ppermute | solution.py:125
  (2 other events, 1.3 us)

commit v17 on v16

--- a/solution.py
+++ b/solution.py
@@ -254,7 +254,12 @@
         )
         return values
 
-    rate_grad = butterfly_sum(partial_rates, (("gz", 1),), [flow_gradient])
+    count_z = lax.axis_size("gz")
+    rate_grad = partial_rates + lax.ppermute(partial_rates, "gz", [(i, i ^ 1) for i in range(count_z)])
+    rate_grad = flow_gradient(rate_grad)
+    rate_grad = rate_grad + sum(
+        lax.ppermute(rate_grad, "gz", [(i, i ^ step) for i in range(count_z)]) for step in (2, 4, 6)
+    )
     grad_rows = later["grad_rows"]
     return (moved, grad_rows, rate_grad)
 

time: 67.7 us -> 68.1 us (level)
  starting transfers between devices: 29 us -> 30.6 us
  waiting for transfers between devices: 19 us -> 17.7 us
    ppermute x0 -> x4, starting transfers between devices: none -> 11.3 us  [the longest x3 9.27 us: per_device(): lax.ppermute(rate_grad, 'gz', [(i, i ^ step) for i in range(count_z)])]
    ppermute x7 -> x4, starting transfers between devices: 15.1 us -> 5.38 us  [butterfly_sum(): values = values + lax.ppermute(values, axis, list(enumerate(targets)))]
    ppermute x7 -> x4, waiting for transfers between devices: 10.5 us -> 5.48 us  [butterfly_sum(): values = values + lax.ppermute(values, axis, list(enumerate(targets)))]
    ppermute x0 -> x4, waiting for transfers between devices: none -> 3.77 us  [the longest x3 2.26 us: per_device(): lax.ppermute(rate_grad, 'gz', [(i, i ^ step) for i in range(count_z)])]
  transfers between devices with their start and end apart: 13 -> 14, of which waited for: 10 -> 9; matrix products, arithmetic and copies ran while one was open for 10% -> 9% of each run, Pallas kernels for 0% -> 0%
where the time goes in v17:
time: 68.1 us; the launch traced here: 67.7 us
  starting transfers between devices  30.6 us (45%)
  waiting for transfers between devices  17.7 us (26%)
  local copies, waits for them, and re-layouts  8.98 us (13%)
  other arithmetic  6.83 us (10%)
  matrix products  2.34 us (3%)
  between operations  1.28 us (2%)
    ppermute x3, starting transfers between devices, per_device(): lax.ppermute(rate_grad, 'gz', [(i, i ^ step) for i in range(count_z)])  9.27 us
    unnamed x58, local copies, waits for them, and re-layouts  6.49 us
    ppermute x4, waiting for transfers between devices, butterfly_sum(): values = values + lax.ppermute(values, axis, list(enumerate(targets)))  5.48 us
    ppermute x4, starting transfers between devices, butterfly_sum(): values = values + lax.ppermute(values, axis, list(enumerate(targets)))  5.38 us
    ppermute x1, starting transfers between devices, per_device(): sent_motion = lax.ppermute(own_motion, 'sec', [(0, 1)])  4.93 us
    ppermute x1, starting transfers between devices, shift_rows(): high = lax.ppermute(field[:, :, :1, :], 'gy', ring('gy', -1))  3.84 us
    ppermute x1, starting transfers between devices, per_device(): other = lax.ppermute(payload, 'sec', [(0, 1), (1, 0)])  2.96 us
    ppermute x1, waiting for transfers between devices, per_device(): other = lax.ppermute(payload, 'sec', [(0, 1), (1, 0)])  2.74 us
  transfers between devices with their start and end apart: 14, of which 9 were waited for; matrix products, arithmetic and copies ran while one was open for 9% of the time, Pallas kernels for 0%

profile of v17, /device:TPU:32, one launch (start us, length us, event | category | flops | bytes accessed | tf_op | source)
XLA Modules:
  0.0 67.7 jit_solution(13744134529942009554)
XLA Ops:
  0.7 1.3 %copy.83 = f32[28,4,8,128]{3,0,2,1:T(8,128)S(1)} copy(f32[28,4,8,128]{3,2,1,0:T(8,128)} %param.22) | data formatting | bytes 917504 | tf_op args[0]
  2.4 4.9 %collective-permute-start = (f32[3,4,8,128]{3,2,1,0:T(8,128)S(1)}, f32[3,4,8,128]{3,2,1,0:T(8,128)S(1)}, u32[]{:S(2)}, u32[]{:S(2)}) collective-permute-start(f32[3,4,8,128]{3,2,1,0:T(8,128)S(1)} %maximum_divide_fusion), channel_id=1, source_target_pairs={{0,128},{1,129},{2,130},{3,131},{4,132},{5,133},{6,134},{7,135},{8... | collective-permute-start | bytes 147464 | tf_op jit(solution)/shard_map/ppermute | solution.py:146
  7.4 0.7 copy-done.3
  10.1 0.7 copy-done.2
  10.7 0.7 %fusion.18 = f32[19,4,8,128]{3,0,2,1:T(8,128)S(1)} fusion(f32[19,19,1,1]{0,1,3,2:T(8,128)S(1)} %copy-done.2, f32[28,4,8,128]{3,0,2,1:T(8,128)S(1)} %copy.83, f32[4,8,128]{2,1,0:T(8,128)S(1)} %broadcast_multiply_fusion.4, f32[4,8,128]{2,1,0:T(8,128)S(1)} %get-tuple-element.117, f32[4,8,128]{2,1,0:T(8,128)S(1)} %get-tuple-element.118, ...), kind=kOutput, calls=%fused_computation.51 | convolution fusion | flops 18833408 | bytes 800768 | tf_op jit(solution)/shard_map/ji,jxyz->ixyz/dot_general | solution.py:169
  11.5 0.6 fusion.1
  12.9 3.8 %collective-permute-start.2 = (f32[56,4,1,128]{3,0,2,1:T(8,128)S(1)}, f32[56,4,1,128]{3,0,2,1:T(8,128)S(1)}, u32[]{:S(2)}, u32[]{:S(2)}) collective-permute-start(f32[56,4,1,128]{3,0,2,1:T(8,128)S(1)} %get-tuple-element.57), channel_id=1, source_target_pairs={{0,120},{8,0},{16,8},{24,16},{32,24},{40,32},{48,40},{56,48},{64,5... | collective-permute-start | bytes 344072 | tf_op jit(solution)/shard_map/ppermute | solution.py:79
  16.8 2.4 %collective-permute-done.1 = f32[56,4,1,128]{3,0,2,1:T(8,128)S(1)} collective-permute-done((f32[56,4,1,128]{3,0,2,1:T(8,128)S(1)}, f32[56,4,1,128]{3,0,2,1:T(8,128)S(1)}, u32[]{:S(2)}, u32[]{:S(2)}) %collective-permute-start.1) | collective-permute-done | bytes 114720 | tf_op jit(solution)/shard_map/ppermute | solution.py:78
  19.2 0.7 %select_reduce_fusion.1 = (f32[56,4,8]{0,2,1:T(8,128)S(1)}, f32[56,4,8]{0,2,1:T(8,128)S(1)}, f32[56,4,8,128]{3,0,2,1:T(8,128)S(1)}) fusion(pred[128]{0:T(512)(128)(4,1)S(1)} %get-tuple-element.136, pred[128]{0:T(512)(128)(4,1)S(1)} %get-tuple-element.137, f32[28,4,8,128]{3,0,2,1:T(8,128)S(1)} %copy.105, f32[28,4,8,128]{3,0,2,1:T(8,128)S(1)} %copy_select_fusion.1, ...), kind=kLoop, calls=%fused_computation.21 | loop fusion | flops 2060800 | bytes 3684720 | tf_op jit(solution)/shard_map/reduce_sum | solution.py:84
  20.2 2.0 %collective-permute-start.3 = (f32[56,4,8]{0,2,1:T(8,128)S(1)}, f32[56,4,8]{0,2,1:T(8,128)S(1)}, u32[]{:S(2)}, u32[]{:S(2)}) collective-permute-start(f32[56,4,8]{0,2,1:T(8,128)S(1)} %get-tuple-element.38), channel_id=1, source_target_pairs={{0,1},{1,2},{2,3},{3,4},{4,5},{5,6},{6,7},{7,0},{8,9},{9,10},{10,1... | collective-permute-start | bytes 21512 | tf_op jit(solution)/shard_map/ppermute | solution.py:86
  22.6 1.4 %collective-permute-done.3 = f32[56,4,8]{0,2,1:T(8,128)S(1)} collective-permute-done((f32[56,4,8]{0,2,1:T(8,128)S(1)}, f32[56,4,8]{0,2,1:T(8,128)S(1)}, u32[]{:S(2)}, u32[]{:S(2)}) %collective-permute-start.3) | collective-permute-done | bytes 7200 | tf_op jit(solution)/shard_map/ppermute | solution.py:86
  24.0 1.9 %collective-permute-done.4 = f32[56,4,8]{0,2,1:T(8,128)S(1)} collective-permute-done((f32[56,4,8]{0,2,1:T(8,128)S(1)}, f32[56,4,8]{0,2,1:T(8,128)S(1)}, u32[]{:S(2)}, u32[]{:S(2)}) %collective-permute-start.4) | collective-permute-done | bytes 7200 | tf_op jit(solution)/shard_map/ppermute | solution.py:87
  25.9 1.2 %fusion.4 = f32[56,4,8,128]{3,0,2,1:T(8,128)S(1)} fusion(f32[56,4,8,127]{3,0,2,1:T(8,128)S(1)} %get-tuple-element.87, f32[56,4,8,1]{3,0,2,1:T(8,128)S(1)} %get-tuple-element.89, f32[56,4,8,128]{3,0,2,1:T(8,128)S(1)} %get-tuple-element.53, f32[56,4,8,1]{3,0,2,1:T(8,128)S(1)} %get-tuple-element.88, f32[56,4,8,127]{3,0,2,1:T(8,128)S(1)} %get-tuple-element.86, ...), kind=kLoop, calls=%fused_computation.15 | loop fusion | flops 1376256 | bytes 3684720 | tf_op jit(solution)/shard_map/jit(_where)/select_n | solution.py:90
  28.5 0.6 copy-done.12
  29.2 0.8 %fusion.72 = (f32[28,4,8,128]{3,0,2,1:T(8,128)S(1)}, f32[28]{0:T(128)S(1)}, f32[28,4,8,128]{3,0,2,1:T(8,128)S(1)}) fusion(f32[56,4,8,128]{3,0,2,1:T(8,128)S(1)} %maximum_select_fusion.2, f32[28,4,8,128]{3,2,1,0:T(8,128)S(1)} %bitcast.96, f32[28,4,8,128]{3,2,1,0:T(8,128)S(1)} %copy-done, pred[4,8,128]{2,1,0:T(8,128)(4,1)S(1)} %broadcast_compare_fusion, ...), kind=kLoop, calls=%fused_computation.165 | loop fusion | flops 688100 | bytes 2756749 | tf_op jit(solution)/shard_map/slice | solution.py:183
  30.8 1.0 %copy.111 = f32[28,4,8,128]{3,2,1,0:T(8,128)} copy(f32[28,4,8,128]{3,0,2,1:T(8,128)S(1)} %get-tuple-element.81) | data formatting | bytes 917504
  32.3 0.8 %collective-permute-start.6 = (f32[19]{0:T(128)S(1)}, f32[19]{0:T(128)S(1)}, u32[]{:S(2)}, u32[]{:S(2)}) collective-permute-start(f32[19]{0:T(128)S(1)} %add.120), channel_id=1, source_target_pairs={{0,16},{8,24},{16,0},{24,8},{32,48},{40,56},{48,32},{56,40},{64,80... | collective-permute-start | bytes 236 | tf_op jit(solution)/shard_map/ppermute | solution.py:125
  33.1 0.6 add_multiply_fusion
  34.3 1.6 %collective-permute-done.6 = f32[19]{0:T(128)S(1)} collective-permute-done((f32[19]{0:T(128)S(1)}, f32[19]{0:T(128)S(1)}, u32[]{:S(2)}, u32[]{:S(2)}) %collective-permute-start.6) | collective-permute-done | bytes 108 | tf_op jit(solution)/shard_map/ppermute | solution.py:125
  36.2 1.6 %collective-permute-start.7 = (f32[19]{0:T(128)S(1)}, f32[19]{0:T(128)S(1)}, u32[]{:S(2)}, u32[]{:S(2)}) collective-permute-start(f32[19]{0:T(128)S(1)} %add.124), channel_id=1, source_target_pairs={{0,32},{8,40},{16,48},{24,56},{32,0},{40,8},{48,16},{56,24},{64,96... | collective-permute-start | bytes 236 | tf_op jit(solution)/shard_map/ppermute | solution.py:125
  37.9 2.0 %collective-permute-done.7 = f32[19]{0:T(128)S(1)} collective-permute-done((f32[19]{0:T(128)S(1)}, f32[19]{0:T(128)S(1)}, u32[]{:S(2)}, u32[]{:S(2)}) %collective-permute-start.7) | collective-permute-done | bytes 108 | tf_op jit(solution)/shard_map/ppermute | solution.py:125
  39.9 2.9 %collective-permute-start.8 = (f32[19]{0:T(128)S(1)}, f32[19]{0:T(128)S(1)}, u32[]{:S(2)}, u32[]{:S(2)}) collective-permute-start(f32[19]{0:T(128)S(1)} %add.125), channel_id=1, source_target_pairs={{0,96},{8,104},{16,112},{24,120},{32,64},{40,72},{48,80},{56,88},{... | collective-permute-start | bytes 236 | tf_op jit(solution)/shard_map/ppermute | solution.py:125
  42.7 1.9 %collective-permute-done.8 = f32[19]{0:T(128)S(1)} collective-permute-done((f32[19]{0:T(128)S(1)}, f32[19]{0:T(128)S(1)}, u32[]{:S(2)}, u32[]{:S(2)}) %collective-permute-start.8) | collective-permute-done | bytes 108 | tf_op jit(solution)/shard_map/ppermute | solution.py:125
  44.6 3.0 %collective-permute-start.9 = (f32[4,4,8,128]{3,2,1,0:T(8,128)S(1)}, f32[4,4,8,128]{3,2,1,0:T(8,128)S(1)}, u32[]{:S(2)}, u32[]{:S(2)}) collective-permute-start(f32[4,4,8,128]{3,2,1,0:T(8,128)S(1)} %select_maximum_fusion), channel_id=1, source_target_pairs={{0,128},{128,0},{1,129},{129,1},{2,130},{130,2},{3,131},{131,3},{4... | collective-permute-start | bytes 196616 | tf_op jit(solution)/shard_map/ppermute | solution.py:241
  47.7 2.7 %collective-permute-done.9 = f32[4,4,8,128]{3,2,1,0:T(8,128)S(1)} collective-permute-done((f32[4,4,8,128]{3,2,1,0:T(8,128)S(1)}, f32[4,4,8,128]{3,2,1,0:T(8,128)S(1)}, u32[]{:S(2)}, u32[]{:S(2)}) %collective-permute-start.9) | collective-permute-done | bytes 65568 | tf_op jit(solution)/shard_map/ppermute | solution.py:241
  50.5 2.0 %collective-permute-start.10 = (f32[19]{0:T(128)S(1)}, f32[19]{0:T(128)S(1)}, u32[]{:S(2)}, u32[]{:S(2)}) collective-permute-start(f32[19]{0:T(128)S(1)} %fusion.57), channel_id=1, source_target_pairs={{0,1},{1,0},{2,3},{3,2},{4,5},{5,4},{6,7},{7,6},{8,9},{9,8},{10,11... | collective-permute-start | bytes 236 | tf_op jit(solution)/shard_map/ppermute | solution.py:258
  52.5 1.5 %collective-permute-done.10 = f32[19]{0:T(128)S(1)} collective-permute-done((f32[19]{0:T(128)S(1)}, f32[19]{0:T(128)S(1)}, u32[]{:S(2)}, u32[]{:S(2)}) %collective-permute-start.10) | collective-permute-done | bytes 108 | tf_op jit(solution)/shard_map/ppermute | solution.py:258
  54.0 5.7 %collective-permute-start.11 = (f32[19]{0:T(128)S(1)}, f32[19]{0:T(128)S(1)}, u32[]{:S(2)}, u32[]{:S(2)}) collective-permute-start(f32[19]{0:T(128)S(1)} %add.128), channel_id=1, source_target_pairs={{0,2},{1,3},{2,0},{3,1},{4,6},{5,7},{6,4},{7,5},{8,10},{9,11},{10,... | collective-permute-start | bytes 236 | tf_op jit(solution)/shard_map/ppermute | solution.py:261
  59.7 1.4 %collective-permute-start.12 = (f32[19]{0:T(128)S(1)}, f32[19]{0:T(128)S(1)}, u32[]{:S(2)}, u32[]{:S(2)}) collective-permute-start(f32[19]{0:T(128)S(1)} %add.128), channel_id=1, source_target_pairs={{0,4},{1,5},{2,6},{3,7},{4,0},{5,1},{6,2},{7,3},{8,12},{9,13},{10,... | collective-permute-start | bytes 236 | tf_op jit(solution)/shard_map/ppermute | solution.py:261
  61.2 2.1 %collective-permute-start.13 = (f32[19]{0:T(128)S(1)}, f32[19]{0:T(128)S(1)}, u32[]{:S(2)}, u32[]{:S(2)}) collective-permute-start(f32[19]{0:T(128)S(1)} %add.128), channel_id=1, source_target_pairs={{0,6},{1,7},{2,4},{3,5},{4,2},{5,3},{6,0},{7,1},{8,14},{9,15},{10,... | collective-permute-start | bytes 236 | tf_op jit(solution)/shard_map/ppermute | solution.py:261
  63.9 1.0 %copy.112 = f32[28,4,8,128]{3,2,1,0:T(8,128)} copy(f32[28,4,8,128]{3,0,2,1:T(8,128)S(1)} %copy_select_fusion) | data formatting | bytes 917504
  64.9 2.2 %collective-permute-done.12 = f32[19]{0:T(128)S(1)} collective-permute-done((f32[19]{0:T(128)S(1)}, f32[19]{0:T(128)S(1)}, u32[]{:S(2)}, u32[]{:S(2)}) %collective-permute-start.12) | collective-permute-done | bytes 108 | tf_op jit(solution)/shard_map/ppermute | solution.py:261
  (121 shorter events, 8.7 us)
Async XLA Ops:
  0.6 1.3 %copy-start.4 = (f32[19]{0:T(128)S(1)}, f32[19]{0:T(128)}, u32[]{:S(2)}) copy-start(f32[19]{0:T(128)} %constant.126) | copy-start | bytes 232
  0.6 1.3 %copy-start.5 = (f32[19]{0:T(128)S(1)}, f32[19]{0:T(128)}, u32[]{:S(2)}) copy-start(f32[19]{0:T(128)} %constant.127) | copy-start | bytes 232
  0.7 1.3 %copy-start.6 = (f32[19]{0:T(128)S(1)}, f32[19]{0:T(128)}, u32[]{:S(2)}) copy-start(f32[19]{0:T(128)} %constant.128) | copy-start | bytes 232
  2.0 5.3 %copy-start = (f32[28,4,8,128]{3,2,1,0:T(8,128)S(1)}, f32[28,4,8,128]{3,2,1,0:T(8,128)}, u32[]{:S(2)}) copy-start(f32[28,4,8,128]{3,2,1,0:T(8,128)} %param.22) | copy-start | bytes 1376260
  2.4 7.6 %collective-permute-start = (f32[3,4,8,128]{3,2,1,0:T(8,128)S(1)}, f32[3,4,8,128]{3,2,1,0:T(8,128)S(1)}, u32[]{:S(2)}, u32[]{:S(2)}) collective-permute-start(f32[3,4,8,128]{3,2,1,0:T(8,128)S(1)} %maximum_divide_fusion), channel_id=1, source_target_pairs={{0,128},{1,129},{2,130},{3,131},{4,132},{5,133},{6,134},{7,135},{8... | collective-permute-start | bytes 147464 | tf_op jit(solution)/shard_map/ppermute | solution.py:146
  7.3 0.7 %copy-start.3 = (s32[4,8,128]{2,1,0:T(8,128)S(1)}, s32[4,8,128]{2,1,0:T(8,128)}, u32[]{:S(2)}) copy-start(s32[4,8,128]{2,1,0:T(8,128)} %param.23) | copy-start | bytes 49156
  8.1 0.7 copy-start.17
  8.1 0.7 copy-start.18
  8.1 0.7 %copy-start.13 = (f32[28,1,1,1]{0,3,2,1:T(1,128)S(1)}, f32[28,1,1,1]{0,3,2,1:T(1,128)}, u32[]{:S(2)}) copy-start(f32[28,1,1,1]{0,3,2,1:T(1,128)} %constant.104.clone) | copy-start | bytes 340
  8.1 0.7 %copy-start.14 = (f32[28,1,1,1]{0,3,2,1:T(1,128)S(1)}, f32[28,1,1,1]{0,3,2,1:T(1,128)}, u32[]{:S(2)}) copy-start(f32[28,1,1,1]{0,3,2,1:T(1,128)} %constant.105.clone) | copy-start | bytes 340
  8.1 0.7 %copy-start.15 = (f32[28,1,1,1]{0,3,2,1:T(1,128)S(1)}, f32[28,1,1,1]{0,3,2,1:T(1,128)}, u32[]{:S(2)}) copy-start(f32[28,1,1,1]{0,3,2,1:T(1,128)} %constant.108.clone) | copy-start | bytes 340
  8.2 0.7 %copy-start.16 = (f32[28,1,1,1]{0,3,2,1:T(1,128)S(1)}, f32[28,1,1,1]{0,3,2,1:T(1,128)}, u32[]{:S(2)}) copy-start(f32[28,1,1,1]{0,3,2,1:T(1,128)} %constant.109.clone) | copy-start | bytes 340
  8.2 0.9 %copy-start.19 = (f32[15]{0:T(128)S(1)}, f32[15]{0:T(128)}, u32[]{:S(2)}) copy-start(f32[15]{0:T(128)} %param.24) | copy-start | bytes 184
  8.2 1.0 %copy-start.1 = (f32[28,4,8,128]{3,2,1,0:T(8,128)S(1)}, f32[28,4,8,128]{3,2,1,0:T(8,128)}, u32[]{:S(2)}) copy-start(f32[28,4,8,128]{3,2,1,0:T(8,128)} %param.26) | copy-start | bytes 1376260
  10.0 0.7 %copy-start.2 = (f32[19,19,1,1]{0,1,3,2:T(8,128)S(1)}, f32[19,19,1,1]{0,1,3,2:T(8,128)}, u32[]{:S(2)}) copy-start(f32[19,19,1,1]{0,1,3,2:T(8,128)} %constant.133) | copy-start | bytes 4336
  10.1 0.7 %copy-start.20 = (f32[19]{0:T(128)S(1)}, f32[19]{0:T(128)}, u32[]{:S(2)}) copy-start(f32[19]{0:T(128)} %constant.125) | copy-start | bytes 232
  11.5 0.7 copy-start.9
  11.5 0.7 copy-start.10
  11.5 0.7 copy-start.11
  12.8 6.4 %collective-permute-start.1 = (f32[56,4,1,128]{3,0,2,1:T(8,128)S(1)}, f32[56,4,1,128]{3,0,2,1:T(8,128)S(1)}, u32[]{:S(2)}, u32[]{:S(2)}) collective-permute-start(f32[56,4,1,128]{3,0,2,1:T(8,128)S(1)} %get-tuple-element.56), channel_id=1, source_target_pairs={{0,8},{8,16},{16,24},{24,32},{32,40},{40,48},{48,56},{56,64},{64,7... | collective-permute-start | bytes 344072 | tf_op jit(solution)/shard_map/ppermute | solution.py:78
  12.9 6.3 %collective-permute-start.2 = (f32[56,4,1,128]{3,0,2,1:T(8,128)S(1)}, f32[56,4,1,128]{3,0,2,1:T(8,128)S(1)}, u32[]{:S(2)}, u32[]{:S(2)}) collective-permute-start(f32[56,4,1,128]{3,0,2,1:T(8,128)S(1)} %get-tuple-element.57), channel_id=1, source_target_pairs={{0,120},{8,0},{16,8},{24,16},{32,24},{40,32},{48,40},{56,48},{64,5... | collective-permute-start | bytes 344072 | tf_op jit(solution)/shard_map/ppermute | solution.py:79
  20.2 3.8 %collective-permute-start.3 = (f32[56,4,8]{0,2,1:T(8,128)S(1)}, f32[56,4,8]{0,2,1:T(8,128)S(1)}, u32[]{:S(2)}, u32[]{:S(2)}) collective-permute-start(f32[56,4,8]{0,2,1:T(8,128)S(1)} %get-tuple-element.38), channel_id=1, source_target_pairs={{0,1},{1,2},{2,3},{3,4},{4,5},{5,6},{6,7},{7,0},{8,9},{9,10},{10,1... | collective-permute-start | bytes 21512 | tf_op jit(solution)/shard_map/ppermute | solution.py:86
  22.2 3.7 %collective-permute-start.4 = (f32[56,4,8]{0,2,1:T(8,128)S(1)}, f32[56,4,8]{0,2,1:T(8,128)S(1)}, u32[]{:S(2)}, u32[]{:S(2)}) collective-permute-start(f32[56,4,8]{0,2,1:T(8,128)S(1)} %get-tuple-element.39), channel_id=1, source_target_pairs={{0,7},{1,0},{2,1},{3,2},{4,3},{5,4},{6,5},{7,6},{8,15},{9,8},{10,9... | collective-permute-start | bytes 21512 | tf_op jit(solution)/shard_map/ppermute | solution.py:87
  30.3 2.0 %collective-permute-start.5 = (f32[19]{0:T(128)S(1)}, f32[19]{0:T(128)S(1)}, u32[]{:S(2)}, u32[]{:S(2)}) collective-permute-start(f32[19]{0:T(128)S(1)} %broadcast_select_fusion.1), channel_id=1, source_target_pairs={{0,8},{8,0},{16,24},{24,16},{32,40},{40,32},{48,56},{56,48},{64,72... | collective-permute-start | bytes 236 | tf_op jit(solution)/shard_map/ppermute | solution.py:125
  32.3 3.6 %collective-permute-start.6 = (f32[19]{0:T(128)S(1)}, f32[19]{0:T(128)S(1)}, u32[]{:S(2)}, u32[]{:S(2)}) collective-permute-start(f32[19]{0:T(128)S(1)} %add.120), channel_id=1, source_target_pairs={{0,16},{8,24},{16,0},{24,8},{32,48},{40,56},{48,32},{56,40},{64,80... | collective-permute-start | bytes 236 | tf_op jit(solution)/shard_map/ppermute | solution.py:125
  36.2 3.6 %collective-permute-start.7 = (f32[19]{0:T(128)S(1)}, f32[19]{0:T(128)S(1)}, u32[]{:S(2)}, u32[]{:S(2)}) collective-permute-start(f32[19]{0:T(128)S(1)} %add.124), channel_id=1, source_target_pairs={{0,32},{8,40},{16,48},{24,56},{32,0},{40,8},{48,16},{56,24},{64,96... | collective-permute-start | bytes 236 | tf_op jit(solution)/shard_map/ppermute | solution.py:125
  39.9 4.8 %collective-permute-start.8 = (f32[19]{0:T(128)S(1)}, f32[19]{0:T(128)S(1)}, u32[]{:S(2)}, u32[]{:S(2)}) collective-permute-start(f32[19]{0:T(128)S(1)} %add.125), channel_id=1, source_target_pairs={{0,96},{8,104},{16,112},{24,120},{32,64},{40,72},{48,80},{56,88},{... | collective-permute-start | bytes 236 | tf_op jit(solution)/shard_map/ppermute | solution.py:125
  44.6 5.9 %collective-permute-start.9 = (f32[4,4,8,128]{3,2,1,0:T(8,128)S(1)}, f32[4,4,8,128]{3,2,1,0:T(8,128)S(1)}, u32[]{:S(2)}, u32[]{:S(2)}) collective-permute-start(f32[4,4,8,128]{3,2,1,0:T(8,128)S(1)} %select_maximum_fusion), channel_id=1, source_target_pairs={{0,128},{128,0},{1,129},{129,1},{2,130},{130,2},{3,131},{131,3},{4... | collective-permute-start | bytes 196616 | tf_op jit(solution)/shard_map/ppermute | solution.py:241
  50.5 3.5 %collective-permute-start.10 = (f32[19]{0:T(128)S(1)}, f32[19]{0:T(128)S(1)}, u32[]{:S(2)}, u32[]{:S(2)}) collective-permute-start(f32[19]{0:T(128)S(1)} %fusion.57), channel_id=1, source_target_pairs={{0,1},{1,0},{2,3},{3,2},{4,5},{5,4},{6,7},{7,6},{8,9},{9,8},{10,11... | collective-permute-start | bytes 236 | tf_op jit(solution)/shard_map/ppermute | solution.py:258
  54.0 10.9 %collective-permute-start.11 = (f32[19]{0:T(128)S(1)}, f32[19]{0:T(128)S(1)}, u32[]{:S(2)}, u32[]{:S(2)}) collective-permute-start(f32[19]{0:T(128)S(1)} %add.128), channel_id=1, source_target_pairs={{0,2},{1,3},{2,0},{3,1},{4,6},{5,7},{6,4},{7,5},{8,10},{9,11},{10,... | collective-permute-start | bytes 236 | tf_op jit(solution)/shard_map/ppermute | solution.py:261
  59.7 7.4 %collective-permute-start.12 = (f32[19]{0:T(128)S(1)}, f32[19]{0:T(128)S(1)}, u32[]{:S(2)}, u32[]{:S(2)}) collective-permute-start(f32[19]{0:T(128)S(1)} %add.128), channel_id=1, source_target_pairs={{0,4},{1,5},{2,6},{3,7},{4,0},{5,1},{6,2},{7,3},{8,12},{9,13},{10,... | collective-permute-start | bytes 236 | tf_op jit(solution)/shard_map/ppermute | solution.py:261
  61.2 6.0 %collective-permute-start.13 = (f32[19]{0:T(128)S(1)}, f32[19]{0:T(128)S(1)}, u32[]{:S(2)}, u32[]{:S(2)}) collective-permute-start(f32[19]{0:T(128)S(1)} %add.128), channel_id=1, source_target_pairs={{0,6},{1,7},{2,4},{3,5},{4,2},{5,3},{6,0},{7,1},{8,14},{9,15},{10,... | collective-permute-start | bytes 236 | tf_op jit(solution)/shard_map/ppermute | solution.py:261
  (3 other events, 2.0 us)
